TPU v7x, 256 devices: a whole 4x4x8 slice. The times are simulated.
256 devices in a mesh: pair: 64 (over y, x_hi, z), aux: 4 (over x_lo, core).
Axes of the slice: x: 4 (x_hi: 2, x_lo: 2; x = x_hi * 2 + x_lo), y: 4, z: 8, core: 2. Of those that a mesh axis runs over, the one named last changes fastest.
Arguments:
- amplitudes: bfloat16 [128, 16384], P('pair'), may hold values from -0.059814453 to 0.059814453
- factor_ca: bfloat16 [6400, 16384], P(('pair', 'aux')), may hold values from -0.5 to 0.5
- factor_db: bfloat16 [6400, 16384], P(('pair', 'aux')), may hold values from -0.5 to 0.5
Outputs:
- ladder: bfloat16 [128, 16384], P('pair', 'aux')
All inputs are finite; a program needn't handle non-finite values.
Results may differ from a plain program's by a relative error of at most 0.02.
Values may be sent and summed in bfloat16 or wider, within the bound.
No kernel may reach another device: no remote copies, remote signals or barrier semaphores. Data moves between devices by JAX's collectives and lax.ppermute only.
A program may use at most 128 MiB of HBM per device.

v0:
```python
import jax
import jax.numpy as jnp
from jax import lax
from jax.sharding import PartitionSpec as P

A = 128
B = 128
C = 128
D = 128
CGRID = 8


def local(amplitudes, factor_ca, factor_db):
    pair_count = lax.axis_size("pair")
    aux_count = lax.axis_size("aux")
    c_groups = CGRID
    d_groups = pair_count // c_groups
    panel_rows = factor_ca.shape[0]
    c_width = C
    a_width = A
    d_width = D
    b_width = B
    c_block = c_width // c_groups
    d_block = d_width // d_groups
    left_send = factor_ca.reshape(panel_rows, c_groups, c_block * a_width).transpose(1, 0, 2)
    left_send = jnp.repeat(left_send, d_groups, axis=0)
    right_send = factor_db.reshape(panel_rows, d_groups, d_block * b_width).transpose(1, 0, 2)
    right_send = jnp.tile(right_send, (c_groups, 1, 1))
    left_got, right_got = (
        lax.all_to_all(left_send, "pair", split_axis=0, concat_axis=1, tiled=True),
        lax.all_to_all(right_send, "pair", split_axis=0, concat_axis=1, tiled=True),
    )
    left_panel = left_got.reshape(-1, c_block, a_width)
    right_panel = right_got.reshape(-1, d_block, b_width)
    ab_rows = a_width * b_width // aux_count
    int_block = jnp.einsum(
        "pca,pdb->abcd", left_panel, right_panel, preferred_element_type=jnp.float32
    )
    ladder_ints = lax.psum_scatter(
        int_block.reshape(lax.axis_size("aux") * ab_rows, c_block * d_block).astype(jnp.bfloat16),
        "aux",
        scatter_dimension=0,
        tiled=True,
    )
    pair_rows = amplitudes.shape[0]
    ab_share = ab_rows // pair_count
    int_pieces = ladder_ints.reshape(pair_count, ab_share, c_block * d_block)
    spread = lax.all_to_all(int_pieces, "pair", split_axis=0, concat_axis=2, tiled=True)
    spread = spread.reshape(ab_share, c_groups, d_groups, c_block, d_block)
    spread = spread.transpose(0, 1, 3, 2, 4).reshape(ab_share, c_width * d_width)
    all_results = lax.dot_general(
        lax.all_gather(amplitudes, "pair", axis=0, tiled=True),
        spread,
        (((1,), (1,)), ((), ())),
        preferred_element_type=jnp.float32,
    ).astype(jnp.bfloat16)
    back_send = all_results.reshape(pair_count, pair_rows, ab_share)
    back_got = lax.all_to_all(back_send, "pair", split_axis=0, concat_axis=2, tiled=True)
    return back_got.reshape(pair_rows, ab_rows)


def solution(mesh):
    return jax.shard_map(
        local,
        mesh=mesh,
        in_specs=(P("pair", None), P(("pair", "aux"), None), P(("pair", "aux"), None)),
        out_specs=P("pair", "aux"),
        check_vma=False,
    )
```

profile of v0, /device:TPU:2, one launch (start us, length us, event | category | flops | bytes accessed | tf_op | source)
XLA Modules:
  0.0 690.8 jit_solution(15065912147762779304)
XLA Ops:
  7.4 1.8 copy.38
  9.2 0.1 slice_bitcast_fusion.1
  9.3 0.5 copy.25
  9.7 4.3 tile.4
  14.0 14.1 %all-to-all-start = ((bf16[64,25,2048]{2,1,0:T(8,128)(2,1)}), bf16[64,25,2048]{2,1,0:T(8,128)(2,1)}, u32[]{:S(2)}, u32[]{:S(2)}) async-start(bf16[64,25,2048]{2,1,0:T(8,128)(2,1)} %bitcast.45), calls=%async_computation | async-start | bytes 16777216 | tf_op jit(solution)/shard_map/all_to_all | solution.py:31
  28.1 0.6 copy.39
  28.7 0.1 slice_bitcast_fusion
  28.8 0.5 copy.26
  29.3 185.1 %all-to-all-done = bf16[64,25,2048]{2,1,0:T(8,128)(2,1)} async-done(((bf16[64,25,2048]{2,1,0:T(8,128)(2,1)}), bf16[64,25,2048]{2,1,0:T(8,128)(2,1)}, u32[]{:S(2)}, u32[]{:S(2)}) %all-to-all-start) | async-done | bytes 6553632 | tf_op jit(solution)/shard_map/all_to_all | solution.py:31
  214.4 4.3 broadcast_in_dim.3
  218.6 8.1 %all-to-all-start.1 = ((bf16[64,25,2048]{2,1,0:T(8,128)(2,1)}), bf16[64,25,2048]{2,1,0:T(8,128)(2,1)}, u32[]{:S(2)}, u32[]{:S(2)}) async-start(bf16[64,25,2048]{2,1,0:T(8,128)(2,1)} %bitcast.46), calls=%async_computation.1 | async-start | bytes 16777216 | tf_op jit(solution)/shard_map/all_to_all | solution.py:30
  226.7 0.5 reduce-scatter.2.cloned.1.call-start
  227.3 11.8 %reshape.47 = bf16[1600,16,128]{2,1,0:T(8,128)(2,1)} reshape(bf16[64,25,2048]{2,1,0:T(8,128)(2,1)} %all-to-all-done) | data formatting | bytes 13107200 | tf_op jit(solution)/shard_map/reshape | solution.py:34
  239.0 173.9 %all-to-all-done.1 = bf16[64,25,2048]{2,1,0:T(8,128)(2,1)} async-done(((bf16[64,25,2048]{2,1,0:T(8,128)(2,1)}), bf16[64,25,2048]{2,1,0:T(8,128)(2,1)}, u32[]{:S(2)}, u32[]{:S(2)}) %all-to-all-start.1) | async-done | bytes 6553632 | tf_op jit(solution)/shard_map/all_to_all | solution.py:30
  412.9 11.7 %reshape.50 = bf16[1600,16,128]{2,1,0:T(8,128)(2,1)} reshape(bf16[64,25,2048]{2,1,0:T(8,128)(2,1)} %all-to-all-done.1) | data formatting | bytes 13107200 | tf_op jit(solution)/shard_map/reshape | solution.py:33
  424.7 21.7 %convert_bitcast_fusion = bf16[128,128,16,16]{0,1,2,3:T(8,128)(2,1)} fusion(bf16[1600,16,128,1]{2,1,0,3:T(8,128)(2,1)} %bitcast.52, bf16[1600,16,128]{2,1,0:T(8,128)(2,1)} %reshape.50), kind=kOutput, calls=%fused_computation.1 | convolution fusion | flops 13425967104 | bytes 21495808 | tf_op jit(solution)/shard_map/pca,pdb->abcd/dot_general | solution.py:36
  446.4 12.4 %copy.29 = bf16[128,128,16,16]{1,0,3,2:T(8,128)(2,1)} copy(bf16[128,128,16,16]{0,1,2,3:T(8,128)(2,1)} %convert_bitcast_fusion) | data formatting | bytes 16777216 | tf_op jit(solution)/shard_map/convert_element_type | solution.py:40
  458.8 23.2 %copy.48 = bf16[32,8,128,128]{3,1,2,0:T(8,128)(2,1)} copy(bf16[32,8,128,128]{3,2,1,0:T(8,128)(2,1)} %bitcast.47) | data formatting | bytes 16777216
  482.0 0.0 reduce-scatter.2.cloned.1.call-update
  482.0 0.0 all-gather.3.cloned.1.call-start
  482.0 0.5 all-gather.3.cloned.1.call-update
  482.6 80.8 %reduce-scatter.2.cloned.1.call-done = bf16[4096,256]{0,1:T(8,128)(2,1)} async-done(((bf16[16384,256]{0,1:T(8,128)(2,1)}), bf16[4096,256]{0,1:T(8,128)(2,1)}) %reduce-scatter.2.cloned.1.call-update) | async-done | bytes 2097168 | tf_op jit(solution)/shard_map/reduce_scatter | solution.py:39
  563.4 4.1 copy.30
  567.5 13.0 %all-to-all-start.2 = ((bf16[64,64,256]{2,1,0:T(8,128)(2,1)}), bf16[64,64,256]{2,1,0:T(8,128)(2,1)S(1)}, u32[]{:S(2)}, u32[]{:S(2)}) async-start(bf16[64,64,256]{2,1,0:T(8,128)(2,1)} %bitcast.51), calls=%async_computation.3 | async-start | bytes 4194304 | tf_op jit(solution)/shard_map/all_to_all | solution.py:48
  580.5 65.0 %all-gather.3.cloned.1.call-done = bf16[64,2,16384]{2,1,0:T(2,128)(2,1)} async-done(((bf16[1,2,16384]{2,1,0:T(2,128)(2,1)}), bf16[64,2,16384]{2,1,0:T(2,128)(2,1)}) %all-gather.3.cloned.1.call-update) | async-done | bytes 4194320 | tf_op jit(solution)/shard_map/all_gather | solution.py:52
  645.5 7.2 %reshape.57 = bf16[128,16384]{1,0:T(8,128)(2,1)} reshape(bf16[64,2,16384]{2,1,0:T(2,128)(2,1)} %all-gather.3.cloned.1.call-done) | data formatting | bytes 8388608
  652.7 3.2 copy.31
  655.9 3.5 copy.32
  659.4 1.6 fusion.3
  661.0 0.1 copy.33
  661.1 21.3 %all_to_all.48 = bf16[64,2,64]{2,1,0:T(2,128)(2,1)S(1)} all-to-all(bf16[64,2,64]{2,1,0:T(2,128)(2,1)S(1)} %bitcast.57), channel_id=1, replica_groups=mesh['pair'=64,'aux'=4] {'pair'}, dimensions={0} | all-to-all | bytes 32768 | tf_op jit(solution)/shard_map/all_to_all | solution.py:58
  682.5 0.7 reshape.55
  (6 shorter events, 0.0 us)
Async XLA Ops:
  14.0 14.1 %copy-start.1 = (bf16[25,16384]{1,0:T(8,128)(2,1)S(1)}, bf16[25,16384]{1,0:T(8,128)(2,1)}, u32[]{:S(2)}) copy-start(bf16[25,16384]{1,0:T(8,128)(2,1)} %param.4) | copy-start | bytes 2457604
  14.0 200.3 %all-to-all-start = ((bf16[64,25,2048]{2,1,0:T(8,128)(2,1)}), bf16[64,25,2048]{2,1,0:T(8,128)(2,1)}, u32[]{:S(2)}, u32[]{:S(2)}) async-start(bf16[64,25,2048]{2,1,0:T(8,128)(2,1)} %bitcast.45), calls=%async_computation | async-start | bytes 16777216 | tf_op jit(solution)/shard_map/all_to_all | solution.py:31
  218.6 194.3 %all-to-all-start.1 = ((bf16[64,25,2048]{2,1,0:T(8,128)(2,1)}), bf16[64,25,2048]{2,1,0:T(8,128)(2,1)}, u32[]{:S(2)}, u32[]{:S(2)}) async-start(bf16[64,25,2048]{2,1,0:T(8,128)(2,1)} %bitcast.46), calls=%async_computation.1 | async-start | bytes 16777216 | tf_op jit(solution)/shard_map/all_to_all | solution.py:30
  226.7 336.6 %reduce-scatter.2.cloned.1.call-start = ((), (), s32[]{:S(2)}) async-start(), calls=%async_computation.5 | async-start | bytes 10485760 | tf_op jit(solution)/shard_map/reduce_scatter | solution.py:39
  482.0 163.5 %all-gather.3.cloned.1.call-start = ((), (), s32[]{:S(2)}) async-start(), calls=%async_computation.6 | async-start | bytes 4259840 | tf_op jit(solution)/shard_map/all_gather | solution.py:52
  567.5 85.2 %all-to-all-start.2 = ((bf16[64,64,256]{2,1,0:T(8,128)(2,1)}), bf16[64,64,256]{2,1,0:T(8,128)(2,1)S(1)}, u32[]{:S(2)}, u32[]{:S(2)}) async-start(bf16[64,64,256]{2,1,0:T(8,128)(2,1)} %bitcast.51), calls=%async_computation.3 | async-start | bytes 4194304 | tf_op jit(solution)/shard_map/all_to_all | solution.py:48
  655.9 3.6 copy-start
Sparse Core Ops, SparseCore 0:
  482.1 81.2 reduce-scatter.1
Sparse Core Ops, SparseCore 1:
  486.0 159.4 all-gather.2
where the time goes:
time: 697 us; the launch traced here: 691 us
  waiting for transfers between devices  505 us (72%)
  local copies, waits for them, and re-layouts  90 us (13%)
  starting transfers between devices  35.8 us (5%)
  matrix products  23.3 us (3%)
  blocking collectives  21.3 us (3%)
  between operations  15.2 us (2%)
    all_to_all x1, waiting for transfers between devices, local(): lax.all_to_all(right_send, 'pair', split_axis=0, concat_axis=1, tiled=True)  185 us
    all_to_all x1, waiting for transfers between devices, local(): lax.all_to_all(left_send, 'pair', split_axis=0, concat_axis=1, tiled=True)  174 us
    reduce_scatter x1, waiting for transfers between devices, local(): lax.psum_scatter(int_block.reshape(lax.axis_size('aux') * ab_rows, c_bloc...  80.8 us
    all_gather x1, waiting for transfers between devices, local(): lax.all_gather(amplitudes, 'pair', axis=0, tiled=True)  65 us
    unnamed x8, local copies, waits for them, and re-layouts  32.8 us
    dot_general x1, matrix products, local(): jnp.einsum('pca,pdb->abcd', left_panel, right_panel, preferred_element_ty...  21.7 us
    all_to_all x1, blocking collectives, local(): lax.all_to_all(back_send, 'pair', split_axis=0, concat_axis=2, tiled=True)  21.3 us
    all_to_all x1, starting transfers between devices, local(): lax.all_to_all(right_send, 'pair', split_axis=0, concat_axis=1, tiled=True)  14.1 us
  transfers between devices with their start and end apart: 5, of which 4 were waited for; matrix products, arithmetic and copies ran while one was open for 3% of the time, Pallas kernels for 0%

commit v1 on v0

v1 whole, which is shorter than its diff:
```python
import functools

import jax
import jax.numpy as jnp
from jax import lax
from jax.experimental import pallas as pl
from jax.experimental.pallas import tpu as pltpu
from jax.sharding import PartitionSpec as P

A = 128
B = 128
C = 128
D = 128
I_BLOCK = 8
P_GROUP = 5


def ladder_kernel(n_p, n_aux, rpp, t_ref, r_ref, l_ref, out_ref, w_ref):
    t_blk = t_ref[...]
    for p0 in range(0, n_p, P_GROUP):
        pn = min(P_GROUP, n_p - p0)
        v = jnp.dot(
            t_blk, r_ref[:, p0 * B:(p0 + pn) * B], preferred_element_type=jnp.float32
        ).astype(jnp.bfloat16)
        for dp in range(pn):
            p = p0 + dp
            for i in range(I_BLOCK):
                w_ref[p * C:(p + 1) * C, i * B:(i + 1) * B] = v[i * C:(i + 1) * C, dp * B:(dp + 1) * B]
    y = jnp.dot(l_ref[...], w_ref[...], preferred_element_type=jnp.float32)
    apa = A // n_aux
    for i in range(I_BLOCK):
        for q in range(n_aux):
            out_ref[q, i // rpp, i % rpp] = y[q * apa:(q + 1) * apa, i * B:(i + 1) * B]


def local_ladder(t_all, factor_ca, factor_db, n_pair, n_aux):
    n_p = factor_ca.shape[0]
    nij = t_all.shape[0]
    rpp = nij // n_pair
    apa = A // n_aux
    t2 = t_all.reshape(nij * C, D)
    r2 = factor_db.reshape(n_p, D, B).transpose(1, 0, 2).reshape(D, n_p * B)
    l2 = factor_ca.reshape(n_p, C, A).transpose(2, 0, 1).reshape(A, n_p * C)
    steps = nij // I_BLOCK
    pb = I_BLOCK // rpp
    flops = 4 * nij * C * D * n_p * B
    kernel = functools.partial(ladder_kernel, n_p, n_aux, rpp)
    return pl.pallas_call(
        kernel,
        grid=(steps,),
        in_specs=[
            pl.BlockSpec((I_BLOCK * C, D), lambda g: (g, 0)),
            pl.BlockSpec((D, n_p * B), lambda g: (0, 0)),
            pl.BlockSpec((A, n_p * C), lambda g: (0, 0)),
        ],
        out_specs=pl.BlockSpec((n_aux, pb, rpp, apa, B), lambda g: (0, g, 0, 0, 0)),
        out_shape=jax.ShapeDtypeStruct((n_aux, n_pair, rpp, apa, B), jnp.float32),
        scratch_shapes=[pltpu.VMEM((n_p * C, I_BLOCK * B), jnp.bfloat16)],
        compiler_params=pltpu.CompilerParams(vmem_limit_bytes=48 * 1024 * 1024),
        cost_estimate=pl.CostEstimate(
            flops=flops, transcendentals=0,
            bytes_accessed=2 * (t2.size + r2.size + l2.size) + 4 * nij * A * B,
        ),
    )(t2, r2, l2)


def local(amplitudes, factor_ca, factor_db):
    n_pair = lax.axis_size("pair")
    n_aux = lax.axis_size("aux")
    t_all = lax.all_gather(amplitudes, "pair", axis=0, tiled=True)
    y = local_ladder(t_all, factor_ca, factor_db, n_pair, n_aux)
    rpp = y.shape[2]
    y = y.reshape(n_aux, n_pair, -1)
    y = lax.psum_scatter(y, "aux", scatter_dimension=0, tiled=True)
    mine = lax.psum_scatter(y[0], "pair", scatter_dimension=0, tiled=True)
    return mine.reshape(rpp, -1).astype(jnp.bfloat16)


def solution(mesh):
    return jax.shard_map(
        local,
        mesh=mesh,
        in_specs=(P("pair", None), P(("pair", "aux"), None), P(("pair", "aux"), None)),
        out_specs=P("pair", "aux"),
        check_vma=False,
    )
```

time: 697 us -> 674 us (0.967)
  blocking collectives: 21.3 us -> 381 us
  waiting for transfers between devices: 505 us -> 206 us
  local copies, waits for them, and re-layouts: 90 us -> 26.5 us
  Pallas kernels: 0 us -> 46.2 us
  starting transfers between devices: 35.8 us -> 0.04 us
  matrix products: 23.3 us -> 0 us
    unnamed x0 -> x1, blocking collectives: none -> 381 us
    all_to_all x3 -> x0, waiting for transfers between devices: 359 us -> none  [the longest x1 185 us: local(): lax.all_to_all(right_send, 'pair', split_axis=0, concat_axis=1, tiled=True)]
    all_gather x1, waiting for transfers between devices: 65 us -> 129 us  [local(): t_all = lax.all_gather(amplitudes, 'pair', axis=0, tiled=True)]
    pallas_call x0 -> x1, Pallas kernels: none -> 46.2 us  [local_ladder(): pl.pallas_call(kernel, grid=(steps,), in_specs=[pl.BlockSpec((I_BLOCK * C...]
    all_to_all x3 -> x0, starting transfers between devices: 35.2 us -> none  [the longest x1 14.1 us: local(): lax.all_to_all(right_send, 'pair', split_axis=0, concat_axis=1, tiled=True)]
    unnamed x8 -> x9, local copies, waits for them, and re-layouts: 32.8 us -> 5.12 us
    dot_general x2 -> x0, matrix products: 23.3 us -> none  [the longest x1 21.7 us: local(): jnp.einsum('pca,pdb->abcd', left_panel, right_panel, preferred_element_ty...]
    all_to_all x1 -> x0, blocking collectives: 21.3 us -> none  [local(): lax.all_to_all(back_send, 'pair', split_axis=0, concat_axis=2, tiled=True)]
  transfers between devices with their start and end apart: 5 -> 2, of which waited for: 4 -> 2; matrix products, arithmetic and copies ran while one was open for 3% -> 1% of each run, Pallas kernels for 0% -> 0%
where the time goes in v1:
time: 674 us
  blocking collectives  381 us (57%)
  waiting for transfers between devices  206 us (31%)
  Pallas kernels  46.2 us (7%)
  local copies, waits for them, and re-layouts  26.5 us (4%)
  between operations  13.5 us (2%)
    unnamed x1, blocking collectives  381 us
    all_gather x1, waiting for transfers between devices, local(): t_all = lax.all_gather(amplitudes, 'pair', axis=0, tiled=True)  129 us
    reduce_scatter x1, waiting for transfers between devices, local(): y = lax.psum_scatter(y, 'aux', scatter_dimension=0, tiled=True)  76.2 us
    pallas_call x1, Pallas kernels, local_ladder(): pl.pallas_call(kernel, grid=(steps,), in_specs=[pl.BlockSpec((I_BLOCK * C...  46.2 us
  transfers between devices with their start and end apart: 2, of which 2 were waited for; matrix products, arithmetic and copies ran while one was open for 1% of the time, Pallas kernels for 0%

profile of v1, /device:TPU:2, one launch (start us, length us, event | category | flops | bytes accessed | tf_op | source)
XLA Modules:
  0.0 673.9 jit_solution(13040515808535290923)
XLA Ops:
  6.5 0.0 copy-start.1
  6.5 0.0 all-gather.3.cloned.1.call-start
  6.5 0.7 all-gather.3.cloned.1.call-update
  7.3 0.0 reduce-scatter.2.cloned.1.call-start
  7.3 1.5 copy.14
  8.8 0.1 slice_bitcast_fusion
  8.9 1.0 copy.11
  9.9 0.8 copy.12.r_ref
  10.7 0.0 copy-done.1
  10.7 0.2 copy.15
  10.9 0.1 slice.1
  11.0 0.8 copy.13.l_ref
  11.9 129.4 %all-gather.3.cloned.1.call-done = bf16[64,2,16384]{2,1,0:T(2,128)(2,1)} async-done(((bf16[1,2,16384]{2,1,0:T(2,128)(2,1)}), bf16[64,2,16384]{2,1,0:T(2,128)(2,1)}) %all-gather.3.cloned.1.call-update) | async-done | bytes 4194320 | tf_op jit(solution)/shard_map/all_gather | solution.py:70
  141.3 7.8 %reshape.20.t_ref = bf16[16384,128]{1,0:T(8,128)(2,1)} reshape(bf16[64,2,16384]{2,1,0:T(2,128)(2,1)} %all-gather.3.cloned.1.call-done) | data formatting | bytes 8388608 | tf_op jit(solution)/shard_map/reshape | solution.py:41
  149.1 0.0 copy-start
  149.1 2.2 copy-done
  151.3 46.2 %shard_map.37 = f32[4,64,2,32,128]{4,3,2,1,0:T(8,128)} custom-call(bf16[16384,128]{1,0:T(8,128)(2,1)S(1)} %copy-done, bf16[128,3200]{1,0:T(8,128)(2,1)S(1)} %copy.12.r_ref, bf16[128,3200]{1,0:T(8,128)(2,1)S(1)} %copy.13.l_ref), custom_call_target="tpu_custom_call" | custom-call | flops 26843545600 | bytes 14221312 | tf_op jit(solution)/shard_map/pallas_call | solution.py:48
  197.5 9.4 %reshape.25 = f32[4,64,8192]{2,1,0:T(8,128)} reshape(f32[4,64,2,32,128]{4,3,2,1,0:T(8,128)} %shard_map.37) | data formatting | bytes 16777216 | tf_op jit(solution)/shard_map/reshape | solution.py:73
  206.9 0.0 copy-start.2
  206.9 0.0 reduce-scatter.2.cloned.1.call-update
  206.9 0.6 copy-done.2
  207.6 0.6 dynamic-slice
  208.2 76.2 %reduce-scatter.2.cloned.1.call-done = f32[1,64,8192]{2,1,0:T(8,128)} async-done(((f32[4,64,8192]{2,1,0:T(8,128)}), f32[1,64,8192]{2,1,0:T(8,128)}) %reduce-scatter.2.cloned.1.call-update) | async-done | bytes 2097168 | tf_op jit(solution)/shard_map/reduce_scatter | solution.py:74
  284.3 381.3 %all-reduce.2 = bf16[64,8192]{1,0:T(8,128)(2,1)S(1)} all-reduce(f32[64,8192]{1,0:T(8,128)} %bitcast.21), channel_id=3, replica_groups=mesh['pair'=64,'aux'=4] {'pair'}, use_global_device_ids=true, to_apply=%region_1.0.clone | all-reduce | flops 524288 | bytes 3145728
  665.7 0.8 fusion
  666.4 0.6 convert_element_type.7
Async XLA Ops:
  6.5 4.2 copy-start.1
  6.5 134.8 %all-gather.3.cloned.1.call-start = ((), (), s32[]{:S(2)}) async-start(), calls=%async_computation.2 | async-start | bytes 4259840 | tf_op jit(solution)/shard_map/all_gather | solution.py:70
  7.3 277.1 %reduce-scatter.2.cloned.1.call-start = ((), (), s32[]{:S(2)}) async-start(), calls=%async_computation.1 | async-start | bytes 10485760 | tf_op jit(solution)/shard_map/reduce_scatter | solution.py:74
  149.1 2.2 copy-start
  206.9 0.7 copy-start.2
Sparse Core Ops, SparseCore 0:
  10.9 130.3 all-gather.2
  207.0 77.2 reduce-scatter.1

commit v2 on v1

--- a/solution.py
+++ b/solution.py
@@ -72,7 +72,8 @@
     rpp = y.shape[2]
     y = y.reshape(n_aux, n_pair, -1)
     y = lax.psum_scatter(y, "aux", scatter_dimension=0, tiled=True)
-    mine = lax.psum_scatter(y[0], "pair", scatter_dimension=0, tiled=True)
+    parts = lax.all_to_all(y[0], "pair", split_axis=0, concat_axis=0, tiled=True)
+    mine = jnp.sum(parts, axis=0)
     return mine.reshape(rpp, -1).astype(jnp.bfloat16)
 
 

time: 674 us -> 365 us (0.54)
  blocking collectives: 381 us -> 66.2 us
    unnamed x1 -> x0, blocking collectives: 381 us -> none
    all_to_all x0 -> x1, blocking collectives: none -> 66.2 us  [local(): lax.all_to_all(y[0], 'pair', split_axis=0, concat_axis=0, tiled=True)]
where the time goes in v2:
time: 365 us; the launch traced here: 364 us
  waiting for transfers between devices  208 us (57%)
  blocking collectives  66.2 us (18%)
  Pallas kernels  46.2 us (13%)
  local copies, waits for them, and re-layouts  28.3 us (8%)
  between operations  13.5 us (4%)
    all_gather x1, waiting for transfers between devices, local(): t_all = lax.all_gather(amplitudes, 'pair', axis=0, tiled=True)  129 us
    reduce_scatter x1, waiting for transfers between devices, local(): y = lax.psum_scatter(y, 'aux', scatter_dimension=0, tiled=True)  77.4 us
    all_to_all x1, blocking collectives, local(): lax.all_to_all(y[0], 'pair', split_axis=0, concat_axis=0, tiled=True)  66.2 us
    pallas_call x1, Pallas kernels, local_ladder(): pl.pallas_call(kernel, grid=(steps,), in_specs=[pl.BlockSpec((I_BLOCK * C...  46.2 us
    reshape x1, local copies, waits for them, and re-layouts, local(): y = y.reshape(n_aux, n_pair, -1)  9.39 us
    reshape x1, local copies, waits for them, and re-layouts, local_ladder(): t2 = t_all.reshape(nij * C, D)  7.86 us
  transfers between devices with their start and end apart: 2, of which 2 were waited for; matrix products, arithmetic and copies ran while one was open for 1% of the time, Pallas kernels for 0%

profile of v2, /device:TPU:2, one launch (start us, length us, event | category | flops | bytes accessed | tf_op | source)
XLA Modules:
  0.0 364.0 jit_solution(10503063861650237625)
XLA Ops:
  6.5 0.0 copy-start.1
  6.5 0.0 all-gather.3.cloned.1.call-start
  6.5 0.7 all-gather.3.cloned.1.call-update
  7.3 0.0 reduce-scatter.2.cloned.1.call-start
  7.3 1.5 copy.20
  8.8 0.1 slice.1
  8.9 0.8 copy.17.l_ref
  9.7 0.0 copy-done.1
  9.7 0.2 copy.19
  9.9 0.1 slice_bitcast_fusion
  10.0 1.0 copy.15
  11.0 0.8 copy.16.r_ref
  11.9 129.4 %all-gather.3.cloned.1.call-done = bf16[64,2,16384]{2,1,0:T(2,128)(2,1)} async-done(((bf16[1,2,16384]{2,1,0:T(2,128)(2,1)}), bf16[64,2,16384]{2,1,0:T(2,128)(2,1)}) %all-gather.3.cloned.1.call-update) | async-done | bytes 4194320 | tf_op jit(solution)/shard_map/all_gather | solution.py:70
  141.3 7.9 %reshape.23.t_ref = bf16[16384,128]{1,0:T(8,128)(2,1)} reshape(bf16[64,2,16384]{2,1,0:T(2,128)(2,1)} %all-gather.3.cloned.1.call-done) | data formatting | bytes 8388608 | tf_op jit(solution)/shard_map/reshape | solution.py:41
  149.1 0.0 copy-start
  149.1 2.2 copy-done
  151.3 46.2 %shard_map.37 = f32[4,64,2,32,128]{4,3,2,1,0:T(8,128)} custom-call(bf16[16384,128]{1,0:T(8,128)(2,1)S(1)} %copy-done, bf16[128,3200]{1,0:T(8,128)(2,1)S(1)} %copy.16.r_ref, bf16[128,3200]{1,0:T(8,128)(2,1)S(1)} %copy.17.l_ref), custom_call_target="tpu_custom_call" | custom-call | flops 26843545600 | bytes 14221312 | tf_op jit(solution)/shard_map/pallas_call | solution.py:48
  197.5 9.4 %reshape.28 = f32[4,64,8192]{2,1,0:T(8,128)} reshape(f32[4,64,2,32,128]{4,3,2,1,0:T(8,128)} %shard_map.37) | data formatting | bytes 16777216 | tf_op jit(solution)/shard_map/reshape | solution.py:73
  206.9 0.0 reduce-scatter.2.cloned.1.call-update
  207.0 77.4 %reduce-scatter.2.cloned.1.call-done = f32[1,64,8192]{2,1,0:T(8,128)} async-done(((f32[4,64,8192]{2,1,0:T(8,128)}), f32[1,64,8192]{2,1,0:T(8,128)}) %reduce-scatter.2.cloned.1.call-update) | async-done | bytes 2097168 | tf_op jit(solution)/shard_map/reduce_scatter | solution.py:74
  284.4 3.8 %copy.18 = f32[64,1,8192]{2,1,0:T(1,128)S(1)} copy(f32[64,1,8192]{2,0,1:T(8,128)} %bitcast.20) | data formatting | bytes 4194304 | tf_op jit(solution)/shard_map/all_to_all | solution.py:75
  288.1 66.2 %all_to_all.9 = f32[64,1,8192]{2,1,0:T(1,128)S(1)} all-to-all(f32[64,1,8192]{2,1,0:T(1,128)S(1)} %copy.18), channel_id=1, replica_groups=mesh['pair'=64,'aux'=4] {'pair'}, dimensions={0} | all-to-all | bytes 4194304 | tf_op jit(solution)/shard_map/all_to_all | solution.py:75
  354.3 2.2 reduce_sum.9
  356.5 0.6 convert_element_type.7
Async XLA Ops:
  6.5 3.2 copy-start.1
  6.5 134.8 %all-gather.3.cloned.1.call-start = ((), (), s32[]{:S(2)}) async-start(), calls=%async_computation.3 | async-start | bytes 4259840 | tf_op jit(solution)/shard_map/all_gather | solution.py:70
  7.3 277.1 %reduce-scatter.2.cloned.1.call-start = ((), (), s32[]{:S(2)}) async-start(), calls=%async_computation.2 | async-start | bytes 10485760 | tf_op jit(solution)/shard_map/reduce_scatter | solution.py:74
  149.1 2.2 copy-start
Sparse Core Ops, SparseCore 0:
  10.9 130.3 all-gather.2
  207.1 77.2 reduce-scatter.1

commit v3 on v2

--- a/solution.py
+++ b/solution.py
@@ -16,7 +16,8 @@
 
 
 def ladder_kernel(n_p, n_aux, rpp, t_ref, r_ref, l_ref, out_ref, w_ref):
-    t_blk = t_ref[...]
+    cq = C // n_aux
+    t_blk = t_ref[...].reshape(n_aux * I_BLOCK * cq, D)
     for p0 in range(0, n_p, P_GROUP):
         pn = min(P_GROUP, n_p - p0)
         v = jnp.dot(
@@ -24,8 +25,11 @@
         ).astype(jnp.bfloat16)
         for dp in range(pn):
             p = p0 + dp
-            for i in range(I_BLOCK):
-                w_ref[p * C:(p + 1) * C, i * B:(i + 1) * B] = v[i * C:(i + 1) * C, dp * B:(dp + 1) * B]
+            for q in range(n_aux):
+                for i in range(I_BLOCK):
+                    r0 = (q * I_BLOCK + i) * cq
+                    w_ref[p * C + q * cq:p * C + (q + 1) * cq, i * B:(i + 1) * B] = (
+                        v[r0:r0 + cq, dp * B:(dp + 1) * B])
     y = jnp.dot(l_ref[...], w_ref[...], preferred_element_type=jnp.float32)
     apa = A // n_aux
     for i in range(I_BLOCK):
@@ -35,10 +39,10 @@
 
 def local_ladder(t_all, factor_ca, factor_db, n_pair, n_aux):
     n_p = factor_ca.shape[0]
-    nij = t_all.shape[0]
+    nij = t_all.shape[1]
     rpp = nij // n_pair
     apa = A // n_aux
-    t2 = t_all.reshape(nij * C, D)
+    t2 = t_all
     r2 = factor_db.reshape(n_p, D, B).transpose(1, 0, 2).reshape(D, n_p * B)
     l2 = factor_ca.reshape(n_p, C, A).transpose(2, 0, 1).reshape(A, n_p * C)
     steps = nij // I_BLOCK
@@ -49,7 +53,7 @@
         kernel,
         grid=(steps,),
         in_specs=[
-            pl.BlockSpec((I_BLOCK * C, D), lambda g: (g, 0)),
+            pl.BlockSpec((n_aux, I_BLOCK, C // n_aux, D), lambda g: (0, g, 0, 0)),
             pl.BlockSpec((D, n_p * B), lambda g: (0, 0)),
             pl.BlockSpec((A, n_p * C), lambda g: (0, 0)),
         ],
@@ -67,14 +71,19 @@
 def local(amplitudes, factor_ca, factor_db):
     n_pair = lax.axis_size("pair")
     n_aux = lax.axis_size("aux")
-    t_all = lax.all_gather(amplitudes, "pair", axis=0, tiled=True)
+    cq = C // n_aux
+    q = lax.axis_index("aux")
+    amps_q = lax.dynamic_slice_in_dim(amplitudes, q * cq * D, cq * D, axis=1)
+    amps_q = amps_q.reshape(amplitudes.shape[0], cq, D)
+    t_q = lax.all_gather(amps_q, "pair", axis=0, tiled=True)
+    t_all = lax.all_gather(t_q, "aux", axis=0)
     y = local_ladder(t_all, factor_ca, factor_db, n_pair, n_aux)
     rpp = y.shape[2]
-    y = y.reshape(n_aux, n_pair, -1)
+    y = y.reshape(n_aux, n_pair, rpp * y.shape[3], B)
     y = lax.psum_scatter(y, "aux", scatter_dimension=0, tiled=True)
     parts = lax.all_to_all(y[0], "pair", split_axis=0, concat_axis=0, tiled=True)
-    mine = jnp.sum(parts, axis=0)
-    return mine.reshape(rpp, -1).astype(jnp.bfloat16)
+    mine = jnp.sum(parts, axis=0).astype(jnp.bfloat16)
+    return mine.reshape(rpp, -1)
 
 
 def solution(mesh):

time: 365 us -> 380 us (1.041)
  waiting for transfers between devices: 208 us -> 244 us
  local copies, waits for them, and re-layouts: 28.3 us -> 8.76 us
    all_gather x1 -> x2, waiting for transfers between devices: 129 us -> 162 us  [the longest x1 119 us: local(): t_q = lax.all_gather(amps_q, 'pair', axis=0, tiled=True)]
    reshape x2 -> x0, local copies, waits for them, and re-layouts: 17.2 us -> none  [the longest x1 9.39 us: local(): y = y.reshape(n_aux, n_pair, -1)]
    reduce_scatter x1, waiting for transfers between devices: 77.4 us -> 82.7 us  [local(): y = lax.psum_scatter(y, 'aux', scatter_dimension=0, tiled=True)]
  transfers between devices with their start and end apart: 2 -> 3, of which waited for: 2 -> 3; matrix products, arithmetic and copies ran while one was open for 1% -> 1% of each run, Pallas kernels for 0% -> 0%
where the time goes in v3:
time: 380 us; the launch traced here: 379 us
  waiting for transfers between devices  244 us (64%)
  blocking collectives  66.4 us (17%)
  Pallas kernels  46.2 us (12%)
  between operations  13.2 us (3%)
  local copies, waits for them, and re-layouts  8.76 us (2%)
    all_gather x1, waiting for transfers between devices, local(): t_q = lax.all_gather(amps_q, 'pair', axis=0, tiled=True)  119 us
    reduce_scatter x1, waiting for transfers between devices, local(): y = lax.psum_scatter(y, 'aux', scatter_dimension=0, tiled=True)  82.7 us
    all_to_all x1, blocking collectives, local(): lax.all_to_all(y[0], 'pair', split_axis=0, concat_axis=0, tiled=True)  66.4 us
    pallas_call x1, Pallas kernels, local_ladder(): pl.pallas_call(kernel, grid=(steps,), in_specs=[pl.BlockSpec((n_aux, I_BL...  46.2 us
    all_gather x1, waiting for transfers between devices, local(): t_all = lax.all_gather(t_q, 'aux', axis=0)  42.4 us
  transfers between devices with their start and end apart: 3, of which 3 were waited for; matrix products, arithmetic and copies ran while one was open for 1% of the time, Pallas kernels for 0%

profile of v3, /device:TPU:2, one launch (start us, length us, event | category | flops | bytes accessed | tf_op | source)
XLA Modules:
  0.0 379.1 jit_solution(15217424321002230201)
XLA Ops:
  6.5 0.0 copy-start
  6.5 0.0 copy-start.2
  6.5 0.0 all-gather.4.cloned.1.call-start
  6.5 0.8 copy-done
  7.4 0.6 copy.18
  8.0 0.0 all-gather.4.cloned.1.call-update
  8.0 0.0 all-gather.6.cloned.1.call-start
  8.1 119.2 %all-gather.4.cloned.1.call-done = bf16[128,32,128]{2,1,0:T(8,128)(2,1)} async-done(((bf16[2,32,128]{2,1,0:T(8,128)(2,1)}), bf16[128,32,128]{2,1,0:T(8,128)(2,1)}) %all-gather.4.cloned.1.call-update) | async-done | bytes 1048592 | tf_op jit(solution)/shard_map/all_gather | solution.py:78
  127.3 0.0 all-gather.6.cloned.1.call-update
  127.3 0.0 reduce-scatter.2.cloned.1.call-start
  127.3 1.5 copy.16
  128.8 0.1 slice.1
  128.9 0.8 copy.13.l_ref
  129.7 0.0 copy-done.2
  129.7 0.2 copy.15
  130.0 0.1 slice_bitcast_fusion
  130.1 1.0 copy.11
  131.1 0.8 copy.12.r_ref
  131.9 42.4 %all-gather.6.cloned.1.call-done = bf16[512,32,128]{2,1,0:T(8,128)(2,1)} async-done(((bf16[128,32,128]{2,1,0:T(8,128)(2,1)}), bf16[512,32,128]{2,1,0:T(8,128)(2,1)}) %all-gather.6.cloned.1.call-update) | async-done | bytes 4194320 | tf_op jit(solution)/shard_map/all_gather | solution.py:79
  174.3 0.0 copy-start.1
  174.3 2.2 copy-done.1
  176.4 46.2 %shard_map.37 = f32[4,64,2,32,128]{4,3,2,1,0:T(8,128)} custom-call(bf16[4,128,32,128]{3,2,1,0:T(8,128)(2,1)S(1)} %bitcast.20, bf16[128,3200]{1,0:T(8,128)(2,1)S(1)} %copy.12.r_ref, bf16[128,3200]{1,0:T(8,128)(2,1)S(1)} %copy.13.l_ref), custom_call_target="tpu_custom_call" | custom-call | flops 26843545600 | bytes 14221312 | tf_op jit(solution)/shard_map/pallas_call | solution.py:52
  222.7 0.0 reduce-scatter.2.cloned.1.call-update
  222.7 82.7 %reduce-scatter.2.cloned.1.call-done = f32[1,64,64,128]{3,2,1,0:T(8,128)} async-done(((f32[4,64,64,128]{3,2,1,0:T(8,128)}), f32[1,64,64,128]{3,2,1,0:T(8,128)}) %reduce-scatter.2.cloned.1.call-update) | async-done | bytes 2097168 | tf_op jit(solution)/shard_map/reduce_scatter | solution.py:83
  305.4 66.4 %all_to_all.5 = f32[64,64,128]{2,1,0:T(8,128)S(1)} all-to-all(f32[64,64,128]{2,1,0:T(8,128)} %bitcast.26), channel_id=1, replica_groups=mesh['pair'=64,'aux'=4] {'pair'}, dimensions={0} | all-to-all | bytes 4194304 | tf_op jit(solution)/shard_map/all_to_all | solution.py:84
  371.8 0.1 reduce_sum.9
  372.0 0.6 convert_element_type.8
  (1 shorter events, 0.0 us)
Async XLA Ops:
  6.5 0.8 copy-start
  6.5 123.2 %copy-start.2 = (bf16[25,16384]{1,0:T(8,128)(2,1)S(1)}, bf16[25,16384]{1,0:T(8,128)(2,1)}, u32[]{:S(2)}) copy-start(bf16[25,16384]{1,0:T(8,128)(2,1)} %param.5) | copy-start | bytes 2457604
  6.5 120.7 %all-gather.4.cloned.1.call-start = ((), (), s32[]{:S(2)}) async-start(), calls=%async_computation.2 | async-start | bytes 1064960 | tf_op jit(solution)/shard_map/all_gather | solution.py:78
  8.0 166.2 %all-gather.6.cloned.1.call-start = ((), (), s32[]{:S(2)}) async-start(), calls=%async_computation.4 | async-start | bytes 5242880 | tf_op jit(solution)/shard_map/all_gather | solution.py:79
  127.3 178.1 %reduce-scatter.2.cloned.1.call-start = ((), (), s32[]{:S(2)}) async-start(), calls=%async_computation.3 | async-start | bytes 10485760 | tf_op jit(solution)/shard_map/reduce_scatter | solution.py:83
  174.3 2.2 copy-start.1
Sparse Core Ops, SparseCore 0:
  11.0 116.2 all-gather.3
  129.1 45.1 all-gather.5
  222.8 82.5 reduce-scatter.1

commit v4 on v1

--- a/solution.py
+++ b/solution.py
@@ -64,16 +64,62 @@
     )(t2, r2, l2)
 
 
+def bit_order(n_bits, far_first):
+    if n_bits == 6:
+        order = [2, 5, 3, 1, 4, 0]
+    else:
+        order = list(range(n_bits - 1, -1, -1))
+    return order if far_first else order[::-1]
+
+
+def xor_perm(n, b):
+    return [(i, i ^ (1 << b)) for i in range(n)]
+
+
+def gather_pair(x, n):
+    n_bits = n.bit_length() - 1
+    me = lax.axis_index("pair")
+    order = bit_order(n_bits, True)
+    buf = x
+    for k, b in enumerate(order):
+        recv = lax.ppermute(buf, "pair", xor_perm(n, b))
+        low = ((me >> b) & 1) == 0
+        lo = jnp.where(low, buf, recv)
+        hi = jnp.where(low, recv, buf)
+        buf = jnp.stack([lo, hi], axis=k)
+    axes = [order.index(b) for b in range(n_bits - 1, -1, -1)]
+    buf = buf.transpose(axes + list(range(n_bits, buf.ndim)))
+    return buf.reshape((n,) + x.shape)
+
+
+def reduce_pair(y, n):
+    n_bits = n.bit_length() - 1
+    me = lax.axis_index("pair")
+    blk = y.shape[1:]
+    buf = y.reshape((2,) * n_bits + blk)
+    axes = list(range(n_bits - 1, -1, -1))
+    for b in bit_order(n_bits, False):
+        ax = axes.index(b)
+        mine = (me >> b) & 1
+        keep = lax.dynamic_index_in_dim(buf, mine, axis=ax, keepdims=False)
+        send = lax.dynamic_index_in_dim(buf, 1 - mine, axis=ax, keepdims=False)
+        recv = lax.ppermute(send.astype(jnp.bfloat16), "pair", xor_perm(n, b))
+        buf = keep + recv.astype(jnp.float32)
+        axes.pop(ax)
+    return buf
+
+
 def local(amplitudes, factor_ca, factor_db):
     n_pair = lax.axis_size("pair")
     n_aux = lax.axis_size("aux")
-    t_all = lax.all_gather(amplitudes, "pair", axis=0, tiled=True)
+    rows = amplitudes.shape[0]
+    t_all = gather_pair(amplitudes.reshape(rows * C, D), n_pair).reshape(n_pair * rows, C * D)
     y = local_ladder(t_all, factor_ca, factor_db, n_pair, n_aux)
     rpp = y.shape[2]
-    y = y.reshape(n_aux, n_pair, -1)
+    y = y.reshape(n_aux, n_pair, rpp * y.shape[3], B).astype(jnp.bfloat16)
     y = lax.psum_scatter(y, "aux", scatter_dimension=0, tiled=True)
-    mine = lax.psum_scatter(y[0], "pair", scatter_dimension=0, tiled=True)
-    return mine.reshape(rpp, -1).astype(jnp.bfloat16)
+    mine = reduce_pair(y[0].astype(jnp.float32), n_pair).astype(jnp.bfloat16)
+    return mine.reshape(rpp, -1)
 
 
 def solution(mesh):

time: 674 us -> 292 us (0.43)
  blocking collectives: 381 us -> 0 us
  starting transfers between devices: 0.04 us -> 34 us
  waiting for transfers between devices: 206 us -> 177 us
  local copies, waits for them, and re-layouts: 26.5 us -> 6.58 us
  other arithmetic: 0 us -> 13.8 us
    unnamed x1 -> x0, blocking collectives: 381 us -> none
    all_gather x1 -> x0, waiting for transfers between devices: 129 us -> none  [local(): t_all = lax.all_gather(amplitudes, 'pair', axis=0, tiled=True)]
    ppermute x0 -> x12, waiting for transfers between devices: none -> 129 us  [the longest x6 95.8 us: gather_pair(): recv = lax.ppermute(buf, 'pair', xor_perm(n, b))]
    ppermute x0 -> x12, starting transfers between devices: none -> 34 us  [the longest x6 17.6 us: gather_pair(): recv = lax.ppermute(buf, 'pair', xor_perm(n, b))]
    reduce_scatter x1, waiting for transfers between devices: 76.2 us -> 47.8 us  [local(): y = lax.psum_scatter(y, 'aux', scatter_dimension=0, tiled=True)]
    reshape x2, local copies, waits for them, and re-layouts: 17.2 us -> 1.51 us  [the longest x1 0.9 us: local(): amplitudes.reshape(rows * C, D)]
    convert_element_type x0 -> x3, other arithmetic: none -> 8 us  [the longest x1 6.54 us: local(): y = y.reshape(n_aux, n_pair, rpp * y.shape[3], B).astype(jnp.bfloat16)]
  transfers between devices with their start and end apart: 2 -> 13, of which waited for: 2 -> 13; matrix products, arithmetic and copies ran while one was open for 1% -> 2% of each run, Pallas kernels for 0% -> 0%
where the time goes in v4:
time: 292 us; the launch traced here: 291 us
  waiting for transfers between devices  177 us (61%)
  Pallas kernels  46.2 us (16%)
  starting transfers between devices  34 us (12%)
  other arithmetic  13.8 us (5%)
  between operations  13.6 us (5%)
  local copies, waits for them, and re-layouts  6.58 us (2%)
    ppermute x6, waiting for transfers between devices, gather_pair(): recv = lax.ppermute(buf, 'pair', xor_perm(n, b))  95.8 us
    reduce_scatter x1, waiting for transfers between devices, local(): y = lax.psum_scatter(y, 'aux', scatter_dimension=0, tiled=True)  47.8 us
    pallas_call x1, Pallas kernels, local_ladder(): pl.pallas_call(kernel, grid=(steps,), in_specs=[pl.BlockSpec((I_BLOCK * C...  46.2 us
    ppermute x6, waiting for transfers between devices, reduce_pair(): recv = lax.ppermute(send.astype(jnp.bfloat16), 'pair', xor_perm(n, b))  33.2 us
    ppermute x6, starting transfers between devices, gather_pair(): recv = lax.ppermute(buf, 'pair', xor_perm(n, b))  17.6 us
    ppermute x6, starting transfers between devices, reduce_pair(): recv = lax.ppermute(send.astype(jnp.bfloat16), 'pair', xor_perm(n, b))  16.4 us
    convert_element_type x1, other arithmetic, local(): y = y.reshape(n_aux, n_pair, rpp * y.shape[3], B).astype(jnp.bfloat16)  6.54 us
  transfers between devices with their start and end apart: 13, of which 13 were waited for; matrix products, arithmetic and copies ran while one was open for 2% of the time, Pallas kernels for 0%

profile of v4, /device:TPU:2, one launch (start us, length us, event | category | flops | bytes accessed | tf_op | source)
XLA Modules:
  0.0 291.1 jit_solution(16386508435547410205)
XLA Ops:
  7.4 7.3 %collective-permute-start = (bf16[256,128]{1,0:T(8,128)(2,1)S(1)}, bf16[256,128]{1,0:T(8,128)(2,1)S(1)}, u32[]{:S(2)}, u32[]{:S(2)}) collective-permute-start(bf16[256,128]{1,0:T(8,128)(2,1)S(1)} %reshape.30), channel_id=1, source_target_pairs={{0,16},{4,20},{8,24},{12,28},{16,0},{20,4},{24,8},{28,12},{32,48},... | collective-permute-start | bytes 196616 | tf_op jit(solution)/shard_map/ppermute | solution.py:85
  14.7 2.4 collective-permute-done
  17.2 3.3 %collective-permute-start.1 = (bf16[2,256,128]{2,1,0:T(8,128)(2,1)S(1)}, bf16[2,256,128]{2,1,0:T(8,128)(2,1)S(1)}, u32[]{:S(2)}, u32[]{:S(2)}) collective-permute-start(bf16[2,256,128]{2,1,0:T(8,128)(2,1)S(1)} %pad_maximum_fusion.5), channel_id=1, source_target_pairs={{0,128},{4,132},{8,136},{12,140},{16,144},{20,148},{24,152},{28,15... | collective-permute-start | bytes 393224 | tf_op jit(solution)/shard_map/ppermute | solution.py:85
  20.5 3.3 %collective-permute-done.1 = bf16[2,256,128]{2,1,0:T(8,128)(2,1)S(1)} collective-permute-done((bf16[2,256,128]{2,1,0:T(8,128)(2,1)S(1)}, bf16[2,256,128]{2,1,0:T(8,128)(2,1)S(1)}, u32[]{:S(2)}, u32[]{:S(2)}) %collective-permute-start.1) | collective-permute-done | bytes 131104 | tf_op jit(solution)/shard_map/ppermute | solution.py:85
  23.8 2.2 collective-permute-start.2
  26.0 5.8 %collective-permute-done.2 = bf16[2,2,256,128]{3,2,0,1:T(8,128)(2,1)S(1)} collective-permute-done((bf16[2,2,256,128]{3,2,0,1:T(8,128)(2,1)S(1)}, bf16[2,2,256,128]{3,2,0,1:T(8,128)(2,1)S(1)}, u32[]{:S(2)}, u32[]{:S(2)}) %collective-permute-start.2) | collective-permute-done | bytes 262176 | tf_op jit(solution)/shard_map/ppermute | solution.py:85
  31.9 3.0 %collective-permute-start.3 = (bf16[2,2,2,256,128]{4,3,0,2,1:T(8,128)(2,1)S(1)}, bf16[2,2,2,256,128]{4,3,0,2,1:T(8,128)(2,1)S(1)}, u32[]{:S(2)}, u32[]{:S(2)}) collective-permute-start(bf16[2,2,2,256,128]{4,3,0,2,1:T(8,128)(2,1)S(1)} %pad_maximum_fusion.3), channel_id=1, source_target_pairs={{0,8},{4,12},{8,0},{12,4},{16,24},{20,28},{24,16},{28,20},{32,40},... | collective-permute-start | bytes 1572872 | tf_op jit(solution)/shard_map/ppermute | solution.py:85
  34.9 19.6 %collective-permute-done.3 = bf16[2,2,2,256,128]{4,3,0,2,1:T(8,128)(2,1)S(1)} collective-permute-done((bf16[2,2,2,256,128]{4,3,0,2,1:T(8,128)(2,1)S(1)}, bf16[2,2,2,256,128]{4,3,0,2,1:T(8,128)(2,1)S(1)}, u32[]{:S(2)}, u32[]{:S(2)}) %collective-permute-start.3) | collective-permute-done | bytes 524320 | tf_op jit(solution)/shard_map/ppermute | solution.py:85
  54.7 1.7 collective-permute-start.4
  56.3 23.1 %collective-permute-done.4 = bf16[2,2,2,2,256,128]{5,4,3,0,2,1:T(8,128)(2,1)S(1)} collective-permute-done((bf16[2,2,2,2,256,128]{5,4,3,0,2,1:T(8,128)(2,1)S(1)}, bf16[2,2,2,2,256,128]{5,4,3,0,2,1:T(8,128)(2,1)S(1)}, u32[]{:S(2)}, u32[]{:S(2)}) %collective-permute-start.4) | collective-permute-done | bytes 1048608 | tf_op jit(solution)/shard_map/ppermute | solution.py:85
  79.6 1.5 pad_maximum_fusion.1
  81.9 1.0 copy.24
  83.7 1.5 copy.31
  86.1 41.6 %collective-permute-done.5 = bf16[2,2,2,2,2,256,128]{6,5,3,0,2,4,1:T(8,128)(2,1)} collective-permute-done((bf16[2,2,2,2,2,256,128]{6,5,3,0,2,4,1:T(8,128)(2,1)}, bf16[2,2,2,2,2,256,128]{6,5,3,0,2,4,1:T(8,128)(2,1)}, u32[]{:S(2)}, u32[]{:S(2)}) %collective-permute-start.5) | collective-permute-done | bytes 2097184 | tf_op jit(solution)/shard_map/ppermute | solution.py:85
  127.8 2.1 select_bitcast_fusion.1
  130.3 46.2 %shard_map.37 = f32[4,64,2,32,128]{4,3,2,1,0:T(8,128)} custom-call(bf16[16384,128]{1,0:T(8,128)(2,1)S(1)} %bitcast.76, bf16[128,3200]{1,0:T(8,128)(2,1)S(1)} %copy.25.r_ref, bf16[128,3200]{1,0:T(8,128)(2,1)S(1)} %copy.26.l_ref), custom_call_target="tpu_custom_call" | custom-call | flops 26843545600 | bytes 14221312 | tf_op jit(solution)/shard_map/pallas_call | solution.py:48
  176.5 6.5 %convert_element_type.70 = bf16[4,64,2,32,128]{4,3,2,1,0:T(8,128)(2,1)} convert(f32[4,64,2,32,128]{4,3,2,1,0:T(8,128)} %shard_map.37) | non-fusion elementwise | flops 2097152 | bytes 12582912 | tf_op jit(solution)/shard_map/convert_element_type | solution.py:119
  183.1 47.8 %reduce-scatter.2.cloned.1.call-done = bf16[1,64,64,128]{3,2,1,0:T(8,128)(2,1)} async-done(((bf16[4,64,64,128]{3,2,1,0:T(8,128)(2,1)}), bf16[1,64,64,128]{3,2,1,0:T(8,128)(2,1)}) %reduce-scatter.2.cloned.1.call-update) | async-done | bytes 1048592 | tf_op jit(solution)/shard_map/reduce_scatter | solution.py:120
  230.9 1.5 convert.1
  232.5 2.4 collective-permute-start.6
  234.8 12.3 %collective-permute-done.6 = bf16[2,2,2,2,2,64,128]{6,5,3,0,2,4,1:T(8,128)(2,1)} collective-permute-done((bf16[2,2,2,2,2,64,128]{6,5,3,0,2,4,1:T(8,128)(2,1)S(1)}, bf16[2,2,2,2,2,64,128]{6,5,3,0,2,4,1:T(8,128)(2,1)}, u32[]{:S(2)}, u32[]{:S(2)}) %collective-permute-start.6) | collective-permute-done | bytes 524320 | tf_op jit(solution)/shard_map/ppermute | solution.py:106
  247.2 1.2 bitcast_add_fusion
  248.4 1.7 collective-permute-start.7
  250.2 6.2 %collective-permute-done.7 = bf16[2,2,2,2,64,128]{5,4,2,0,1,3:T(8,128)(2,1)S(1)} collective-permute-done((bf16[2,2,2,2,64,128]{5,4,2,0,1,3:T(8,128)(2,1)S(1)}, bf16[2,2,2,2,64,128]{5,4,2,0,1,3:T(8,128)(2,1)S(1)}, u32[]{:S(2)}, u32[]{:S(2)}) %collective-permute-start.7) | collective-permute-done | bytes 262176 | tf_op jit(solution)/shard_map/ppermute | solution.py:106
  256.5 2.5 collective-permute-start.8
  259.0 5.4 %collective-permute-done.8 = bf16[2,2,2,64,128]{4,3,2,0,1:T(8,128)(2,1)S(1)} collective-permute-done((bf16[2,2,2,64,128]{4,3,2,0,1:T(8,128)(2,1)S(1)}, bf16[2,2,2,64,128]{4,3,2,0,1:T(8,128)(2,1)S(1)}, u32[]{:S(2)}, u32[]{:S(2)}) %collective-permute-start.8) | collective-permute-done | bytes 131104 | tf_op jit(solution)/shard_map/ppermute | solution.py:106
  264.4 1.9 collective-permute-start.9
  266.3 4.0 %collective-permute-done.9 = bf16[2,2,64,128]{3,2,1,0:T(8,128)(2,1)S(1)} collective-permute-done((bf16[2,2,64,128]{3,2,1,0:T(8,128)(2,1)S(1)}, bf16[2,2,64,128]{3,2,1,0:T(8,128)(2,1)S(1)}, u32[]{:S(2)}, u32[]{:S(2)}) %collective-permute-start.9) | collective-permute-done | bytes 65568 | tf_op jit(solution)/shard_map/ppermute | solution.py:106
  270.3 2.6 collective-permute-start.10
  272.9 2.9 %collective-permute-done.10 = bf16[2,64,128]{2,1,0:T(8,128)(2,1)S(1)} collective-permute-done((bf16[2,64,128]{2,1,0:T(8,128)(2,1)S(1)}, bf16[2,64,128]{2,1,0:T(8,128)(2,1)S(1)}, u32[]{:S(2)}, u32[]{:S(2)}) %collective-permute-start.10) | collective-permute-done | bytes 32800 | tf_op jit(solution)/shard_map/ppermute | solution.py:106
  275.9 5.3 %collective-permute-start.11 = (bf16[64,128]{1,0:T(8,128)(2,1)S(1)}, bf16[64,128]{1,0:T(8,128)(2,1)S(1)}, u32[]{:S(2)}, u32[]{:S(2)}) collective-permute-start(bf16[64,128]{1,0:T(8,128)(2,1)S(1)} %fusion.6), channel_id=1, source_target_pairs={{0,16},{4,20},{8,24},{12,28},{16,0},{20,4},{24,8},{28,12},{32,48},... | collective-permute-start | bytes 49160 | tf_op jit(solution)/shard_map/ppermute | solution.py:106
  281.2 2.4 collective-permute-done.11
  (35 shorter events, 5.3 us)
Async XLA Ops:
  6.5 224.4 %reduce-scatter.2.cloned.1.call-start = ((), (), s32[]{:S(2)}) async-start(), calls=%async_computation.1 | async-start | bytes 5242880 | tf_op jit(solution)/shard_map/reduce_scatter | solution.py:120
  7.4 9.7 %collective-permute-start = (bf16[256,128]{1,0:T(8,128)(2,1)S(1)}, bf16[256,128]{1,0:T(8,128)(2,1)S(1)}, u32[]{:S(2)}, u32[]{:S(2)}) collective-permute-start(bf16[256,128]{1,0:T(8,128)(2,1)S(1)} %reshape.30), channel_id=1, source_target_pairs={{0,16},{4,20},{8,24},{12,28},{16,0},{20,4},{24,8},{28,12},{32,48},... | collective-permute-start | bytes 196616 | tf_op jit(solution)/shard_map/ppermute | solution.py:85
  17.2 6.6 %collective-permute-start.1 = (bf16[2,256,128]{2,1,0:T(8,128)(2,1)S(1)}, bf16[2,256,128]{2,1,0:T(8,128)(2,1)S(1)}, u32[]{:S(2)}, u32[]{:S(2)}) collective-permute-start(bf16[2,256,128]{2,1,0:T(8,128)(2,1)S(1)} %pad_maximum_fusion.5), channel_id=1, source_target_pairs={{0,128},{4,132},{8,136},{12,140},{16,144},{20,148},{24,152},{28,15... | collective-permute-start | bytes 393224 | tf_op jit(solution)/shard_map/ppermute | solution.py:85
  23.8 8.0 %collective-permute-start.2 = (bf16[2,2,256,128]{3,2,0,1:T(8,128)(2,1)S(1)}, bf16[2,2,256,128]{3,2,0,1:T(8,128)(2,1)S(1)}, u32[]{:S(2)}, u32[]{:S(2)}) collective-permute-start(bf16[2,2,256,128]{3,2,0,1:T(8,128)(2,1)S(1)} %pad_maximum_fusion.4), channel_id=1, source_target_pairs={{0,32},{4,36},{8,40},{12,44},{16,48},{20,52},{24,56},{28,60},{32,0... | collective-permute-start | bytes 786440 | tf_op jit(solution)/shard_map/ppermute | solution.py:85
  31.9 22.6 %collective-permute-start.3 = (bf16[2,2,2,256,128]{4,3,0,2,1:T(8,128)(2,1)S(1)}, bf16[2,2,2,256,128]{4,3,0,2,1:T(8,128)(2,1)S(1)}, u32[]{:S(2)}, u32[]{:S(2)}) collective-permute-start(bf16[2,2,2,256,128]{4,3,0,2,1:T(8,128)(2,1)S(1)} %pad_maximum_fusion.3), channel_id=1, source_target_pairs={{0,8},{4,12},{8,0},{12,4},{16,24},{20,28},{24,16},{28,20},{32,40},... | collective-permute-start | bytes 1572872 | tf_op jit(solution)/shard_map/ppermute | solution.py:85
  54.7 24.7 %collective-permute-start.4 = (bf16[2,2,2,2,256,128]{5,4,3,0,2,1:T(8,128)(2,1)S(1)}, bf16[2,2,2,2,256,128]{5,4,3,0,2,1:T(8,128)(2,1)S(1)}, u32[]{:S(2)}, u32[]{:S(2)}) collective-permute-start(bf16[2,2,2,2,256,128]{5,4,3,0,2,1:T(8,128)(2,1)S(1)} %pad_maximum_fusion.2), channel_id=1, source_target_pairs={{0,64},{4,68},{8,72},{12,76},{16,80},{20,84},{24,88},{28,92},{32,9... | collective-permute-start | bytes 3145736 | tf_op jit(solution)/shard_map/ppermute | solution.py:85
  79.6 1.7 copy-start
  79.6 2.0 copy-start.1
  81.2 46.5 %collective-permute-start.5 = (bf16[2,2,2,2,2,256,128]{6,5,3,0,2,4,1:T(8,128)(2,1)}, bf16[2,2,2,2,2,256,128]{6,5,3,0,2,4,1:T(8,128)(2,1)}, u32[]{:S(2)}, u32[]{:S(2)}) collective-permute-start(bf16[2,2,2,2,2,256,128]{6,5,3,0,2,4,1:T(8,128)(2,1)} %pad_maximum_fusion.1), channel_id=1, source_target_pairs={{0,4},{4,0},{8,12},{12,8},{16,20},{20,16},{24,28},{28,24},{32,36},... | collective-permute-start | bytes 6291464 | tf_op jit(solution)/shard_map/ppermute | solution.py:85
  232.5 14.7 %collective-permute-start.6 = (bf16[2,2,2,2,2,64,128]{6,5,3,0,2,4,1:T(8,128)(2,1)S(1)}, bf16[2,2,2,2,2,64,128]{6,5,3,0,2,4,1:T(8,128)(2,1)}, u32[]{:S(2)}, u32[]{:S(2)}) collective-permute-start(bf16[2,2,2,2,2,64,128]{6,5,3,0,2,4,1:T(8,128)(2,1)S(1)} %fusion), channel_id=1, source_target_pairs={{0,4},{4,0},{8,12},{12,8},{16,20},{20,16},{24,28},{28,24},{32,36},... | collective-permute-start | bytes 1572872 | tf_op jit(solution)/shard_map/ppermute | solution.py:106
  248.4 7.9 %collective-permute-start.7 = (bf16[2,2,2,2,64,128]{5,4,2,0,1,3:T(8,128)(2,1)S(1)}, bf16[2,2,2,2,64,128]{5,4,2,0,1,3:T(8,128)(2,1)S(1)}, u32[]{:S(2)}, u32[]{:S(2)}) collective-permute-start(bf16[2,2,2,2,64,128]{5,4,2,0,1,3:T(8,128)(2,1)S(1)} %fusion.1), channel_id=1, source_target_pairs={{0,64},{4,68},{8,72},{12,76},{16,80},{20,84},{24,88},{28,92},{32,9... | collective-permute-start | bytes 786440 | tf_op jit(solution)/shard_map/ppermute | solution.py:106
  256.5 7.9 %collective-permute-start.8 = (bf16[2,2,2,64,128]{4,3,2,0,1:T(8,128)(2,1)S(1)}, bf16[2,2,2,64,128]{4,3,2,0,1:T(8,128)(2,1)S(1)}, u32[]{:S(2)}, u32[]{:S(2)}) collective-permute-start(bf16[2,2,2,64,128]{4,3,2,0,1:T(8,128)(2,1)S(1)} %fusion.2), channel_id=1, source_target_pairs={{0,8},{4,12},{8,0},{12,4},{16,24},{20,28},{24,16},{28,20},{32,40},... | collective-permute-start | bytes 393224 | tf_op jit(solution)/shard_map/ppermute | solution.py:106
  264.4 5.9 %collective-permute-start.9 = (bf16[2,2,64,128]{3,2,1,0:T(8,128)(2,1)S(1)}, bf16[2,2,64,128]{3,2,1,0:T(8,128)(2,1)S(1)}, u32[]{:S(2)}, u32[]{:S(2)}) collective-permute-start(bf16[2,2,64,128]{3,2,1,0:T(8,128)(2,1)S(1)} %fusion.3), channel_id=1, source_target_pairs={{0,32},{4,36},{8,40},{12,44},{16,48},{20,52},{24,56},{28,60},{32,0... | collective-permute-start | bytes 196616 | tf_op jit(solution)/shard_map/ppermute | solution.py:106
  270.3 5.5 %collective-permute-start.10 = (bf16[2,64,128]{2,1,0:T(8,128)(2,1)S(1)}, bf16[2,64,128]{2,1,0:T(8,128)(2,1)S(1)}, u32[]{:S(2)}, u32[]{:S(2)}) collective-permute-start(bf16[2,64,128]{2,1,0:T(8,128)(2,1)S(1)} %fusion.4), channel_id=1, source_target_pairs={{0,128},{4,132},{8,136},{12,140},{16,144},{20,148},{24,152},{28,15... | collective-permute-start | bytes 98312 | tf_op jit(solution)/shard_map/ppermute | solution.py:106
  275.9 7.7 %collective-permute-start.11 = (bf16[64,128]{1,0:T(8,128)(2,1)S(1)}, bf16[64,128]{1,0:T(8,128)(2,1)S(1)}, u32[]{:S(2)}, u32[]{:S(2)}) collective-permute-start(bf16[64,128]{1,0:T(8,128)(2,1)S(1)} %fusion.6), channel_id=1, source_target_pairs={{0,16},{4,20},{8,24},{12,28},{16,0},{20,4},{24,8},{28,12},{32,48},... | collective-permute-start | bytes 49160 | tf_op jit(solution)/shard_map/ppermute | solution.py:106
Sparse Core Ops, SparseCore 0:
  183.2 47.6 reduce-scatter.1

commit v5 on v3

--- a/solution.py
+++ b/solution.py
@@ -13,6 +13,7 @@
 D = 128
 I_BLOCK = 8
 P_GROUP = 5
+SMALL_SEND = 131072
 
 
 def ladder_kernel(n_p, n_aux, rpp, t_ref, r_ref, l_ref, out_ref, w_ref):
@@ -34,7 +35,7 @@
     apa = A // n_aux
     for i in range(I_BLOCK):
         for q in range(n_aux):
-            out_ref[q, i // rpp, i % rpp] = y[q * apa:(q + 1) * apa, i * B:(i + 1) * B]
+            out_ref[q, i // rpp, i % rpp] = y[q * apa:(q + 1) * apa, i * B:(i + 1) * B].astype(out_ref.dtype)
 
 
 def local_ladder(t_all, factor_ca, factor_db, n_pair, n_aux):
@@ -58,31 +59,77 @@
             pl.BlockSpec((A, n_p * C), lambda g: (0, 0)),
         ],
         out_specs=pl.BlockSpec((n_aux, pb, rpp, apa, B), lambda g: (0, g, 0, 0, 0)),
-        out_shape=jax.ShapeDtypeStruct((n_aux, n_pair, rpp, apa, B), jnp.float32),
+        out_shape=jax.ShapeDtypeStruct((n_aux, n_pair, rpp, apa, B), jnp.bfloat16),
         scratch_shapes=[pltpu.VMEM((n_p * C, I_BLOCK * B), jnp.bfloat16)],
         compiler_params=pltpu.CompilerParams(vmem_limit_bytes=48 * 1024 * 1024),
         cost_estimate=pl.CostEstimate(
             flops=flops, transcendentals=0,
-            bytes_accessed=2 * (t2.size + r2.size + l2.size) + 4 * nij * A * B,
+            bytes_accessed=2 * (t2.size + r2.size + l2.size) + 2 * nij * A * B,
         ),
     )(t2, r2, l2)
+
+
+def bit_order(axis, n_bits, far_first):
+    if axis == "pair" and n_bits == 6:
+        order = [2, 5, 3, 1, 4, 0]
+    else:
+        order = list(range(n_bits - 1, -1, -1))
+    return order if far_first else order[::-1]
+
+
+def xor_perm(n, b):
+    return [(i, i ^ (1 << b)) for i in range(n)]
+
+
+def gather_axis(x, axis, n):
+    n_bits = n.bit_length() - 1
+    me = lax.axis_index(axis)
+    order = bit_order(axis, n_bits, True)
+    buf = x
+    for k, b in enumerate(order):
+        recv = lax.ppermute(buf, axis, xor_perm(n, b))
+        low = ((me >> b) & 1) == 0
+        lo = jnp.where(low, buf, recv)
+        hi = jnp.where(low, recv, buf)
+        buf = jnp.stack([lo, hi], axis=k)
+    axes = [order.index(b) for b in range(n_bits - 1, -1, -1)]
+    buf = buf.transpose(axes + list(range(n_bits, buf.ndim)))
+    return buf.reshape((n,) + x.shape)
+
+
+def reduce_axis(y, axis, n):
+    n_bits = n.bit_length() - 1
+    me = lax.axis_index(axis)
+    blk = y.shape[1:]
+    buf = y.reshape((2,) * n_bits + blk)
+    axes = list(range(n_bits - 1, -1, -1))
+    for b in bit_order(axis, n_bits, False):
+        ax = axes.index(b)
+        mine = (me >> b) & 1
+        keep = lax.dynamic_index_in_dim(buf, mine, axis=ax, keepdims=False)
+        send = lax.dynamic_index_in_dim(buf, 1 - mine, axis=ax, keepdims=False)
+        wire = jnp.bfloat16 if send.size > SMALL_SEND else jnp.float32
+        recv = lax.ppermute(send.astype(wire), axis, xor_perm(n, b))
+        buf = keep.astype(jnp.float32) + recv.astype(jnp.float32)
+        axes.pop(ax)
+    return buf
 
 
 def local(amplitudes, factor_ca, factor_db):
     n_pair = lax.axis_size("pair")
     n_aux = lax.axis_size("aux")
+    rows = amplitudes.shape[0]
     cq = C // n_aux
     q = lax.axis_index("aux")
     amps_q = lax.dynamic_slice_in_dim(amplitudes, q * cq * D, cq * D, axis=1)
-    amps_q = amps_q.reshape(amplitudes.shape[0], cq, D)
-    t_q = lax.all_gather(amps_q, "pair", axis=0, tiled=True)
-    t_all = lax.all_gather(t_q, "aux", axis=0)
+    amps_q = amps_q.reshape(rows * cq, D)
+    t_q = gather_axis(amps_q, "pair", n_pair).reshape(n_pair * rows, cq, D)
+    t_all = gather_axis(t_q, "aux", n_aux)
     y = local_ladder(t_all, factor_ca, factor_db, n_pair, n_aux)
     rpp = y.shape[2]
     y = y.reshape(n_aux, n_pair, rpp * y.shape[3], B)
-    y = lax.psum_scatter(y, "aux", scatter_dimension=0, tiled=True)
-    parts = lax.all_to_all(y[0], "pair", split_axis=0, concat_axis=0, tiled=True)
-    mine = jnp.sum(parts, axis=0).astype(jnp.bfloat16)
+    y = reduce_axis(y, "aux", n_aux)
+    mine = reduce_axis(y, "pair", n_pair).astype(jnp.bfloat16)
     return mine.reshape(rpp, -1)
 
 

time: 380 us -> 222 us (0.58)
  waiting for transfers between devices: 244 us -> 117 us
  blocking collectives: 66.4 us -> 0 us
  starting transfers between devices: 0.08 us -> 33.2 us
  between operations: 13.2 us -> 0.3 us
  other arithmetic: 0.14 us -> 12.8 us
    all_gather x2 -> x0, waiting for transfers between devices: 162 us -> none  [the longest x1 119 us: local(): t_q = lax.all_gather(amps_q, 'pair', axis=0, tiled=True)]
    ppermute x0 -> x16, waiting for transfers between devices: none -> 117 us  [the longest x8 72.9 us: reduce_axis(): recv = lax.ppermute(send.astype(wire), axis, xor_perm(n, b))]
    reduce_scatter x1 -> x0, waiting for transfers between devices: 82.7 us -> none  [local(): y = lax.psum_scatter(y, 'aux', scatter_dimension=0, tiled=True)]
    all_to_all x1 -> x0, blocking collectives: 66.4 us -> none  [local(): lax.all_to_all(y[0], 'pair', split_axis=0, concat_axis=0, tiled=True)]
    ppermute x0 -> x16, starting transfers between devices: none -> 33.2 us  [the longest x8 17.8 us: gather_axis(): recv = lax.ppermute(buf, axis, xor_perm(n, b))]
    another operation x0 -> x16, other arithmetic: none -> 6.45 us  [gather_axis(): buf = jnp.stack([lo, hi], axis=k)]
    add x0 -> x7, other arithmetic: none -> 6.33 us  [reduce_axis(): buf = keep.astype(jnp.float32) + recv.astype(jnp.float32)]
  transfers between devices with their start and end apart: 3 -> 16, of which waited for: 3 -> 15; matrix products, arithmetic and copies ran while one was open for 1% -> 3% of each run, Pallas kernels for 0% -> 0%
where the time goes in v5:
time: 222 us
  waiting for transfers between devices  117 us (53%)
  Pallas kernels  46.4 us (21%)
  starting transfers between devices  33.2 us (15%)
  other arithmetic  12.8 us (6%)
  local copies, waits for them, and re-layouts  12.4 us (6%)
    ppermute x8, waiting for transfers between devices, reduce_axis(): recv = lax.ppermute(send.astype(wire), axis, xor_perm(n, b))  72.9 us
    pallas_call x1, Pallas kernels, local_ladder(): pl.pallas_call(kernel, grid=(steps,), in_specs=[pl.BlockSpec((n_aux, I_BL...  46.4 us
    ppermute x8, waiting for transfers between devices, gather_axis(): recv = lax.ppermute(buf, axis, xor_perm(n, b))  44 us
    ppermute x8, starting transfers between devices, gather_axis(): recv = lax.ppermute(buf, axis, xor_perm(n, b))  17.8 us
    ppermute x8, starting transfers between devices, reduce_axis(): recv = lax.ppermute(send.astype(wire), axis, xor_perm(n, b))  15.4 us
    unnamed x12, local copies, waits for them, and re-layouts  6.74 us
    another operation x16, other arithmetic, gather_axis(): buf = jnp.stack([lo, hi], axis=k)  6.45 us
    add x7, other arithmetic, reduce_axis(): buf = keep.astype(jnp.float32) + recv.astype(jnp.float32)  6.33 us
  transfers between devices with their start and end apart: 16, of which 15 were waited for; matrix products, arithmetic and copies ran while one was open for 3% of the time, Pallas kernels for 0%

profile of v5, /device:TPU:2, one launch (start us, length us, event | category | flops | bytes accessed | tf_op | source)
XLA Modules:
  0.0 222.0 jit_solution(8962018822599789431)
XLA Ops:
  0.9 7.3 %collective-permute-start = (bf16[64,128]{1,0:T(8,128)(2,1)S(1)}, bf16[64,128]{1,0:T(8,128)(2,1)S(1)}, u32[]{:S(2)}, u32[]{:S(2)}) collective-permute-start(bf16[64,128]{1,0:T(8,128)(2,1)S(1)} %reshape.28), channel_id=1, source_target_pairs={{0,16},{4,20},{8,24},{12,28},{16,0},{20,4},{24,8},{28,12},{32,48},... | collective-permute-start | bytes 49160 | tf_op jit(solution)/shard_map/ppermute | solution.py:90
  8.2 1.7 collective-permute-done
  9.9 3.3 %collective-permute-start.1 = (bf16[2,64,128]{2,1,0:T(8,128)(2,1)S(1)}, bf16[2,64,128]{2,1,0:T(8,128)(2,1)S(1)}, u32[]{:S(2)}, u32[]{:S(2)}) collective-permute-start(bf16[2,64,128]{2,1,0:T(8,128)(2,1)S(1)} %pad_maximum_fusion.7), channel_id=1, source_target_pairs={{0,128},{4,132},{8,136},{12,140},{16,144},{20,148},{24,152},{28,15... | collective-permute-start | bytes 98312 | tf_op jit(solution)/shard_map/ppermute | solution.py:90
  13.2 2.2 %collective-permute-done.1 = bf16[2,64,128]{2,1,0:T(8,128)(2,1)S(1)} collective-permute-done((bf16[2,64,128]{2,1,0:T(8,128)(2,1)S(1)}, bf16[2,64,128]{2,1,0:T(8,128)(2,1)S(1)}, u32[]{:S(2)}, u32[]{:S(2)}) %collective-permute-start.1) | collective-permute-done | bytes 32800 | tf_op jit(solution)/shard_map/ppermute | solution.py:90
  15.4 2.2 collective-permute-start.2
  17.6 3.6 %collective-permute-done.2 = bf16[2,2,64,128]{3,2,0,1:T(8,128)(2,1)S(1)} collective-permute-done((bf16[2,2,64,128]{3,2,0,1:T(8,128)(2,1)S(1)}, bf16[2,2,64,128]{3,2,0,1:T(8,128)(2,1)S(1)}, u32[]{:S(2)}, u32[]{:S(2)}) %collective-permute-start.2) | collective-permute-done | bytes 65568 | tf_op jit(solution)/shard_map/ppermute | solution.py:90
  21.3 2.1 collective-permute-start.3
  23.4 5.3 %collective-permute-done.3 = bf16[2,2,2,64,128]{4,3,0,2,1:T(8,128)(2,1)S(1)} collective-permute-done((bf16[2,2,2,64,128]{4,3,0,2,1:T(8,128)(2,1)S(1)}, bf16[2,2,2,64,128]{4,3,0,2,1:T(8,128)(2,1)S(1)}, u32[]{:S(2)}, u32[]{:S(2)}) %collective-permute-start.3) | collective-permute-done | bytes 131104 | tf_op jit(solution)/shard_map/ppermute | solution.py:90
  28.7 1.7 collective-permute-start.4
  30.4 4.8 %collective-permute-done.4 = bf16[2,2,2,2,64,128]{5,4,3,0,2,1:T(8,128)(2,1)S(1)} collective-permute-done((bf16[2,2,2,2,64,128]{5,4,3,0,2,1:T(8,128)(2,1)S(1)}, bf16[2,2,2,2,64,128]{5,4,3,0,2,1:T(8,128)(2,1)S(1)}, u32[]{:S(2)}, u32[]{:S(2)}) %collective-permute-start.4) | collective-permute-done | bytes 262176 | tf_op jit(solution)/shard_map/ppermute | solution.py:90
  35.5 9.1 %collective-permute-done.5 = bf16[2,2,2,2,2,64,128]{6,5,3,0,2,4,1:T(8,128)(2,1)S(1)} collective-permute-done((bf16[2,2,2,2,2,64,128]{6,5,3,0,2,4,1:T(8,128)(2,1)S(1)}, bf16[2,2,2,2,2,64,128]{6,5,3,0,2,4,1:T(8,128)(2,1)S(1)}, u32[]{:S(2)}, u32[]{:S(2)}) %collective-permute-start.5) | collective-permute-done | bytes 524320 | tf_op jit(solution)/shard_map/ppermute | solution.py:90
  45.8 17.3 %collective-permute-done.6 = bf16[128,32,128]{2,1,0:T(8,128)(2,1)S(1)} collective-permute-done((bf16[128,32,128]{2,1,0:T(8,128)(2,1)S(1)}, bf16[128,32,128]{2,1,0:T(8,128)(2,1)S(1)}, u32[]{:S(2)}, u32[]{:S(2)}) %collective-permute-start.6) | collective-permute-done | bytes 1048608 | tf_op jit(solution)/shard_map/ppermute | solution.py:90
  69.9 1.5 copy.27.l_ref
  71.5 2.1 select_bitcast_fusion.1
  73.6 2.3 %pad_maximum_fusion = bf16[2,2,128,32,128]{4,3,2,1,0:T(8,128)(2,1)} fusion(bf16[2,1,128,32,128]{4,3,2,1,0:T(8,128)(2,1)S(1)} %get-tuple-element.6, bf16[2,1,128,32,128]{4,3,2,1,0:T(8,128)(2,1)S(1)} %get-tuple-element.5), kind=kLoop, calls=%fused_computation | loop fusion | flops 2097152 | bytes 8388608 | tf_op jit(solution)/shard_map/stack | solution.py:94
  75.9 46.4 %shard_map.37 = bf16[4,64,2,32,128]{4,3,2,1,0:T(8,128)(2,1)S(1)} custom-call(bf16[4,128,32,128]{3,2,1,0:T(8,128)(2,1)} %bitcast.101, bf16[128,3200]{1,0:T(8,128)(2,1)S(1)} %copy.26.r_ref, bf16[128,3200]{1,0:T(8,128)(2,1)S(1)} %copy.27.l_ref), custom_call_target="tpu_custom_call" | custom-call | flops 26843545600 | bytes 10027008 | tf_op jit(solution)/shard_map/pallas_call | solution.py:53
  122.5 1.7 copy-done.1
  124.4 4.1 %collective-permute-done.8 = bf16[2,64,64,128]{3,2,1,0:T(8,128)(2,1)} collective-permute-done((bf16[2,64,64,128]{3,2,1,0:T(8,128)(2,1)S(1)}, bf16[2,64,64,128]{3,2,1,0:T(8,128)(2,1)}, u32[]{:S(2)}, u32[]{:S(2)}) %collective-permute-start.8) | collective-permute-done | bytes 2097184 | tf_op jit(solution)/shard_map/ppermute | solution.py:112
  128.5 3.1 %convert_add_fusion = f32[2,64,64,128]{3,2,1,0:T(8,128)S(1)} fusion(bf16[2,64,64,128]{3,2,1,0:T(8,128)(2,1)} %collective-permute-done.8, bf16[2,2,64,64,128]{4,3,2,1,0:T(8,128)(2,1)} %bitcast.96, s32[]{:T(128)S(6)} %select_n.180), kind=kLoop, calls=%fused_computation.1 | loop fusion | flops 3145728 | bytes 8388612 | tf_op jit(solution)/shard_map/add | solution.py:113
  131.6 1.9 copy-done.2
  134.6 24.7 %collective-permute-done.9 = bf16[64,64,128]{2,1,0:T(8,128)(2,1)S(1)} collective-permute-done((bf16[64,64,128]{2,1,0:T(8,128)(2,1)S(1)}, bf16[64,64,128]{2,1,0:T(8,128)(2,1)S(1)}, u32[]{:S(2)}, u32[]{:S(2)}) %collective-permute-start.9) | collective-permute-done | bytes 1048608 | tf_op jit(solution)/shard_map/ppermute | solution.py:112
  159.3 1.9 bitcast_add_fusion
  161.6 13.0 %collective-permute-done.10 = bf16[2,2,2,2,2,64,128]{6,5,3,2,0,4,1:T(8,128)(2,1)} collective-permute-done((bf16[2,2,2,2,2,64,128]{6,5,3,2,0,4,1:T(8,128)(2,1)S(1)}, bf16[2,2,2,2,2,64,128]{6,5,3,2,0,4,1:T(8,128)(2,1)}, u32[]{:S(2)}, u32[]{:S(2)}) %collective-permute-start.10) | collective-permute-done | bytes 524320 | tf_op jit(solution)/shard_map/ppermute | solution.py:112
  176.0 1.7 collective-permute-start.11
  177.6 10.7 %collective-permute-done.11 = f32[2,2,2,2,64,128]{5,4,2,1,0,3:T(8,128)S(1)} collective-permute-done((f32[2,2,2,2,64,128]{5,4,2,1,0,3:T(8,128)S(1)}, f32[2,2,2,2,64,128]{5,4,2,1,0,3:T(8,128)S(1)}, u32[]{:S(2)}, u32[]{:S(2)}) %collective-permute-start.11) | collective-permute-done | bytes 524320 | tf_op jit(solution)/shard_map/ppermute | solution.py:112
  190.0 10.8 %collective-permute-done.12 = f32[2,2,2,64,128]{4,3,2,1,0:T(8,128)S(1)} collective-permute-done((f32[2,2,2,64,128]{4,3,2,1,0:T(8,128)S(1)}, f32[2,2,2,64,128]{4,3,2,1,0:T(8,128)S(1)}, u32[]{:S(2)}, u32[]{:S(2)}) %collective-permute-start.12) | collective-permute-done | bytes 262176 | tf_op jit(solution)/shard_map/ppermute | solution.py:112
  200.8 2.2 collective-permute-start.13
  203.0 4.4 %collective-permute-done.13 = f32[2,2,64,128]{3,2,1,0:T(8,128)S(1)} collective-permute-done((f32[2,2,64,128]{3,2,1,0:T(8,128)S(1)}, f32[2,2,64,128]{3,2,1,0:T(8,128)S(1)}, u32[]{:S(2)}, u32[]{:S(2)}) %collective-permute-start.13) | collective-permute-done | bytes 131104 | tf_op jit(solution)/shard_map/ppermute | solution.py:112
  207.5 3.3 %collective-permute-start.14 = (f32[2,64,128]{2,1,0:T(8,128)S(1)}, f32[2,64,128]{2,1,0:T(8,128)S(1)}, u32[]{:S(2)}, u32[]{:S(2)}) collective-permute-start(f32[2,64,128]{2,1,0:T(8,128)S(1)} %dynamic-slice_bitcast_fusion.4), channel_id=1, source_target_pairs={{0,128},{4,132},{8,136},{12,140},{16,144},{20,148},{24,152},{28,15... | collective-permute-start | bytes 196616 | tf_op jit(solution)/shard_map/ppermute | solution.py:112
  210.8 2.6 %collective-permute-done.14 = f32[2,64,128]{2,1,0:T(8,128)S(1)} collective-permute-done((f32[2,64,128]{2,1,0:T(8,128)S(1)}, f32[2,64,128]{2,1,0:T(8,128)S(1)}, u32[]{:S(2)}, u32[]{:S(2)}) %collective-permute-start.14) | collective-permute-done | bytes 65568 | tf_op jit(solution)/shard_map/ppermute | solution.py:112
  213.4 5.4 %collective-permute-start.15 = (f32[64,128]{1,0:T(8,128)S(1)}, f32[64,128]{1,0:T(8,128)S(1)}, u32[]{:S(2)}, u32[]{:S(2)}) collective-permute-start(f32[64,128]{1,0:T(8,128)S(1)} %dynamic-slice_bitcast_fusion.5), channel_id=1, source_target_pairs={{0,16},{4,20},{8,24},{12,28},{16,0},{20,4},{24,8},{28,12},{32,48},... | collective-permute-start | bytes 98312 | tf_op jit(solution)/shard_map/ppermute | solution.py:112
  218.8 2.5 %collective-permute-done.15 = f32[64,128]{1,0:T(8,128)S(1)} collective-permute-done((f32[64,128]{1,0:T(8,128)S(1)}, f32[64,128]{1,0:T(8,128)S(1)}, u32[]{:S(2)}, u32[]{:S(2)}) %collective-permute-start.15) | collective-permute-done | bytes 32800 | tf_op jit(solution)/shard_map/ppermute | solution.py:112
  (53 shorter events, 14.6 us)
Async XLA Ops:
  0.0 0.8 copy-start
  0.9 9.0 %collective-permute-start = (bf16[64,128]{1,0:T(8,128)(2,1)S(1)}, bf16[64,128]{1,0:T(8,128)(2,1)S(1)}, u32[]{:S(2)}, u32[]{:S(2)}) collective-permute-start(bf16[64,128]{1,0:T(8,128)(2,1)S(1)} %reshape.28), channel_id=1, source_target_pairs={{0,16},{4,20},{8,24},{12,28},{16,0},{20,4},{24,8},{28,12},{32,48},... | collective-permute-start | bytes 49160 | tf_op jit(solution)/shard_map/ppermute | solution.py:90
  9.9 5.5 %collective-permute-start.1 = (bf16[2,64,128]{2,1,0:T(8,128)(2,1)S(1)}, bf16[2,64,128]{2,1,0:T(8,128)(2,1)S(1)}, u32[]{:S(2)}, u32[]{:S(2)}) collective-permute-start(bf16[2,64,128]{2,1,0:T(8,128)(2,1)S(1)} %pad_maximum_fusion.7), channel_id=1, source_target_pairs={{0,128},{4,132},{8,136},{12,140},{16,144},{20,148},{24,152},{28,15... | collective-permute-start | bytes 98312 | tf_op jit(solution)/shard_map/ppermute | solution.py:90
  15.4 5.9 %collective-permute-start.2 = (bf16[2,2,64,128]{3,2,0,1:T(8,128)(2,1)S(1)}, bf16[2,2,64,128]{3,2,0,1:T(8,128)(2,1)S(1)}, u32[]{:S(2)}, u32[]{:S(2)}) collective-permute-start(bf16[2,2,64,128]{3,2,0,1:T(8,128)(2,1)S(1)} %pad_maximum_fusion.6), channel_id=1, source_target_pairs={{0,32},{4,36},{8,40},{12,44},{16,48},{20,52},{24,56},{28,60},{32,0... | collective-permute-start | bytes 196616 | tf_op jit(solution)/shard_map/ppermute | solution.py:90
  21.3 7.4 %collective-permute-start.3 = (bf16[2,2,2,64,128]{4,3,0,2,1:T(8,128)(2,1)S(1)}, bf16[2,2,2,64,128]{4,3,0,2,1:T(8,128)(2,1)S(1)}, u32[]{:S(2)}, u32[]{:S(2)}) collective-permute-start(bf16[2,2,2,64,128]{4,3,0,2,1:T(8,128)(2,1)S(1)} %pad_maximum_fusion.5), channel_id=1, source_target_pairs={{0,8},{4,12},{8,0},{12,4},{16,24},{20,28},{24,16},{28,20},{32,40},... | collective-permute-start | bytes 393224 | tf_op jit(solution)/shard_map/ppermute | solution.py:90
  28.7 6.5 %collective-permute-start.4 = (bf16[2,2,2,2,64,128]{5,4,3,0,2,1:T(8,128)(2,1)S(1)}, bf16[2,2,2,2,64,128]{5,4,3,0,2,1:T(8,128)(2,1)S(1)}, u32[]{:S(2)}, u32[]{:S(2)}) collective-permute-start(bf16[2,2,2,2,64,128]{5,4,3,0,2,1:T(8,128)(2,1)S(1)} %pad_maximum_fusion.4), channel_id=1, source_target_pairs={{0,64},{4,68},{8,72},{12,76},{16,80},{20,84},{24,88},{28,92},{32,9... | collective-permute-start | bytes 786440 | tf_op jit(solution)/shard_map/ppermute | solution.py:90
  35.3 9.3 %collective-permute-start.5 = (bf16[2,2,2,2,2,64,128]{6,5,3,0,2,4,1:T(8,128)(2,1)S(1)}, bf16[2,2,2,2,2,64,128]{6,5,3,0,2,4,1:T(8,128)(2,1)S(1)}, u32[]{:S(2)}, u32[]{:S(2)}) collective-permute-start(bf16[2,2,2,2,2,64,128]{6,5,3,0,2,4,1:T(8,128)(2,1)S(1)} %pad_maximum_fusion.3), channel_id=1, source_target_pairs={{0,4},{4,0},{8,12},{12,8},{16,20},{20,16},{24,28},{28,24},{32,36},... | collective-permute-start | bytes 1572872 | tf_op jit(solution)/shard_map/ppermute | solution.py:90
  44.8 18.4 %collective-permute-start.6 = (bf16[128,32,128]{2,1,0:T(8,128)(2,1)S(1)}, bf16[128,32,128]{2,1,0:T(8,128)(2,1)S(1)}, u32[]{:S(2)}, u32[]{:S(2)}) collective-permute-start(bf16[128,32,128]{2,1,0:T(8,128)(2,1)S(1)} %bitcast.99), channel_id=1, source_target_pairs={{0,2},{1,3},{2,0},{3,1},{4,6},{5,7},{6,4},{7,5},{8,10},{9,11},{10,... | collective-permute-start | bytes 3145736 | tf_op jit(solution)/shard_map/ppermute | solution.py:90
  63.3 1.7 copy-start.3
  63.3 2.0 copy-start.4
  65.0 6.5 %collective-permute-start.7 = (bf16[2,128,32,128]{3,2,1,0:T(8,128)(2,1)}, bf16[2,128,32,128]{3,2,1,0:T(8,128)(2,1)}, u32[]{:S(2)}, u32[]{:S(2)}) collective-permute-start(bf16[2,128,32,128]{3,2,1,0:T(8,128)(2,1)} %pad_maximum_fusion.1), channel_id=1, source_target_pairs={{0,1},{1,0},{2,3},{3,2},{4,5},{5,4},{6,7},{7,6},{8,9},{9,8},{10,11... | collective-permute-start | bytes 6291464 | tf_op jit(solution)/shard_map/ppermute | solution.py:90
  122.3 1.9 copy-start.1
  124.2 4.3 %collective-permute-start.8 = (bf16[2,64,64,128]{3,2,1,0:T(8,128)(2,1)S(1)}, bf16[2,64,64,128]{3,2,1,0:T(8,128)(2,1)}, u32[]{:S(2)}, u32[]{:S(2)}) collective-permute-start(bf16[2,64,64,128]{3,2,1,0:T(8,128)(2,1)S(1)} %dynamic-slice_bitcast_fusion), channel_id=1, source_target_pairs={{0,1},{1,0},{2,3},{3,2},{4,5},{5,4},{6,7},{7,6},{8,9},{9,8},{10,11... | collective-permute-start | bytes 6291464 | tf_op jit(solution)/shard_map/ppermute | solution.py:112
  131.6 1.9 copy-start.2
  133.8 25.5 %collective-permute-start.9 = (bf16[64,64,128]{2,1,0:T(8,128)(2,1)S(1)}, bf16[64,64,128]{2,1,0:T(8,128)(2,1)S(1)}, u32[]{:S(2)}, u32[]{:S(2)}) collective-permute-start(bf16[64,64,128]{2,1,0:T(8,128)(2,1)S(1)} %fusion), channel_id=1, source_target_pairs={{0,2},{1,3},{2,0},{3,1},{4,6},{5,7},{6,4},{7,5},{8,10},{9,11},{10,... | collective-permute-start | bytes 3145736 | tf_op jit(solution)/shard_map/ppermute | solution.py:112
  161.3 13.4 %collective-permute-start.10 = (bf16[2,2,2,2,2,64,128]{6,5,3,2,0,4,1:T(8,128)(2,1)S(1)}, bf16[2,2,2,2,2,64,128]{6,5,3,2,0,4,1:T(8,128)(2,1)}, u32[]{:S(2)}, u32[]{:S(2)}) collective-permute-start(bf16[2,2,2,2,2,64,128]{6,5,3,2,0,4,1:T(8,128)(2,1)S(1)} %fusion.1), channel_id=1, source_target_pairs={{0,4},{4,0},{8,12},{12,8},{16,20},{20,16},{24,28},{28,24},{32,36},... | collective-permute-start | bytes 1572872 | tf_op jit(solution)/shard_map/ppermute | solution.py:112
  176.0 12.4 %collective-permute-start.11 = (f32[2,2,2,2,64,128]{5,4,2,1,0,3:T(8,128)S(1)}, f32[2,2,2,2,64,128]{5,4,2,1,0,3:T(8,128)S(1)}, u32[]{:S(2)}, u32[]{:S(2)}) collective-permute-start(f32[2,2,2,2,64,128]{5,4,2,1,0,3:T(8,128)S(1)} %dynamic-slice_bitcast_fusion.1), channel_id=1, source_target_pairs={{0,64},{4,68},{8,72},{12,76},{16,80},{20,84},{24,88},{28,92},{32,9... | collective-permute-start | bytes 1572872 | tf_op jit(solution)/shard_map/ppermute | solution.py:112
  188.4 12.3 %collective-permute-start.12 = (f32[2,2,2,64,128]{4,3,2,1,0:T(8,128)S(1)}, f32[2,2,2,64,128]{4,3,2,1,0:T(8,128)S(1)}, u32[]{:S(2)}, u32[]{:S(2)}) collective-permute-start(f32[2,2,2,64,128]{4,3,2,1,0:T(8,128)S(1)} %dynamic-slice_bitcast_fusion.2), channel_id=1, source_target_pairs={{0,8},{4,12},{8,0},{12,4},{16,24},{20,28},{24,16},{28,20},{32,40},... | collective-permute-start | bytes 786440 | tf_op jit(solution)/shard_map/ppermute | solution.py:112
  200.8 6.7 %collective-permute-start.13 = (f32[2,2,64,128]{3,2,1,0:T(8,128)S(1)}, f32[2,2,64,128]{3,2,1,0:T(8,128)S(1)}, u32[]{:S(2)}, u32[]{:S(2)}) collective-permute-start(f32[2,2,64,128]{3,2,1,0:T(8,128)S(1)} %dynamic-slice_bitcast_fusion.3), channel_id=1, source_target_pairs={{0,32},{4,36},{8,40},{12,44},{16,48},{20,52},{24,56},{28,60},{32,0... | collective-permute-start | bytes 393224 | tf_op jit(solution)/shard_map/ppermute | solution.py:112
  207.5 5.9 %collective-permute-start.14 = (f32[2,64,128]{2,1,0:T(8,128)S(1)}, f32[2,64,128]{2,1,0:T(8,128)S(1)}, u32[]{:S(2)}, u32[]{:S(2)}) collective-permute-start(f32[2,64,128]{2,1,0:T(8,128)S(1)} %dynamic-slice_bitcast_fusion.4), channel_id=1, source_target_pairs={{0,128},{4,132},{8,136},{12,140},{16,144},{20,148},{24,152},{28,15... | collective-permute-start | bytes 196616 | tf_op jit(solution)/shard_map/ppermute | solution.py:112
  213.4 7.9 %collective-permute-start.15 = (f32[64,128]{1,0:T(8,128)S(1)}, f32[64,128]{1,0:T(8,128)S(1)}, u32[]{:S(2)}, u32[]{:S(2)}) collective-permute-start(f32[64,128]{1,0:T(8,128)S(1)} %dynamic-slice_bitcast_fusion.5), channel_id=1, source_target_pairs={{0,16},{4,20},{8,24},{12,28},{16,0},{20,4},{24,8},{28,12},{32,48},... | collective-permute-start | bytes 98312 | tf_op jit(solution)/shard_map/ppermute | solution.py:112

commit v6 on v5

--- a/solution.py
+++ b/solution.py
@@ -13,7 +13,7 @@
 D = 128
 I_BLOCK = 8
 P_GROUP = 5
-SMALL_SEND = 131072
+SMALL_SEND = 65536
 
 
 def ladder_kernel(n_p, n_aux, rpp, t_ref, r_ref, l_ref, out_ref, w_ref):
@@ -35,7 +35,7 @@
     apa = A // n_aux
     for i in range(I_BLOCK):
         for q in range(n_aux):
-            out_ref[q, i // rpp, i % rpp] = y[q * apa:(q + 1) * apa, i * B:(i + 1) * B].astype(out_ref.dtype)
+            out_ref[i // rpp, q, i % rpp] = y[q * apa:(q + 1) * apa, i * B:(i + 1) * B].astype(out_ref.dtype)
 
 
 def local_ladder(t_all, factor_ca, factor_db, n_pair, n_aux):
@@ -58,8 +58,8 @@
             pl.BlockSpec((D, n_p * B), lambda g: (0, 0)),
             pl.BlockSpec((A, n_p * C), lambda g: (0, 0)),
         ],
-        out_specs=pl.BlockSpec((n_aux, pb, rpp, apa, B), lambda g: (0, g, 0, 0, 0)),
-        out_shape=jax.ShapeDtypeStruct((n_aux, n_pair, rpp, apa, B), jnp.bfloat16),
+        out_specs=pl.BlockSpec((pb, n_aux, rpp, apa, B), lambda g: (g, 0, 0, 0, 0)),
+        out_shape=jax.ShapeDtypeStruct((n_pair, n_aux, rpp, apa, B), jnp.bfloat16),
         scratch_shapes=[pltpu.VMEM((n_p * C, I_BLOCK * B), jnp.bfloat16)],
         compiler_params=pltpu.CompilerParams(vmem_limit_bytes=48 * 1024 * 1024),
         cost_estimate=pl.CostEstimate(
@@ -69,67 +69,79 @@
     )(t2, r2, l2)
 
 
-def bit_order(axis, n_bits, far_first):
-    if axis == "pair" and n_bits == 6:
-        order = [2, 5, 3, 1, 4, 0]
-    else:
-        order = list(range(n_bits - 1, -1, -1))
-    return order if far_first else order[::-1]
+def two_orders(n_pair, n_aux):
+    if (n_pair, n_aux) == (64, 4):
+        return [0, 1, 2, 6, 3, 5, 7, 4], [0, 2, 1, 3, 6, 7, 5, 4]
+    n_bits = (n_pair * n_aux).bit_length() - 1
+    first = list(range(n_bits))
+    return first, first[1:] + first[:1]
 
 
 def xor_perm(n, b):
     return [(i, i ^ (1 << b)) for i in range(n)]
 
 
-def gather_axis(x, axis, n):
+def gather_bits(x, axes, n, order, target):
     n_bits = n.bit_length() - 1
-    me = lax.axis_index(axis)
-    order = bit_order(axis, n_bits, True)
+    me = lax.axis_index(axes)
     buf = x
     for k, b in enumerate(order):
-        recv = lax.ppermute(buf, axis, xor_perm(n, b))
+        recv = lax.ppermute(buf, axes, xor_perm(n, b))
         low = ((me >> b) & 1) == 0
         lo = jnp.where(low, buf, recv)
         hi = jnp.where(low, recv, buf)
         buf = jnp.stack([lo, hi], axis=k)
-    axes = [order.index(b) for b in range(n_bits - 1, -1, -1)]
-    buf = buf.transpose(axes + list(range(n_bits, buf.ndim)))
-    return buf.reshape((n,) + x.shape)
+    perm = [order.index(b) for b in target]
+    return buf.transpose(perm + list(range(n_bits, buf.ndim)))
 
 
-def reduce_axis(y, axis, n):
+def reduce_bits(y, axes, n, order):
     n_bits = n.bit_length() - 1
-    me = lax.axis_index(axis)
+    me = lax.axis_index(axes)
     blk = y.shape[1:]
     buf = y.reshape((2,) * n_bits + blk)
-    axes = list(range(n_bits - 1, -1, -1))
-    for b in bit_order(axis, n_bits, False):
-        ax = axes.index(b)
+    live = list(range(n_bits - 1, -1, -1))
+    for b in order:
+        ax = live.index(b)
         mine = (me >> b) & 1
         keep = lax.dynamic_index_in_dim(buf, mine, axis=ax, keepdims=False)
         send = lax.dynamic_index_in_dim(buf, 1 - mine, axis=ax, keepdims=False)
         wire = jnp.bfloat16 if send.size > SMALL_SEND else jnp.float32
-        recv = lax.ppermute(send.astype(wire), axis, xor_perm(n, b))
+        recv = lax.ppermute(send.astype(wire), axes, xor_perm(n, b))
         buf = keep.astype(jnp.float32) + recv.astype(jnp.float32)
-        axes.pop(ax)
+        live.pop(ax)
     return buf
 
 
 def local(amplitudes, factor_ca, factor_db):
     n_pair = lax.axis_size("pair")
     n_aux = lax.axis_size("aux")
+    n = n_pair * n_aux
+    both = ("pair", "aux")
+    order_a, order_b = two_orders(n_pair, n_aux)
     rows = amplitudes.shape[0]
     cq = C // n_aux
     q = lax.axis_index("aux")
     amps_q = lax.dynamic_slice_in_dim(amplitudes, q * cq * D, cq * D, axis=1)
-    amps_q = amps_q.reshape(rows * cq, D)
-    t_q = gather_axis(amps_q, "pair", n_pair).reshape(n_pair * rows, cq, D)
-    t_all = gather_axis(t_q, "aux", n_aux)
+    amps_q = amps_q.reshape(rows, cq, D)
+    half = cq // 2
+    n_bits = n.bit_length() - 1
+    aux_bits = n_aux.bit_length() - 1
+    target = list(range(aux_bits - 1, -1, -1)) + list(range(n_bits - 1, aux_bits - 1, -1))
+    t_halves = [
+        gather_bits(amps_q[:, h * half:(h + 1) * half], both, n, order[::-1], target)
+        .reshape(n_aux, n_pair * rows, half, D)
+        for h, order in enumerate((order_a, order_b))
+    ]
+    t_all = jnp.concatenate(t_halves, axis=2)
     y = local_ladder(t_all, factor_ca, factor_db, n_pair, n_aux)
     rpp = y.shape[2]
-    y = y.reshape(n_aux, n_pair, rpp * y.shape[3], B)
-    y = reduce_axis(y, "aux", n_aux)
-    mine = reduce_axis(y, "pair", n_pair).astype(jnp.bfloat16)
+    y = y.reshape(n, rpp * y.shape[3], B)
+    split = y.shape[1] // 2
+    mine = jnp.concatenate([
+        reduce_bits(y[:, h * split:(h + 1) * split], both, n, order)
+        for h, order in enumerate((order_a, order_b))
+    ], axis=0).astype(jnp.bfloat16)
     return mine.reshape(rpp, -1)
 
 

time: 222 us -> 201 us (0.905)
  waiting for transfers between devices: 117 us -> 59.3 us
  starting transfers between devices: 33.2 us -> 63.2 us
  local copies, waits for them, and re-layouts: 12.4 us -> 15.6 us
    ppermute x16 -> x32, waiting for transfers between devices: 117 us -> 59.3 us  [the longest x16 35.6 us: reduce_bits(): recv = lax.ppermute(send.astype(wire), axes, xor_perm(n, b))]
    ppermute x16 -> x32, starting transfers between devices: 33.2 us -> 63.2 us  [the longest x16 33.1 us: gather_bits(): recv = lax.ppermute(buf, axes, xor_perm(n, b))]
    concatenate x0 -> x2, other arithmetic: none -> 2.76 us  [the longest x1 2.75 us: local(): t_all = jnp.concatenate(t_halves, axis=2)]
    unnamed x12 -> x18, local copies, waits for them, and re-layouts: 6.74 us -> 4.72 us
    another operation x16 -> x33, other arithmetic: 6.45 us -> 5.19 us  [the longest x31 5.17 us: gather_bits(): buf = jnp.stack([lo, hi], axis=k)]
    add x7 -> x14, other arithmetic: 6.33 us -> 6.36 us  [reduce_bits(): buf = keep.astype(jnp.float32) + recv.astype(jnp.float32)]
  transfers between devices with their start and end apart: 16 -> 32, of which waited for: 15 -> 22; matrix products, arithmetic and copies ran while one was open for 3% -> 10% of each run, Pallas kernels for 0% -> 0%
where the time goes in v6:
time: 201 us; the launch traced here: 199 us
  starting transfers between devices  63.2 us (31%)
  waiting for transfers between devices  59.3 us (30%)
  Pallas kernels  46.2 us (23%)
  local copies, waits for them, and re-layouts  15.6 us (8%)
  other arithmetic  14.5 us (7%)
    pallas_call x1, Pallas kernels, local_ladder(): pl.pallas_call(kernel, grid=(steps,), in_specs=[pl.BlockSpec((n_aux, I_BL...  46.2 us
    ppermute x16, waiting for transfers between devices, reduce_bits(): recv = lax.ppermute(send.astype(wire), axes, xor_perm(n, b))  35.6 us
    ppermute x16, starting transfers between devices, gather_bits(): recv = lax.ppermute(buf, axes, xor_perm(n, b))  33.1 us
    ppermute x16, starting transfers between devices, reduce_bits(): recv = lax.ppermute(send.astype(wire), axes, xor_perm(n, b))  30.1 us
    ppermute x16, waiting for transfers between devices, gather_bits(): recv = lax.ppermute(buf, axes, xor_perm(n, b))  23.7 us
    add x14, other arithmetic, reduce_bits(): buf = keep.astype(jnp.float32) + recv.astype(jnp.float32)  6.36 us
    another operation x31, other arithmetic, gather_bits(): buf = jnp.stack([lo, hi], axis=k)  5.17 us
    unnamed x18, local copies, waits for them, and re-layouts  4.72 us
  transfers between devices with their start and end apart: 32, of which 22 were waited for; matrix products, arithmetic and copies ran while one was open for 10% of the time, Pallas kernels for 0%

profile of v6, /device:TPU:2, one launch (start us, length us, event | category | flops | bytes accessed | tf_op | source)
XLA Modules:
  0.0 199.4 jit_solution(3096119467425540000)
XLA Ops:
  0.9 7.3 %collective-permute-start = (bf16[2,16,128]{2,1,0:T(8,128)(2,1)S(1)}, bf16[2,16,128]{2,1,0:T(8,128)(2,1)S(1)}, u32[]{:S(2)}, u32[]{:S(2)}) collective-permute-start(bf16[2,16,128]{2,1,0:T(8,128)(2,1)S(1)} %slice.16), channel_id=1, source_target_pairs={{0,16},{1,17},{2,18},{3,19},{4,20},{5,21},{6,22},{7,23},{8,24},{9,... | collective-permute-start | bytes 24584 | tf_op jit(solution)/shard_map/ppermute | solution.py:89
  9.8 5.9 %collective-permute-start.8 = (bf16[2,16,128]{2,1,0:T(8,128)(2,1)S(1)}, bf16[2,16,128]{2,1,0:T(8,128)(2,1)S(1)}, u32[]{:S(2)}, u32[]{:S(2)}) collective-permute-start(bf16[2,16,128]{2,1,0:T(8,128)(2,1)S(1)} %get-tuple-element.41), channel_id=1, source_target_pairs={{0,16},{1,17},{2,18},{3,19},{4,20},{5,21},{6,22},{7,23},{8,24},{9,... | collective-permute-start | bytes 24584 | tf_op jit(solution)/shard_map/ppermute | solution.py:89
  15.7 3.2 %collective-permute-start.1 = (bf16[2,2,16,128]{3,2,1,0:T(8,128)(2,1)S(1)}, bf16[2,2,16,128]{3,2,1,0:T(8,128)(2,1)S(1)}, u32[]{:S(2)}, u32[]{:S(2)}) collective-permute-start(bf16[2,2,16,128]{3,2,1,0:T(8,128)(2,1)S(1)} %pad_maximum_fusion.14), channel_id=1, source_target_pairs={{0,128},{1,129},{2,130},{3,131},{4,132},{5,133},{6,134},{7,135},{8... | collective-permute-start | bytes 49160 | tf_op jit(solution)/shard_map/ppermute | solution.py:89
  18.9 2.2 %collective-permute-start.9 = (bf16[2,2,16,128]{3,2,1,0:T(8,128)(2,1)S(1)}, bf16[2,2,16,128]{3,2,1,0:T(8,128)(2,1)S(1)}, u32[]{:S(2)}, u32[]{:S(2)}) collective-permute-start(bf16[2,2,16,128]{3,2,1,0:T(8,128)(2,1)S(1)} %pad_maximum_fusion.15), channel_id=1, source_target_pairs={{0,32},{1,33},{2,34},{3,35},{4,36},{5,37},{6,38},{7,39},{8,40},{9,... | collective-permute-start | bytes 49160 | tf_op jit(solution)/shard_map/ppermute | solution.py:89
  21.2 2.0 %collective-permute-start.2 = (bf16[2,2,2,16,128]{4,3,2,0,1:T(8,128)(2,1)S(1)}, bf16[2,2,2,16,128]{4,3,2,0,1:T(8,128)(2,1)S(1)}, u32[]{:S(2)}, u32[]{:S(2)}) collective-permute-start(bf16[2,2,2,16,128]{4,3,2,0,1:T(8,128)(2,1)S(1)} %pad_maximum_fusion.12), channel_id=1, source_target_pairs={{0,32},{1,33},{2,34},{3,35},{4,36},{5,37},{6,38},{7,39},{8,40},{9,... | collective-permute-start | bytes 98312 | tf_op jit(solution)/shard_map/ppermute | solution.py:89
  24.3 2.2 %collective-permute-start.10 = (bf16[2,2,2,16,128]{4,3,2,0,1:T(8,128)(2,1)S(1)}, bf16[2,2,2,16,128]{4,3,2,0,1:T(8,128)(2,1)S(1)}, u32[]{:S(2)}, u32[]{:S(2)}) collective-permute-start(bf16[2,2,2,16,128]{4,3,2,0,1:T(8,128)(2,1)S(1)} %pad_maximum_fusion.13), channel_id=1, source_target_pairs={{0,128},{1,129},{2,130},{3,131},{4,132},{5,133},{6,134},{7,135},{8... | collective-permute-start | bytes 98312 | tf_op jit(solution)/shard_map/ppermute | solution.py:89
  30.9 1.7 collective-permute-done.3
  32.7 3.0 %collective-permute-start.4 = (bf16[2,2,2,2,2,16,128]{6,5,4,0,1,3,2:T(8,128)(2,1)S(1)}, bf16[2,2,2,2,2,16,128]{6,5,4,0,1,3,2:T(8,128)(2,1)S(1)}, u32[]{:S(2)}, u32[]{:S(2)}) collective-permute-start(bf16[2,2,2,2,2,16,128]{6,5,4,0,1,3,2:T(8,128)(2,1)S(1)} %pad_maximum_fusion.8), channel_id=1, source_target_pairs={{0,64},{1,65},{2,66},{3,67},{4,68},{5,69},{6,70},{7,71},{8,72},{9,... | collective-permute-start | bytes 393224 | tf_op jit(solution)/shard_map/ppermute | solution.py:89
  35.9 2.8 %collective-permute-done.4 = bf16[2,2,2,2,2,16,128]{6,5,4,0,1,3,2:T(8,128)(2,1)S(1)} collective-permute-done((bf16[2,2,2,2,2,16,128]{6,5,4,0,1,3,2:T(8,128)(2,1)S(1)}, bf16[2,2,2,2,2,16,128]{6,5,4,0,1,3,2:T(8,128)(2,1)S(1)}, u32[]{:S(2)}, u32[]{:S(2)}) %collective-permute-start.4) | collective-permute-done | bytes 131104 | tf_op jit(solution)/shard_map/ppermute | solution.py:89
  38.8 3.4 %collective-permute-done.12 = bf16[2,2,2,2,2,16,128]{6,5,4,0,1,2,3:T(8,128)(2,1)S(1)} collective-permute-done((bf16[2,2,2,2,2,16,128]{6,5,4,0,1,2,3:T(8,128)(2,1)S(1)}, bf16[2,2,2,2,2,16,128]{6,5,4,0,1,2,3:T(8,128)(2,1)S(1)}, u32[]{:S(2)}, u32[]{:S(2)}) %collective-permute-start.12) | collective-permute-done | bytes 131104 | tf_op jit(solution)/shard_map/ppermute | solution.py:89
  43.1 2.9 %collective-permute-done.5 = bf16[2,2,2,2,2,2,16,128]{7,6,5,4,0,1,3,2:T(8,128)(2,1)S(1)} collective-permute-done((bf16[2,2,2,2,2,2,16,128]{7,6,5,4,0,1,3,2:T(8,128)(2,1)S(1)}, bf16[2,2,2,2,2,2,16,128]{7,6,5,4,0,1,3,2:T(8,128)(2,1)S(1)}, u32[]{:S(2)}, u32[]{:S(2)}) %collective-permute-start.5) | collective-permute-done | bytes 262176 | tf_op jit(solution)/shard_map/ppermute | solution.py:89
  46.1 3.2 %collective-permute-start.6 = (bf16[2,2,2,2,2,2,2,16,128]{8,7,6,4,0,1,3,2,5:T(8,128)(2,1)S(1)}, bf16[2,2,2,2,2,2,2,16,128]{8,7,6,4,0,1,3,2,5:T(8,128)(2,1)S(1)}, u32[]{:S(2)}, u32[]{:S(2)}) collective-permute-start(bf16[2,2,2,2,2,2,2,16,128]{8,7,6,4,0,1,3,2,5:T(8,128)(2,1)S(1)} %pad_maximum_fusion.4), channel_id=1, source_target_pairs={{0,2},{1,3},{2,0},{3,1},{4,6},{5,7},{6,4},{7,5},{8,10},{9,11},{10,... | collective-permute-start | bytes 1572872 | tf_op jit(solution)/shard_map/ppermute | solution.py:89
  50.5 6.0 %collective-permute-done.6 = bf16[2,2,2,2,2,2,2,16,128]{8,7,6,4,0,1,3,2,5:T(8,128)(2,1)S(1)} collective-permute-done((bf16[2,2,2,2,2,2,2,16,128]{8,7,6,4,0,1,3,2,5:T(8,128)(2,1)S(1)}, bf16[2,2,2,2,2,2,2,16,128]{8,7,6,4,0,1,3,2,5:T(8,128)(2,1)S(1)}, u32[]{:S(2)}, u32[]{:S(2)}) %collective-permute-start.6) | collective-permute-done | bytes 524320 | tf_op jit(solution)/shard_map/ppermute | solution.py:89
  57.7 1.7 collective-permute-done.14
  70.0 1.9 select_bitcast_fusion.1
  72.1 2.8 %pad_maximum_fusion.t_ref = bf16[4,128,32,128]{3,2,1,0:T(8,128)(2,1)} fusion(bf16[4,128,16,128]{3,2,1,0:T(8,128)(2,1)S(1)} %bitcast.176, bf16[4,128,16,128]{3,2,1,0:T(8,128)(2,1)S(1)} %bitcast.175), kind=kLoop, calls=%fused_computation | loop fusion | flops 8388608 | bytes 8388608 | tf_op jit(solution)/shard_map/concatenate | solution.py:136
  74.9 46.2 %shard_map.37 = bf16[64,4,2,32,128]{4,3,2,1,0:T(8,128)(2,1)S(1)} custom-call(bf16[4,128,32,128]{3,2,1,0:T(8,128)(2,1)} %pad_maximum_fusion.t_ref, bf16[128,3200]{1,0:T(8,128)(2,1)S(1)} %copy.32.r_ref, bf16[128,3200]{1,0:T(8,128)(2,1)S(1)} %copy.33.l_ref), custom_call_target="tpu_custom_call" | custom-call | flops 26843545600 | bytes 10027008 | tf_op jit(solution)/shard_map/pallas_call | solution.py:53
  129.8 1.7 convert_add_fusion
  133.6 8.8 %collective-permute-done.17 = bf16[2,2,2,2,2,2,32,128]{7,6,3,2,0,4,1,5:T(8,128)(2,1)} collective-permute-done((bf16[2,2,2,2,2,2,32,128]{7,6,3,2,0,4,1,5:T(8,128)(2,1)S(1)}, bf16[2,2,2,2,2,2,32,128]{7,6,3,2,0,4,1,5:T(8,128)(2,1)}, u32[]{:S(2)}, u32[]{:S(2)}) %collective-permute-start.17) | collective-permute-done | bytes 524320 | tf_op jit(solution)/shard_map/ppermute | solution.py:110
  144.4 2.9 %collective-permute-done.25 = bf16[2,2,2,2,2,2,32,128]{7,6,5,4,3,2,1,0:T(8,128)(2,1)} collective-permute-done((bf16[2,2,2,2,2,2,32,128]{7,6,5,4,3,2,1,0:T(8,128)(2,1)S(1)}, bf16[2,2,2,2,2,2,32,128]{7,6,5,4,3,2,1,0:T(8,128)(2,1)}, u32[]{:S(2)}, u32[]{:S(2)}) %collective-permute-start.25) | collective-permute-done | bytes 524320 | tf_op jit(solution)/shard_map/ppermute | solution.py:110
  148.6 1.7 collective-permute-start.26
  150.3 1.9 collective-permute-done.18
  153.4 2.1 %collective-permute-done.26 = bf16[2,2,2,2,2,32,128]{6,5,4,3,2,1,0:T(8,128)(2,1)S(1)} collective-permute-done((bf16[2,2,2,2,2,32,128]{6,5,4,3,2,1,0:T(8,128)(2,1)S(1)}, bf16[2,2,2,2,2,32,128]{6,5,4,3,2,1,0:T(8,128)(2,1)S(1)}, u32[]{:S(2)}, u32[]{:S(2)}) %collective-permute-start.26) | collective-permute-done | bytes 262176 | tf_op jit(solution)/shard_map/ppermute | solution.py:110
  156.9 2.8 %collective-permute-done.19 = f32[2,2,2,2,32,128]{5,4,2,1,0,3:T(8,128)S(1)} collective-permute-done((f32[2,2,2,2,32,128]{5,4,2,1,0,3:T(8,128)S(1)}, f32[2,2,2,2,32,128]{5,4,2,1,0,3:T(8,128)S(1)}, u32[]{:S(2)}, u32[]{:S(2)}) %collective-permute-start.19) | collective-permute-done | bytes 262176 | tf_op jit(solution)/shard_map/ppermute | solution.py:110
  161.2 10.3 %collective-permute-done.27 = f32[2,2,2,2,32,128]{5,4,3,2,1,0:T(8,128)S(1)} collective-permute-done((f32[2,2,2,2,32,128]{5,4,3,2,1,0:T(8,128)S(1)}, f32[2,2,2,2,32,128]{5,4,3,2,1,0:T(8,128)S(1)}, u32[]{:S(2)}, u32[]{:S(2)}) %collective-permute-start.27) | collective-permute-done | bytes 262176 | tf_op jit(solution)/shard_map/ppermute | solution.py:110
  173.2 3.0 %collective-permute-start.21 = (f32[2,2,32,128]{3,2,1,0:T(8,128)S(1)}, f32[2,2,32,128]{3,2,1,0:T(8,128)S(1)}, u32[]{:S(2)}, u32[]{:S(2)}) collective-permute-start(f32[2,2,32,128]{3,2,1,0:T(8,128)S(1)} %dynamic-slice_bitcast_fusion.6), channel_id=1, source_target_pairs={{0,32},{1,33},{2,34},{3,35},{4,36},{5,37},{6,38},{7,39},{8,40},{9,... | collective-permute-start | bytes 196616 | tf_op jit(solution)/shard_map/ppermute | solution.py:110
  176.7 3.1 %collective-permute-start.29 = (f32[2,2,32,128]{3,2,1,0:T(8,128)S(1)}, f32[2,2,32,128]{3,2,1,0:T(8,128)S(1)}, u32[]{:S(2)}, u32[]{:S(2)}) collective-permute-start(f32[2,2,32,128]{3,2,1,0:T(8,128)S(1)} %dynamic-slice_bitcast_fusion.5), channel_id=1, source_target_pairs={{0,128},{1,129},{2,130},{3,131},{4,132},{5,133},{6,134},{7,135},{8... | collective-permute-start | bytes 196616 | tf_op jit(solution)/shard_map/ppermute | solution.py:110
  179.8 3.0 %collective-permute-start.22 = (f32[2,32,128]{2,1,0:T(8,128)S(1)}, f32[2,32,128]{2,1,0:T(8,128)S(1)}, u32[]{:S(2)}, u32[]{:S(2)}) collective-permute-start(f32[2,32,128]{2,1,0:T(8,128)S(1)} %dynamic-slice_bitcast_fusion.8), channel_id=1, source_target_pairs={{0,128},{1,129},{2,130},{3,131},{4,132},{5,133},{6,134},{7,135},{8... | collective-permute-start | bytes 98312 | tf_op jit(solution)/shard_map/ppermute | solution.py:110
  182.9 2.3 %collective-permute-start.30 = (f32[2,32,128]{2,1,0:T(8,128)S(1)}, f32[2,32,128]{2,1,0:T(8,128)S(1)}, u32[]{:S(2)}, u32[]{:S(2)}) collective-permute-start(f32[2,32,128]{2,1,0:T(8,128)S(1)} %dynamic-slice_bitcast_fusion.7), channel_id=1, source_target_pairs={{0,32},{1,33},{2,34},{3,35},{4,36},{5,37},{6,38},{7,39},{8,40},{9,... | collective-permute-start | bytes 98312 | tf_op jit(solution)/shard_map/ppermute | solution.py:110
  185.3 5.6 %collective-permute-start.23 = (f32[32,128]{1,0:T(8,128)S(1)}, f32[32,128]{1,0:T(8,128)S(1)}, u32[]{:S(2)}, u32[]{:S(2)}) collective-permute-start(f32[32,128]{1,0:T(8,128)S(1)} %dynamic-slice_bitcast_fusion.10), channel_id=1, source_target_pairs={{0,16},{1,17},{2,18},{3,19},{4,20},{5,21},{6,22},{7,23},{8,24},{9,... | collective-permute-start | bytes 49160 | tf_op jit(solution)/shard_map/ppermute | solution.py:110
  191.0 3.0 %collective-permute-start.31 = (f32[32,128]{1,0:T(8,128)S(1)}, f32[32,128]{1,0:T(8,128)S(1)}, u32[]{:S(2)}, u32[]{:S(2)}) collective-permute-start(f32[32,128]{1,0:T(8,128)S(1)} %dynamic-slice_bitcast_fusion.9), channel_id=1, source_target_pairs={{0,16},{1,17},{2,18},{3,19},{4,20},{5,21},{6,22},{7,23},{8,24},{9,... | collective-permute-start | bytes 49160 | tf_op jit(solution)/shard_map/ppermute | solution.py:110
  194.0 4.7 %collective-permute-done.31 = f32[32,128]{1,0:T(8,128)S(1)} collective-permute-done((f32[32,128]{1,0:T(8,128)S(1)}, f32[32,128]{1,0:T(8,128)S(1)}, u32[]{:S(2)}, u32[]{:S(2)}) %collective-permute-start.31) | collective-permute-done | bytes 16416 | tf_op jit(solution)/shard_map/ppermute | solution.py:110
  (128 shorter events, 43.2 us)
Async XLA Ops:
  0.9 8.9 %collective-permute-start = (bf16[2,16,128]{2,1,0:T(8,128)(2,1)S(1)}, bf16[2,16,128]{2,1,0:T(8,128)(2,1)S(1)}, u32[]{:S(2)}, u32[]{:S(2)}) collective-permute-start(bf16[2,16,128]{2,1,0:T(8,128)(2,1)S(1)} %slice.16), channel_id=1, source_target_pairs={{0,16},{1,17},{2,18},{3,19},{4,20},{5,21},{6,22},{7,23},{8,24},{9,... | collective-permute-start | bytes 24584 | tf_op jit(solution)/shard_map/ppermute | solution.py:89
  9.8 9.1 %collective-permute-start.8 = (bf16[2,16,128]{2,1,0:T(8,128)(2,1)S(1)}, bf16[2,16,128]{2,1,0:T(8,128)(2,1)S(1)}, u32[]{:S(2)}, u32[]{:S(2)}) collective-permute-start(bf16[2,16,128]{2,1,0:T(8,128)(2,1)S(1)} %get-tuple-element.41), channel_id=1, source_target_pairs={{0,16},{1,17},{2,18},{3,19},{4,20},{5,21},{6,22},{7,23},{8,24},{9,... | collective-permute-start | bytes 24584 | tf_op jit(solution)/shard_map/ppermute | solution.py:89
  15.7 5.4 %collective-permute-start.1 = (bf16[2,2,16,128]{3,2,1,0:T(8,128)(2,1)S(1)}, bf16[2,2,16,128]{3,2,1,0:T(8,128)(2,1)S(1)}, u32[]{:S(2)}, u32[]{:S(2)}) collective-permute-start(bf16[2,2,16,128]{3,2,1,0:T(8,128)(2,1)S(1)} %pad_maximum_fusion.14), channel_id=1, source_target_pairs={{0,128},{1,129},{2,130},{3,131},{4,132},{5,133},{6,134},{7,135},{8... | collective-permute-start | bytes 49160 | tf_op jit(solution)/shard_map/ppermute | solution.py:89
  18.9 5.3 %collective-permute-start.9 = (bf16[2,2,16,128]{3,2,1,0:T(8,128)(2,1)S(1)}, bf16[2,2,16,128]{3,2,1,0:T(8,128)(2,1)S(1)}, u32[]{:S(2)}, u32[]{:S(2)}) collective-permute-start(bf16[2,2,16,128]{3,2,1,0:T(8,128)(2,1)S(1)} %pad_maximum_fusion.15), channel_id=1, source_target_pairs={{0,32},{1,33},{2,34},{3,35},{4,36},{5,37},{6,38},{7,39},{8,40},{9,... | collective-permute-start | bytes 49160 | tf_op jit(solution)/shard_map/ppermute | solution.py:89
  21.2 5.5 %collective-permute-start.2 = (bf16[2,2,2,16,128]{4,3,2,0,1:T(8,128)(2,1)S(1)}, bf16[2,2,2,16,128]{4,3,2,0,1:T(8,128)(2,1)S(1)}, u32[]{:S(2)}, u32[]{:S(2)}) collective-permute-start(bf16[2,2,2,16,128]{4,3,2,0,1:T(8,128)(2,1)S(1)} %pad_maximum_fusion.12), channel_id=1, source_target_pairs={{0,32},{1,33},{2,34},{3,35},{4,36},{5,37},{6,38},{7,39},{8,40},{9,... | collective-permute-start | bytes 98312 | tf_op jit(solution)/shard_map/ppermute | solution.py:89
  24.3 5.6 %collective-permute-start.10 = (bf16[2,2,2,16,128]{4,3,2,0,1:T(8,128)(2,1)S(1)}, bf16[2,2,2,16,128]{4,3,2,0,1:T(8,128)(2,1)S(1)}, u32[]{:S(2)}, u32[]{:S(2)}) collective-permute-start(bf16[2,2,2,16,128]{4,3,2,0,1:T(8,128)(2,1)S(1)} %pad_maximum_fusion.13), channel_id=1, source_target_pairs={{0,128},{1,129},{2,130},{3,131},{4,132},{5,133},{6,134},{7,135},{8... | collective-permute-start | bytes 98312 | tf_op jit(solution)/shard_map/ppermute | solution.py:89
  26.7 6.0 %collective-permute-start.3 = (bf16[2,2,2,2,16,128]{5,4,3,0,1,2:T(8,128)(2,1)S(1)}, bf16[2,2,2,2,16,128]{5,4,3,0,1,2:T(8,128)(2,1)S(1)}, u32[]{:S(2)}, u32[]{:S(2)}) collective-permute-start(bf16[2,2,2,2,16,128]{5,4,3,0,1,2:T(8,128)(2,1)S(1)} %pad_maximum_fusion.10), channel_id=1, source_target_pairs={{0,8},{1,9},{2,10},{3,11},{4,12},{5,13},{6,14},{7,15},{8,0},{9,1},... | collective-permute-start | bytes 196616 | tf_op jit(solution)/shard_map/ppermute | solution.py:89
  29.9 5.8 %collective-permute-start.11 = (bf16[2,2,2,2,16,128]{5,4,3,0,1,2:T(8,128)(2,1)S(1)}, bf16[2,2,2,2,16,128]{5,4,3,0,1,2:T(8,128)(2,1)S(1)}, u32[]{:S(2)}, u32[]{:S(2)}) collective-permute-start(bf16[2,2,2,2,16,128]{5,4,3,0,1,2:T(8,128)(2,1)S(1)} %pad_maximum_fusion.11), channel_id=1, source_target_pairs={{0,64},{1,65},{2,66},{3,67},{4,68},{5,69},{6,70},{7,71},{8,72},{9,... | collective-permute-start | bytes 196616 | tf_op jit(solution)/shard_map/ppermute | solution.py:89
  32.7 6.0 %collective-permute-start.4 = (bf16[2,2,2,2,2,16,128]{6,5,4,0,1,3,2:T(8,128)(2,1)S(1)}, bf16[2,2,2,2,2,16,128]{6,5,4,0,1,3,2:T(8,128)(2,1)S(1)}, u32[]{:S(2)}, u32[]{:S(2)}) collective-permute-start(bf16[2,2,2,2,2,16,128]{6,5,4,0,1,3,2:T(8,128)(2,1)S(1)} %pad_maximum_fusion.8), channel_id=1, source_target_pairs={{0,64},{1,65},{2,66},{3,67},{4,68},{5,69},{6,70},{7,71},{8,72},{9,... | collective-permute-start | bytes 393224 | tf_op jit(solution)/shard_map/ppermute | solution.py:89
  35.8 6.5 %collective-permute-start.12 = (bf16[2,2,2,2,2,16,128]{6,5,4,0,1,2,3:T(8,128)(2,1)S(1)}, bf16[2,2,2,2,2,16,128]{6,5,4,0,1,2,3:T(8,128)(2,1)S(1)}, u32[]{:S(2)}, u32[]{:S(2)}) collective-permute-start(bf16[2,2,2,2,2,16,128]{6,5,4,0,1,2,3:T(8,128)(2,1)S(1)} %pad_maximum_fusion.9), channel_id=1, source_target_pairs={{0,8},{1,9},{2,10},{3,11},{4,12},{5,13},{6,14},{7,15},{8,0},{9,1},... | collective-permute-start | bytes 393224 | tf_op jit(solution)/shard_map/ppermute | solution.py:89
  38.7 7.3 %collective-permute-start.5 = (bf16[2,2,2,2,2,2,16,128]{7,6,5,4,0,1,3,2:T(8,128)(2,1)S(1)}, bf16[2,2,2,2,2,2,16,128]{7,6,5,4,0,1,3,2:T(8,128)(2,1)S(1)}, u32[]{:S(2)}, u32[]{:S(2)}) collective-permute-start(bf16[2,2,2,2,2,2,16,128]{7,6,5,4,0,1,3,2:T(8,128)(2,1)S(1)} %pad_maximum_fusion.6), channel_id=1, source_target_pairs={{0,4},{1,5},{2,6},{3,7},{4,0},{5,1},{6,2},{7,3},{8,12},{9,13},{10,... | collective-permute-start | bytes 786440 | tf_op jit(solution)/shard_map/ppermute | solution.py:89
  42.3 7.7 %collective-permute-start.13 = (bf16[2,2,2,2,2,2,16,128]{7,6,5,0,1,2,3,4:T(8,128)(2,1)S(1)}, bf16[2,2,2,2,2,2,16,128]{7,6,5,0,1,2,3,4:T(8,128)(2,1)S(1)}, u32[]{:S(2)}, u32[]{:S(2)}) collective-permute-start(bf16[2,2,2,2,2,2,16,128]{7,6,5,0,1,2,3,4:T(8,128)(2,1)S(1)} %pad_maximum_fusion.7), channel_id=1, source_target_pairs={{0,2},{1,3},{2,0},{3,1},{4,6},{5,7},{6,4},{7,5},{8,10},{9,11},{10,... | collective-permute-start | bytes 786440 | tf_op jit(solution)/shard_map/ppermute | solution.py:89
  46.1 10.4 %collective-permute-start.6 = (bf16[2,2,2,2,2,2,2,16,128]{8,7,6,4,0,1,3,2,5:T(8,128)(2,1)S(1)}, bf16[2,2,2,2,2,2,2,16,128]{8,7,6,4,0,1,3,2,5:T(8,128)(2,1)S(1)}, u32[]{:S(2)}, u32[]{:S(2)}) collective-permute-start(bf16[2,2,2,2,2,2,2,16,128]{8,7,6,4,0,1,3,2,5:T(8,128)(2,1)S(1)} %pad_maximum_fusion.4), channel_id=1, source_target_pairs={{0,2},{1,3},{2,0},{3,1},{4,6},{5,7},{6,4},{7,5},{8,10},{9,11},{10,... | collective-permute-start | bytes 1572872 | tf_op jit(solution)/shard_map/ppermute | solution.py:89
  50.1 9.3 %collective-permute-start.14 = (bf16[2,2,2,2,2,2,2,16,128]{8,7,6,0,1,2,3,4,5:T(8,128)(2,1)S(1)}, bf16[2,2,2,2,2,2,2,16,128]{8,7,6,0,1,2,3,4,5:T(8,128)(2,1)S(1)}, u32[]{:S(2)}, u32[]{:S(2)}) collective-permute-start(bf16[2,2,2,2,2,2,2,16,128]{8,7,6,0,1,2,3,4,5:T(8,128)(2,1)S(1)} %pad_maximum_fusion.5), channel_id=1, source_target_pairs={{0,4},{1,5},{2,6},{3,7},{4,0},{5,1},{6,2},{7,3},{8,12},{9,13},{10,... | collective-permute-start | bytes 1572872 | tf_op jit(solution)/shard_map/ppermute | solution.py:89
  57.7 9.7 %collective-permute-start.7 = (bf16[2,2,2,2,2,2,2,2,16,128]{9,8,7,6,4,0,1,3,2,5:T(8,128)(2,1)}, bf16[2,2,2,2,2,2,2,2,16,128]{9,8,7,6,4,0,1,3,2,5:T(8,128)(2,1)}, u32[]{:S(2)}, u32[]{:S(2)}) collective-permute-start(bf16[2,2,2,2,2,2,2,2,16,128]{9,8,7,6,4,0,1,3,2,5:T(8,128)(2,1)} %pad_maximum_fusion.2), channel_id=1, source_target_pairs={{0,1},{1,0},{2,3},{3,2},{4,5},{5,4},{6,7},{7,6},{8,9},{9,8},{10,11... | collective-permute-start | bytes 3145736 | tf_op jit(solution)/shard_map/ppermute | solution.py:89
  60.8 8.9 %collective-permute-start.15 = (bf16[2,2,2,2,2,2,2,2,16,128]{9,8,7,6,4,0,1,3,2,5:T(8,128)(2,1)}, bf16[2,2,2,2,2,2,2,2,16,128]{9,8,7,6,4,0,1,3,2,5:T(8,128)(2,1)}, u32[]{:S(2)}, u32[]{:S(2)}) collective-permute-start(bf16[2,2,2,2,2,2,2,2,16,128]{9,8,7,6,4,0,1,3,2,5:T(8,128)(2,1)} %copy.36), channel_id=1, source_target_pairs={{0,1},{1,0},{2,3},{3,2},{4,5},{5,4},{6,7},{7,6},{8,9},{9,8},{10,11... | collective-permute-start | bytes 3145736 | tf_op jit(solution)/shard_map/ppermute | solution.py:89
  123.5 3.0 %collective-permute-start.16 = (bf16[2,2,2,2,2,2,2,32,128]{8,7,3,2,0,4,1,5,6:T(8,128)(2,1)}, bf16[2,2,2,2,2,2,2,32,128]{8,7,3,2,0,4,1,5,6:T(8,128)(2,1)}, u32[]{:S(2)}, u32[]{:S(2)}) collective-permute-start(bf16[2,2,2,2,2,2,2,32,128]{8,7,3,2,0,4,1,5,6:T(8,128)(2,1)} %bitcast.169), channel_id=1, source_target_pairs={{0,1},{1,0},{2,3},{3,2},{4,5},{5,4},{6,7},{7,6},{8,9},{9,8},{10,11... | collective-permute-start | bytes 3145736 | tf_op jit(solution)/shard_map/ppermute | solution.py:110
  124.7 5.1 %collective-permute-start.24 = (bf16[2,2,2,2,2,2,2,32,128]{8,7,6,5,4,3,2,1,0:T(8,128)(2,1)}, bf16[2,2,2,2,2,2,2,32,128]{8,7,6,5,4,3,2,1,0:T(8,128)(2,1)}, u32[]{:S(2)}, u32[]{:S(2)}) collective-permute-start(bf16[2,2,2,2,2,2,2,32,128]{8,7,6,5,4,3,2,1,0:T(8,128)(2,1)} %dynamic-slice_bitcast_fusion), channel_id=1, source_target_pairs={{0,1},{1,0},{2,3},{3,2},{4,5},{5,4},{6,7},{7,6},{8,9},{9,8},{10,11... | collective-permute-start | bytes 3145736 | tf_op jit(solution)/shard_map/ppermute | solution.py:110
  128.2 14.2 %collective-permute-start.17 = (bf16[2,2,2,2,2,2,32,128]{7,6,3,2,0,4,1,5:T(8,128)(2,1)S(1)}, bf16[2,2,2,2,2,2,32,128]{7,6,3,2,0,4,1,5:T(8,128)(2,1)}, u32[]{:S(2)}, u32[]{:S(2)}) collective-permute-start(bf16[2,2,2,2,2,2,32,128]{7,6,3,2,0,4,1,5:T(8,128)(2,1)S(1)} %fusion), channel_id=1, source_target_pairs={{0,2},{1,3},{2,0},{3,1},{4,6},{5,7},{6,4},{7,5},{8,10},{9,11},{10,... | collective-permute-start | bytes 1572872 | tf_op jit(solution)/shard_map/ppermute | solution.py:110
  132.9 14.4 %collective-permute-start.25 = (bf16[2,2,2,2,2,2,32,128]{7,6,5,4,3,2,1,0:T(8,128)(2,1)S(1)}, bf16[2,2,2,2,2,2,32,128]{7,6,5,4,3,2,1,0:T(8,128)(2,1)}, u32[]{:S(2)}, u32[]{:S(2)}) collective-permute-start(bf16[2,2,2,2,2,2,32,128]{7,6,5,4,3,2,1,0:T(8,128)(2,1)S(1)} %fusion.1), channel_id=1, source_target_pairs={{0,4},{1,5},{2,6},{3,7},{4,0},{5,1},{6,2},{7,3},{8,12},{9,13},{10,... | collective-permute-start | bytes 1572872 | tf_op jit(solution)/shard_map/ppermute | solution.py:110
  144.0 8.3 %collective-permute-start.18 = (bf16[2,2,2,2,2,32,128]{6,5,3,2,0,4,1:T(8,128)(2,1)S(1)}, bf16[2,2,2,2,2,32,128]{6,5,3,2,0,4,1:T(8,128)(2,1)S(1)}, u32[]{:S(2)}, u32[]{:S(2)}) collective-permute-start(bf16[2,2,2,2,2,32,128]{6,5,3,2,0,4,1:T(8,128)(2,1)S(1)} %fusion.2), channel_id=1, source_target_pairs={{0,4},{1,5},{2,6},{3,7},{4,0},{5,1},{6,2},{7,3},{8,12},{9,13},{10,... | collective-permute-start | bytes 786440 | tf_op jit(solution)/shard_map/ppermute | solution.py:110
  148.6 6.9 %collective-permute-start.26 = (bf16[2,2,2,2,2,32,128]{6,5,4,3,2,1,0:T(8,128)(2,1)S(1)}, bf16[2,2,2,2,2,32,128]{6,5,4,3,2,1,0:T(8,128)(2,1)S(1)}, u32[]{:S(2)}, u32[]{:S(2)}) collective-permute-start(bf16[2,2,2,2,2,32,128]{6,5,4,3,2,1,0:T(8,128)(2,1)S(1)} %fusion.3), channel_id=1, source_target_pairs={{0,2},{1,3},{2,0},{3,1},{4,6},{5,7},{6,4},{7,5},{8,10},{9,11},{10,... | collective-permute-start | bytes 786440 | tf_op jit(solution)/shard_map/ppermute | solution.py:110
  152.4 7.3 %collective-permute-start.19 = (f32[2,2,2,2,32,128]{5,4,2,1,0,3:T(8,128)S(1)}, f32[2,2,2,2,32,128]{5,4,2,1,0,3:T(8,128)S(1)}, u32[]{:S(2)}, u32[]{:S(2)}) collective-permute-start(f32[2,2,2,2,32,128]{5,4,2,1,0,3:T(8,128)S(1)} %dynamic-slice_bitcast_fusion.2), channel_id=1, source_target_pairs={{0,64},{1,65},{2,66},{3,67},{4,68},{5,69},{6,70},{7,71},{8,72},{9,... | collective-permute-start | bytes 786440 | tf_op jit(solution)/shard_map/ppermute | solution.py:110
  155.6 15.8 %collective-permute-start.27 = (f32[2,2,2,2,32,128]{5,4,3,2,1,0:T(8,128)S(1)}, f32[2,2,2,2,32,128]{5,4,3,2,1,0:T(8,128)S(1)}, u32[]{:S(2)}, u32[]{:S(2)}) collective-permute-start(f32[2,2,2,2,32,128]{5,4,3,2,1,0:T(8,128)S(1)} %dynamic-slice_bitcast_fusion.1), channel_id=1, source_target_pairs={{0,8},{1,9},{2,10},{3,11},{4,12},{5,13},{6,14},{7,15},{8,0},{9,1},... | collective-permute-start | bytes 786440 | tf_op jit(solution)/shard_map/ppermute | solution.py:110
  159.8 13.4 %collective-permute-start.20 = (f32[2,2,2,32,128]{4,3,2,1,0:T(8,128)S(1)}, f32[2,2,2,32,128]{4,3,2,1,0:T(8,128)S(1)}, u32[]{:S(2)}, u32[]{:S(2)}) collective-permute-start(f32[2,2,2,32,128]{4,3,2,1,0:T(8,128)S(1)} %dynamic-slice_bitcast_fusion.4), channel_id=1, source_target_pairs={{0,8},{1,9},{2,10},{3,11},{4,12},{5,13},{6,14},{7,15},{8,0},{9,1},... | collective-permute-start | bytes 393224 | tf_op jit(solution)/shard_map/ppermute | solution.py:110
  171.6 5.1 %collective-permute-start.28 = (f32[2,2,2,32,128]{4,3,2,1,0:T(8,128)S(1)}, f32[2,2,2,32,128]{4,3,2,1,0:T(8,128)S(1)}, u32[]{:S(2)}, u32[]{:S(2)}) collective-permute-start(f32[2,2,2,32,128]{4,3,2,1,0:T(8,128)S(1)} %dynamic-slice_bitcast_fusion.3), channel_id=1, source_target_pairs={{0,64},{1,65},{2,66},{3,67},{4,68},{5,69},{6,70},{7,71},{8,72},{9,... | collective-permute-start | bytes 393224 | tf_op jit(solution)/shard_map/ppermute | solution.py:110
  173.2 6.6 %collective-permute-start.21 = (f32[2,2,32,128]{3,2,1,0:T(8,128)S(1)}, f32[2,2,32,128]{3,2,1,0:T(8,128)S(1)}, u32[]{:S(2)}, u32[]{:S(2)}) collective-permute-start(f32[2,2,32,128]{3,2,1,0:T(8,128)S(1)} %dynamic-slice_bitcast_fusion.6), channel_id=1, source_target_pairs={{0,32},{1,33},{2,34},{3,35},{4,36},{5,37},{6,38},{7,39},{8,40},{9,... | collective-permute-start | bytes 196616 | tf_op jit(solution)/shard_map/ppermute | solution.py:110
  176.7 6.2 %collective-permute-start.29 = (f32[2,2,32,128]{3,2,1,0:T(8,128)S(1)}, f32[2,2,32,128]{3,2,1,0:T(8,128)S(1)}, u32[]{:S(2)}, u32[]{:S(2)}) collective-permute-start(f32[2,2,32,128]{3,2,1,0:T(8,128)S(1)} %dynamic-slice_bitcast_fusion.5), channel_id=1, source_target_pairs={{0,128},{1,129},{2,130},{3,131},{4,132},{5,133},{6,134},{7,135},{8... | collective-permute-start | bytes 196616 | tf_op jit(solution)/shard_map/ppermute | solution.py:110
  179.8 5.5 %collective-permute-start.22 = (f32[2,32,128]{2,1,0:T(8,128)S(1)}, f32[2,32,128]{2,1,0:T(8,128)S(1)}, u32[]{:S(2)}, u32[]{:S(2)}) collective-permute-start(f32[2,32,128]{2,1,0:T(8,128)S(1)} %dynamic-slice_bitcast_fusion.8), channel_id=1, source_target_pairs={{0,128},{1,129},{2,130},{3,131},{4,132},{5,133},{6,134},{7,135},{8... | collective-permute-start | bytes 98312 | tf_op jit(solution)/shard_map/ppermute | solution.py:110
  182.9 8.1 %collective-permute-start.30 = (f32[2,32,128]{2,1,0:T(8,128)S(1)}, f32[2,32,128]{2,1,0:T(8,128)S(1)}, u32[]{:S(2)}, u32[]{:S(2)}) collective-permute-start(f32[2,32,128]{2,1,0:T(8,128)S(1)} %dynamic-slice_bitcast_fusion.7), channel_id=1, source_target_pairs={{0,32},{1,33},{2,34},{3,35},{4,36},{5,37},{6,38},{7,39},{8,40},{9,... | collective-permute-start | bytes 98312 | tf_op jit(solution)/shard_map/ppermute | solution.py:110
  185.3 8.7 %collective-permute-start.23 = (f32[32,128]{1,0:T(8,128)S(1)}, f32[32,128]{1,0:T(8,128)S(1)}, u32[]{:S(2)}, u32[]{:S(2)}) collective-permute-start(f32[32,128]{1,0:T(8,128)S(1)} %dynamic-slice_bitcast_fusion.10), channel_id=1, source_target_pairs={{0,16},{1,17},{2,18},{3,19},{4,20},{5,21},{6,22},{7,23},{8,24},{9,... | collective-permute-start | bytes 49160 | tf_op jit(solution)/shard_map/ppermute | solution.py:110
  191.0 7.7 %collective-permute-start.31 = (f32[32,128]{1,0:T(8,128)S(1)}, f32[32,128]{1,0:T(8,128)S(1)}, u32[]{:S(2)}, u32[]{:S(2)}) collective-permute-start(f32[32,128]{1,0:T(8,128)S(1)} %dynamic-slice_bitcast_fusion.9), channel_id=1, source_target_pairs={{0,16},{1,17},{2,18},{3,19},{4,20},{5,21},{6,22},{7,23},{8,24},{9,... | collective-permute-start | bytes 49160 | tf_op jit(solution)/shard_map/ppermute | solution.py:110
  (7 other events, 22.5 us)

commit v7 on v3

--- a/solution.py
+++ b/solution.py
@@ -13,6 +13,7 @@
 D = 128
 I_BLOCK = 8
 P_GROUP = 5
+SMALL_SEND = 65536
 
 
 def ladder_kernel(n_p, n_aux, rpp, t_ref, r_ref, l_ref, out_ref, w_ref):
@@ -34,7 +35,7 @@
     apa = A // n_aux
     for i in range(I_BLOCK):
         for q in range(n_aux):
-            out_ref[q, i // rpp, i % rpp] = y[q * apa:(q + 1) * apa, i * B:(i + 1) * B]
+            out_ref[i // rpp, q, i % rpp] = y[q * apa:(q + 1) * apa, i * B:(i + 1) * B].astype(out_ref.dtype)
 
 
 def local_ladder(t_all, factor_ca, factor_db, n_pair, n_aux):
@@ -57,32 +58,110 @@
             pl.BlockSpec((D, n_p * B), lambda g: (0, 0)),
             pl.BlockSpec((A, n_p * C), lambda g: (0, 0)),
         ],
-        out_specs=pl.BlockSpec((n_aux, pb, rpp, apa, B), lambda g: (0, g, 0, 0, 0)),
-        out_shape=jax.ShapeDtypeStruct((n_aux, n_pair, rpp, apa, B), jnp.float32),
+        out_specs=pl.BlockSpec((pb, n_aux, rpp, apa, B), lambda g: (g, 0, 0, 0, 0)),
+        out_shape=jax.ShapeDtypeStruct((n_pair, n_aux, rpp, apa, B), jnp.bfloat16),
         scratch_shapes=[pltpu.VMEM((n_p * C, I_BLOCK * B), jnp.bfloat16)],
         compiler_params=pltpu.CompilerParams(vmem_limit_bytes=48 * 1024 * 1024),
         cost_estimate=pl.CostEstimate(
             flops=flops, transcendentals=0,
-            bytes_accessed=2 * (t2.size + r2.size + l2.size) + 4 * nij * A * B,
+            bytes_accessed=2 * (t2.size + r2.size + l2.size) + 2 * nij * A * B,
         ),
     )(t2, r2, l2)
+
+
+def plan(n_pair, n_aux):
+    if (n_pair, n_aux) == (64, 4):
+        return [0], ([1, 2], [2, 1]), [6, 3, 5, 7, 4]
+    n_bits = (n_pair * n_aux).bit_length() - 1
+    rest = list(range(2, n_bits))
+    return [0], ([1], [1]), rest
+
+
+def xor_perm(n, b):
+    return [(i, i ^ (1 << b)) for i in range(n)]
+
+
+def gather_step(buf, axes, n, me, b, k):
+    recv = lax.ppermute(buf, axes, xor_perm(n, b))
+    low = ((me >> b) & 1) == 0
+    lo = jnp.where(low, buf, recv)
+    hi = jnp.where(low, recv, buf)
+    return jnp.stack([lo, hi], axis=k)
+
+
+def gather_bits(x, axes, n, first, pair_orders, last, target, split_axis):
+    n_bits = n.bit_length() - 1
+    me = lax.axis_index(axes)
+    buf = x
+    for k, b in enumerate(first):
+        buf = gather_step(buf, axes, n, me, b, k)
+    ax = len(first) + split_axis
+    size = buf.shape[ax] // 2
+    halves = []
+    for h, tail in enumerate(pair_orders):
+        part = lax.slice_in_dim(buf, h * size, (h + 1) * size, axis=ax)
+        order = first + tail + last
+        for k, b in enumerate(tail + last):
+            part = gather_step(part, axes, n, me, b, len(first) + k)
+        perm = [order.index(b) for b in target]
+        halves.append(part.transpose(perm + list(range(n_bits, part.ndim))))
+    return jnp.concatenate(halves, axis=n_bits + split_axis)
+
+
+def reduce_step(buf, axes, n, me, live, b):
+    ax = live.index(b)
+    mine = (me >> b) & 1
+    keep = lax.dynamic_index_in_dim(buf, mine, axis=ax, keepdims=False)
+    send = lax.dynamic_index_in_dim(buf, 1 - mine, axis=ax, keepdims=False)
+    wire = jnp.bfloat16 if send.size > SMALL_SEND else jnp.float32
+    recv = lax.ppermute(send.astype(wire), axes, xor_perm(n, b))
+    live.pop(ax)
+    return keep.astype(jnp.float32) + recv.astype(jnp.float32)
+
+
+def reduce_bits(y, axes, n, first, pair_orders, last):
+    n_bits = n.bit_length() - 1
+    me = lax.axis_index(axes)
+    buf = y.reshape((2,) * n_bits + y.shape[1:])
+    live = list(range(n_bits - 1, -1, -1))
+    for b in first:
+        buf = reduce_step(buf, axes, n, me, live, b)
+    ax = len(live)
+    size = buf.shape[ax] // 2
+    halves = []
+    for order in pair_orders:
+        part = lax.slice_in_dim(buf, size * len(halves), size * (len(halves) + 1), axis=ax)
+        part_live = list(live)
+        for b in order:
+            part = reduce_step(part, axes, n, me, part_live, b)
+        halves.append(part)
+    live = part_live
+    buf = jnp.concatenate(halves, axis=len(live))
+    for b in last:
+        buf = reduce_step(buf, axes, n, me, live, b)
+    return buf
 
 
 def local(amplitudes, factor_ca, factor_db):
     n_pair = lax.axis_size("pair")
     n_aux = lax.axis_size("aux")
+    n = n_pair * n_aux
+    both = ("pair", "aux")
+    first, pair_orders, last = plan(n_pair, n_aux)
+    rows = amplitudes.shape[0]
     cq = C // n_aux
     q = lax.axis_index("aux")
     amps_q = lax.dynamic_slice_in_dim(amplitudes, q * cq * D, cq * D, axis=1)
-    amps_q = amps_q.reshape(amplitudes.shape[0], cq, D)
-    t_q = lax.all_gather(amps_q, "pair", axis=0, tiled=True)
-    t_all = lax.all_gather(t_q, "aux", axis=0)
+    amps_q = amps_q.reshape(rows, cq, D)
+    n_bits = n.bit_length() - 1
+    aux_bits = n_aux.bit_length() - 1
+    target = list(range(aux_bits - 1, -1, -1)) + list(range(n_bits - 1, aux_bits - 1, -1))
+    t_all = gather_bits(amps_q, both, n, last[::-1], [o[::-1] for o in pair_orders], first[::-1], target, 1)
+    t_all = t_all.reshape(n_aux, n_pair * rows, cq, D)
     y = local_ladder(t_all, factor_ca, factor_db, n_pair, n_aux)
     rpp = y.shape[2]
-    y = y.reshape(n_aux, n_pair, rpp * y.shape[3], B)
-    y = lax.psum_scatter(y, "aux", scatter_dimension=0, tiled=True)
-    parts = lax.all_to_all(y[0], "pair", split_axis=0, concat_axis=0, tiled=True)
-    mine = jnp.sum(parts, axis=0).astype(jnp.bfloat16)
+    y = y.reshape(n, rpp * y.shape[3], B)
+    mine = reduce_bits(y, both, n, first, pair_orders, last).astype(jnp.bfloat16)
     return mine.reshape(rpp, -1)
 
 

time: 380 us -> 197 us (0.52)
  waiting for transfers between devices: 244 us -> 79.2 us
  blocking collectives: 66.4 us -> 0 us
  starting transfers between devices: 0.08 us -> 39 us
  other arithmetic: 0.14 us -> 15.5 us
  between operations: 13.2 us -> 0.39 us
  local copies, waits for them, and re-layouts: 8.76 us -> 16 us
    all_gather x2 -> x0, waiting for transfers between devices: 162 us -> none  [the longest x1 119 us: local(): t_q = lax.all_gather(amps_q, 'pair', axis=0, tiled=True)]
    reduce_scatter x1 -> x0, waiting for transfers between devices: 82.7 us -> none  [local(): y = lax.psum_scatter(y, 'aux', scatter_dimension=0, tiled=True)]
    ppermute x0 -> x21, waiting for transfers between devices: none -> 79.2 us  [the longest x10 45.4 us: reduce_step(): recv = lax.ppermute(send.astype(wire), axes, xor_perm(n, b))]
    all_to_all x1 -> x0, blocking collectives: 66.4 us -> none  [local(): lax.all_to_all(y[0], 'pair', split_axis=0, concat_axis=0, tiled=True)]
    ppermute x0 -> x21, starting transfers between devices: none -> 39 us  [the longest x10 19.7 us: reduce_step(): recv = lax.ppermute(send.astype(wire), axes, xor_perm(n, b))]
    add x0 -> x9, other arithmetic: none -> 7.31 us  [reduce_step(): return keep.astype(jnp.float32) + recv.astype(jnp.float32)]
    another operation x0 -> x20, other arithmetic: none -> 5.44 us  [gather_step(): return jnp.stack([lo, hi], axis=k)]
    unnamed x10 -> x18, local copies, waits for them, and re-layouts: 5.35 us -> 8.16 us
  transfers between devices with their start and end apart: 3 -> 21, of which waited for: 3 -> 17; matrix products, arithmetic and copies ran while one was open for 1% -> 8% of each run, Pallas kernels for 0% -> 0%
where the time goes in v7:
time: 197 us; the launch traced here: 196 us
  waiting for transfers between devices  79.2 us (40%)
  Pallas kernels  46.2 us (23%)
  starting transfers between devices  39 us (20%)
  local copies, waits for them, and re-layouts  16 us (8%)
  other arithmetic  15.5 us (8%)
    pallas_call x1, Pallas kernels, local_ladder(): pl.pallas_call(kernel, grid=(steps,), in_specs=[pl.BlockSpec((n_aux, I_BL...  46.2 us
    ppermute x10, waiting for transfers between devices, reduce_step(): recv = lax.ppermute(send.astype(wire), axes, xor_perm(n, b))  45.4 us
    ppermute x11, waiting for transfers between devices, gather_step(): recv = lax.ppermute(buf, axes, xor_perm(n, b))  33.7 us
    ppermute x10, starting transfers between devices, reduce_step(): recv = lax.ppermute(send.astype(wire), axes, xor_perm(n, b))  19.7 us
    ppermute x11, starting transfers between devices, gather_step(): recv = lax.ppermute(buf, axes, xor_perm(n, b))  19.3 us
    unnamed x18, local copies, waits for them, and re-layouts  8.16 us
    add x9, other arithmetic, reduce_step(): return keep.astype(jnp.float32) + recv.astype(jnp.float32)  7.31 us
    another operation x20, other arithmetic, gather_step(): return jnp.stack([lo, hi], axis=k)  5.44 us
  transfers between devices with their start and end apart: 21, of which 17 were waited for; matrix products, arithmetic and copies ran while one was open for 8% of the time, Pallas kernels for 0%

profile of v7, /device:TPU:2, one launch (start us, length us, event | category | flops | bytes accessed | tf_op | source)
XLA Modules:
  0.0 196.3 jit_solution(15370389671116905270)
XLA Ops:
  0.9 7.3 %collective-permute-start = (bf16[2,32,128]{2,1,0:T(8,128)(2,1)S(1)}, bf16[2,32,128]{2,1,0:T(8,128)(2,1)S(1)}, u32[]{:S(2)}, u32[]{:S(2)}) collective-permute-start(bf16[2,32,128]{2,1,0:T(8,128)(2,1)S(1)} %bitcast.143), channel_id=1, source_target_pairs={{0,16},{1,17},{2,18},{3,19},{4,20},{5,21},{6,22},{7,23},{8,24},{9,... | collective-permute-start | bytes 49160 | tf_op jit(solution)/shard_map/ppermute | solution.py:85
  8.1 1.7 collective-permute-done
  9.9 3.3 %collective-permute-start.1 = (bf16[2,2,32,128]{3,2,1,0:T(8,128)(2,1)S(1)}, bf16[2,2,32,128]{3,2,1,0:T(8,128)(2,1)S(1)}, u32[]{:S(2)}, u32[]{:S(2)}) collective-permute-start(bf16[2,2,32,128]{3,2,1,0:T(8,128)(2,1)S(1)} %pad_maximum_fusion.9), channel_id=1, source_target_pairs={{0,128},{1,129},{2,130},{3,131},{4,132},{5,133},{6,134},{7,135},{8... | collective-permute-start | bytes 98312 | tf_op jit(solution)/shard_map/ppermute | solution.py:85
  13.2 2.2 %collective-permute-done.1 = bf16[2,2,32,128]{3,2,1,0:T(8,128)(2,1)S(1)} collective-permute-done((bf16[2,2,32,128]{3,2,1,0:T(8,128)(2,1)S(1)}, bf16[2,2,32,128]{3,2,1,0:T(8,128)(2,1)S(1)}, u32[]{:S(2)}, u32[]{:S(2)}) %collective-permute-start.1) | collective-permute-done | bytes 32800 | tf_op jit(solution)/shard_map/ppermute | solution.py:85
  15.4 2.2 %collective-permute-start.2 = (bf16[2,2,2,32,128]{4,3,2,0,1:T(8,128)(2,1)S(1)}, bf16[2,2,2,32,128]{4,3,2,0,1:T(8,128)(2,1)S(1)}, u32[]{:S(2)}, u32[]{:S(2)}) collective-permute-start(bf16[2,2,2,32,128]{4,3,2,0,1:T(8,128)(2,1)S(1)} %pad_maximum_fusion.8), channel_id=1, source_target_pairs={{0,32},{1,33},{2,34},{3,35},{4,36},{5,37},{6,38},{7,39},{8,40},{9,... | collective-permute-start | bytes 196616 | tf_op jit(solution)/shard_map/ppermute | solution.py:85
  17.6 3.6 %collective-permute-done.2 = bf16[2,2,2,32,128]{4,3,2,0,1:T(8,128)(2,1)S(1)} collective-permute-done((bf16[2,2,2,32,128]{4,3,2,0,1:T(8,128)(2,1)S(1)}, bf16[2,2,2,32,128]{4,3,2,0,1:T(8,128)(2,1)S(1)}, u32[]{:S(2)}, u32[]{:S(2)}) %collective-permute-start.2) | collective-permute-done | bytes 65568 | tf_op jit(solution)/shard_map/ppermute | solution.py:85
  21.3 2.1 %collective-permute-start.3 = (bf16[2,2,2,2,32,128]{5,4,3,0,2,1:T(8,128)(2,1)S(1)}, bf16[2,2,2,2,32,128]{5,4,3,0,2,1:T(8,128)(2,1)S(1)}, u32[]{:S(2)}, u32[]{:S(2)}) collective-permute-start(bf16[2,2,2,2,32,128]{5,4,3,0,2,1:T(8,128)(2,1)S(1)} %pad_maximum_fusion.7), channel_id=1, source_target_pairs={{0,8},{1,9},{2,10},{3,11},{4,12},{5,13},{6,14},{7,15},{8,0},{9,1},... | collective-permute-start | bytes 393224 | tf_op jit(solution)/shard_map/ppermute | solution.py:85
  23.4 5.3 %collective-permute-done.3 = bf16[2,2,2,2,32,128]{5,4,3,0,2,1:T(8,128)(2,1)S(1)} collective-permute-done((bf16[2,2,2,2,32,128]{5,4,3,0,2,1:T(8,128)(2,1)S(1)}, bf16[2,2,2,2,32,128]{5,4,3,0,2,1:T(8,128)(2,1)S(1)}, u32[]{:S(2)}, u32[]{:S(2)}) %collective-permute-start.3) | collective-permute-done | bytes 131104 | tf_op jit(solution)/shard_map/ppermute | solution.py:85
  28.7 1.7 collective-permute-start.4
  30.4 4.8 %collective-permute-done.4 = bf16[2,2,2,2,2,32,128]{6,5,4,3,0,2,1:T(8,128)(2,1)S(1)} collective-permute-done((bf16[2,2,2,2,2,32,128]{6,5,4,3,0,2,1:T(8,128)(2,1)S(1)}, bf16[2,2,2,2,2,32,128]{6,5,4,3,0,2,1:T(8,128)(2,1)S(1)}, u32[]{:S(2)}, u32[]{:S(2)}) %collective-permute-start.4) | collective-permute-done | bytes 262176 | tf_op jit(solution)/shard_map/ppermute | solution.py:85
  36.4 8.1 %collective-permute-done.8 = bf16[2,2,2,2,2,2,16,128]{7,6,5,3,0,2,4,1:T(8,128)(2,1)S(1)} collective-permute-done((bf16[2,2,2,2,2,2,16,128]{7,6,5,3,0,2,4,1:T(8,128)(2,1)S(1)}, bf16[2,2,2,2,2,2,16,128]{7,6,5,3,0,2,4,1:T(8,128)(2,1)S(1)}, u32[]{:S(2)}, u32[]{:S(2)}) %collective-permute-start.8) | collective-permute-done | bytes 262176 | tf_op jit(solution)/shard_map/ppermute | solution.py:85
  46.8 7.0 %collective-permute-done.9 = bf16[2,2,2,2,2,2,2,16,128]{8,7,6,3,0,2,4,1,5:T(8,128)(2,1)S(1)} collective-permute-done((bf16[2,2,2,2,2,2,2,16,128]{8,7,6,3,0,2,4,1,5:T(8,128)(2,1)S(1)}, bf16[2,2,2,2,2,2,2,16,128]{8,7,6,3,0,2,4,1,5:T(8,128)(2,1)S(1)}, u32[]{:S(2)}, u32[]{:S(2)}) %collective-permute-start.9) | collective-permute-done | bytes 524320 | tf_op jit(solution)/shard_map/ppermute | solution.py:85
  62.2 1.5 copy.36.l_ref
  67.5 2.5 %pad_maximum_fusion = bf16[2,2,2,2,2,2,2,2,2,32,128]{10,9,8,7,6,5,4,3,2,1,0:T(8,128)(2,1)} fusion(bf16[2,2,2,2,2,2,2,2,2,16,128]{10,9,8,7,6,5,4,3,2,1,0:T(8,128)(2,1)S(1)} %maximum_bitcast_fusion.1, bf16[2,2,2,2,2,2,2,1,2,16,128]{10,9,8,6,3,0,2,4,1,5,7:T(8,128)(2,1)S(1)} %get-tuple-element.8, ...), kind=kLoop, calls=%fused_computation | loop fusion | flops 9437184 | bytes 8388608 | tf_op jit(solution)/shard_map/concatenate | solution.py:108
  70.0 46.2 %shard_map.37 = bf16[64,4,2,32,128]{4,3,2,1,0:T(8,128)(2,1)S(1)} custom-call(bf16[4,128,32,128]{3,2,1,0:T(8,128)(2,1)} %bitcast.136, bf16[128,3200]{1,0:T(8,128)(2,1)S(1)} %copy.35.r_ref, bf16[128,3200]{1,0:T(8,128)(2,1)S(1)} %copy.36.l_ref), custom_call_target="tpu_custom_call" | custom-call | flops 26843545600 | bytes 10027008 | tf_op jit(solution)/shard_map/pallas_call | solution.py:53
  116.5 1.7 copy-done.1
  118.2 4.3 %collective-permute-done.11 = bf16[2,2,2,2,2,2,2,64,128]{8,7,6,5,4,3,2,1,0:T(8,128)(2,1)} collective-permute-done((bf16[2,2,2,2,2,2,2,64,128]{8,7,6,5,4,3,2,1,0:T(8,128)(2,1)S(1)}, bf16[2,2,2,2,2,2,2,64,128]{8,7,6,5,4,3,2,1,0:T(8,128)(2,1)}, u32[]{:S(2)}, u32[]{:S(2)}) %collective-permute-start.11) | collective-permute-done | bytes 2097184 | tf_op jit(solution)/shard_map/ppermute | solution.py:117
  122.5 3.2 %convert_add_fusion = f32[2,2,2,2,2,2,2,64,128]{8,7,6,5,4,3,2,1,0:T(8,128)S(1)} fusion(bf16[2,2,2,2,2,2,2,64,128]{8,7,6,5,4,3,2,1,0:T(8,128)(2,1)} %collective-permute-done.11, bf16[2,2,2,2,2,2,2,2,64,128]{9,8,7,6,5,4,3,2,1,0:T(8,128)(2,1)} %bitcast.135, s32[]{:T(128)S(6)} %select_n.221), kind=kLoop, calls=%fused_computation.1 | loop fusion | flops 3145728 | bytes 8388612 | tf_op jit(solution)/shard_map/add | solution.py:119
  130.5 11.5 %collective-permute-done.14 = bf16[2,2,2,2,2,2,32,128]{7,6,5,4,3,2,1,0:T(8,128)(2,1)} collective-permute-done((bf16[2,2,2,2,2,2,32,128]{7,6,5,4,3,2,1,0:T(8,128)(2,1)S(1)}, bf16[2,2,2,2,2,2,32,128]{7,6,5,4,3,2,1,0:T(8,128)(2,1)}, u32[]{:S(2)}, u32[]{:S(2)}) %collective-permute-start.14) | collective-permute-done | bytes 524320 | tf_op jit(solution)/shard_map/ppermute | solution.py:117
  142.0 1.6 bitcast_add_fusion
  148.6 3.5 %collective-permute-done.15 = bf16[2,2,2,2,2,32,128]{6,5,4,3,2,1,0:T(8,128)(2,1)S(1)} collective-permute-done((bf16[2,2,2,2,2,32,128]{6,5,4,3,2,1,0:T(8,128)(2,1)}, bf16[2,2,2,2,2,32,128]{6,5,4,3,2,1,0:T(8,128)(2,1)S(1)}, u32[]{:S(2)}, u32[]{:S(2)}) %collective-permute-start.15) | collective-permute-done | bytes 262176 | tf_op jit(solution)/shard_map/ppermute | solution.py:117
  152.1 2.8 %collective-permute-done.13 = bf16[2,2,2,2,2,32,128]{6,5,4,3,2,1,0:T(8,128)(2,1)S(1)} collective-permute-done((bf16[2,2,2,2,2,32,128]{6,5,4,3,2,1,0:T(8,128)(2,1)S(1)}, bf16[2,2,2,2,2,32,128]{6,5,4,3,2,1,0:T(8,128)(2,1)S(1)}, u32[]{:S(2)}, u32[]{:S(2)}) %collective-permute-start.13) | collective-permute-done | bytes 262176 | tf_op jit(solution)/shard_map/ppermute | solution.py:117
  156.1 1.8 collective-permute-start.16
  157.9 4.8 %collective-permute-done.16 = bf16[2,2,2,2,64,128]{5,4,3,2,1,0:T(8,128)(2,1)S(1)} collective-permute-done((bf16[2,2,2,2,64,128]{5,4,3,2,1,0:T(8,128)(2,1)S(1)}, bf16[2,2,2,2,64,128]{5,4,3,2,1,0:T(8,128)(2,1)S(1)}, u32[]{:S(2)}, u32[]{:S(2)}) %collective-permute-start.16) | collective-permute-done | bytes 262176 | tf_op jit(solution)/shard_map/ppermute | solution.py:117
  162.8 2.4 %collective-permute-start.17 = (f32[2,2,2,64,128]{4,3,2,1,0:T(8,128)S(1)}, f32[2,2,2,64,128]{4,3,2,1,0:T(8,128)S(1)}, u32[]{:S(2)}, u32[]{:S(2)}) collective-permute-start(f32[2,2,2,64,128]{4,3,2,1,0:T(8,128)S(1)} %dynamic-slice_bitcast_fusion.1), channel_id=1, source_target_pairs={{0,8},{1,9},{2,10},{3,11},{4,12},{5,13},{6,14},{7,15},{8,0},{9,1},... | collective-permute-start | bytes 786440 | tf_op jit(solution)/shard_map/ppermute | solution.py:117
  165.1 9.9 %collective-permute-done.17 = f32[2,2,2,64,128]{4,3,2,1,0:T(8,128)S(1)} collective-permute-done((f32[2,2,2,64,128]{4,3,2,1,0:T(8,128)S(1)}, f32[2,2,2,64,128]{4,3,2,1,0:T(8,128)S(1)}, u32[]{:S(2)}, u32[]{:S(2)}) %collective-permute-start.17) | collective-permute-done | bytes 262176 | tf_op jit(solution)/shard_map/ppermute | solution.py:117
  175.1 2.1 %collective-permute-start.18 = (f32[2,2,64,128]{3,2,1,0:T(8,128)S(1)}, f32[2,2,64,128]{3,2,1,0:T(8,128)S(1)}, u32[]{:S(2)}, u32[]{:S(2)}) collective-permute-start(f32[2,2,64,128]{3,2,1,0:T(8,128)S(1)} %dynamic-slice_bitcast_fusion.2), channel_id=1, source_target_pairs={{0,32},{1,33},{2,34},{3,35},{4,36},{5,37},{6,38},{7,39},{8,40},{9,... | collective-permute-start | bytes 393224 | tf_op jit(solution)/shard_map/ppermute | solution.py:117
  177.2 4.5 %collective-permute-done.18 = f32[2,2,64,128]{3,2,1,0:T(8,128)S(1)} collective-permute-done((f32[2,2,64,128]{3,2,1,0:T(8,128)S(1)}, f32[2,2,64,128]{3,2,1,0:T(8,128)S(1)}, u32[]{:S(2)}, u32[]{:S(2)}) %collective-permute-start.18) | collective-permute-done | bytes 131104 | tf_op jit(solution)/shard_map/ppermute | solution.py:117
  181.7 3.5 %collective-permute-start.19 = (f32[2,64,128]{2,1,0:T(8,128)S(1)}, f32[2,64,128]{2,1,0:T(8,128)S(1)}, u32[]{:S(2)}, u32[]{:S(2)}) collective-permute-start(f32[2,64,128]{2,1,0:T(8,128)S(1)} %dynamic-slice_bitcast_fusion.3), channel_id=1, source_target_pairs={{0,128},{1,129},{2,130},{3,131},{4,132},{5,133},{6,134},{7,135},{8... | collective-permute-start | bytes 196616 | tf_op jit(solution)/shard_map/ppermute | solution.py:117
  185.1 2.4 %collective-permute-done.19 = f32[2,64,128]{2,1,0:T(8,128)S(1)} collective-permute-done((f32[2,64,128]{2,1,0:T(8,128)S(1)}, f32[2,64,128]{2,1,0:T(8,128)S(1)}, u32[]{:S(2)}, u32[]{:S(2)}) %collective-permute-start.19) | collective-permute-done | bytes 65568 | tf_op jit(solution)/shard_map/ppermute | solution.py:117
  187.6 6.2 %collective-permute-start.20 = (f32[64,128]{1,0:T(8,128)S(1)}, f32[64,128]{1,0:T(8,128)S(1)}, u32[]{:S(2)}, u32[]{:S(2)}) collective-permute-start(f32[64,128]{1,0:T(8,128)S(1)} %dynamic-slice_bitcast_fusion.4), channel_id=1, source_target_pairs={{0,16},{1,17},{2,18},{3,19},{4,20},{5,21},{6,22},{7,23},{8,24},{9,... | collective-permute-start | bytes 98312 | tf_op jit(solution)/shard_map/ppermute | solution.py:117
  193.8 1.9 collective-permute-done.20
  (78 shorter events, 28.5 us)
Async XLA Ops:
  0.0 0.8 copy-start
  0.9 9.0 %collective-permute-start = (bf16[2,32,128]{2,1,0:T(8,128)(2,1)S(1)}, bf16[2,32,128]{2,1,0:T(8,128)(2,1)S(1)}, u32[]{:S(2)}, u32[]{:S(2)}) collective-permute-start(bf16[2,32,128]{2,1,0:T(8,128)(2,1)S(1)} %bitcast.143), channel_id=1, source_target_pairs={{0,16},{1,17},{2,18},{3,19},{4,20},{5,21},{6,22},{7,23},{8,24},{9,... | collective-permute-start | bytes 49160 | tf_op jit(solution)/shard_map/ppermute | solution.py:85
  9.9 5.5 %collective-permute-start.1 = (bf16[2,2,32,128]{3,2,1,0:T(8,128)(2,1)S(1)}, bf16[2,2,32,128]{3,2,1,0:T(8,128)(2,1)S(1)}, u32[]{:S(2)}, u32[]{:S(2)}) collective-permute-start(bf16[2,2,32,128]{3,2,1,0:T(8,128)(2,1)S(1)} %pad_maximum_fusion.9), channel_id=1, source_target_pairs={{0,128},{1,129},{2,130},{3,131},{4,132},{5,133},{6,134},{7,135},{8... | collective-permute-start | bytes 98312 | tf_op jit(solution)/shard_map/ppermute | solution.py:85
  15.4 5.9 %collective-permute-start.2 = (bf16[2,2,2,32,128]{4,3,2,0,1:T(8,128)(2,1)S(1)}, bf16[2,2,2,32,128]{4,3,2,0,1:T(8,128)(2,1)S(1)}, u32[]{:S(2)}, u32[]{:S(2)}) collective-permute-start(bf16[2,2,2,32,128]{4,3,2,0,1:T(8,128)(2,1)S(1)} %pad_maximum_fusion.8), channel_id=1, source_target_pairs={{0,32},{1,33},{2,34},{3,35},{4,36},{5,37},{6,38},{7,39},{8,40},{9,... | collective-permute-start | bytes 196616 | tf_op jit(solution)/shard_map/ppermute | solution.py:85
  21.3 7.4 %collective-permute-start.3 = (bf16[2,2,2,2,32,128]{5,4,3,0,2,1:T(8,128)(2,1)S(1)}, bf16[2,2,2,2,32,128]{5,4,3,0,2,1:T(8,128)(2,1)S(1)}, u32[]{:S(2)}, u32[]{:S(2)}) collective-permute-start(bf16[2,2,2,2,32,128]{5,4,3,0,2,1:T(8,128)(2,1)S(1)} %pad_maximum_fusion.7), channel_id=1, source_target_pairs={{0,8},{1,9},{2,10},{3,11},{4,12},{5,13},{6,14},{7,15},{8,0},{9,1},... | collective-permute-start | bytes 393224 | tf_op jit(solution)/shard_map/ppermute | solution.py:85
  28.7 6.5 %collective-permute-start.4 = (bf16[2,2,2,2,2,32,128]{6,5,4,3,0,2,1:T(8,128)(2,1)S(1)}, bf16[2,2,2,2,2,32,128]{6,5,4,3,0,2,1:T(8,128)(2,1)S(1)}, u32[]{:S(2)}, u32[]{:S(2)}) collective-permute-start(bf16[2,2,2,2,2,32,128]{6,5,4,3,0,2,1:T(8,128)(2,1)S(1)} %pad_maximum_fusion.6), channel_id=1, source_target_pairs={{0,64},{1,65},{2,66},{3,67},{4,68},{5,69},{6,70},{7,71},{8,72},{9,... | collective-permute-start | bytes 786440 | tf_op jit(solution)/shard_map/ppermute | solution.py:85
  35.3 9.2 %collective-permute-start.8 = (bf16[2,2,2,2,2,2,16,128]{7,6,5,3,0,2,4,1:T(8,128)(2,1)S(1)}, bf16[2,2,2,2,2,2,16,128]{7,6,5,3,0,2,4,1:T(8,128)(2,1)S(1)}, u32[]{:S(2)}, u32[]{:S(2)}) collective-permute-start(bf16[2,2,2,2,2,2,16,128]{7,6,5,3,0,2,4,1:T(8,128)(2,1)S(1)} %get-tuple-element.18), channel_id=1, source_target_pairs={{0,2},{1,3},{2,0},{3,1},{4,6},{5,7},{6,4},{7,5},{8,10},{9,11},{10,... | collective-permute-start | bytes 786440 | tf_op jit(solution)/shard_map/ppermute | solution.py:85
  36.4 9.2 %collective-permute-start.5 = (bf16[2,2,2,2,2,2,16,128]{7,6,5,3,0,2,4,1:T(8,128)(2,1)S(1)}, bf16[2,2,2,2,2,2,16,128]{7,6,5,3,0,2,4,1:T(8,128)(2,1)S(1)}, u32[]{:S(2)}, u32[]{:S(2)}) collective-permute-start(bf16[2,2,2,2,2,2,16,128]{7,6,5,3,0,2,4,1:T(8,128)(2,1)S(1)} %get-tuple-element.17), channel_id=1, source_target_pairs={{0,4},{1,5},{2,6},{3,7},{4,0},{5,1},{6,2},{7,3},{8,12},{9,13},{10,... | collective-permute-start | bytes 786440 | tf_op jit(solution)/shard_map/ppermute | solution.py:85
  44.6 9.3 %collective-permute-start.9 = (bf16[2,2,2,2,2,2,2,16,128]{8,7,6,3,0,2,4,1,5:T(8,128)(2,1)S(1)}, bf16[2,2,2,2,2,2,2,16,128]{8,7,6,3,0,2,4,1,5:T(8,128)(2,1)S(1)}, u32[]{:S(2)}, u32[]{:S(2)}) collective-permute-start(bf16[2,2,2,2,2,2,2,16,128]{8,7,6,3,0,2,4,1,5:T(8,128)(2,1)S(1)} %pad_maximum_fusion.4), channel_id=1, source_target_pairs={{0,4},{1,5},{2,6},{3,7},{4,0},{5,1},{6,2},{7,3},{8,12},{9,13},{10,... | collective-permute-start | bytes 1572872 | tf_op jit(solution)/shard_map/ppermute | solution.py:85
  45.7 9.3 %collective-permute-start.6 = (bf16[2,2,2,2,2,2,2,16,128]{8,7,6,3,0,2,4,1,5:T(8,128)(2,1)S(1)}, bf16[2,2,2,2,2,2,2,16,128]{8,7,6,3,0,2,4,1,5:T(8,128)(2,1)S(1)}, u32[]{:S(2)}, u32[]{:S(2)}) collective-permute-start(bf16[2,2,2,2,2,2,2,16,128]{8,7,6,3,0,2,4,1,5:T(8,128)(2,1)S(1)} %pad_maximum_fusion.3), channel_id=1, source_target_pairs={{0,2},{1,3},{2,0},{3,1},{4,6},{5,7},{6,4},{7,5},{8,10},{9,11},{10,... | collective-permute-start | bytes 1572872 | tf_op jit(solution)/shard_map/ppermute | solution.py:85
  55.0 2.5 %copy-start.6 = (bf16[25,16384]{1,0:T(8,128)(2,1)S(1)}, bf16[25,16384]{1,0:T(8,128)(2,1)}, u32[]{:S(2)}) copy-start(bf16[25,16384]{1,0:T(8,128)(2,1)} %param.5) | copy-start | bytes 2457604
  55.0 8.7 %collective-permute-start.10 = (bf16[2,2,2,2,2,2,2,2,16,128]{9,8,7,6,3,0,2,4,1,5:T(8,128)(2,1)}, bf16[2,2,2,2,2,2,2,2,16,128]{9,8,7,6,3,0,2,4,1,5:T(8,128)(2,1)}, u32[]{:S(2)}, u32[]{:S(2)}) collective-permute-start(bf16[2,2,2,2,2,2,2,2,16,128]{9,8,7,6,3,0,2,4,1,5:T(8,128)(2,1)} %pad_maximum_fusion.2), channel_id=1, source_target_pairs={{0,1},{1,0},{2,3},{3,2},{4,5},{5,4},{6,7},{7,6},{8,9},{9,8},{10,11... | collective-permute-start | bytes 3145736 | tf_op jit(solution)/shard_map/ppermute | solution.py:85
  55.1 0.8 copy-start.3
  57.0 8.3 %collective-permute-start.7 = (bf16[2,2,2,2,2,2,2,2,16,128]{9,8,7,6,3,0,2,4,1,5:T(8,128)(2,1)}, bf16[2,2,2,2,2,2,2,2,16,128]{9,8,7,6,3,0,2,4,1,5:T(8,128)(2,1)}, u32[]{:S(2)}, u32[]{:S(2)}) collective-permute-start(bf16[2,2,2,2,2,2,2,2,16,128]{9,8,7,6,3,0,2,4,1,5:T(8,128)(2,1)} %pad_maximum_fusion.1), channel_id=1, source_target_pairs={{0,1},{1,0},{2,3},{3,2},{4,5},{5,4},{6,7},{7,6},{8,9},{9,8},{10,11... | collective-permute-start | bytes 3145736 | tf_op jit(solution)/shard_map/ppermute | solution.py:85
  65.1 1.0 copy-start.4
  116.2 2.0 %copy-start.1 = (bf16[64,4,2,32,128]{4,3,2,1,0:T(8,128)(2,1)}, bf16[64,4,2,32,128]{4,3,2,1,0:T(8,128)(2,1)S(1)}, u32[]{:S(2)}) copy-start(bf16[64,4,2,32,128]{4,3,2,1,0:T(8,128)(2,1)S(1)} %shard_map.37) | copy-start | bytes 12582916
  118.2 4.3 %collective-permute-start.11 = (bf16[2,2,2,2,2,2,2,64,128]{8,7,6,5,4,3,2,1,0:T(8,128)(2,1)S(1)}, bf16[2,2,2,2,2,2,2,64,128]{8,7,6,5,4,3,2,1,0:T(8,128)(2,1)}, u32[]{:S(2)}, u32[]{:S(2)}) collective-permute-start(bf16[2,2,2,2,2,2,2,64,128]{8,7,6,5,4,3,2,1,0:T(8,128)(2,1)S(1)} %dynamic-slice_bitcast_fusion), channel_id=1, source_target_pairs={{0,1},{1,0},{2,3},{3,2},{4,5},{5,4},{6,7},{7,6},{8,9},{9,8},{10,11... | collective-permute-start | bytes 6291464 | tf_op jit(solution)/shard_map/ppermute | solution.py:117
  126.3 1.4 copy-start.2
  127.8 14.2 %collective-permute-start.14 = (bf16[2,2,2,2,2,2,32,128]{7,6,5,4,3,2,1,0:T(8,128)(2,1)S(1)}, bf16[2,2,2,2,2,2,32,128]{7,6,5,4,3,2,1,0:T(8,128)(2,1)}, u32[]{:S(2)}, u32[]{:S(2)}) collective-permute-start(bf16[2,2,2,2,2,2,32,128]{7,6,5,4,3,2,1,0:T(8,128)(2,1)S(1)} %fusion.1), channel_id=1, source_target_pairs={{0,4},{1,5},{2,6},{3,7},{4,0},{5,1},{6,2},{7,3},{8,12},{9,13},{10,... | collective-permute-start | bytes 1572872 | tf_op jit(solution)/shard_map/ppermute | solution.py:117
  129.5 15.7 %collective-permute-start.12 = (bf16[2,2,2,2,2,2,32,128]{7,6,4,3,2,1,0,5:T(8,128)(2,1)}, bf16[2,2,2,2,2,2,32,128]{7,6,4,3,2,1,0,5:T(8,128)(2,1)}, u32[]{:S(2)}, u32[]{:S(2)}) collective-permute-start(bf16[2,2,2,2,2,2,32,128]{7,6,4,3,2,1,0,5:T(8,128)(2,1)} %fusion.2), channel_id=1, source_target_pairs={{0,2},{1,3},{2,0},{3,1},{4,6},{5,7},{6,4},{7,5},{8,10},{9,11},{10,... | collective-permute-start | bytes 1572872 | tf_op jit(solution)/shard_map/ppermute | solution.py:117
  144.3 7.7 %collective-permute-start.15 = (bf16[2,2,2,2,2,32,128]{6,5,4,3,2,1,0:T(8,128)(2,1)}, bf16[2,2,2,2,2,32,128]{6,5,4,3,2,1,0:T(8,128)(2,1)S(1)}, u32[]{:S(2)}, u32[]{:S(2)}) collective-permute-start(bf16[2,2,2,2,2,32,128]{6,5,4,3,2,1,0:T(8,128)(2,1)} %fusion.9), channel_id=1, source_target_pairs={{0,2},{1,3},{2,0},{3,1},{4,6},{5,7},{6,4},{7,5},{8,10},{9,11},{10,... | collective-permute-start | bytes 786440 | tf_op jit(solution)/shard_map/ppermute | solution.py:117
  146.5 1.0 copy-start.5
  147.5 7.3 %collective-permute-start.13 = (bf16[2,2,2,2,2,32,128]{6,5,4,3,2,1,0:T(8,128)(2,1)S(1)}, bf16[2,2,2,2,2,32,128]{6,5,4,3,2,1,0:T(8,128)(2,1)S(1)}, u32[]{:S(2)}, u32[]{:S(2)}) collective-permute-start(bf16[2,2,2,2,2,32,128]{6,5,4,3,2,1,0:T(8,128)(2,1)S(1)} %fusion.8), channel_id=1, source_target_pairs={{0,4},{1,5},{2,6},{3,7},{4,0},{5,1},{6,2},{7,3},{8,12},{9,13},{10,... | collective-permute-start | bytes 786440 | tf_op jit(solution)/shard_map/ppermute | solution.py:117
  156.1 6.6 %collective-permute-start.16 = (bf16[2,2,2,2,64,128]{5,4,3,2,1,0:T(8,128)(2,1)S(1)}, bf16[2,2,2,2,64,128]{5,4,3,2,1,0:T(8,128)(2,1)S(1)}, u32[]{:S(2)}, u32[]{:S(2)}) collective-permute-start(bf16[2,2,2,2,64,128]{5,4,3,2,1,0:T(8,128)(2,1)S(1)} %fusion.11), channel_id=1, source_target_pairs={{0,64},{1,65},{2,66},{3,67},{4,68},{5,69},{6,70},{7,71},{8,72},{9,... | collective-permute-start | bytes 786440 | tf_op jit(solution)/shard_map/ppermute | solution.py:117
  162.8 12.2 %collective-permute-start.17 = (f32[2,2,2,64,128]{4,3,2,1,0:T(8,128)S(1)}, f32[2,2,2,64,128]{4,3,2,1,0:T(8,128)S(1)}, u32[]{:S(2)}, u32[]{:S(2)}) collective-permute-start(f32[2,2,2,64,128]{4,3,2,1,0:T(8,128)S(1)} %dynamic-slice_bitcast_fusion.1), channel_id=1, source_target_pairs={{0,8},{1,9},{2,10},{3,11},{4,12},{5,13},{6,14},{7,15},{8,0},{9,1},... | collective-permute-start | bytes 786440 | tf_op jit(solution)/shard_map/ppermute | solution.py:117
  175.1 6.6 %collective-permute-start.18 = (f32[2,2,64,128]{3,2,1,0:T(8,128)S(1)}, f32[2,2,64,128]{3,2,1,0:T(8,128)S(1)}, u32[]{:S(2)}, u32[]{:S(2)}) collective-permute-start(f32[2,2,64,128]{3,2,1,0:T(8,128)S(1)} %dynamic-slice_bitcast_fusion.2), channel_id=1, source_target_pairs={{0,32},{1,33},{2,34},{3,35},{4,36},{5,37},{6,38},{7,39},{8,40},{9,... | collective-permute-start | bytes 393224 | tf_op jit(solution)/shard_map/ppermute | solution.py:117
  181.7 5.9 %collective-permute-start.19 = (f32[2,64,128]{2,1,0:T(8,128)S(1)}, f32[2,64,128]{2,1,0:T(8,128)S(1)}, u32[]{:S(2)}, u32[]{:S(2)}) collective-permute-start(f32[2,64,128]{2,1,0:T(8,128)S(1)} %dynamic-slice_bitcast_fusion.3), channel_id=1, source_target_pairs={{0,128},{1,129},{2,130},{3,131},{4,132},{5,133},{6,134},{7,135},{8... | collective-permute-start | bytes 196616 | tf_op jit(solution)/shard_map/ppermute | solution.py:117
  187.6 8.1 %collective-permute-start.20 = (f32[64,128]{1,0:T(8,128)S(1)}, f32[64,128]{1,0:T(8,128)S(1)}, u32[]{:S(2)}, u32[]{:S(2)}) collective-permute-start(f32[64,128]{1,0:T(8,128)S(1)} %dynamic-slice_bitcast_fusion.4), channel_id=1, source_target_pairs={{0,16},{1,17},{2,18},{3,19},{4,20},{5,21},{6,22},{7,23},{8,24},{9,... | collective-permute-start | bytes 98312 | tf_op jit(solution)/shard_map/ppermute | solution.py:117

commit v8 on v7

--- a/solution.py
+++ b/solution.py
@@ -16,7 +16,13 @@
 SMALL_SEND = 65536
 
 
-def ladder_kernel(n_p, n_aux, rpp, t_ref, r_ref, l_ref, out_ref, w_ref):
+def ladder_kernel(n_p, n_aux, rpp, t_ref, fb_ref, fa_ref, out_ref, w_ref, r_ref, l_ref):
+    @pl.when(pl.program_id(0) == 0)
+    def _():
+        for p in range(n_p):
+            r_ref[:, p * B:(p + 1) * B] = fb_ref[p]
+            l_ref[:, p * C:(p + 1) * C] = fa_ref[p].astype(jnp.float32).T.astype(jnp.bfloat16)
+
     cq = C // n_aux
     t_blk = t_ref[...].reshape(n_aux * I_BLOCK * cq, D)
     for p0 in range(0, n_p, P_GROUP):
@@ -44,8 +50,8 @@
     rpp = nij // n_pair
     apa = A // n_aux
     t2 = t_all
-    r2 = factor_db.reshape(n_p, D, B).transpose(1, 0, 2).reshape(D, n_p * B)
-    l2 = factor_ca.reshape(n_p, C, A).transpose(2, 0, 1).reshape(A, n_p * C)
+    r2 = factor_db.reshape(n_p, D, B)
+    l2 = factor_ca.reshape(n_p, C, A)
     steps = nij // I_BLOCK
     pb = I_BLOCK // rpp
     flops = 4 * nij * C * D * n_p * B
@@ -55,13 +61,18 @@
         grid=(steps,),
         in_specs=[
             pl.BlockSpec((n_aux, I_BLOCK, C // n_aux, D), lambda g: (0, g, 0, 0)),
-            pl.BlockSpec((D, n_p * B), lambda g: (0, 0)),
-            pl.BlockSpec((A, n_p * C), lambda g: (0, 0)),
+            pl.BlockSpec((n_p, D, B), lambda g: (0, 0, 0)),
+            pl.BlockSpec((n_p, C, A), lambda g: (0, 0, 0)),
         ],
         out_specs=pl.BlockSpec((pb, n_aux, rpp, apa, B), lambda g: (g, 0, 0, 0, 0)),
         out_shape=jax.ShapeDtypeStruct((n_pair, n_aux, rpp, apa, B), jnp.bfloat16),
-        scratch_shapes=[pltpu.VMEM((n_p * C, I_BLOCK * B), jnp.bfloat16)],
-        compiler_params=pltpu.CompilerParams(vmem_limit_bytes=48 * 1024 * 1024),
+        scratch_shapes=[
+            pltpu.VMEM((n_p * C, I_BLOCK * B), jnp.bfloat16),
+            pltpu.VMEM((D, n_p * B), jnp.bfloat16),
+            pltpu.VMEM((A, n_p * C), jnp.bfloat16),
+        ],
+        compiler_params=pltpu.CompilerParams(
+            dimension_semantics=("arbitrary",), vmem_limit_bytes=48 * 1024 * 1024),
         cost_estimate=pl.CostEstimate(
             flops=flops, transcendentals=0,
             bytes_accessed=2 * (t2.size + r2.size + l2.size) + 2 * nij * A * B,

time: 197 us -> 193 us (0.980)
  local copies, waits for them, and re-layouts: 16 us -> 11.4 us
    reshape x3 -> x2, local copies, waits for them, and re-layouts: 3.36 us -> 0.15 us  [the longest x1 0.07 us: local_ladder(): r2 = factor_db.reshape(n_p, D, B)]
    unnamed x18 -> x20, local copies, waits for them, and re-layouts: 8.16 us -> 7.83 us
  transfers between devices with their start and end apart: 21 -> 21, of which waited for: 17 -> 17; matrix products, arithmetic and copies ran while one was open for 8% -> 5% of each run, Pallas kernels for 0% -> 0%
where the time goes in v8:
time: 193 us; the launch traced here: 192 us
  waiting for transfers between devices  79.1 us (41%)
  Pallas kernels  46.7 us (24%)
  starting transfers between devices  39 us (20%)
  other arithmetic  15.5 us (8%)
  local copies, waits for them, and re-layouts  11.4 us (6%)
    pallas_call x1, Pallas kernels, local_ladder(): pl.pallas_call(kernel, grid=(steps,), in_specs=[pl.BlockSpec((n_aux, I_BL...  46.7 us
    ppermute x10, waiting for transfers between devices, reduce_step(): recv = lax.ppermute(send.astype(wire), axes, xor_perm(n, b))  45.4 us
    ppermute x11, waiting for transfers between devices, gather_step(): recv = lax.ppermute(buf, axes, xor_perm(n, b))  33.7 us
    ppermute x10, starting transfers between devices, reduce_step(): recv = lax.ppermute(send.astype(wire), axes, xor_perm(n, b))  19.7 us
    ppermute x11, starting transfers between devices, gather_step(): recv = lax.ppermute(buf, axes, xor_perm(n, b))  19.3 us
    unnamed x20, local copies, waits for them, and re-layouts  7.83 us
    add x9, other arithmetic, reduce_step(): return keep.astype(jnp.float32) + recv.astype(jnp.float32)  7.31 us
    another operation x20, other arithmetic, gather_step(): return jnp.stack([lo, hi], axis=k)  5.44 us
  transfers between devices with their start and end apart: 21, of which 17 were waited for; matrix products, arithmetic and copies ran while one was open for 5% of the time, Pallas kernels for 0%

profile of v8, /device:TPU:2, one launch (start us, length us, event | category | flops | bytes accessed | tf_op | source)
XLA Modules:
  0.0 192.1 jit_solution(2641913732484469317)
XLA Ops:
  0.9 7.3 %collective-permute-start = (bf16[2,32,128]{2,1,0:T(8,128)(2,1)S(1)}, bf16[2,32,128]{2,1,0:T(8,128)(2,1)S(1)}, u32[]{:S(2)}, u32[]{:S(2)}) collective-permute-start(bf16[2,32,128]{2,1,0:T(8,128)(2,1)S(1)} %bitcast.135), channel_id=1, source_target_pairs={{0,16},{1,17},{2,18},{3,19},{4,20},{5,21},{6,22},{7,23},{8,24},{9,... | collective-permute-start | bytes 49160 | tf_op jit(solution)/shard_map/ppermute | solution.py:96
  8.1 1.7 collective-permute-done
  9.9 3.3 %collective-permute-start.1 = (bf16[2,2,32,128]{3,2,1,0:T(8,128)(2,1)S(1)}, bf16[2,2,32,128]{3,2,1,0:T(8,128)(2,1)S(1)}, u32[]{:S(2)}, u32[]{:S(2)}) collective-permute-start(bf16[2,2,32,128]{3,2,1,0:T(8,128)(2,1)S(1)} %pad_maximum_fusion.9), channel_id=1, source_target_pairs={{0,128},{1,129},{2,130},{3,131},{4,132},{5,133},{6,134},{7,135},{8... | collective-permute-start | bytes 98312 | tf_op jit(solution)/shard_map/ppermute | solution.py:96
  13.2 2.2 %collective-permute-done.1 = bf16[2,2,32,128]{3,2,1,0:T(8,128)(2,1)S(1)} collective-permute-done((bf16[2,2,32,128]{3,2,1,0:T(8,128)(2,1)S(1)}, bf16[2,2,32,128]{3,2,1,0:T(8,128)(2,1)S(1)}, u32[]{:S(2)}, u32[]{:S(2)}) %collective-permute-start.1) | collective-permute-done | bytes 32800 | tf_op jit(solution)/shard_map/ppermute | solution.py:96
  15.4 2.2 %collective-permute-start.2 = (bf16[2,2,2,32,128]{4,3,2,0,1:T(8,128)(2,1)S(1)}, bf16[2,2,2,32,128]{4,3,2,0,1:T(8,128)(2,1)S(1)}, u32[]{:S(2)}, u32[]{:S(2)}) collective-permute-start(bf16[2,2,2,32,128]{4,3,2,0,1:T(8,128)(2,1)S(1)} %pad_maximum_fusion.8), channel_id=1, source_target_pairs={{0,32},{1,33},{2,34},{3,35},{4,36},{5,37},{6,38},{7,39},{8,40},{9,... | collective-permute-start | bytes 196616 | tf_op jit(solution)/shard_map/ppermute | solution.py:96
  17.6 3.6 %collective-permute-done.2 = bf16[2,2,2,32,128]{4,3,2,0,1:T(8,128)(2,1)S(1)} collective-permute-done((bf16[2,2,2,32,128]{4,3,2,0,1:T(8,128)(2,1)S(1)}, bf16[2,2,2,32,128]{4,3,2,0,1:T(8,128)(2,1)S(1)}, u32[]{:S(2)}, u32[]{:S(2)}) %collective-permute-start.2) | collective-permute-done | bytes 65568 | tf_op jit(solution)/shard_map/ppermute | solution.py:96
  21.3 2.1 %collective-permute-start.3 = (bf16[2,2,2,2,32,128]{5,4,3,0,2,1:T(8,128)(2,1)S(1)}, bf16[2,2,2,2,32,128]{5,4,3,0,2,1:T(8,128)(2,1)S(1)}, u32[]{:S(2)}, u32[]{:S(2)}) collective-permute-start(bf16[2,2,2,2,32,128]{5,4,3,0,2,1:T(8,128)(2,1)S(1)} %pad_maximum_fusion.7), channel_id=1, source_target_pairs={{0,8},{1,9},{2,10},{3,11},{4,12},{5,13},{6,14},{7,15},{8,0},{9,1},... | collective-permute-start | bytes 393224 | tf_op jit(solution)/shard_map/ppermute | solution.py:96
  23.4 5.3 %collective-permute-done.3 = bf16[2,2,2,2,32,128]{5,4,3,0,2,1:T(8,128)(2,1)S(1)} collective-permute-done((bf16[2,2,2,2,32,128]{5,4,3,0,2,1:T(8,128)(2,1)S(1)}, bf16[2,2,2,2,32,128]{5,4,3,0,2,1:T(8,128)(2,1)S(1)}, u32[]{:S(2)}, u32[]{:S(2)}) %collective-permute-start.3) | collective-permute-done | bytes 131104 | tf_op jit(solution)/shard_map/ppermute | solution.py:96
  28.7 1.7 collective-permute-start.4
  30.4 4.8 %collective-permute-done.4 = bf16[2,2,2,2,2,32,128]{6,5,4,3,0,2,1:T(8,128)(2,1)S(1)} collective-permute-done((bf16[2,2,2,2,2,32,128]{6,5,4,3,0,2,1:T(8,128)(2,1)S(1)}, bf16[2,2,2,2,2,32,128]{6,5,4,3,0,2,1:T(8,128)(2,1)S(1)}, u32[]{:S(2)}, u32[]{:S(2)}) %collective-permute-start.4) | collective-permute-done | bytes 262176 | tf_op jit(solution)/shard_map/ppermute | solution.py:96
  36.4 8.1 %collective-permute-done.8 = bf16[2,2,2,2,2,2,16,128]{7,6,5,3,0,2,4,1:T(8,128)(2,1)S(1)} collective-permute-done((bf16[2,2,2,2,2,2,16,128]{7,6,5,3,0,2,4,1:T(8,128)(2,1)S(1)}, bf16[2,2,2,2,2,2,16,128]{7,6,5,3,0,2,4,1:T(8,128)(2,1)S(1)}, u32[]{:S(2)}, u32[]{:S(2)}) %collective-permute-start.8) | collective-permute-done | bytes 262176 | tf_op jit(solution)/shard_map/ppermute | solution.py:96
  46.8 7.0 %collective-permute-done.9 = bf16[2,2,2,2,2,2,2,16,128]{8,7,6,3,0,2,4,1,5:T(8,128)(2,1)S(1)} collective-permute-done((bf16[2,2,2,2,2,2,2,16,128]{8,7,6,3,0,2,4,1,5:T(8,128)(2,1)S(1)}, bf16[2,2,2,2,2,2,2,16,128]{8,7,6,3,0,2,4,1,5:T(8,128)(2,1)S(1)}, u32[]{:S(2)}, u32[]{:S(2)}) %collective-permute-start.9) | collective-permute-done | bytes 524320 | tf_op jit(solution)/shard_map/ppermute | solution.py:96
  59.1 1.4 select_bitcast_fusion.1
  62.9 2.5 %pad_maximum_fusion = bf16[2,2,2,2,2,2,2,2,2,32,128]{10,9,8,7,6,5,4,3,2,1,0:T(8,128)(2,1)} fusion(bf16[2,2,2,2,2,2,2,2,2,16,128]{10,9,8,7,6,5,4,3,2,1,0:T(8,128)(2,1)S(1)} %maximum_bitcast_fusion.1, bf16[2,2,2,2,2,2,2,1,2,16,128]{10,9,8,6,3,0,2,4,1,5,7:T(8,128)(2,1)S(1)} %get-tuple-element.8, ...), kind=kLoop, calls=%fused_computation | loop fusion | flops 9437184 | bytes 8388608 | tf_op jit(solution)/shard_map/concatenate | solution.py:119
  65.4 46.7 %shard_map.37 = bf16[64,4,2,32,128]{4,3,2,1,0:T(8,128)(2,1)S(1)} custom-call(bf16[4,128,32,128]{3,2,1,0:T(8,128)(2,1)} %bitcast.130, bf16[25,128,128]{2,1,0:T(8,128)(2,1)S(1)} %slice.20.fb_ref, bf16[25,128,128]{2,1,0:T(8,128)(2,1)S(1)} %slice.21.fa_ref), custom_call_target="tpu_custom_call" | custom-call | flops 26843545600 | bytes 10027008 | tf_op jit(solution)/shard_map/pallas_call | solution.py:59
  112.4 1.7 copy-done.1
  114.0 4.3 %collective-permute-done.11 = bf16[2,2,2,2,2,2,2,64,128]{8,7,6,5,4,3,2,1,0:T(8,128)(2,1)} collective-permute-done((bf16[2,2,2,2,2,2,2,64,128]{8,7,6,5,4,3,2,1,0:T(8,128)(2,1)S(1)}, bf16[2,2,2,2,2,2,2,64,128]{8,7,6,5,4,3,2,1,0:T(8,128)(2,1)}, u32[]{:S(2)}, u32[]{:S(2)}) %collective-permute-start.11) | collective-permute-done | bytes 2097184 | tf_op jit(solution)/shard_map/ppermute | solution.py:128
  118.3 3.2 %convert_add_fusion = f32[2,2,2,2,2,2,2,64,128]{8,7,6,5,4,3,2,1,0:T(8,128)S(1)} fusion(bf16[2,2,2,2,2,2,2,64,128]{8,7,6,5,4,3,2,1,0:T(8,128)(2,1)} %collective-permute-done.11, bf16[2,2,2,2,2,2,2,2,64,128]{9,8,7,6,5,4,3,2,1,0:T(8,128)(2,1)} %bitcast.129, s32[]{:T(128)S(6)} %select_n.221), kind=kLoop, calls=%fused_computation.1 | loop fusion | flops 3145728 | bytes 8388612 | tf_op jit(solution)/shard_map/add | solution.py:130
  126.3 11.5 %collective-permute-done.14 = bf16[2,2,2,2,2,2,32,128]{7,6,5,4,3,2,1,0:T(8,128)(2,1)} collective-permute-done((bf16[2,2,2,2,2,2,32,128]{7,6,5,4,3,2,1,0:T(8,128)(2,1)S(1)}, bf16[2,2,2,2,2,2,32,128]{7,6,5,4,3,2,1,0:T(8,128)(2,1)}, u32[]{:S(2)}, u32[]{:S(2)}) %collective-permute-start.14) | collective-permute-done | bytes 524320 | tf_op jit(solution)/shard_map/ppermute | solution.py:128
  137.8 1.6 bitcast_add_fusion
  144.4 3.5 %collective-permute-done.15 = bf16[2,2,2,2,2,32,128]{6,5,4,3,2,1,0:T(8,128)(2,1)S(1)} collective-permute-done((bf16[2,2,2,2,2,32,128]{6,5,4,3,2,1,0:T(8,128)(2,1)}, bf16[2,2,2,2,2,32,128]{6,5,4,3,2,1,0:T(8,128)(2,1)S(1)}, u32[]{:S(2)}, u32[]{:S(2)}) %collective-permute-start.15) | collective-permute-done | bytes 262176 | tf_op jit(solution)/shard_map/ppermute | solution.py:128
  147.9 2.8 %collective-permute-done.13 = bf16[2,2,2,2,2,32,128]{6,5,4,3,2,1,0:T(8,128)(2,1)S(1)} collective-permute-done((bf16[2,2,2,2,2,32,128]{6,5,4,3,2,1,0:T(8,128)(2,1)S(1)}, bf16[2,2,2,2,2,32,128]{6,5,4,3,2,1,0:T(8,128)(2,1)S(1)}, u32[]{:S(2)}, u32[]{:S(2)}) %collective-permute-start.13) | collective-permute-done | bytes 262176 | tf_op jit(solution)/shard_map/ppermute | solution.py:128
  151.9 1.8 collective-permute-start.16
  153.7 4.8 %collective-permute-done.16 = bf16[2,2,2,2,64,128]{5,4,3,2,1,0:T(8,128)(2,1)S(1)} collective-permute-done((bf16[2,2,2,2,64,128]{5,4,3,2,1,0:T(8,128)(2,1)S(1)}, bf16[2,2,2,2,64,128]{5,4,3,2,1,0:T(8,128)(2,1)S(1)}, u32[]{:S(2)}, u32[]{:S(2)}) %collective-permute-start.16) | collective-permute-done | bytes 262176 | tf_op jit(solution)/shard_map/ppermute | solution.py:128
  158.6 2.4 %collective-permute-start.17 = (f32[2,2,2,64,128]{4,3,2,1,0:T(8,128)S(1)}, f32[2,2,2,64,128]{4,3,2,1,0:T(8,128)S(1)}, u32[]{:S(2)}, u32[]{:S(2)}) collective-permute-start(f32[2,2,2,64,128]{4,3,2,1,0:T(8,128)S(1)} %dynamic-slice_bitcast_fusion.1), channel_id=1, source_target_pairs={{0,8},{1,9},{2,10},{3,11},{4,12},{5,13},{6,14},{7,15},{8,0},{9,1},... | collective-permute-start | bytes 786440 | tf_op jit(solution)/shard_map/ppermute | solution.py:128
  160.9 9.8 %collective-permute-done.17 = f32[2,2,2,64,128]{4,3,2,1,0:T(8,128)S(1)} collective-permute-done((f32[2,2,2,64,128]{4,3,2,1,0:T(8,128)S(1)}, f32[2,2,2,64,128]{4,3,2,1,0:T(8,128)S(1)}, u32[]{:S(2)}, u32[]{:S(2)}) %collective-permute-start.17) | collective-permute-done | bytes 262176 | tf_op jit(solution)/shard_map/ppermute | solution.py:128
  170.8 2.1 %collective-permute-start.18 = (f32[2,2,64,128]{3,2,1,0:T(8,128)S(1)}, f32[2,2,64,128]{3,2,1,0:T(8,128)S(1)}, u32[]{:S(2)}, u32[]{:S(2)}) collective-permute-start(f32[2,2,64,128]{3,2,1,0:T(8,128)S(1)} %dynamic-slice_bitcast_fusion.2), channel_id=1, source_target_pairs={{0,32},{1,33},{2,34},{3,35},{4,36},{5,37},{6,38},{7,39},{8,40},{9,... | collective-permute-start | bytes 393224 | tf_op jit(solution)/shard_map/ppermute | solution.py:128
  173.0 4.4 %collective-permute-done.18 = f32[2,2,64,128]{3,2,1,0:T(8,128)S(1)} collective-permute-done((f32[2,2,64,128]{3,2,1,0:T(8,128)S(1)}, f32[2,2,64,128]{3,2,1,0:T(8,128)S(1)}, u32[]{:S(2)}, u32[]{:S(2)}) %collective-permute-start.18) | collective-permute-done | bytes 131104 | tf_op jit(solution)/shard_map/ppermute | solution.py:128
  177.4 3.5 %collective-permute-start.19 = (f32[2,64,128]{2,1,0:T(8,128)S(1)}, f32[2,64,128]{2,1,0:T(8,128)S(1)}, u32[]{:S(2)}, u32[]{:S(2)}) collective-permute-start(f32[2,64,128]{2,1,0:T(8,128)S(1)} %dynamic-slice_bitcast_fusion.3), channel_id=1, source_target_pairs={{0,128},{1,129},{2,130},{3,131},{4,132},{5,133},{6,134},{7,135},{8... | collective-permute-start | bytes 196616 | tf_op jit(solution)/shard_map/ppermute | solution.py:128
  180.9 2.4 %collective-permute-done.19 = f32[2,64,128]{2,1,0:T(8,128)S(1)} collective-permute-done((f32[2,64,128]{2,1,0:T(8,128)S(1)}, f32[2,64,128]{2,1,0:T(8,128)S(1)}, u32[]{:S(2)}, u32[]{:S(2)}) %collective-permute-start.19) | collective-permute-done | bytes 65568 | tf_op jit(solution)/shard_map/ppermute | solution.py:128
  183.3 6.2 %collective-permute-start.20 = (f32[64,128]{1,0:T(8,128)S(1)}, f32[64,128]{1,0:T(8,128)S(1)}, u32[]{:S(2)}, u32[]{:S(2)}) collective-permute-start(f32[64,128]{1,0:T(8,128)S(1)} %dynamic-slice_bitcast_fusion.4), channel_id=1, source_target_pairs={{0,16},{1,17},{2,18},{3,19},{4,20},{5,21},{6,22},{7,23},{8,24},{9,... | collective-permute-start | bytes 98312 | tf_op jit(solution)/shard_map/ppermute | solution.py:128
  189.6 1.9 collective-permute-done.20
  (77 shorter events, 24.1 us)
Async XLA Ops:
  0.0 0.8 copy-start
  0.9 9.0 %collective-permute-start = (bf16[2,32,128]{2,1,0:T(8,128)(2,1)S(1)}, bf16[2,32,128]{2,1,0:T(8,128)(2,1)S(1)}, u32[]{:S(2)}, u32[]{:S(2)}) collective-permute-start(bf16[2,32,128]{2,1,0:T(8,128)(2,1)S(1)} %bitcast.135), channel_id=1, source_target_pairs={{0,16},{1,17},{2,18},{3,19},{4,20},{5,21},{6,22},{7,23},{8,24},{9,... | collective-permute-start | bytes 49160 | tf_op jit(solution)/shard_map/ppermute | solution.py:96
  9.9 5.5 %collective-permute-start.1 = (bf16[2,2,32,128]{3,2,1,0:T(8,128)(2,1)S(1)}, bf16[2,2,32,128]{3,2,1,0:T(8,128)(2,1)S(1)}, u32[]{:S(2)}, u32[]{:S(2)}) collective-permute-start(bf16[2,2,32,128]{3,2,1,0:T(8,128)(2,1)S(1)} %pad_maximum_fusion.9), channel_id=1, source_target_pairs={{0,128},{1,129},{2,130},{3,131},{4,132},{5,133},{6,134},{7,135},{8... | collective-permute-start | bytes 98312 | tf_op jit(solution)/shard_map/ppermute | solution.py:96
  15.4 5.9 %collective-permute-start.2 = (bf16[2,2,2,32,128]{4,3,2,0,1:T(8,128)(2,1)S(1)}, bf16[2,2,2,32,128]{4,3,2,0,1:T(8,128)(2,1)S(1)}, u32[]{:S(2)}, u32[]{:S(2)}) collective-permute-start(bf16[2,2,2,32,128]{4,3,2,0,1:T(8,128)(2,1)S(1)} %pad_maximum_fusion.8), channel_id=1, source_target_pairs={{0,32},{1,33},{2,34},{3,35},{4,36},{5,37},{6,38},{7,39},{8,40},{9,... | collective-permute-start | bytes 196616 | tf_op jit(solution)/shard_map/ppermute | solution.py:96
  21.3 7.4 %collective-permute-start.3 = (bf16[2,2,2,2,32,128]{5,4,3,0,2,1:T(8,128)(2,1)S(1)}, bf16[2,2,2,2,32,128]{5,4,3,0,2,1:T(8,128)(2,1)S(1)}, u32[]{:S(2)}, u32[]{:S(2)}) collective-permute-start(bf16[2,2,2,2,32,128]{5,4,3,0,2,1:T(8,128)(2,1)S(1)} %pad_maximum_fusion.7), channel_id=1, source_target_pairs={{0,8},{1,9},{2,10},{3,11},{4,12},{5,13},{6,14},{7,15},{8,0},{9,1},... | collective-permute-start | bytes 393224 | tf_op jit(solution)/shard_map/ppermute | solution.py:96
  28.7 6.5 %collective-permute-start.4 = (bf16[2,2,2,2,2,32,128]{6,5,4,3,0,2,1:T(8,128)(2,1)S(1)}, bf16[2,2,2,2,2,32,128]{6,5,4,3,0,2,1:T(8,128)(2,1)S(1)}, u32[]{:S(2)}, u32[]{:S(2)}) collective-permute-start(bf16[2,2,2,2,2,32,128]{6,5,4,3,0,2,1:T(8,128)(2,1)S(1)} %pad_maximum_fusion.6), channel_id=1, source_target_pairs={{0,64},{1,65},{2,66},{3,67},{4,68},{5,69},{6,70},{7,71},{8,72},{9,... | collective-permute-start | bytes 786440 | tf_op jit(solution)/shard_map/ppermute | solution.py:96
  35.3 9.2 %collective-permute-start.8 = (bf16[2,2,2,2,2,2,16,128]{7,6,5,3,0,2,4,1:T(8,128)(2,1)S(1)}, bf16[2,2,2,2,2,2,16,128]{7,6,5,3,0,2,4,1:T(8,128)(2,1)S(1)}, u32[]{:S(2)}, u32[]{:S(2)}) collective-permute-start(bf16[2,2,2,2,2,2,16,128]{7,6,5,3,0,2,4,1:T(8,128)(2,1)S(1)} %get-tuple-element.18), channel_id=1, source_target_pairs={{0,2},{1,3},{2,0},{3,1},{4,6},{5,7},{6,4},{7,5},{8,10},{9,11},{10,... | collective-permute-start | bytes 786440 | tf_op jit(solution)/shard_map/ppermute | solution.py:96
  36.4 9.2 %collective-permute-start.5 = (bf16[2,2,2,2,2,2,16,128]{7,6,5,3,0,2,4,1:T(8,128)(2,1)S(1)}, bf16[2,2,2,2,2,2,16,128]{7,6,5,3,0,2,4,1:T(8,128)(2,1)S(1)}, u32[]{:S(2)}, u32[]{:S(2)}) collective-permute-start(bf16[2,2,2,2,2,2,16,128]{7,6,5,3,0,2,4,1:T(8,128)(2,1)S(1)} %get-tuple-element.17), channel_id=1, source_target_pairs={{0,4},{1,5},{2,6},{3,7},{4,0},{5,1},{6,2},{7,3},{8,12},{9,13},{10,... | collective-permute-start | bytes 786440 | tf_op jit(solution)/shard_map/ppermute | solution.py:96
  44.6 9.3 %collective-permute-start.9 = (bf16[2,2,2,2,2,2,2,16,128]{8,7,6,3,0,2,4,1,5:T(8,128)(2,1)S(1)}, bf16[2,2,2,2,2,2,2,16,128]{8,7,6,3,0,2,4,1,5:T(8,128)(2,1)S(1)}, u32[]{:S(2)}, u32[]{:S(2)}) collective-permute-start(bf16[2,2,2,2,2,2,2,16,128]{8,7,6,3,0,2,4,1,5:T(8,128)(2,1)S(1)} %pad_maximum_fusion.4), channel_id=1, source_target_pairs={{0,4},{1,5},{2,6},{3,7},{4,0},{5,1},{6,2},{7,3},{8,12},{9,13},{10,... | collective-permute-start | bytes 1572872 | tf_op jit(solution)/shard_map/ppermute | solution.py:96
  45.7 9.3 %collective-permute-start.6 = (bf16[2,2,2,2,2,2,2,16,128]{8,7,6,3,0,2,4,1,5:T(8,128)(2,1)S(1)}, bf16[2,2,2,2,2,2,2,16,128]{8,7,6,3,0,2,4,1,5:T(8,128)(2,1)S(1)}, u32[]{:S(2)}, u32[]{:S(2)}) collective-permute-start(bf16[2,2,2,2,2,2,2,16,128]{8,7,6,3,0,2,4,1,5:T(8,128)(2,1)S(1)} %pad_maximum_fusion.3), channel_id=1, source_target_pairs={{0,2},{1,3},{2,0},{3,1},{4,6},{5,7},{6,4},{7,5},{8,10},{9,11},{10,... | collective-permute-start | bytes 1572872 | tf_op jit(solution)/shard_map/ppermute | solution.py:96
  55.0 2.5 %copy-start.6 = (bf16[25,16384]{1,0:T(8,128)(2,1)S(1)}, bf16[25,16384]{1,0:T(8,128)(2,1)}, u32[]{:S(2)}) copy-start(bf16[25,16384]{1,0:T(8,128)(2,1)} %param.5) | copy-start | bytes 2457604
  55.1 4.0 %collective-permute-start.10 = (bf16[2,2,2,2,2,2,2,2,16,128]{9,8,7,6,3,0,2,4,1,5:T(8,128)(2,1)}, bf16[2,2,2,2,2,2,2,2,16,128]{9,8,7,6,3,0,2,4,1,5:T(8,128)(2,1)}, u32[]{:S(2)}, u32[]{:S(2)}) collective-permute-start(bf16[2,2,2,2,2,2,2,2,16,128]{9,8,7,6,3,0,2,4,1,5:T(8,128)(2,1)} %pad_maximum_fusion.2), channel_id=1, source_target_pairs={{0,1},{1,0},{2,3},{3,2},{4,5},{5,4},{6,7},{7,6},{8,9},{9,8},{10,11... | collective-permute-start | bytes 3145736 | tf_op jit(solution)/shard_map/ppermute | solution.py:96
  55.1 0.8 copy-start.3
  57.0 3.6 %collective-permute-start.7 = (bf16[2,2,2,2,2,2,2,2,16,128]{9,8,7,6,3,0,2,4,1,5:T(8,128)(2,1)}, bf16[2,2,2,2,2,2,2,2,16,128]{9,8,7,6,3,0,2,4,1,5:T(8,128)(2,1)}, u32[]{:S(2)}, u32[]{:S(2)}) collective-permute-start(bf16[2,2,2,2,2,2,2,2,16,128]{9,8,7,6,3,0,2,4,1,5:T(8,128)(2,1)} %pad_maximum_fusion.1), channel_id=1, source_target_pairs={{0,1},{1,0},{2,3},{3,2},{4,5},{5,4},{6,7},{7,6},{8,9},{9,8},{10,11... | collective-permute-start | bytes 3145736 | tf_op jit(solution)/shard_map/ppermute | solution.py:96
  57.5 1.2 copy-start.7
  60.5 1.0 copy-start.4
  112.0 2.0 %copy-start.1 = (bf16[64,4,2,32,128]{4,3,2,1,0:T(8,128)(2,1)}, bf16[64,4,2,32,128]{4,3,2,1,0:T(8,128)(2,1)S(1)}, u32[]{:S(2)}) copy-start(bf16[64,4,2,32,128]{4,3,2,1,0:T(8,128)(2,1)S(1)} %shard_map.37) | copy-start | bytes 12582916
  114.0 4.3 %collective-permute-start.11 = (bf16[2,2,2,2,2,2,2,64,128]{8,7,6,5,4,3,2,1,0:T(8,128)(2,1)S(1)}, bf16[2,2,2,2,2,2,2,64,128]{8,7,6,5,4,3,2,1,0:T(8,128)(2,1)}, u32[]{:S(2)}, u32[]{:S(2)}) collective-permute-start(bf16[2,2,2,2,2,2,2,64,128]{8,7,6,5,4,3,2,1,0:T(8,128)(2,1)S(1)} %dynamic-slice_bitcast_fusion), channel_id=1, source_target_pairs={{0,1},{1,0},{2,3},{3,2},{4,5},{5,4},{6,7},{7,6},{8,9},{9,8},{10,11... | collective-permute-start | bytes 6291464 | tf_op jit(solution)/shard_map/ppermute | solution.py:128
  122.1 1.4 copy-start.2
  123.6 14.2 %collective-permute-start.14 = (bf16[2,2,2,2,2,2,32,128]{7,6,5,4,3,2,1,0:T(8,128)(2,1)S(1)}, bf16[2,2,2,2,2,2,32,128]{7,6,5,4,3,2,1,0:T(8,128)(2,1)}, u32[]{:S(2)}, u32[]{:S(2)}) collective-permute-start(bf16[2,2,2,2,2,2,32,128]{7,6,5,4,3,2,1,0:T(8,128)(2,1)S(1)} %fusion.1), channel_id=1, source_target_pairs={{0,4},{1,5},{2,6},{3,7},{4,0},{5,1},{6,2},{7,3},{8,12},{9,13},{10,... | collective-permute-start | bytes 1572872 | tf_op jit(solution)/shard_map/ppermute | solution.py:128
  125.3 15.8 %collective-permute-start.12 = (bf16[2,2,2,2,2,2,32,128]{7,6,4,3,2,1,0,5:T(8,128)(2,1)}, bf16[2,2,2,2,2,2,32,128]{7,6,4,3,2,1,0,5:T(8,128)(2,1)}, u32[]{:S(2)}, u32[]{:S(2)}) collective-permute-start(bf16[2,2,2,2,2,2,32,128]{7,6,4,3,2,1,0,5:T(8,128)(2,1)} %fusion.2), channel_id=1, source_target_pairs={{0,2},{1,3},{2,0},{3,1},{4,6},{5,7},{6,4},{7,5},{8,10},{9,11},{10,... | collective-permute-start | bytes 1572872 | tf_op jit(solution)/shard_map/ppermute | solution.py:128
  140.1 7.7 %collective-permute-start.15 = (bf16[2,2,2,2,2,32,128]{6,5,4,3,2,1,0:T(8,128)(2,1)}, bf16[2,2,2,2,2,32,128]{6,5,4,3,2,1,0:T(8,128)(2,1)S(1)}, u32[]{:S(2)}, u32[]{:S(2)}) collective-permute-start(bf16[2,2,2,2,2,32,128]{6,5,4,3,2,1,0:T(8,128)(2,1)} %fusion.9), channel_id=1, source_target_pairs={{0,2},{1,3},{2,0},{3,1},{4,6},{5,7},{6,4},{7,5},{8,10},{9,11},{10,... | collective-permute-start | bytes 786440 | tf_op jit(solution)/shard_map/ppermute | solution.py:128
  142.3 1.0 copy-start.5
  143.4 7.3 %collective-permute-start.13 = (bf16[2,2,2,2,2,32,128]{6,5,4,3,2,1,0:T(8,128)(2,1)S(1)}, bf16[2,2,2,2,2,32,128]{6,5,4,3,2,1,0:T(8,128)(2,1)S(1)}, u32[]{:S(2)}, u32[]{:S(2)}) collective-permute-start(bf16[2,2,2,2,2,32,128]{6,5,4,3,2,1,0:T(8,128)(2,1)S(1)} %fusion.8), channel_id=1, source_target_pairs={{0,4},{1,5},{2,6},{3,7},{4,0},{5,1},{6,2},{7,3},{8,12},{9,13},{10,... | collective-permute-start | bytes 786440 | tf_op jit(solution)/shard_map/ppermute | solution.py:128
  151.9 6.6 %collective-permute-start.16 = (bf16[2,2,2,2,64,128]{5,4,3,2,1,0:T(8,128)(2,1)S(1)}, bf16[2,2,2,2,64,128]{5,4,3,2,1,0:T(8,128)(2,1)S(1)}, u32[]{:S(2)}, u32[]{:S(2)}) collective-permute-start(bf16[2,2,2,2,64,128]{5,4,3,2,1,0:T(8,128)(2,1)S(1)} %fusion.11), channel_id=1, source_target_pairs={{0,64},{1,65},{2,66},{3,67},{4,68},{5,69},{6,70},{7,71},{8,72},{9,... | collective-permute-start | bytes 786440 | tf_op jit(solution)/shard_map/ppermute | solution.py:128
  158.6 12.2 %collective-permute-start.17 = (f32[2,2,2,64,128]{4,3,2,1,0:T(8,128)S(1)}, f32[2,2,2,64,128]{4,3,2,1,0:T(8,128)S(1)}, u32[]{:S(2)}, u32[]{:S(2)}) collective-permute-start(f32[2,2,2,64,128]{4,3,2,1,0:T(8,128)S(1)} %dynamic-slice_bitcast_fusion.1), channel_id=1, source_target_pairs={{0,8},{1,9},{2,10},{3,11},{4,12},{5,13},{6,14},{7,15},{8,0},{9,1},... | collective-permute-start | bytes 786440 | tf_op jit(solution)/shard_map/ppermute | solution.py:128
  170.8 6.6 %collective-permute-start.18 = (f32[2,2,64,128]{3,2,1,0:T(8,128)S(1)}, f32[2,2,64,128]{3,2,1,0:T(8,128)S(1)}, u32[]{:S(2)}, u32[]{:S(2)}) collective-permute-start(f32[2,2,64,128]{3,2,1,0:T(8,128)S(1)} %dynamic-slice_bitcast_fusion.2), channel_id=1, source_target_pairs={{0,32},{1,33},{2,34},{3,35},{4,36},{5,37},{6,38},{7,39},{8,40},{9,... | collective-permute-start | bytes 393224 | tf_op jit(solution)/shard_map/ppermute | solution.py:128
  177.4 5.9 %collective-permute-start.19 = (f32[2,64,128]{2,1,0:T(8,128)S(1)}, f32[2,64,128]{2,1,0:T(8,128)S(1)}, u32[]{:S(2)}, u32[]{:S(2)}) collective-permute-start(f32[2,64,128]{2,1,0:T(8,128)S(1)} %dynamic-slice_bitcast_fusion.3), channel_id=1, source_target_pairs={{0,128},{1,129},{2,130},{3,131},{4,132},{5,133},{6,134},{7,135},{8... | collective-permute-start | bytes 196616 | tf_op jit(solution)/shard_map/ppermute | solution.py:128
  183.3 8.1 %collective-permute-start.20 = (f32[64,128]{1,0:T(8,128)S(1)}, f32[64,128]{1,0:T(8,128)S(1)}, u32[]{:S(2)}, u32[]{:S(2)}) collective-permute-start(f32[64,128]{1,0:T(8,128)S(1)} %dynamic-slice_bitcast_fusion.4), channel_id=1, source_target_pairs={{0,16},{1,17},{2,18},{3,19},{4,20},{5,21},{6,22},{7,23},{8,24},{9,... | collective-permute-start | bytes 98312 | tf_op jit(solution)/shard_map/ppermute | solution.py:128

commit v9 on v8

--- a/solution.py
+++ b/solution.py
@@ -11,7 +11,7 @@
 B = 128
 C = 128
 D = 128
-I_BLOCK = 8
+I_BLOCK = 16
 P_GROUP = 5
 SMALL_SEND = 65536
 

time: 193 us -> 191 us (0.990)
  no operation moved by 1% of the time
where the time goes in v9:
time: 191 us
  waiting for transfers between devices  79.2 us (41%)
  Pallas kernels  45.2 us (24%)
  starting transfers between devices  39 us (20%)
  other arithmetic  15.5 us (8%)
  local copies, waits for them, and re-layouts  11.4 us (6%)
    ppermute x10, waiting for transfers between devices, reduce_step(): recv = lax.ppermute(send.astype(wire), axes, xor_perm(n, b))  45.4 us
    pallas_call x1, Pallas kernels, local_ladder(): pl.pallas_call(kernel, grid=(steps,), in_specs=[pl.BlockSpec((n_aux, I_BL...  45.2 us
    ppermute x11, waiting for transfers between devices, gather_step(): recv = lax.ppermute(buf, axes, xor_perm(n, b))  33.7 us
    ppermute x10, starting transfers between devices, reduce_step(): recv = lax.ppermute(send.astype(wire), axes, xor_perm(n, b))  19.7 us
    ppermute x11, starting transfers between devices, gather_step(): recv = lax.ppermute(buf, axes, xor_perm(n, b))  19.3 us
    unnamed x20, local copies, waits for them, and re-layouts  7.83 us
    add x9, other arithmetic, reduce_step(): return keep.astype(jnp.float32) + recv.astype(jnp.float32)  7.31 us
    another operation x20, other arithmetic, gather_step(): return jnp.stack([lo, hi], axis=k)  5.44 us
  transfers between devices with their start and end apart: 21, of which 17 were waited for; matrix products, arithmetic and copies ran while one was open for 5% of the time, Pallas kernels for 0%

profile of v9, /device:TPU:2, one launch (start us, length us, event | category | flops | bytes accessed | tf_op | source)
XLA Modules:
  0.0 190.7 jit_solution(13969110929438610662)
XLA Ops:
  0.9 7.3 %collective-permute-start = (bf16[2,32,128]{2,1,0:T(8,128)(2,1)S(1)}, bf16[2,32,128]{2,1,0:T(8,128)(2,1)S(1)}, u32[]{:S(2)}, u32[]{:S(2)}) collective-permute-start(bf16[2,32,128]{2,1,0:T(8,128)(2,1)S(1)} %bitcast.135), channel_id=1, source_target_pairs={{0,16},{1,17},{2,18},{3,19},{4,20},{5,21},{6,22},{7,23},{8,24},{9,... | collective-permute-start | bytes 49160 | tf_op jit(solution)/shard_map/ppermute | solution.py:96
  8.1 1.7 collective-permute-done
  9.9 3.3 %collective-permute-start.1 = (bf16[2,2,32,128]{3,2,1,0:T(8,128)(2,1)S(1)}, bf16[2,2,32,128]{3,2,1,0:T(8,128)(2,1)S(1)}, u32[]{:S(2)}, u32[]{:S(2)}) collective-permute-start(bf16[2,2,32,128]{3,2,1,0:T(8,128)(2,1)S(1)} %pad_maximum_fusion.9), channel_id=1, source_target_pairs={{0,128},{1,129},{2,130},{3,131},{4,132},{5,133},{6,134},{7,135},{8... | collective-permute-start | bytes 98312 | tf_op jit(solution)/shard_map/ppermute | solution.py:96
  13.2 2.2 %collective-permute-done.1 = bf16[2,2,32,128]{3,2,1,0:T(8,128)(2,1)S(1)} collective-permute-done((bf16[2,2,32,128]{3,2,1,0:T(8,128)(2,1)S(1)}, bf16[2,2,32,128]{3,2,1,0:T(8,128)(2,1)S(1)}, u32[]{:S(2)}, u32[]{:S(2)}) %collective-permute-start.1) | collective-permute-done | bytes 32800 | tf_op jit(solution)/shard_map/ppermute | solution.py:96
  15.4 2.2 %collective-permute-start.2 = (bf16[2,2,2,32,128]{4,3,2,0,1:T(8,128)(2,1)S(1)}, bf16[2,2,2,32,128]{4,3,2,0,1:T(8,128)(2,1)S(1)}, u32[]{:S(2)}, u32[]{:S(2)}) collective-permute-start(bf16[2,2,2,32,128]{4,3,2,0,1:T(8,128)(2,1)S(1)} %pad_maximum_fusion.8), channel_id=1, source_target_pairs={{0,32},{1,33},{2,34},{3,35},{4,36},{5,37},{6,38},{7,39},{8,40},{9,... | collective-permute-start | bytes 196616 | tf_op jit(solution)/shard_map/ppermute | solution.py:96
  17.6 3.6 %collective-permute-done.2 = bf16[2,2,2,32,128]{4,3,2,0,1:T(8,128)(2,1)S(1)} collective-permute-done((bf16[2,2,2,32,128]{4,3,2,0,1:T(8,128)(2,1)S(1)}, bf16[2,2,2,32,128]{4,3,2,0,1:T(8,128)(2,1)S(1)}, u32[]{:S(2)}, u32[]{:S(2)}) %collective-permute-start.2) | collective-permute-done | bytes 65568 | tf_op jit(solution)/shard_map/ppermute | solution.py:96
  21.3 2.1 %collective-permute-start.3 = (bf16[2,2,2,2,32,128]{5,4,3,0,2,1:T(8,128)(2,1)S(1)}, bf16[2,2,2,2,32,128]{5,4,3,0,2,1:T(8,128)(2,1)S(1)}, u32[]{:S(2)}, u32[]{:S(2)}) collective-permute-start(bf16[2,2,2,2,32,128]{5,4,3,0,2,1:T(8,128)(2,1)S(1)} %pad_maximum_fusion.7), channel_id=1, source_target_pairs={{0,8},{1,9},{2,10},{3,11},{4,12},{5,13},{6,14},{7,15},{8,0},{9,1},... | collective-permute-start | bytes 393224 | tf_op jit(solution)/shard_map/ppermute | solution.py:96
  23.4 5.3 %collective-permute-done.3 = bf16[2,2,2,2,32,128]{5,4,3,0,2,1:T(8,128)(2,1)S(1)} collective-permute-done((bf16[2,2,2,2,32,128]{5,4,3,0,2,1:T(8,128)(2,1)S(1)}, bf16[2,2,2,2,32,128]{5,4,3,0,2,1:T(8,128)(2,1)S(1)}, u32[]{:S(2)}, u32[]{:S(2)}) %collective-permute-start.3) | collective-permute-done | bytes 131104 | tf_op jit(solution)/shard_map/ppermute | solution.py:96
  28.7 1.7 collective-permute-start.4
  30.4 4.8 %collective-permute-done.4 = bf16[2,2,2,2,2,32,128]{6,5,4,3,0,2,1:T(8,128)(2,1)S(1)} collective-permute-done((bf16[2,2,2,2,2,32,128]{6,5,4,3,0,2,1:T(8,128)(2,1)S(1)}, bf16[2,2,2,2,2,32,128]{6,5,4,3,0,2,1:T(8,128)(2,1)S(1)}, u32[]{:S(2)}, u32[]{:S(2)}) %collective-permute-start.4) | collective-permute-done | bytes 262176 | tf_op jit(solution)/shard_map/ppermute | solution.py:96
  36.4 8.1 %collective-permute-done.8 = bf16[2,2,2,2,2,2,16,128]{7,6,5,3,0,2,4,1:T(8,128)(2,1)S(1)} collective-permute-done((bf16[2,2,2,2,2,2,16,128]{7,6,5,3,0,2,4,1:T(8,128)(2,1)S(1)}, bf16[2,2,2,2,2,2,16,128]{7,6,5,3,0,2,4,1:T(8,128)(2,1)S(1)}, u32[]{:S(2)}, u32[]{:S(2)}) %collective-permute-start.8) | collective-permute-done | bytes 262176 | tf_op jit(solution)/shard_map/ppermute | solution.py:96
  46.8 7.0 %collective-permute-done.9 = bf16[2,2,2,2,2,2,2,16,128]{8,7,6,3,0,2,4,1,5:T(8,128)(2,1)S(1)} collective-permute-done((bf16[2,2,2,2,2,2,2,16,128]{8,7,6,3,0,2,4,1,5:T(8,128)(2,1)S(1)}, bf16[2,2,2,2,2,2,2,16,128]{8,7,6,3,0,2,4,1,5:T(8,128)(2,1)S(1)}, u32[]{:S(2)}, u32[]{:S(2)}) %collective-permute-start.9) | collective-permute-done | bytes 524320 | tf_op jit(solution)/shard_map/ppermute | solution.py:96
  59.1 1.4 select_bitcast_fusion.1
  62.9 2.5 %pad_maximum_fusion = bf16[2,2,2,2,2,2,2,2,2,32,128]{10,9,8,7,6,5,4,3,2,1,0:T(8,128)(2,1)} fusion(bf16[2,2,2,2,2,2,2,2,2,16,128]{10,9,8,7,6,5,4,3,2,1,0:T(8,128)(2,1)S(1)} %maximum_bitcast_fusion.1, bf16[2,2,2,2,2,2,2,1,2,16,128]{10,9,8,6,3,0,2,4,1,5,7:T(8,128)(2,1)S(1)} %get-tuple-element.8, ...), kind=kLoop, calls=%fused_computation | loop fusion | flops 9437184 | bytes 8388608 | tf_op jit(solution)/shard_map/concatenate | solution.py:119
  65.4 45.2 %shard_map.37 = bf16[64,4,2,32,128]{4,3,2,1,0:T(8,128)(2,1)S(1)} custom-call(bf16[4,128,32,128]{3,2,1,0:T(8,128)(2,1)} %bitcast.130, bf16[25,128,128]{2,1,0:T(8,128)(2,1)S(1)} %slice.20.fb_ref, bf16[25,128,128]{2,1,0:T(8,128)(2,1)S(1)} %slice.21.fa_ref), custom_call_target="tpu_custom_call" | custom-call | flops 26843545600 | bytes 10027008 | tf_op jit(solution)/shard_map/pallas_call | solution.py:59
  110.9 1.7 copy-done.1
  112.6 4.3 %collective-permute-done.11 = bf16[2,2,2,2,2,2,2,64,128]{8,7,6,5,4,3,2,1,0:T(8,128)(2,1)} collective-permute-done((bf16[2,2,2,2,2,2,2,64,128]{8,7,6,5,4,3,2,1,0:T(8,128)(2,1)S(1)}, bf16[2,2,2,2,2,2,2,64,128]{8,7,6,5,4,3,2,1,0:T(8,128)(2,1)}, u32[]{:S(2)}, u32[]{:S(2)}) %collective-permute-start.11) | collective-permute-done | bytes 2097184 | tf_op jit(solution)/shard_map/ppermute | solution.py:128
  116.9 3.2 %convert_add_fusion = f32[2,2,2,2,2,2,2,64,128]{8,7,6,5,4,3,2,1,0:T(8,128)S(1)} fusion(bf16[2,2,2,2,2,2,2,64,128]{8,7,6,5,4,3,2,1,0:T(8,128)(2,1)} %collective-permute-done.11, bf16[2,2,2,2,2,2,2,2,64,128]{9,8,7,6,5,4,3,2,1,0:T(8,128)(2,1)} %bitcast.129, s32[]{:T(128)S(6)} %select_n.221), kind=kLoop, calls=%fused_computation.1 | loop fusion | flops 3145728 | bytes 8388612 | tf_op jit(solution)/shard_map/add | solution.py:130
  124.8 11.5 %collective-permute-done.14 = bf16[2,2,2,2,2,2,32,128]{7,6,5,4,3,2,1,0:T(8,128)(2,1)} collective-permute-done((bf16[2,2,2,2,2,2,32,128]{7,6,5,4,3,2,1,0:T(8,128)(2,1)S(1)}, bf16[2,2,2,2,2,2,32,128]{7,6,5,4,3,2,1,0:T(8,128)(2,1)}, u32[]{:S(2)}, u32[]{:S(2)}) %collective-permute-start.14) | collective-permute-done | bytes 524320 | tf_op jit(solution)/shard_map/ppermute | solution.py:128
  136.3 1.6 bitcast_add_fusion
  142.9 3.5 %collective-permute-done.15 = bf16[2,2,2,2,2,32,128]{6,5,4,3,2,1,0:T(8,128)(2,1)S(1)} collective-permute-done((bf16[2,2,2,2,2,32,128]{6,5,4,3,2,1,0:T(8,128)(2,1)}, bf16[2,2,2,2,2,32,128]{6,5,4,3,2,1,0:T(8,128)(2,1)S(1)}, u32[]{:S(2)}, u32[]{:S(2)}) %collective-permute-start.15) | collective-permute-done | bytes 262176 | tf_op jit(solution)/shard_map/ppermute | solution.py:128
  146.5 2.8 %collective-permute-done.13 = bf16[2,2,2,2,2,32,128]{6,5,4,3,2,1,0:T(8,128)(2,1)S(1)} collective-permute-done((bf16[2,2,2,2,2,32,128]{6,5,4,3,2,1,0:T(8,128)(2,1)S(1)}, bf16[2,2,2,2,2,32,128]{6,5,4,3,2,1,0:T(8,128)(2,1)S(1)}, u32[]{:S(2)}, u32[]{:S(2)}) %collective-permute-start.13) | collective-permute-done | bytes 262176 | tf_op jit(solution)/shard_map/ppermute | solution.py:128
  150.4 1.8 collective-permute-start.16
  152.2 4.8 %collective-permute-done.16 = bf16[2,2,2,2,64,128]{5,4,3,2,1,0:T(8,128)(2,1)S(1)} collective-permute-done((bf16[2,2,2,2,64,128]{5,4,3,2,1,0:T(8,128)(2,1)S(1)}, bf16[2,2,2,2,64,128]{5,4,3,2,1,0:T(8,128)(2,1)S(1)}, u32[]{:S(2)}, u32[]{:S(2)}) %collective-permute-start.16) | collective-permute-done | bytes 262176 | tf_op jit(solution)/shard_map/ppermute | solution.py:128
  157.1 2.4 %collective-permute-start.17 = (f32[2,2,2,64,128]{4,3,2,1,0:T(8,128)S(1)}, f32[2,2,2,64,128]{4,3,2,1,0:T(8,128)S(1)}, u32[]{:S(2)}, u32[]{:S(2)}) collective-permute-start(f32[2,2,2,64,128]{4,3,2,1,0:T(8,128)S(1)} %dynamic-slice_bitcast_fusion.1), channel_id=1, source_target_pairs={{0,8},{1,9},{2,10},{3,11},{4,12},{5,13},{6,14},{7,15},{8,0},{9,1},... | collective-permute-start | bytes 786440 | tf_op jit(solution)/shard_map/ppermute | solution.py:128
  159.5 9.9 %collective-permute-done.17 = f32[2,2,2,64,128]{4,3,2,1,0:T(8,128)S(1)} collective-permute-done((f32[2,2,2,64,128]{4,3,2,1,0:T(8,128)S(1)}, f32[2,2,2,64,128]{4,3,2,1,0:T(8,128)S(1)}, u32[]{:S(2)}, u32[]{:S(2)}) %collective-permute-start.17) | collective-permute-done | bytes 262176 | tf_op jit(solution)/shard_map/ppermute | solution.py:128
  169.4 2.1 %collective-permute-start.18 = (f32[2,2,64,128]{3,2,1,0:T(8,128)S(1)}, f32[2,2,64,128]{3,2,1,0:T(8,128)S(1)}, u32[]{:S(2)}, u32[]{:S(2)}) collective-permute-start(f32[2,2,64,128]{3,2,1,0:T(8,128)S(1)} %dynamic-slice_bitcast_fusion.2), channel_id=1, source_target_pairs={{0,32},{1,33},{2,34},{3,35},{4,36},{5,37},{6,38},{7,39},{8,40},{9,... | collective-permute-start | bytes 393224 | tf_op jit(solution)/shard_map/ppermute | solution.py:128
  171.5 4.5 %collective-permute-done.18 = f32[2,2,64,128]{3,2,1,0:T(8,128)S(1)} collective-permute-done((f32[2,2,64,128]{3,2,1,0:T(8,128)S(1)}, f32[2,2,64,128]{3,2,1,0:T(8,128)S(1)}, u32[]{:S(2)}, u32[]{:S(2)}) %collective-permute-start.18) | collective-permute-done | bytes 131104 | tf_op jit(solution)/shard_map/ppermute | solution.py:128
  176.0 3.5 %collective-permute-start.19 = (f32[2,64,128]{2,1,0:T(8,128)S(1)}, f32[2,64,128]{2,1,0:T(8,128)S(1)}, u32[]{:S(2)}, u32[]{:S(2)}) collective-permute-start(f32[2,64,128]{2,1,0:T(8,128)S(1)} %dynamic-slice_bitcast_fusion.3), channel_id=1, source_target_pairs={{0,128},{1,129},{2,130},{3,131},{4,132},{5,133},{6,134},{7,135},{8... | collective-permute-start | bytes 196616 | tf_op jit(solution)/shard_map/ppermute | solution.py:128
  179.5 2.4 %collective-permute-done.19 = f32[2,64,128]{2,1,0:T(8,128)S(1)} collective-permute-done((f32[2,64,128]{2,1,0:T(8,128)S(1)}, f32[2,64,128]{2,1,0:T(8,128)S(1)}, u32[]{:S(2)}, u32[]{:S(2)}) %collective-permute-start.19) | collective-permute-done | bytes 65568 | tf_op jit(solution)/shard_map/ppermute | solution.py:128
  181.9 6.2 %collective-permute-start.20 = (f32[64,128]{1,0:T(8,128)S(1)}, f32[64,128]{1,0:T(8,128)S(1)}, u32[]{:S(2)}, u32[]{:S(2)}) collective-permute-start(f32[64,128]{1,0:T(8,128)S(1)} %dynamic-slice_bitcast_fusion.4), channel_id=1, source_target_pairs={{0,16},{1,17},{2,18},{3,19},{4,20},{5,21},{6,22},{7,23},{8,24},{9,... | collective-permute-start | bytes 98312 | tf_op jit(solution)/shard_map/ppermute | solution.py:128
  188.1 1.9 collective-permute-done.20
  (77 shorter events, 24.1 us)
Async XLA Ops:
  0.0 0.8 copy-start
  0.9 9.0 %collective-permute-start = (bf16[2,32,128]{2,1,0:T(8,128)(2,1)S(1)}, bf16[2,32,128]{2,1,0:T(8,128)(2,1)S(1)}, u32[]{:S(2)}, u32[]{:S(2)}) collective-permute-start(bf16[2,32,128]{2,1,0:T(8,128)(2,1)S(1)} %bitcast.135), channel_id=1, source_target_pairs={{0,16},{1,17},{2,18},{3,19},{4,20},{5,21},{6,22},{7,23},{8,24},{9,... | collective-permute-start | bytes 49160 | tf_op jit(solution)/shard_map/ppermute | solution.py:96
  9.9 5.5 %collective-permute-start.1 = (bf16[2,2,32,128]{3,2,1,0:T(8,128)(2,1)S(1)}, bf16[2,2,32,128]{3,2,1,0:T(8,128)(2,1)S(1)}, u32[]{:S(2)}, u32[]{:S(2)}) collective-permute-start(bf16[2,2,32,128]{3,2,1,0:T(8,128)(2,1)S(1)} %pad_maximum_fusion.9), channel_id=1, source_target_pairs={{0,128},{1,129},{2,130},{3,131},{4,132},{5,133},{6,134},{7,135},{8... | collective-permute-start | bytes 98312 | tf_op jit(solution)/shard_map/ppermute | solution.py:96
  15.4 5.9 %collective-permute-start.2 = (bf16[2,2,2,32,128]{4,3,2,0,1:T(8,128)(2,1)S(1)}, bf16[2,2,2,32,128]{4,3,2,0,1:T(8,128)(2,1)S(1)}, u32[]{:S(2)}, u32[]{:S(2)}) collective-permute-start(bf16[2,2,2,32,128]{4,3,2,0,1:T(8,128)(2,1)S(1)} %pad_maximum_fusion.8), channel_id=1, source_target_pairs={{0,32},{1,33},{2,34},{3,35},{4,36},{5,37},{6,38},{7,39},{8,40},{9,... | collective-permute-start | bytes 196616 | tf_op jit(solution)/shard_map/ppermute | solution.py:96
  21.3 7.4 %collective-permute-start.3 = (bf16[2,2,2,2,32,128]{5,4,3,0,2,1:T(8,128)(2,1)S(1)}, bf16[2,2,2,2,32,128]{5,4,3,0,2,1:T(8,128)(2,1)S(1)}, u32[]{:S(2)}, u32[]{:S(2)}) collective-permute-start(bf16[2,2,2,2,32,128]{5,4,3,0,2,1:T(8,128)(2,1)S(1)} %pad_maximum_fusion.7), channel_id=1, source_target_pairs={{0,8},{1,9},{2,10},{3,11},{4,12},{5,13},{6,14},{7,15},{8,0},{9,1},... | collective-permute-start | bytes 393224 | tf_op jit(solution)/shard_map/ppermute | solution.py:96
  28.7 6.5 %collective-permute-start.4 = (bf16[2,2,2,2,2,32,128]{6,5,4,3,0,2,1:T(8,128)(2,1)S(1)}, bf16[2,2,2,2,2,32,128]{6,5,4,3,0,2,1:T(8,128)(2,1)S(1)}, u32[]{:S(2)}, u32[]{:S(2)}) collective-permute-start(bf16[2,2,2,2,2,32,128]{6,5,4,3,0,2,1:T(8,128)(2,1)S(1)} %pad_maximum_fusion.6), channel_id=1, source_target_pairs={{0,64},{1,65},{2,66},{3,67},{4,68},{5,69},{6,70},{7,71},{8,72},{9,... | collective-permute-start | bytes 786440 | tf_op jit(solution)/shard_map/ppermute | solution.py:96
  35.3 9.2 %collective-permute-start.8 = (bf16[2,2,2,2,2,2,16,128]{7,6,5,3,0,2,4,1:T(8,128)(2,1)S(1)}, bf16[2,2,2,2,2,2,16,128]{7,6,5,3,0,2,4,1:T(8,128)(2,1)S(1)}, u32[]{:S(2)}, u32[]{:S(2)}) collective-permute-start(bf16[2,2,2,2,2,2,16,128]{7,6,5,3,0,2,4,1:T(8,128)(2,1)S(1)} %get-tuple-element.18), channel_id=1, source_target_pairs={{0,2},{1,3},{2,0},{3,1},{4,6},{5,7},{6,4},{7,5},{8,10},{9,11},{10,... | collective-permute-start | bytes 786440 | tf_op jit(solution)/shard_map/ppermute | solution.py:96
  36.4 9.2 %collective-permute-start.5 = (bf16[2,2,2,2,2,2,16,128]{7,6,5,3,0,2,4,1:T(8,128)(2,1)S(1)}, bf16[2,2,2,2,2,2,16,128]{7,6,5,3,0,2,4,1:T(8,128)(2,1)S(1)}, u32[]{:S(2)}, u32[]{:S(2)}) collective-permute-start(bf16[2,2,2,2,2,2,16,128]{7,6,5,3,0,2,4,1:T(8,128)(2,1)S(1)} %get-tuple-element.17), channel_id=1, source_target_pairs={{0,4},{1,5},{2,6},{3,7},{4,0},{5,1},{6,2},{7,3},{8,12},{9,13},{10,... | collective-permute-start | bytes 786440 | tf_op jit(solution)/shard_map/ppermute | solution.py:96
  44.6 9.3 %collective-permute-start.9 = (bf16[2,2,2,2,2,2,2,16,128]{8,7,6,3,0,2,4,1,5:T(8,128)(2,1)S(1)}, bf16[2,2,2,2,2,2,2,16,128]{8,7,6,3,0,2,4,1,5:T(8,128)(2,1)S(1)}, u32[]{:S(2)}, u32[]{:S(2)}) collective-permute-start(bf16[2,2,2,2,2,2,2,16,128]{8,7,6,3,0,2,4,1,5:T(8,128)(2,1)S(1)} %pad_maximum_fusion.4), channel_id=1, source_target_pairs={{0,4},{1,5},{2,6},{3,7},{4,0},{5,1},{6,2},{7,3},{8,12},{9,13},{10,... | collective-permute-start | bytes 1572872 | tf_op jit(solution)/shard_map/ppermute | solution.py:96
  45.7 9.3 %collective-permute-start.6 = (bf16[2,2,2,2,2,2,2,16,128]{8,7,6,3,0,2,4,1,5:T(8,128)(2,1)S(1)}, bf16[2,2,2,2,2,2,2,16,128]{8,7,6,3,0,2,4,1,5:T(8,128)(2,1)S(1)}, u32[]{:S(2)}, u32[]{:S(2)}) collective-permute-start(bf16[2,2,2,2,2,2,2,16,128]{8,7,6,3,0,2,4,1,5:T(8,128)(2,1)S(1)} %pad_maximum_fusion.3), channel_id=1, source_target_pairs={{0,2},{1,3},{2,0},{3,1},{4,6},{5,7},{6,4},{7,5},{8,10},{9,11},{10,... | collective-permute-start | bytes 1572872 | tf_op jit(solution)/shard_map/ppermute | solution.py:96
  55.0 2.5 %copy-start.6 = (bf16[25,16384]{1,0:T(8,128)(2,1)S(1)}, bf16[25,16384]{1,0:T(8,128)(2,1)}, u32[]{:S(2)}) copy-start(bf16[25,16384]{1,0:T(8,128)(2,1)} %param.5) | copy-start | bytes 2457604
  55.1 4.0 %collective-permute-start.10 = (bf16[2,2,2,2,2,2,2,2,16,128]{9,8,7,6,3,0,2,4,1,5:T(8,128)(2,1)}, bf16[2,2,2,2,2,2,2,2,16,128]{9,8,7,6,3,0,2,4,1,5:T(8,128)(2,1)}, u32[]{:S(2)}, u32[]{:S(2)}) collective-permute-start(bf16[2,2,2,2,2,2,2,2,16,128]{9,8,7,6,3,0,2,4,1,5:T(8,128)(2,1)} %pad_maximum_fusion.2), channel_id=1, source_target_pairs={{0,1},{1,0},{2,3},{3,2},{4,5},{5,4},{6,7},{7,6},{8,9},{9,8},{10,11... | collective-permute-start | bytes 3145736 | tf_op jit(solution)/shard_map/ppermute | solution.py:96
  55.1 0.8 copy-start.3
  57.0 3.6 %collective-permute-start.7 = (bf16[2,2,2,2,2,2,2,2,16,128]{9,8,7,6,3,0,2,4,1,5:T(8,128)(2,1)}, bf16[2,2,2,2,2,2,2,2,16,128]{9,8,7,6,3,0,2,4,1,5:T(8,128)(2,1)}, u32[]{:S(2)}, u32[]{:S(2)}) collective-permute-start(bf16[2,2,2,2,2,2,2,2,16,128]{9,8,7,6,3,0,2,4,1,5:T(8,128)(2,1)} %pad_maximum_fusion.1), channel_id=1, source_target_pairs={{0,1},{1,0},{2,3},{3,2},{4,5},{5,4},{6,7},{7,6},{8,9},{9,8},{10,11... | collective-permute-start | bytes 3145736 | tf_op jit(solution)/shard_map/ppermute | solution.py:96
  57.5 1.2 copy-start.7
  60.5 1.0 copy-start.4
  110.6 2.0 %copy-start.1 = (bf16[64,4,2,32,128]{4,3,2,1,0:T(8,128)(2,1)}, bf16[64,4,2,32,128]{4,3,2,1,0:T(8,128)(2,1)S(1)}, u32[]{:S(2)}) copy-start(bf16[64,4,2,32,128]{4,3,2,1,0:T(8,128)(2,1)S(1)} %shard_map.37) | copy-start | bytes 12582916
  112.6 4.3 %collective-permute-start.11 = (bf16[2,2,2,2,2,2,2,64,128]{8,7,6,5,4,3,2,1,0:T(8,128)(2,1)S(1)}, bf16[2,2,2,2,2,2,2,64,128]{8,7,6,5,4,3,2,1,0:T(8,128)(2,1)}, u32[]{:S(2)}, u32[]{:S(2)}) collective-permute-start(bf16[2,2,2,2,2,2,2,64,128]{8,7,6,5,4,3,2,1,0:T(8,128)(2,1)S(1)} %dynamic-slice_bitcast_fusion), channel_id=1, source_target_pairs={{0,1},{1,0},{2,3},{3,2},{4,5},{5,4},{6,7},{7,6},{8,9},{9,8},{10,11... | collective-permute-start | bytes 6291464 | tf_op jit(solution)/shard_map/ppermute | solution.py:128
  120.7 1.4 copy-start.2
  122.2 14.2 %collective-permute-start.14 = (bf16[2,2,2,2,2,2,32,128]{7,6,5,4,3,2,1,0:T(8,128)(2,1)S(1)}, bf16[2,2,2,2,2,2,32,128]{7,6,5,4,3,2,1,0:T(8,128)(2,1)}, u32[]{:S(2)}, u32[]{:S(2)}) collective-permute-start(bf16[2,2,2,2,2,2,32,128]{7,6,5,4,3,2,1,0:T(8,128)(2,1)S(1)} %fusion.1), channel_id=1, source_target_pairs={{0,4},{1,5},{2,6},{3,7},{4,0},{5,1},{6,2},{7,3},{8,12},{9,13},{10,... | collective-permute-start | bytes 1572872 | tf_op jit(solution)/shard_map/ppermute | solution.py:128
  123.9 15.8 %collective-permute-start.12 = (bf16[2,2,2,2,2,2,32,128]{7,6,4,3,2,1,0,5:T(8,128)(2,1)}, bf16[2,2,2,2,2,2,32,128]{7,6,4,3,2,1,0,5:T(8,128)(2,1)}, u32[]{:S(2)}, u32[]{:S(2)}) collective-permute-start(bf16[2,2,2,2,2,2,32,128]{7,6,4,3,2,1,0,5:T(8,128)(2,1)} %fusion.2), channel_id=1, source_target_pairs={{0,2},{1,3},{2,0},{3,1},{4,6},{5,7},{6,4},{7,5},{8,10},{9,11},{10,... | collective-permute-start | bytes 1572872 | tf_op jit(solution)/shard_map/ppermute | solution.py:128
  138.7 7.7 %collective-permute-start.15 = (bf16[2,2,2,2,2,32,128]{6,5,4,3,2,1,0:T(8,128)(2,1)}, bf16[2,2,2,2,2,32,128]{6,5,4,3,2,1,0:T(8,128)(2,1)S(1)}, u32[]{:S(2)}, u32[]{:S(2)}) collective-permute-start(bf16[2,2,2,2,2,32,128]{6,5,4,3,2,1,0:T(8,128)(2,1)} %fusion.9), channel_id=1, source_target_pairs={{0,2},{1,3},{2,0},{3,1},{4,6},{5,7},{6,4},{7,5},{8,10},{9,11},{10,... | collective-permute-start | bytes 786440 | tf_op jit(solution)/shard_map/ppermute | solution.py:128
  140.9 1.0 copy-start.5
  141.9 7.3 %collective-permute-start.13 = (bf16[2,2,2,2,2,32,128]{6,5,4,3,2,1,0:T(8,128)(2,1)S(1)}, bf16[2,2,2,2,2,32,128]{6,5,4,3,2,1,0:T(8,128)(2,1)S(1)}, u32[]{:S(2)}, u32[]{:S(2)}) collective-permute-start(bf16[2,2,2,2,2,32,128]{6,5,4,3,2,1,0:T(8,128)(2,1)S(1)} %fusion.8), channel_id=1, source_target_pairs={{0,4},{1,5},{2,6},{3,7},{4,0},{5,1},{6,2},{7,3},{8,12},{9,13},{10,... | collective-permute-start | bytes 786440 | tf_op jit(solution)/shard_map/ppermute | solution.py:128
  150.4 6.6 %collective-permute-start.16 = (bf16[2,2,2,2,64,128]{5,4,3,2,1,0:T(8,128)(2,1)S(1)}, bf16[2,2,2,2,64,128]{5,4,3,2,1,0:T(8,128)(2,1)S(1)}, u32[]{:S(2)}, u32[]{:S(2)}) collective-permute-start(bf16[2,2,2,2,64,128]{5,4,3,2,1,0:T(8,128)(2,1)S(1)} %fusion.11), channel_id=1, source_target_pairs={{0,64},{1,65},{2,66},{3,67},{4,68},{5,69},{6,70},{7,71},{8,72},{9,... | collective-permute-start | bytes 786440 | tf_op jit(solution)/shard_map/ppermute | solution.py:128
  157.1 12.2 %collective-permute-start.17 = (f32[2,2,2,64,128]{4,3,2,1,0:T(8,128)S(1)}, f32[2,2,2,64,128]{4,3,2,1,0:T(8,128)S(1)}, u32[]{:S(2)}, u32[]{:S(2)}) collective-permute-start(f32[2,2,2,64,128]{4,3,2,1,0:T(8,128)S(1)} %dynamic-slice_bitcast_fusion.1), channel_id=1, source_target_pairs={{0,8},{1,9},{2,10},{3,11},{4,12},{5,13},{6,14},{7,15},{8,0},{9,1},... | collective-permute-start | bytes 786440 | tf_op jit(solution)/shard_map/ppermute | solution.py:128
  169.4 6.6 %collective-permute-start.18 = (f32[2,2,64,128]{3,2,1,0:T(8,128)S(1)}, f32[2,2,64,128]{3,2,1,0:T(8,128)S(1)}, u32[]{:S(2)}, u32[]{:S(2)}) collective-permute-start(f32[2,2,64,128]{3,2,1,0:T(8,128)S(1)} %dynamic-slice_bitcast_fusion.2), channel_id=1, source_target_pairs={{0,32},{1,33},{2,34},{3,35},{4,36},{5,37},{6,38},{7,39},{8,40},{9,... | collective-permute-start | bytes 393224 | tf_op jit(solution)/shard_map/ppermute | solution.py:128
  176.0 5.9 %collective-permute-start.19 = (f32[2,64,128]{2,1,0:T(8,128)S(1)}, f32[2,64,128]{2,1,0:T(8,128)S(1)}, u32[]{:S(2)}, u32[]{:S(2)}) collective-permute-start(f32[2,64,128]{2,1,0:T(8,128)S(1)} %dynamic-slice_bitcast_fusion.3), channel_id=1, source_target_pairs={{0,128},{1,129},{2,130},{3,131},{4,132},{5,133},{6,134},{7,135},{8... | collective-permute-start | bytes 196616 | tf_op jit(solution)/shard_map/ppermute | solution.py:128
  181.9 8.1 %collective-permute-start.20 = (f32[64,128]{1,0:T(8,128)S(1)}, f32[64,128]{1,0:T(8,128)S(1)}, u32[]{:S(2)}, u32[]{:S(2)}) collective-permute-start(f32[64,128]{1,0:T(8,128)S(1)} %dynamic-slice_bitcast_fusion.4), channel_id=1, source_target_pairs={{0,16},{1,17},{2,18},{3,19},{4,20},{5,21},{6,22},{7,23},{8,24},{9,... | collective-permute-start | bytes 98312 | tf_op jit(solution)/shard_map/ppermute | solution.py:128

commit v10 on v9

--- a/solution.py
+++ b/solution.py
@@ -13,7 +13,7 @@
 D = 128
 I_BLOCK = 16
 P_GROUP = 5
-SMALL_SEND = 65536
+SMALL_SEND = 0
 
 
 def ladder_kernel(n_p, n_aux, rpp, t_ref, fb_ref, fa_ref, out_ref, w_ref, r_ref, l_ref):

time: 191 us -> 185 us (0.969)
  waiting for transfers between devices: 79.2 us -> 73.2 us
    ppermute x10, waiting for transfers between devices: 45.4 us -> 39.5 us  [reduce_step(): recv = lax.ppermute(send.astype(wire), axes, xor_perm(n, b))]
where the time goes in v10:
time: 185 us
  waiting for transfers between devices  73.2 us (40%)
  Pallas kernels  45.2 us (24%)
  starting transfers between devices  38.8 us (21%)
  other arithmetic  15.5 us (8%)
  local copies, waits for them, and re-layouts  11.4 us (6%)
    pallas_call x1, Pallas kernels, local_ladder(): pl.pallas_call(kernel, grid=(steps,), in_specs=[pl.BlockSpec((n_aux, I_BL...  45.2 us
    ppermute x10, waiting for transfers between devices, reduce_step(): recv = lax.ppermute(send.astype(wire), axes, xor_perm(n, b))  39.5 us
    ppermute x11, waiting for transfers between devices, gather_step(): recv = lax.ppermute(buf, axes, xor_perm(n, b))  33.7 us
    ppermute x10, starting transfers between devices, reduce_step(): recv = lax.ppermute(send.astype(wire), axes, xor_perm(n, b))  19.5 us
    ppermute x11, starting transfers between devices, gather_step(): recv = lax.ppermute(buf, axes, xor_perm(n, b))  19.3 us
    unnamed x20, local copies, waits for them, and re-layouts  7.83 us
    add x9, other arithmetic, reduce_step(): return keep.astype(jnp.float32) + recv.astype(jnp.float32)  7.31 us
    another operation x20, other arithmetic, gather_step(): return jnp.stack([lo, hi], axis=k)  5.44 us
  transfers between devices with their start and end apart: 21, of which 17 were waited for; matrix products, arithmetic and copies ran while one was open for 5% of the time, Pallas kernels for 0%

profile of v10, /device:TPU:2, one launch (start us, length us, event | category | flops | bytes accessed | tf_op | source)
XLA Modules:
  0.0 184.5 jit_solution(8329332905988287200)
XLA Ops:
  0.9 7.3 %collective-permute-start = (bf16[2,32,128]{2,1,0:T(8,128)(2,1)S(1)}, bf16[2,32,128]{2,1,0:T(8,128)(2,1)S(1)}, u32[]{:S(2)}, u32[]{:S(2)}) collective-permute-start(bf16[2,32,128]{2,1,0:T(8,128)(2,1)S(1)} %bitcast.135), channel_id=1, source_target_pairs={{0,16},{1,17},{2,18},{3,19},{4,20},{5,21},{6,22},{7,23},{8,24},{9,... | collective-permute-start | bytes 49160 | tf_op jit(solution)/shard_map/ppermute | solution.py:96
  8.1 1.7 collective-permute-done
  9.9 3.3 %collective-permute-start.1 = (bf16[2,2,32,128]{3,2,1,0:T(8,128)(2,1)S(1)}, bf16[2,2,32,128]{3,2,1,0:T(8,128)(2,1)S(1)}, u32[]{:S(2)}, u32[]{:S(2)}) collective-permute-start(bf16[2,2,32,128]{3,2,1,0:T(8,128)(2,1)S(1)} %pad_maximum_fusion.9), channel_id=1, source_target_pairs={{0,128},{1,129},{2,130},{3,131},{4,132},{5,133},{6,134},{7,135},{8... | collective-permute-start | bytes 98312 | tf_op jit(solution)/shard_map/ppermute | solution.py:96
  13.2 2.2 %collective-permute-done.1 = bf16[2,2,32,128]{3,2,1,0:T(8,128)(2,1)S(1)} collective-permute-done((bf16[2,2,32,128]{3,2,1,0:T(8,128)(2,1)S(1)}, bf16[2,2,32,128]{3,2,1,0:T(8,128)(2,1)S(1)}, u32[]{:S(2)}, u32[]{:S(2)}) %collective-permute-start.1) | collective-permute-done | bytes 32800 | tf_op jit(solution)/shard_map/ppermute | solution.py:96
  15.4 2.2 %collective-permute-start.2 = (bf16[2,2,2,32,128]{4,3,2,0,1:T(8,128)(2,1)S(1)}, bf16[2,2,2,32,128]{4,3,2,0,1:T(8,128)(2,1)S(1)}, u32[]{:S(2)}, u32[]{:S(2)}) collective-permute-start(bf16[2,2,2,32,128]{4,3,2,0,1:T(8,128)(2,1)S(1)} %pad_maximum_fusion.8), channel_id=1, source_target_pairs={{0,32},{1,33},{2,34},{3,35},{4,36},{5,37},{6,38},{7,39},{8,40},{9,... | collective-permute-start | bytes 196616 | tf_op jit(solution)/shard_map/ppermute | solution.py:96
  17.6 3.6 %collective-permute-done.2 = bf16[2,2,2,32,128]{4,3,2,0,1:T(8,128)(2,1)S(1)} collective-permute-done((bf16[2,2,2,32,128]{4,3,2,0,1:T(8,128)(2,1)S(1)}, bf16[2,2,2,32,128]{4,3,2,0,1:T(8,128)(2,1)S(1)}, u32[]{:S(2)}, u32[]{:S(2)}) %collective-permute-start.2) | collective-permute-done | bytes 65568 | tf_op jit(solution)/shard_map/ppermute | solution.py:96
  21.3 2.1 %collective-permute-start.3 = (bf16[2,2,2,2,32,128]{5,4,3,0,2,1:T(8,128)(2,1)S(1)}, bf16[2,2,2,2,32,128]{5,4,3,0,2,1:T(8,128)(2,1)S(1)}, u32[]{:S(2)}, u32[]{:S(2)}) collective-permute-start(bf16[2,2,2,2,32,128]{5,4,3,0,2,1:T(8,128)(2,1)S(1)} %pad_maximum_fusion.7), channel_id=1, source_target_pairs={{0,8},{1,9},{2,10},{3,11},{4,12},{5,13},{6,14},{7,15},{8,0},{9,1},... | collective-permute-start | bytes 393224 | tf_op jit(solution)/shard_map/ppermute | solution.py:96
  23.4 5.3 %collective-permute-done.3 = bf16[2,2,2,2,32,128]{5,4,3,0,2,1:T(8,128)(2,1)S(1)} collective-permute-done((bf16[2,2,2,2,32,128]{5,4,3,0,2,1:T(8,128)(2,1)S(1)}, bf16[2,2,2,2,32,128]{5,4,3,0,2,1:T(8,128)(2,1)S(1)}, u32[]{:S(2)}, u32[]{:S(2)}) %collective-permute-start.3) | collective-permute-done | bytes 131104 | tf_op jit(solution)/shard_map/ppermute | solution.py:96
  28.7 1.7 collective-permute-start.4
  30.4 4.8 %collective-permute-done.4 = bf16[2,2,2,2,2,32,128]{6,5,4,3,0,2,1:T(8,128)(2,1)S(1)} collective-permute-done((bf16[2,2,2,2,2,32,128]{6,5,4,3,0,2,1:T(8,128)(2,1)S(1)}, bf16[2,2,2,2,2,32,128]{6,5,4,3,0,2,1:T(8,128)(2,1)S(1)}, u32[]{:S(2)}, u32[]{:S(2)}) %collective-permute-start.4) | collective-permute-done | bytes 262176 | tf_op jit(solution)/shard_map/ppermute | solution.py:96
  36.4 8.1 %collective-permute-done.8 = bf16[2,2,2,2,2,2,16,128]{7,6,5,3,0,2,4,1:T(8,128)(2,1)S(1)} collective-permute-done((bf16[2,2,2,2,2,2,16,128]{7,6,5,3,0,2,4,1:T(8,128)(2,1)S(1)}, bf16[2,2,2,2,2,2,16,128]{7,6,5,3,0,2,4,1:T(8,128)(2,1)S(1)}, u32[]{:S(2)}, u32[]{:S(2)}) %collective-permute-start.8) | collective-permute-done | bytes 262176 | tf_op jit(solution)/shard_map/ppermute | solution.py:96
  46.8 7.0 %collective-permute-done.9 = bf16[2,2,2,2,2,2,2,16,128]{8,7,6,3,0,2,4,1,5:T(8,128)(2,1)S(1)} collective-permute-done((bf16[2,2,2,2,2,2,2,16,128]{8,7,6,3,0,2,4,1,5:T(8,128)(2,1)S(1)}, bf16[2,2,2,2,2,2,2,16,128]{8,7,6,3,0,2,4,1,5:T(8,128)(2,1)S(1)}, u32[]{:S(2)}, u32[]{:S(2)}) %collective-permute-start.9) | collective-permute-done | bytes 524320 | tf_op jit(solution)/shard_map/ppermute | solution.py:96
  59.1 1.4 select_bitcast_fusion.1
  62.9 2.5 %pad_maximum_fusion = bf16[2,2,2,2,2,2,2,2,2,32,128]{10,9,8,7,6,5,4,3,2,1,0:T(8,128)(2,1)} fusion(bf16[2,2,2,2,2,2,2,2,2,16,128]{10,9,8,7,6,5,4,3,2,1,0:T(8,128)(2,1)S(1)} %maximum_bitcast_fusion.1, bf16[2,2,2,2,2,2,2,1,2,16,128]{10,9,8,6,3,0,2,4,1,5,7:T(8,128)(2,1)S(1)} %get-tuple-element.8, ...), kind=kLoop, calls=%fused_computation | loop fusion | flops 9437184 | bytes 8388608 | tf_op jit(solution)/shard_map/concatenate | solution.py:119
  65.4 45.2 %shard_map.37 = bf16[64,4,2,32,128]{4,3,2,1,0:T(8,128)(2,1)S(1)} custom-call(bf16[4,128,32,128]{3,2,1,0:T(8,128)(2,1)} %bitcast.130, bf16[25,128,128]{2,1,0:T(8,128)(2,1)S(1)} %slice.20.fb_ref, bf16[25,128,128]{2,1,0:T(8,128)(2,1)S(1)} %slice.21.fa_ref), custom_call_target="tpu_custom_call" | custom-call | flops 26843545600 | bytes 10027008 | tf_op jit(solution)/shard_map/pallas_call | solution.py:59
  110.9 1.7 copy-done.1
  112.6 4.3 %collective-permute-done.11 = bf16[2,2,2,2,2,2,2,64,128]{8,7,6,5,4,3,2,1,0:T(8,128)(2,1)} collective-permute-done((bf16[2,2,2,2,2,2,2,64,128]{8,7,6,5,4,3,2,1,0:T(8,128)(2,1)S(1)}, bf16[2,2,2,2,2,2,2,64,128]{8,7,6,5,4,3,2,1,0:T(8,128)(2,1)}, u32[]{:S(2)}, u32[]{:S(2)}) %collective-permute-start.11) | collective-permute-done | bytes 2097184 | tf_op jit(solution)/shard_map/ppermute | solution.py:128
  116.9 3.2 %convert_add_fusion = f32[2,2,2,2,2,2,2,64,128]{8,7,6,5,4,3,2,1,0:T(8,128)S(1)} fusion(bf16[2,2,2,2,2,2,2,64,128]{8,7,6,5,4,3,2,1,0:T(8,128)(2,1)} %collective-permute-done.11, bf16[2,2,2,2,2,2,2,2,64,128]{9,8,7,6,5,4,3,2,1,0:T(8,128)(2,1)} %bitcast.129, s32[]{:T(128)S(6)} %select_n.221), kind=kLoop, calls=%fused_computation.1 | loop fusion | flops 3145728 | bytes 8388612 | tf_op jit(solution)/shard_map/add | solution.py:130
  124.8 11.5 %collective-permute-done.14 = bf16[2,2,2,2,2,2,32,128]{7,6,5,4,3,2,1,0:T(8,128)(2,1)} collective-permute-done((bf16[2,2,2,2,2,2,32,128]{7,6,5,4,3,2,1,0:T(8,128)(2,1)S(1)}, bf16[2,2,2,2,2,2,32,128]{7,6,5,4,3,2,1,0:T(8,128)(2,1)}, u32[]{:S(2)}, u32[]{:S(2)}) %collective-permute-start.14) | collective-permute-done | bytes 524320 | tf_op jit(solution)/shard_map/ppermute | solution.py:128
  136.3 1.6 bitcast_add_fusion
  142.9 3.5 %collective-permute-done.15 = bf16[2,2,2,2,2,32,128]{6,5,4,3,2,1,0:T(8,128)(2,1)S(1)} collective-permute-done((bf16[2,2,2,2,2,32,128]{6,5,4,3,2,1,0:T(8,128)(2,1)}, bf16[2,2,2,2,2,32,128]{6,5,4,3,2,1,0:T(8,128)(2,1)S(1)}, u32[]{:S(2)}, u32[]{:S(2)}) %collective-permute-start.15) | collective-permute-done | bytes 262176 | tf_op jit(solution)/shard_map/ppermute | solution.py:128
  146.5 2.8 %collective-permute-done.13 = bf16[2,2,2,2,2,32,128]{6,5,4,3,2,1,0:T(8,128)(2,1)S(1)} collective-permute-done((bf16[2,2,2,2,2,32,128]{6,5,4,3,2,1,0:T(8,128)(2,1)S(1)}, bf16[2,2,2,2,2,32,128]{6,5,4,3,2,1,0:T(8,128)(2,1)S(1)}, u32[]{:S(2)}, u32[]{:S(2)}) %collective-permute-start.13) | collective-permute-done | bytes 262176 | tf_op jit(solution)/shard_map/ppermute | solution.py:128
  150.4 1.8 collective-permute-start.16
  152.2 4.8 %collective-permute-done.16 = bf16[2,2,2,2,64,128]{5,4,3,2,1,0:T(8,128)(2,1)S(1)} collective-permute-done((bf16[2,2,2,2,64,128]{5,4,3,2,1,0:T(8,128)(2,1)S(1)}, bf16[2,2,2,2,64,128]{5,4,3,2,1,0:T(8,128)(2,1)S(1)}, u32[]{:S(2)}, u32[]{:S(2)}) %collective-permute-start.16) | collective-permute-done | bytes 262176 | tf_op jit(solution)/shard_map/ppermute | solution.py:128
  157.1 2.4 %collective-permute-start.17 = (bf16[2,2,2,64,128]{4,3,2,1,0:T(8,128)(2,1)S(1)}, bf16[2,2,2,64,128]{4,3,2,1,0:T(8,128)(2,1)S(1)}, u32[]{:S(2)}, u32[]{:S(2)}) collective-permute-start(bf16[2,2,2,64,128]{4,3,2,1,0:T(8,128)(2,1)S(1)} %fusion.12), channel_id=1, source_target_pairs={{0,8},{1,9},{2,10},{3,11},{4,12},{5,13},{6,14},{7,15},{8,0},{9,1},... | collective-permute-start | bytes 393224 | tf_op jit(solution)/shard_map/ppermute | solution.py:128
  159.5 5.0 %collective-permute-done.17 = bf16[2,2,2,64,128]{4,3,2,1,0:T(8,128)(2,1)S(1)} collective-permute-done((bf16[2,2,2,64,128]{4,3,2,1,0:T(8,128)(2,1)S(1)}, bf16[2,2,2,64,128]{4,3,2,1,0:T(8,128)(2,1)S(1)}, u32[]{:S(2)}, u32[]{:S(2)}) %collective-permute-start.17) | collective-permute-done | bytes 131104 | tf_op jit(solution)/shard_map/ppermute | solution.py:128
  164.6 2.0 %collective-permute-start.18 = (bf16[2,2,64,128]{3,2,1,0:T(8,128)(2,1)S(1)}, bf16[2,2,64,128]{3,2,1,0:T(8,128)(2,1)S(1)}, u32[]{:S(2)}, u32[]{:S(2)}) collective-permute-start(bf16[2,2,64,128]{3,2,1,0:T(8,128)(2,1)S(1)} %fusion.13), channel_id=1, source_target_pairs={{0,32},{1,33},{2,34},{3,35},{4,36},{5,37},{6,38},{7,39},{8,40},{9,... | collective-permute-start | bytes 196616 | tf_op jit(solution)/shard_map/ppermute | solution.py:128
  166.5 3.9 %collective-permute-done.18 = bf16[2,2,64,128]{3,2,1,0:T(8,128)(2,1)S(1)} collective-permute-done((bf16[2,2,64,128]{3,2,1,0:T(8,128)(2,1)S(1)}, bf16[2,2,64,128]{3,2,1,0:T(8,128)(2,1)S(1)}, u32[]{:S(2)}, u32[]{:S(2)}) %collective-permute-start.18) | collective-permute-done | bytes 65568 | tf_op jit(solution)/shard_map/ppermute | solution.py:128
  170.5 3.4 %collective-permute-start.19 = (bf16[2,64,128]{2,1,0:T(8,128)(2,1)S(1)}, bf16[2,64,128]{2,1,0:T(8,128)(2,1)S(1)}, u32[]{:S(2)}, u32[]{:S(2)}) collective-permute-start(bf16[2,64,128]{2,1,0:T(8,128)(2,1)S(1)} %fusion.14), channel_id=1, source_target_pairs={{0,128},{1,129},{2,130},{3,131},{4,132},{5,133},{6,134},{7,135},{8... | collective-permute-start | bytes 98312 | tf_op jit(solution)/shard_map/ppermute | solution.py:128
  173.9 2.1 %collective-permute-done.19 = bf16[2,64,128]{2,1,0:T(8,128)(2,1)S(1)} collective-permute-done((bf16[2,64,128]{2,1,0:T(8,128)(2,1)S(1)}, bf16[2,64,128]{2,1,0:T(8,128)(2,1)S(1)}, u32[]{:S(2)}, u32[]{:S(2)}) %collective-permute-start.19) | collective-permute-done | bytes 32800 | tf_op jit(solution)/shard_map/ppermute | solution.py:128
  176.0 6.2 %collective-permute-start.20 = (bf16[64,128]{1,0:T(8,128)(2,1)S(1)}, bf16[64,128]{1,0:T(8,128)(2,1)S(1)}, u32[]{:S(2)}, u32[]{:S(2)}) collective-permute-start(bf16[64,128]{1,0:T(8,128)(2,1)S(1)} %fusion.16), channel_id=1, source_target_pairs={{0,16},{1,17},{2,18},{3,19},{4,20},{5,21},{6,22},{7,23},{8,24},{9,... | collective-permute-start | bytes 49160 | tf_op jit(solution)/shard_map/ppermute | solution.py:128
  182.2 1.7 collective-permute-done.20
  (77 shorter events, 24.1 us)
Async XLA Ops:
  0.0 0.8 copy-start
  0.9 9.0 %collective-permute-start = (bf16[2,32,128]{2,1,0:T(8,128)(2,1)S(1)}, bf16[2,32,128]{2,1,0:T(8,128)(2,1)S(1)}, u32[]{:S(2)}, u32[]{:S(2)}) collective-permute-start(bf16[2,32,128]{2,1,0:T(8,128)(2,1)S(1)} %bitcast.135), channel_id=1, source_target_pairs={{0,16},{1,17},{2,18},{3,19},{4,20},{5,21},{6,22},{7,23},{8,24},{9,... | collective-permute-start | bytes 49160 | tf_op jit(solution)/shard_map/ppermute | solution.py:96
  9.9 5.5 %collective-permute-start.1 = (bf16[2,2,32,128]{3,2,1,0:T(8,128)(2,1)S(1)}, bf16[2,2,32,128]{3,2,1,0:T(8,128)(2,1)S(1)}, u32[]{:S(2)}, u32[]{:S(2)}) collective-permute-start(bf16[2,2,32,128]{3,2,1,0:T(8,128)(2,1)S(1)} %pad_maximum_fusion.9), channel_id=1, source_target_pairs={{0,128},{1,129},{2,130},{3,131},{4,132},{5,133},{6,134},{7,135},{8... | collective-permute-start | bytes 98312 | tf_op jit(solution)/shard_map/ppermute | solution.py:96
  15.4 5.9 %collective-permute-start.2 = (bf16[2,2,2,32,128]{4,3,2,0,1:T(8,128)(2,1)S(1)}, bf16[2,2,2,32,128]{4,3,2,0,1:T(8,128)(2,1)S(1)}, u32[]{:S(2)}, u32[]{:S(2)}) collective-permute-start(bf16[2,2,2,32,128]{4,3,2,0,1:T(8,128)(2,1)S(1)} %pad_maximum_fusion.8), channel_id=1, source_target_pairs={{0,32},{1,33},{2,34},{3,35},{4,36},{5,37},{6,38},{7,39},{8,40},{9,... | collective-permute-start | bytes 196616 | tf_op jit(solution)/shard_map/ppermute | solution.py:96
  21.3 7.4 %collective-permute-start.3 = (bf16[2,2,2,2,32,128]{5,4,3,0,2,1:T(8,128)(2,1)S(1)}, bf16[2,2,2,2,32,128]{5,4,3,0,2,1:T(8,128)(2,1)S(1)}, u32[]{:S(2)}, u32[]{:S(2)}) collective-permute-start(bf16[2,2,2,2,32,128]{5,4,3,0,2,1:T(8,128)(2,1)S(1)} %pad_maximum_fusion.7), channel_id=1, source_target_pairs={{0,8},{1,9},{2,10},{3,11},{4,12},{5,13},{6,14},{7,15},{8,0},{9,1},... | collective-permute-start | bytes 393224 | tf_op jit(solution)/shard_map/ppermute | solution.py:96
  28.7 6.5 %collective-permute-start.4 = (bf16[2,2,2,2,2,32,128]{6,5,4,3,0,2,1:T(8,128)(2,1)S(1)}, bf16[2,2,2,2,2,32,128]{6,5,4,3,0,2,1:T(8,128)(2,1)S(1)}, u32[]{:S(2)}, u32[]{:S(2)}) collective-permute-start(bf16[2,2,2,2,2,32,128]{6,5,4,3,0,2,1:T(8,128)(2,1)S(1)} %pad_maximum_fusion.6), channel_id=1, source_target_pairs={{0,64},{1,65},{2,66},{3,67},{4,68},{5,69},{6,70},{7,71},{8,72},{9,... | collective-permute-start | bytes 786440 | tf_op jit(solution)/shard_map/ppermute | solution.py:96
  35.3 9.2 %collective-permute-start.8 = (bf16[2,2,2,2,2,2,16,128]{7,6,5,3,0,2,4,1:T(8,128)(2,1)S(1)}, bf16[2,2,2,2,2,2,16,128]{7,6,5,3,0,2,4,1:T(8,128)(2,1)S(1)}, u32[]{:S(2)}, u32[]{:S(2)}) collective-permute-start(bf16[2,2,2,2,2,2,16,128]{7,6,5,3,0,2,4,1:T(8,128)(2,1)S(1)} %get-tuple-element.18), channel_id=1, source_target_pairs={{0,2},{1,3},{2,0},{3,1},{4,6},{5,7},{6,4},{7,5},{8,10},{9,11},{10,... | collective-permute-start | bytes 786440 | tf_op jit(solution)/shard_map/ppermute | solution.py:96
  36.4 9.2 %collective-permute-start.5 = (bf16[2,2,2,2,2,2,16,128]{7,6,5,3,0,2,4,1:T(8,128)(2,1)S(1)}, bf16[2,2,2,2,2,2,16,128]{7,6,5,3,0,2,4,1:T(8,128)(2,1)S(1)}, u32[]{:S(2)}, u32[]{:S(2)}) collective-permute-start(bf16[2,2,2,2,2,2,16,128]{7,6,5,3,0,2,4,1:T(8,128)(2,1)S(1)} %get-tuple-element.17), channel_id=1, source_target_pairs={{0,4},{1,5},{2,6},{3,7},{4,0},{5,1},{6,2},{7,3},{8,12},{9,13},{10,... | collective-permute-start | bytes 786440 | tf_op jit(solution)/shard_map/ppermute | solution.py:96
  44.6 9.3 %collective-permute-start.9 = (bf16[2,2,2,2,2,2,2,16,128]{8,7,6,3,0,2,4,1,5:T(8,128)(2,1)S(1)}, bf16[2,2,2,2,2,2,2,16,128]{8,7,6,3,0,2,4,1,5:T(8,128)(2,1)S(1)}, u32[]{:S(2)}, u32[]{:S(2)}) collective-permute-start(bf16[2,2,2,2,2,2,2,16,128]{8,7,6,3,0,2,4,1,5:T(8,128)(2,1)S(1)} %pad_maximum_fusion.4), channel_id=1, source_target_pairs={{0,4},{1,5},{2,6},{3,7},{4,0},{5,1},{6,2},{7,3},{8,12},{9,13},{10,... | collective-permute-start | bytes 1572872 | tf_op jit(solution)/shard_map/ppermute | solution.py:96
  45.7 9.3 %collective-permute-start.6 = (bf16[2,2,2,2,2,2,2,16,128]{8,7,6,3,0,2,4,1,5:T(8,128)(2,1)S(1)}, bf16[2,2,2,2,2,2,2,16,128]{8,7,6,3,0,2,4,1,5:T(8,128)(2,1)S(1)}, u32[]{:S(2)}, u32[]{:S(2)}) collective-permute-start(bf16[2,2,2,2,2,2,2,16,128]{8,7,6,3,0,2,4,1,5:T(8,128)(2,1)S(1)} %pad_maximum_fusion.3), channel_id=1, source_target_pairs={{0,2},{1,3},{2,0},{3,1},{4,6},{5,7},{6,4},{7,5},{8,10},{9,11},{10,... | collective-permute-start | bytes 1572872 | tf_op jit(solution)/shard_map/ppermute | solution.py:96
  55.0 2.5 %copy-start.6 = (bf16[25,16384]{1,0:T(8,128)(2,1)S(1)}, bf16[25,16384]{1,0:T(8,128)(2,1)}, u32[]{:S(2)}) copy-start(bf16[25,16384]{1,0:T(8,128)(2,1)} %param.5) | copy-start | bytes 2457604
  55.1 4.0 %collective-permute-start.10 = (bf16[2,2,2,2,2,2,2,2,16,128]{9,8,7,6,3,0,2,4,1,5:T(8,128)(2,1)}, bf16[2,2,2,2,2,2,2,2,16,128]{9,8,7,6,3,0,2,4,1,5:T(8,128)(2,1)}, u32[]{:S(2)}, u32[]{:S(2)}) collective-permute-start(bf16[2,2,2,2,2,2,2,2,16,128]{9,8,7,6,3,0,2,4,1,5:T(8,128)(2,1)} %pad_maximum_fusion.2), channel_id=1, source_target_pairs={{0,1},{1,0},{2,3},{3,2},{4,5},{5,4},{6,7},{7,6},{8,9},{9,8},{10,11... | collective-permute-start | bytes 3145736 | tf_op jit(solution)/shard_map/ppermute | solution.py:96
  55.1 0.8 copy-start.3
  57.0 3.6 %collective-permute-start.7 = (bf16[2,2,2,2,2,2,2,2,16,128]{9,8,7,6,3,0,2,4,1,5:T(8,128)(2,1)}, bf16[2,2,2,2,2,2,2,2,16,128]{9,8,7,6,3,0,2,4,1,5:T(8,128)(2,1)}, u32[]{:S(2)}, u32[]{:S(2)}) collective-permute-start(bf16[2,2,2,2,2,2,2,2,16,128]{9,8,7,6,3,0,2,4,1,5:T(8,128)(2,1)} %pad_maximum_fusion.1), channel_id=1, source_target_pairs={{0,1},{1,0},{2,3},{3,2},{4,5},{5,4},{6,7},{7,6},{8,9},{9,8},{10,11... | collective-permute-start | bytes 3145736 | tf_op jit(solution)/shard_map/ppermute | solution.py:96
  57.5 1.2 copy-start.7
  60.5 1.0 copy-start.4
  110.6 2.0 %copy-start.1 = (bf16[64,4,2,32,128]{4,3,2,1,0:T(8,128)(2,1)}, bf16[64,4,2,32,128]{4,3,2,1,0:T(8,128)(2,1)S(1)}, u32[]{:S(2)}) copy-start(bf16[64,4,2,32,128]{4,3,2,1,0:T(8,128)(2,1)S(1)} %shard_map.37) | copy-start | bytes 12582916
  112.6 4.3 %collective-permute-start.11 = (bf16[2,2,2,2,2,2,2,64,128]{8,7,6,5,4,3,2,1,0:T(8,128)(2,1)S(1)}, bf16[2,2,2,2,2,2,2,64,128]{8,7,6,5,4,3,2,1,0:T(8,128)(2,1)}, u32[]{:S(2)}, u32[]{:S(2)}) collective-permute-start(bf16[2,2,2,2,2,2,2,64,128]{8,7,6,5,4,3,2,1,0:T(8,128)(2,1)S(1)} %dynamic-slice_bitcast_fusion), channel_id=1, source_target_pairs={{0,1},{1,0},{2,3},{3,2},{4,5},{5,4},{6,7},{7,6},{8,9},{9,8},{10,11... | collective-permute-start | bytes 6291464 | tf_op jit(solution)/shard_map/ppermute | solution.py:128
  120.7 1.4 copy-start.2
  122.2 14.2 %collective-permute-start.14 = (bf16[2,2,2,2,2,2,32,128]{7,6,5,4,3,2,1,0:T(8,128)(2,1)S(1)}, bf16[2,2,2,2,2,2,32,128]{7,6,5,4,3,2,1,0:T(8,128)(2,1)}, u32[]{:S(2)}, u32[]{:S(2)}) collective-permute-start(bf16[2,2,2,2,2,2,32,128]{7,6,5,4,3,2,1,0:T(8,128)(2,1)S(1)} %fusion.1), channel_id=1, source_target_pairs={{0,4},{1,5},{2,6},{3,7},{4,0},{5,1},{6,2},{7,3},{8,12},{9,13},{10,... | collective-permute-start | bytes 1572872 | tf_op jit(solution)/shard_map/ppermute | solution.py:128
  123.9 15.8 %collective-permute-start.12 = (bf16[2,2,2,2,2,2,32,128]{7,6,4,3,2,1,0,5:T(8,128)(2,1)}, bf16[2,2,2,2,2,2,32,128]{7,6,4,3,2,1,0,5:T(8,128)(2,1)}, u32[]{:S(2)}, u32[]{:S(2)}) collective-permute-start(bf16[2,2,2,2,2,2,32,128]{7,6,4,3,2,1,0,5:T(8,128)(2,1)} %fusion.2), channel_id=1, source_target_pairs={{0,2},{1,3},{2,0},{3,1},{4,6},{5,7},{6,4},{7,5},{8,10},{9,11},{10,... | collective-permute-start | bytes 1572872 | tf_op jit(solution)/shard_map/ppermute | solution.py:128
  138.7 7.7 %collective-permute-start.15 = (bf16[2,2,2,2,2,32,128]{6,5,4,3,2,1,0:T(8,128)(2,1)}, bf16[2,2,2,2,2,32,128]{6,5,4,3,2,1,0:T(8,128)(2,1)S(1)}, u32[]{:S(2)}, u32[]{:S(2)}) collective-permute-start(bf16[2,2,2,2,2,32,128]{6,5,4,3,2,1,0:T(8,128)(2,1)} %fusion.9), channel_id=1, source_target_pairs={{0,2},{1,3},{2,0},{3,1},{4,6},{5,7},{6,4},{7,5},{8,10},{9,11},{10,... | collective-permute-start | bytes 786440 | tf_op jit(solution)/shard_map/ppermute | solution.py:128
  140.9 1.0 copy-start.5
  141.9 7.3 %collective-permute-start.13 = (bf16[2,2,2,2,2,32,128]{6,5,4,3,2,1,0:T(8,128)(2,1)S(1)}, bf16[2,2,2,2,2,32,128]{6,5,4,3,2,1,0:T(8,128)(2,1)S(1)}, u32[]{:S(2)}, u32[]{:S(2)}) collective-permute-start(bf16[2,2,2,2,2,32,128]{6,5,4,3,2,1,0:T(8,128)(2,1)S(1)} %fusion.8), channel_id=1, source_target_pairs={{0,4},{1,5},{2,6},{3,7},{4,0},{5,1},{6,2},{7,3},{8,12},{9,13},{10,... | collective-permute-start | bytes 786440 | tf_op jit(solution)/shard_map/ppermute | solution.py:128
  150.4 6.6 %collective-permute-start.16 = (bf16[2,2,2,2,64,128]{5,4,3,2,1,0:T(8,128)(2,1)S(1)}, bf16[2,2,2,2,64,128]{5,4,3,2,1,0:T(8,128)(2,1)S(1)}, u32[]{:S(2)}, u32[]{:S(2)}) collective-permute-start(bf16[2,2,2,2,64,128]{5,4,3,2,1,0:T(8,128)(2,1)S(1)} %fusion.11), channel_id=1, source_target_pairs={{0,64},{1,65},{2,66},{3,67},{4,68},{5,69},{6,70},{7,71},{8,72},{9,... | collective-permute-start | bytes 786440 | tf_op jit(solution)/shard_map/ppermute | solution.py:128
  157.1 7.4 %collective-permute-start.17 = (bf16[2,2,2,64,128]{4,3,2,1,0:T(8,128)(2,1)S(1)}, bf16[2,2,2,64,128]{4,3,2,1,0:T(8,128)(2,1)S(1)}, u32[]{:S(2)}, u32[]{:S(2)}) collective-permute-start(bf16[2,2,2,64,128]{4,3,2,1,0:T(8,128)(2,1)S(1)} %fusion.12), channel_id=1, source_target_pairs={{0,8},{1,9},{2,10},{3,11},{4,12},{5,13},{6,14},{7,15},{8,0},{9,1},... | collective-permute-start | bytes 393224 | tf_op jit(solution)/shard_map/ppermute | solution.py:128
  164.6 5.9 %collective-permute-start.18 = (bf16[2,2,64,128]{3,2,1,0:T(8,128)(2,1)S(1)}, bf16[2,2,64,128]{3,2,1,0:T(8,128)(2,1)S(1)}, u32[]{:S(2)}, u32[]{:S(2)}) collective-permute-start(bf16[2,2,64,128]{3,2,1,0:T(8,128)(2,1)S(1)} %fusion.13), channel_id=1, source_target_pairs={{0,32},{1,33},{2,34},{3,35},{4,36},{5,37},{6,38},{7,39},{8,40},{9,... | collective-permute-start | bytes 196616 | tf_op jit(solution)/shard_map/ppermute | solution.py:128
  170.5 5.5 %collective-permute-start.19 = (bf16[2,64,128]{2,1,0:T(8,128)(2,1)S(1)}, bf16[2,64,128]{2,1,0:T(8,128)(2,1)S(1)}, u32[]{:S(2)}, u32[]{:S(2)}) collective-permute-start(bf16[2,64,128]{2,1,0:T(8,128)(2,1)S(1)} %fusion.14), channel_id=1, source_target_pairs={{0,128},{1,129},{2,130},{3,131},{4,132},{5,133},{6,134},{7,135},{8... | collective-permute-start | bytes 98312 | tf_op jit(solution)/shard_map/ppermute | solution.py:128
  176.0 7.9 %collective-permute-start.20 = (bf16[64,128]{1,0:T(8,128)(2,1)S(1)}, bf16[64,128]{1,0:T(8,128)(2,1)S(1)}, u32[]{:S(2)}, u32[]{:S(2)}) collective-permute-start(bf16[64,128]{1,0:T(8,128)(2,1)S(1)} %fusion.16), channel_id=1, source_target_pairs={{0,16},{1,17},{2,18},{3,19},{4,20},{5,21},{6,22},{7,23},{8,24},{9,... | collective-permute-start | bytes 49160 | tf_op jit(solution)/shard_map/ppermute | solution.py:128

commit v11 on v10

--- a/solution.py
+++ b/solution.py
@@ -82,10 +82,10 @@
 
 def plan(n_pair, n_aux):
     if (n_pair, n_aux) == (64, 4):
-        return [0], ([1, 2], [2, 1]), [6, 3, 5, 7, 4]
+        return [0], ([1, 2], [2, 1]), [[6, 3], [5, 7], [4]]
     n_bits = (n_pair * n_aux).bit_length() - 1
     rest = list(range(2, n_bits))
-    return [0], ([1], [1]), rest
+    return [0], ([1], [1]), [rest[k:k + 2] for k in range(0, len(rest), 2)]
 
 
 def xor_perm(n, b):
@@ -100,12 +100,34 @@
     return jnp.stack([lo, hi], axis=k)
 
 
-def gather_bits(x, axes, n, first, pair_orders, last, target, split_axis):
+def gather_step4(buf, axes, n, me, b1, b2, k):
+    r1 = lax.ppermute(buf, axes, xor_perm(n, b1))
+    r2 = lax.ppermute(buf, axes, xor_perm(n, b2))
+    r3 = lax.ppermute(buf, axes, [(i, i ^ (1 << b1) ^ (1 << b2)) for i in range(n)])
+    my1 = ((me >> b1) & 1) == 1
+    my2 = ((me >> b2) & 1) == 1
+    rows = []
+    for x1 in (False, True):
+        d1 = my1 != x1
+        row = []
+        for x2 in (False, True):
+            d2 = my2 != x2
+            row.append(jnp.where(d1, jnp.where(d2, r3, r1), jnp.where(d2, r2, buf)))
+        rows.append(jnp.stack(row, axis=k))
+    return jnp.stack(rows, axis=k)
+
+
+def gather_bits(x, axes, n, first_groups, pair_orders, last, target, split_axis):
     n_bits = n.bit_length() - 1
     me = lax.axis_index(axes)
     buf = x
-    for k, b in enumerate(first):
-        buf = gather_step(buf, axes, n, me, b, k)
+    first = []
+    for grp in first_groups:
+        if len(grp) == 2:
+            buf = gather_step4(buf, axes, n, me, grp[0], grp[1], len(first))
+        else:
+            buf = gather_step(buf, axes, n, me, grp[0], len(first))
+        first = first + list(grp)
     ax = len(first) + split_axis
     size = buf.shape[ax] // 2
     halves = []
@@ -128,6 +150,31 @@
     recv = lax.ppermute(send.astype(wire), axes, xor_perm(n, b))
     live.pop(ax)
     return keep.astype(jnp.float32) + recv.astype(jnp.float32)
+
+
+def reduce_step4(buf, axes, n, me, live, b1, b2):
+    my1 = (me >> b1) & 1
+    my2 = (me >> b2) & 1
+    ax1 = live.index(b1)
+    ax2 = live.index(b2) - (1 if live.index(b2) > ax1 else 0)
+
+    def part(v1, v2):
+        blk = lax.dynamic_index_in_dim(buf, v1, axis=ax1, keepdims=False)
+        blk = lax.dynamic_index_in_dim(blk, v2, axis=ax2, keepdims=False)
+        return blk
+
+    total = part(my1, my2).astype(jnp.float32)
+    for v1, v2, perm in (
+        (1 - my1, my2, xor_perm(n, b1)),
+        (my1, 1 - my2, xor_perm(n, b2)),
+        (1 - my1, 1 - my2, [(i, i ^ (1 << b1) ^ (1 << b2)) for i in range(n)]),
+    ):
+        send = part(v1, v2)
+        wire = jnp.bfloat16 if send.size > SMALL_SEND else jnp.float32
+        total = total + lax.ppermute(send.astype(wire), axes, perm).astype(jnp.float32)
+    live.remove(b1)
+    live.remove(b2)
+    return total
 
 
 def reduce_bits(y, axes, n, first, pair_orders, last):
@@ -148,8 +195,11 @@
         halves.append(part)
     live = part_live
     buf = jnp.concatenate(halves, axis=len(live))
-    for b in last:
-        buf = reduce_step(buf, axes, n, me, live, b)
+    for grp in last:
+        if len(grp) == 2:
+            buf = reduce_step4(buf, axes, n, me, live, grp[0], grp[1])
+        else:
+            buf = reduce_step(buf, axes, n, me, live, grp[0])
     return buf
 
 
@@ -167,7 +217,8 @@
     n_bits = n.bit_length() - 1
     aux_bits = n_aux.bit_length() - 1
     target = list(range(aux_bits - 1, -1, -1)) + list(range(n_bits - 1, aux_bits - 1, -1))
-    t_all = gather_bits(amps_q, both, n, last[::-1], [o[::-1] for o in pair_orders], first[::-1], target, 1)
+    head = [grp[::-1] for grp in last[::-1]]
+    t_all = gather_bits(amps_q, both, n, head, [o[::-1] for o in pair_orders], first[::-1], target, 1)
     t_all = t_all.reshape(n_aux, n_pair * rows, cq, D)
     y = local_ladder(t_all, factor_ca, factor_db, n_pair, n_aux)
     rpp = y.shape[2]

time: 185 us -> 188 us (1.016)
  starting transfers between devices: 38.8 us -> 41.6 us
  waiting for transfers between devices: 73.2 us -> 71 us
    ppermute x0 -> x12, waiting for transfers between devices: none -> 28.1 us  [the longest x6 15.3 us: reduce_step4(): lax.ppermute(send.astype(wire), axes, perm).astype(jnp.float32)]
    ppermute x0 -> x12, starting transfers between devices: none -> 22.6 us  [the longest x6 11.5 us: reduce_step4(): lax.ppermute(send.astype(wire), axes, perm).astype(jnp.float32)]
    ppermute x11 -> x7, waiting for transfers between devices: 33.7 us -> 18.5 us  [gather_step(): recv = lax.ppermute(buf, axes, xor_perm(n, b))]
    ppermute x10 -> x6, waiting for transfers between devices: 39.5 us -> 24.4 us  [reduce_step(): recv = lax.ppermute(send.astype(wire), axes, xor_perm(n, b))]
    ppermute x10 -> x6, starting transfers between devices: 19.5 us -> 9.08 us  [reduce_step(): recv = lax.ppermute(send.astype(wire), axes, xor_perm(n, b))]
    ppermute x11 -> x7, starting transfers between devices: 19.3 us -> 9.88 us  [gather_step(): recv = lax.ppermute(buf, axes, xor_perm(n, b))]
    add x9 -> x5, other arithmetic: 7.31 us -> 8.19 us  [reduce_step(): return keep.astype(jnp.float32) + recv.astype(jnp.float32)]
    unnamed x20 -> x14, local copies, waits for them, and re-layouts: 7.83 us -> 8.41 us
  transfers between devices with their start and end apart: 21 -> 25, of which waited for: 17 -> 19; matrix products, arithmetic and copies ran while one was open for 5% -> 7% of each run, Pallas kernels for 0% -> 0%
where the time goes in v11:
time: 188 us
  waiting for transfers between devices  71 us (38%)
  Pallas kernels  45.2 us (24%)
  starting transfers between devices  41.6 us (22%)
  other arithmetic  16.5 us (9%)
  local copies, waits for them, and re-layouts  13 us (7%)
    pallas_call x1, Pallas kernels, local_ladder(): pl.pallas_call(kernel, grid=(steps,), in_specs=[pl.BlockSpec((n_aux, I_BL...  45.2 us
    ppermute x6, waiting for transfers between devices, reduce_step(): recv = lax.ppermute(send.astype(wire), axes, xor_perm(n, b))  24.4 us
    ppermute x7, waiting for transfers between devices, gather_step(): recv = lax.ppermute(buf, axes, xor_perm(n, b))  18.5 us
    ppermute x6, waiting for transfers between devices, reduce_step4(): lax.ppermute(send.astype(wire), axes, perm).astype(jnp.float32)  15.3 us
    ppermute x6, starting transfers between devices, reduce_step4(): lax.ppermute(send.astype(wire), axes, perm).astype(jnp.float32)  11.5 us
    ppermute x7, starting transfers between devices, gather_step(): recv = lax.ppermute(buf, axes, xor_perm(n, b))  9.88 us
    ppermute x6, starting transfers between devices, reduce_step(): recv = lax.ppermute(send.astype(wire), axes, xor_perm(n, b))  9.08 us
    ppermute x2, waiting for transfers between devices, gather_step4(): r3 = lax.ppermute(buf, axes, [(i, i ^ 1 << b1 ^ 1 << b2) for i in range(n)])  8.69 us
  transfers between devices with their start and end apart: 25, of which 19 were waited for; matrix products, arithmetic and copies ran while one was open for 7% of the time, Pallas kernels for 0%

profile of v11, /device:TPU:2, one launch (start us, length us, event | category | flops | bytes accessed | tf_op | source)
XLA Modules:
  0.0 187.6 jit_solution(15246836350804237798)
XLA Ops:
  0.9 7.3 %collective-permute-start = (bf16[2,32,128]{2,1,0:T(8,128)(2,1)S(1)}, bf16[2,32,128]{2,1,0:T(8,128)(2,1)S(1)}, u32[]{:S(2)}, u32[]{:S(2)}) collective-permute-start(bf16[2,32,128]{2,1,0:T(8,128)(2,1)S(1)} %bitcast.161), channel_id=1, source_target_pairs={{0,16},{1,17},{2,18},{3,19},{4,20},{5,21},{6,22},{7,23},{8,24},{9,... | collective-permute-start | bytes 49160 | tf_op jit(solution)/shard_map/ppermute | solution.py:96
  8.1 1.7 collective-permute-done
  9.9 4.8 %collective-permute-start.1 = (bf16[2,2,32,128]{3,2,1,0:T(8,128)(2,1)S(1)}, bf16[2,2,32,128]{3,2,1,0:T(8,128)(2,1)S(1)}, u32[]{:S(2)}, u32[]{:S(2)}) collective-permute-start(bf16[2,2,32,128]{3,2,1,0:T(8,128)(2,1)S(1)} %pad_maximum_fusion.7), channel_id=1, source_target_pairs={{0,160},{1,161},{2,162},{3,163},{4,164},{5,165},{6,166},{7,167},{8... | collective-permute-start | bytes 98312 | tf_op jit(solution)/shard_map/ppermute | solution.py:106
  15.1 1.4 collective-permute-start.3
  17.8 2.3 %collective-permute-done.2 = bf16[2,2,32,128]{3,2,1,0:T(8,128)(2,1)S(1)} collective-permute-done((bf16[2,2,32,128]{3,2,1,0:T(8,128)(2,1)S(1)}, bf16[2,2,32,128]{3,2,1,0:T(8,128)(2,1)S(1)}, u32[]{:S(2)}, u32[]{:S(2)}) %collective-permute-start.2) | collective-permute-done | bytes 32800 | tf_op jit(solution)/shard_map/ppermute | solution.py:104
  20.5 3.1 %collective-permute-start.4 = (bf16[2,2,2,2,32,128]{5,4,3,0,2,1:T(8,128)(2,1)S(1)}, bf16[2,2,2,2,32,128]{5,4,3,0,2,1:T(8,128)(2,1)S(1)}, u32[]{:S(2)}, u32[]{:S(2)}) collective-permute-start(bf16[2,2,2,2,32,128]{5,4,3,0,2,1:T(8,128)(2,1)S(1)} %pad_maximum_fusion.6), channel_id=1, source_target_pairs={{0,72},{1,73},{2,74},{3,75},{4,76},{5,77},{6,78},{7,79},{8,64},{9,... | collective-permute-start | bytes 393224 | tf_op jit(solution)/shard_map/ppermute | solution.py:106
  25.0 7.3 %collective-permute-done.4 = bf16[2,2,2,2,32,128]{5,4,3,0,2,1:T(8,128)(2,1)S(1)} collective-permute-done((bf16[2,2,2,2,32,128]{5,4,3,0,2,1:T(8,128)(2,1)S(1)}, bf16[2,2,2,2,32,128]{5,4,3,0,2,1:T(8,128)(2,1)S(1)}, u32[]{:S(2)}, u32[]{:S(2)}) %collective-permute-start.4) | collective-permute-done | bytes 131104 | tf_op jit(solution)/shard_map/ppermute | solution.py:106
  32.4 1.4 collective-permute-done.5
  35.3 5.4 %collective-permute-done.10 = bf16[2,2,2,2,2,2,16,128]{7,6,5,3,0,2,4,1:T(8,128)(2,1)S(1)} collective-permute-done((bf16[2,2,2,2,2,2,16,128]{7,6,5,3,0,2,4,1:T(8,128)(2,1)S(1)}, bf16[2,2,2,2,2,2,16,128]{7,6,5,3,0,2,4,1:T(8,128)(2,1)S(1)}, u32[]{:S(2)}, u32[]{:S(2)}) %collective-permute-start.10) | collective-permute-done | bytes 262176 | tf_op jit(solution)/shard_map/ppermute | solution.py:96
  42.7 10.3 %collective-permute-done.11 = bf16[2,2,2,2,2,2,2,16,128]{8,7,6,3,0,2,4,1,5:T(8,128)(2,1)S(1)} collective-permute-done((bf16[2,2,2,2,2,2,2,16,128]{8,7,6,3,0,2,4,1,5:T(8,128)(2,1)S(1)}, bf16[2,2,2,2,2,2,2,16,128]{8,7,6,3,0,2,4,1,5:T(8,128)(2,1)S(1)}, u32[]{:S(2)}, u32[]{:S(2)}) %collective-permute-start.11) | collective-permute-done | bytes 524320 | tf_op jit(solution)/shard_map/ppermute | solution.py:96
  56.6 1.5 copy.20
  58.2 1.5 copy.21
  59.8 1.4 select_bitcast_fusion.1
  63.5 2.5 %pad_maximum_fusion = bf16[2,2,2,2,2,2,2,2,2,32,128]{10,9,8,7,6,5,4,3,2,1,0:T(8,128)(2,1)} fusion(bf16[2,2,2,2,2,2,2,2,2,16,128]{10,9,8,7,6,5,4,3,2,1,0:T(8,128)(2,1)S(1)} %maximum_bitcast_fusion.1, bf16[2,2,2,2,2,2,2,1,2,16,128]{10,9,8,6,3,0,2,4,1,5,7:T(8,128)(2,1)S(1)} %get-tuple-element.8, ...), kind=kLoop, calls=%fused_computation | loop fusion | flops 9437184 | bytes 8388608 | tf_op jit(solution)/shard_map/concatenate | solution.py:141
  66.0 45.2 %shard_map.37 = bf16[64,4,2,32,128]{4,3,2,1,0:T(8,128)(2,1)S(1)} custom-call(bf16[4,128,32,128]{3,2,1,0:T(8,128)(2,1)} %bitcast.156, bf16[25,128,128]{2,1,0:T(8,128)(2,1)S(1)} %slice.20.fb_ref, bf16[25,128,128]{2,1,0:T(8,128)(2,1)S(1)} %slice.21.fa_ref), custom_call_target="tpu_custom_call" | custom-call | flops 26843545600 | bytes 10027008 | tf_op jit(solution)/shard_map/pallas_call | solution.py:59
  111.6 1.7 copy-done.1
  113.2 4.3 %collective-permute-done.13 = bf16[2,2,2,2,2,2,2,64,128]{8,7,6,5,4,3,2,1,0:T(8,128)(2,1)} collective-permute-done((bf16[2,2,2,2,2,2,2,64,128]{8,7,6,5,4,3,2,1,0:T(8,128)(2,1)S(1)}, bf16[2,2,2,2,2,2,2,64,128]{8,7,6,5,4,3,2,1,0:T(8,128)(2,1)}, u32[]{:S(2)}, u32[]{:S(2)}) %collective-permute-start.13) | collective-permute-done | bytes 2097184 | tf_op jit(solution)/shard_map/ppermute | solution.py:150
  117.5 3.2 %convert_add_fusion = f32[2,2,2,2,2,2,2,64,128]{8,7,6,5,4,3,2,1,0:T(8,128)S(1)} fusion(bf16[2,2,2,2,2,2,2,64,128]{8,7,6,5,4,3,2,1,0:T(8,128)(2,1)} %collective-permute-done.13, bf16[2,2,2,2,2,2,2,2,64,128]{9,8,7,6,5,4,3,2,1,0:T(8,128)(2,1)} %bitcast.155, s32[]{:T(128)S(6)} %select_n.309), kind=kLoop, calls=%fused_computation.1 | loop fusion | flops 3145728 | bytes 8388612 | tf_op jit(solution)/shard_map/add | solution.py:152
  125.1 11.9 %collective-permute-done.16 = bf16[2,2,2,2,2,2,32,128]{7,6,5,4,3,2,1,0:T(8,128)(2,1)} collective-permute-done((bf16[2,2,2,2,2,2,32,128]{7,6,5,4,3,2,1,0:T(8,128)(2,1)S(1)}, bf16[2,2,2,2,2,2,32,128]{7,6,5,4,3,2,1,0:T(8,128)(2,1)}, u32[]{:S(2)}, u32[]{:S(2)}) %collective-permute-start.16) | collective-permute-done | bytes 524320 | tf_op jit(solution)/shard_map/ppermute | solution.py:150
  137.0 1.6 bitcast_add_fusion
  140.1 2.2 %fusion = f32[2,2,2,2,2,2,32,128]{7,6,4,3,2,1,0,5:T(8,128)} fusion(bf16[2,2,2,2,2,2,32,128]{7,6,4,3,2,1,0,5:T(8,128)(2,1)} %collective-permute-done.14, f32[2,2,2,2,2,2,2,32,128]{8,7,6,5,4,3,2,1,0:T(8,128)S(1)} %get-tuple-element.6, s32[]{:T(128)S(6)} %select_n.311), kind=kLoop, calls=%fused_computation.17 | loop fusion | flops 524288 | bytes 2621444 | tf_op jit(solution)/shard_map/add | solution.py:152
  144.1 3.0 %collective-permute-done.17 = bf16[2,2,2,2,2,32,128]{6,5,4,3,2,1,0:T(8,128)(2,1)S(1)} collective-permute-done((bf16[2,2,2,2,2,32,128]{6,5,4,3,2,1,0:T(8,128)(2,1)}, bf16[2,2,2,2,2,32,128]{6,5,4,3,2,1,0:T(8,128)(2,1)S(1)}, u32[]{:S(2)}, u32[]{:S(2)}) %collective-permute-start.17) | collective-permute-done | bytes 262176 | tf_op jit(solution)/shard_map/ppermute | solution.py:150
  147.2 3.5 %collective-permute-done.15 = bf16[2,2,2,2,2,32,128]{6,5,4,3,2,1,0:T(8,128)(2,1)S(1)} collective-permute-done((bf16[2,2,2,2,2,32,128]{6,5,4,3,2,1,0:T(8,128)(2,1)S(1)}, bf16[2,2,2,2,2,32,128]{6,5,4,3,2,1,0:T(8,128)(2,1)S(1)}, u32[]{:S(2)}, u32[]{:S(2)}) %collective-permute-start.15) | collective-permute-done | bytes 262176 | tf_op jit(solution)/shard_map/ppermute | solution.py:150
  152.7 2.6 %collective-permute-start.19 = (bf16[2,2,2,64,128]{4,3,2,1,0:T(8,128)(2,1)S(1)}, bf16[2,2,2,64,128]{4,3,2,1,0:T(8,128)(2,1)S(1)}, u32[]{:S(2)}, u32[]{:S(2)}) collective-permute-start(bf16[2,2,2,64,128]{4,3,2,1,0:T(8,128)(2,1)S(1)} %get-tuple-element.12), channel_id=1, source_target_pairs={{0,8},{1,9},{2,10},{3,11},{4,12},{5,13},{6,14},{7,15},{8,0},{9,1},... | collective-permute-start | bytes 393224 | tf_op jit(solution)/shard_map/ppermute | solution.py:174
  157.2 6.9 %collective-permute-done.19 = bf16[2,2,2,64,128]{4,3,2,1,0:T(8,128)(2,1)S(1)} collective-permute-done((bf16[2,2,2,64,128]{4,3,2,1,0:T(8,128)(2,1)S(1)}, bf16[2,2,2,64,128]{4,3,2,1,0:T(8,128)(2,1)S(1)}, u32[]{:S(2)}, u32[]{:S(2)}) %collective-permute-start.19) | collective-permute-done | bytes 131104 | tf_op jit(solution)/shard_map/ppermute | solution.py:174
  164.1 2.1 %collective-permute-done.20 = bf16[2,2,2,64,128]{4,3,2,1,0:T(8,128)(2,1)S(1)} collective-permute-done((bf16[2,2,2,64,128]{4,3,2,1,0:T(8,128)(2,1)S(1)}, bf16[2,2,2,64,128]{4,3,2,1,0:T(8,128)(2,1)S(1)}, u32[]{:S(2)}, u32[]{:S(2)}) %collective-permute-start.20) | collective-permute-done | bytes 131104 | tf_op jit(solution)/shard_map/ppermute | solution.py:174
  166.4 2.0 %collective-permute-start.21 = (bf16[2,64,128]{2,1,0:T(8,128)(2,1)S(1)}, bf16[2,64,128]{2,1,0:T(8,128)(2,1)S(1)}, u32[]{:S(2)}, u32[]{:S(2)}) collective-permute-start(bf16[2,64,128]{2,1,0:T(8,128)(2,1)S(1)} %get-tuple-element.28), channel_id=1, source_target_pairs={{0,32},{1,33},{2,34},{3,35},{4,36},{5,37},{6,38},{7,39},{8,40},{9,... | collective-permute-start | bytes 98312 | tf_op jit(solution)/shard_map/ppermute | solution.py:174
  168.3 2.7 %collective-permute-start.22 = (bf16[2,64,128]{2,1,0:T(8,128)(2,1)S(1)}, bf16[2,64,128]{2,1,0:T(8,128)(2,1)S(1)}, u32[]{:S(2)}, u32[]{:S(2)}) collective-permute-start(bf16[2,64,128]{2,1,0:T(8,128)(2,1)S(1)} %get-tuple-element.30), channel_id=1, source_target_pairs={{0,128},{1,129},{2,130},{3,131},{4,132},{5,133},{6,134},{7,135},{8... | collective-permute-start | bytes 98312 | tf_op jit(solution)/shard_map/ppermute | solution.py:174
  171.1 2.1 %collective-permute-start.23 = (bf16[2,64,128]{2,1,0:T(8,128)(2,1)S(1)}, bf16[2,64,128]{2,1,0:T(8,128)(2,1)S(1)}, u32[]{:S(2)}, u32[]{:S(2)}) collective-permute-start(bf16[2,64,128]{2,1,0:T(8,128)(2,1)S(1)} %get-tuple-element.29), channel_id=1, source_target_pairs={{0,160},{1,161},{2,162},{3,163},{4,164},{5,165},{6,166},{7,167},{8... | collective-permute-start | bytes 98312 | tf_op jit(solution)/shard_map/ppermute | solution.py:174
  173.8 5.1 %collective-permute-done.23 = bf16[2,64,128]{2,1,0:T(8,128)(2,1)S(1)} collective-permute-done((bf16[2,64,128]{2,1,0:T(8,128)(2,1)S(1)}, bf16[2,64,128]{2,1,0:T(8,128)(2,1)S(1)}, u32[]{:S(2)}, u32[]{:S(2)}) %collective-permute-start.23) | collective-permute-done | bytes 32800 | tf_op jit(solution)/shard_map/ppermute | solution.py:174
  178.9 6.3 %collective-permute-start.24 = (bf16[64,128]{1,0:T(8,128)(2,1)S(1)}, bf16[64,128]{1,0:T(8,128)(2,1)S(1)}, u32[]{:S(2)}, u32[]{:S(2)}) collective-permute-start(bf16[64,128]{1,0:T(8,128)(2,1)S(1)} %fusion.28), channel_id=1, source_target_pairs={{0,16},{1,17},{2,18},{3,19},{4,20},{5,21},{6,22},{7,23},{8,24},{9,... | collective-permute-start | bytes 49160 | tf_op jit(solution)/shard_map/ppermute | solution.py:150
  185.3 1.7 collective-permute-done.24
  (73 shorter events, 27.2 us)
Async XLA Ops:
  0.0 0.8 copy-start
  0.9 9.0 %collective-permute-start = (bf16[2,32,128]{2,1,0:T(8,128)(2,1)S(1)}, bf16[2,32,128]{2,1,0:T(8,128)(2,1)S(1)}, u32[]{:S(2)}, u32[]{:S(2)}) collective-permute-start(bf16[2,32,128]{2,1,0:T(8,128)(2,1)S(1)} %bitcast.161), channel_id=1, source_target_pairs={{0,16},{1,17},{2,18},{3,19},{4,20},{5,21},{6,22},{7,23},{8,24},{9,... | collective-permute-start | bytes 49160 | tf_op jit(solution)/shard_map/ppermute | solution.py:96
  9.9 7.9 %collective-permute-start.1 = (bf16[2,2,32,128]{3,2,1,0:T(8,128)(2,1)S(1)}, bf16[2,2,32,128]{3,2,1,0:T(8,128)(2,1)S(1)}, u32[]{:S(2)}, u32[]{:S(2)}) collective-permute-start(bf16[2,2,32,128]{3,2,1,0:T(8,128)(2,1)S(1)} %pad_maximum_fusion.7), channel_id=1, source_target_pairs={{0,160},{1,161},{2,162},{3,163},{4,164},{5,165},{6,166},{7,167},{8... | collective-permute-start | bytes 98312 | tf_op jit(solution)/shard_map/ppermute | solution.py:106
  14.7 5.4 %collective-permute-start.2 = (bf16[2,2,32,128]{3,2,1,0:T(8,128)(2,1)S(1)}, bf16[2,2,32,128]{3,2,1,0:T(8,128)(2,1)S(1)}, u32[]{:S(2)}, u32[]{:S(2)}) collective-permute-start(bf16[2,2,32,128]{3,2,1,0:T(8,128)(2,1)S(1)} %pad_maximum_fusion.7), channel_id=1, source_target_pairs={{0,128},{1,129},{2,130},{3,131},{4,132},{5,133},{6,134},{7,135},{8... | collective-permute-start | bytes 98312 | tf_op jit(solution)/shard_map/ppermute | solution.py:104
  15.1 5.4 %collective-permute-start.3 = (bf16[2,2,32,128]{3,2,1,0:T(8,128)(2,1)S(1)}, bf16[2,2,32,128]{3,2,1,0:T(8,128)(2,1)S(1)}, u32[]{:S(2)}, u32[]{:S(2)}) collective-permute-start(bf16[2,2,32,128]{3,2,1,0:T(8,128)(2,1)S(1)} %pad_maximum_fusion.7), channel_id=1, source_target_pairs={{0,32},{1,33},{2,34},{3,35},{4,36},{5,37},{6,38},{7,39},{8,40},{9,... | collective-permute-start | bytes 98312 | tf_op jit(solution)/shard_map/ppermute | solution.py:105
  20.5 11.8 %collective-permute-start.4 = (bf16[2,2,2,2,32,128]{5,4,3,0,2,1:T(8,128)(2,1)S(1)}, bf16[2,2,2,2,32,128]{5,4,3,0,2,1:T(8,128)(2,1)S(1)}, u32[]{:S(2)}, u32[]{:S(2)}) collective-permute-start(bf16[2,2,2,2,32,128]{5,4,3,0,2,1:T(8,128)(2,1)S(1)} %pad_maximum_fusion.6), channel_id=1, source_target_pairs={{0,72},{1,73},{2,74},{3,75},{4,76},{5,77},{6,78},{7,79},{8,64},{9,... | collective-permute-start | bytes 393224 | tf_op jit(solution)/shard_map/ppermute | solution.py:106
  23.7 10.1 %collective-permute-start.5 = (bf16[2,2,2,2,32,128]{5,4,3,0,2,1:T(8,128)(2,1)S(1)}, bf16[2,2,2,2,32,128]{5,4,3,0,2,1:T(8,128)(2,1)S(1)}, u32[]{:S(2)}, u32[]{:S(2)}) collective-permute-start(bf16[2,2,2,2,32,128]{5,4,3,0,2,1:T(8,128)(2,1)S(1)} %pad_maximum_fusion.6), channel_id=1, source_target_pairs={{0,8},{1,9},{2,10},{3,11},{4,12},{5,13},{6,14},{7,15},{8,0},{9,1},... | collective-permute-start | bytes 393224 | tf_op jit(solution)/shard_map/ppermute | solution.py:104
  24.6 9.2 %collective-permute-start.6 = (bf16[2,2,2,2,32,128]{5,4,3,0,2,1:T(8,128)(2,1)S(1)}, bf16[2,2,2,2,32,128]{5,4,3,0,2,1:T(8,128)(2,1)S(1)}, u32[]{:S(2)}, u32[]{:S(2)}) collective-permute-start(bf16[2,2,2,2,32,128]{5,4,3,0,2,1:T(8,128)(2,1)S(1)} %pad_maximum_fusion.6), channel_id=1, source_target_pairs={{0,64},{1,65},{2,66},{3,67},{4,68},{5,69},{6,70},{7,71},{8,72},{9,... | collective-permute-start | bytes 393224 | tf_op jit(solution)/shard_map/ppermute | solution.py:105
  33.9 6.7 %collective-permute-start.10 = (bf16[2,2,2,2,2,2,16,128]{7,6,5,3,0,2,4,1:T(8,128)(2,1)S(1)}, bf16[2,2,2,2,2,2,16,128]{7,6,5,3,0,2,4,1:T(8,128)(2,1)S(1)}, u32[]{:S(2)}, u32[]{:S(2)}) collective-permute-start(bf16[2,2,2,2,2,2,16,128]{7,6,5,3,0,2,4,1:T(8,128)(2,1)S(1)} %get-tuple-element.21), channel_id=1, source_target_pairs={{0,2},{1,3},{2,0},{3,1},{4,6},{5,7},{6,4},{7,5},{8,10},{9,11},{10,... | collective-permute-start | bytes 786440 | tf_op jit(solution)/shard_map/ppermute | solution.py:96
  35.3 7.2 %collective-permute-start.7 = (bf16[2,2,2,2,2,2,16,128]{7,6,5,3,0,2,4,1:T(8,128)(2,1)S(1)}, bf16[2,2,2,2,2,2,16,128]{7,6,5,3,0,2,4,1:T(8,128)(2,1)S(1)}, u32[]{:S(2)}, u32[]{:S(2)}) collective-permute-start(bf16[2,2,2,2,2,2,16,128]{7,6,5,3,0,2,4,1:T(8,128)(2,1)S(1)} %get-tuple-element.20), channel_id=1, source_target_pairs={{0,4},{1,5},{2,6},{3,7},{4,0},{5,1},{6,2},{7,3},{8,12},{9,13},{10,... | collective-permute-start | bytes 786440 | tf_op jit(solution)/shard_map/ppermute | solution.py:96
  40.8 12.2 %collective-permute-start.11 = (bf16[2,2,2,2,2,2,2,16,128]{8,7,6,3,0,2,4,1,5:T(8,128)(2,1)S(1)}, bf16[2,2,2,2,2,2,2,16,128]{8,7,6,3,0,2,4,1,5:T(8,128)(2,1)S(1)}, u32[]{:S(2)}, u32[]{:S(2)}) collective-permute-start(bf16[2,2,2,2,2,2,2,16,128]{8,7,6,3,0,2,4,1,5:T(8,128)(2,1)S(1)} %pad_maximum_fusion.4), channel_id=1, source_target_pairs={{0,4},{1,5},{2,6},{3,7},{4,0},{5,1},{6,2},{7,3},{8,12},{9,13},{10,... | collective-permute-start | bytes 1572872 | tf_op jit(solution)/shard_map/ppermute | solution.py:96
  42.6 11.5 %collective-permute-start.8 = (bf16[2,2,2,2,2,2,2,16,128]{8,7,6,3,0,2,4,1,5:T(8,128)(2,1)S(1)}, bf16[2,2,2,2,2,2,2,16,128]{8,7,6,3,0,2,4,1,5:T(8,128)(2,1)S(1)}, u32[]{:S(2)}, u32[]{:S(2)}) collective-permute-start(bf16[2,2,2,2,2,2,2,16,128]{8,7,6,3,0,2,4,1,5:T(8,128)(2,1)S(1)} %pad_maximum_fusion.3), channel_id=1, source_target_pairs={{0,2},{1,3},{2,0},{3,1},{4,6},{5,7},{6,4},{7,5},{8,10},{9,11},{10,... | collective-permute-start | bytes 1572872 | tf_op jit(solution)/shard_map/ppermute | solution.py:96
  54.2 5.6 %collective-permute-start.12 = (bf16[2,2,2,2,2,2,2,2,16,128]{9,8,7,6,3,0,2,4,1,5:T(8,128)(2,1)}, bf16[2,2,2,2,2,2,2,2,16,128]{9,8,7,6,3,0,2,4,1,5:T(8,128)(2,1)}, u32[]{:S(2)}, u32[]{:S(2)}) collective-permute-start(bf16[2,2,2,2,2,2,2,2,16,128]{9,8,7,6,3,0,2,4,1,5:T(8,128)(2,1)} %pad_maximum_fusion.2), channel_id=1, source_target_pairs={{0,1},{1,0},{2,3},{3,2},{4,5},{5,4},{6,7},{7,6},{8,9},{9,8},{10,11... | collective-permute-start | bytes 3145736 | tf_op jit(solution)/shard_map/ppermute | solution.py:96
  54.3 0.8 copy-start.3
  56.1 5.2 %collective-permute-start.9 = (bf16[2,2,2,2,2,2,2,2,16,128]{9,8,7,6,3,0,2,4,1,5:T(8,128)(2,1)}, bf16[2,2,2,2,2,2,2,2,16,128]{9,8,7,6,3,0,2,4,1,5:T(8,128)(2,1)}, u32[]{:S(2)}, u32[]{:S(2)}) collective-permute-start(bf16[2,2,2,2,2,2,2,2,16,128]{9,8,7,6,3,0,2,4,1,5:T(8,128)(2,1)} %pad_maximum_fusion.1), channel_id=1, source_target_pairs={{0,1},{1,0},{2,3},{3,2},{4,5},{5,4},{6,7},{7,6},{8,9},{9,8},{10,11... | collective-permute-start | bytes 3145736 | tf_op jit(solution)/shard_map/ppermute | solution.py:96
  61.1 1.0 copy-start.4
  111.3 2.0 %copy-start.1 = (bf16[64,4,2,32,128]{4,3,2,1,0:T(8,128)(2,1)}, bf16[64,4,2,32,128]{4,3,2,1,0:T(8,128)(2,1)S(1)}, u32[]{:S(2)}) copy-start(bf16[64,4,2,32,128]{4,3,2,1,0:T(8,128)(2,1)S(1)} %shard_map.37) | copy-start | bytes 12582916
  113.2 4.3 %collective-permute-start.13 = (bf16[2,2,2,2,2,2,2,64,128]{8,7,6,5,4,3,2,1,0:T(8,128)(2,1)S(1)}, bf16[2,2,2,2,2,2,2,64,128]{8,7,6,5,4,3,2,1,0:T(8,128)(2,1)}, u32[]{:S(2)}, u32[]{:S(2)}) collective-permute-start(bf16[2,2,2,2,2,2,2,64,128]{8,7,6,5,4,3,2,1,0:T(8,128)(2,1)S(1)} %dynamic-slice_bitcast_fusion), channel_id=1, source_target_pairs={{0,1},{1,0},{2,3},{3,2},{4,5},{5,4},{6,7},{7,6},{8,9},{9,8},{10,11... | collective-permute-start | bytes 6291464 | tf_op jit(solution)/shard_map/ppermute | solution.py:150
  121.4 1.4 copy-start.2
  122.9 14.2 %collective-permute-start.16 = (bf16[2,2,2,2,2,2,32,128]{7,6,5,4,3,2,1,0:T(8,128)(2,1)S(1)}, bf16[2,2,2,2,2,2,32,128]{7,6,5,4,3,2,1,0:T(8,128)(2,1)}, u32[]{:S(2)}, u32[]{:S(2)}) collective-permute-start(bf16[2,2,2,2,2,2,32,128]{7,6,5,4,3,2,1,0:T(8,128)(2,1)S(1)} %fusion.1), channel_id=1, source_target_pairs={{0,4},{1,5},{2,6},{3,7},{4,0},{5,1},{6,2},{7,3},{8,12},{9,13},{10,... | collective-permute-start | bytes 1572872 | tf_op jit(solution)/shard_map/ppermute | solution.py:150
  124.3 15.8 %collective-permute-start.14 = (bf16[2,2,2,2,2,2,32,128]{7,6,4,3,2,1,0,5:T(8,128)(2,1)}, bf16[2,2,2,2,2,2,32,128]{7,6,4,3,2,1,0,5:T(8,128)(2,1)}, u32[]{:S(2)}, u32[]{:S(2)}) collective-permute-start(bf16[2,2,2,2,2,2,32,128]{7,6,4,3,2,1,0,5:T(8,128)(2,1)} %fusion.2), channel_id=1, source_target_pairs={{0,2},{1,3},{2,0},{3,1},{4,6},{5,7},{6,4},{7,5},{8,10},{9,11},{10,... | collective-permute-start | bytes 1572872 | tf_op jit(solution)/shard_map/ppermute | solution.py:150
  139.4 7.7 %collective-permute-start.17 = (bf16[2,2,2,2,2,32,128]{6,5,4,3,2,1,0:T(8,128)(2,1)}, bf16[2,2,2,2,2,32,128]{6,5,4,3,2,1,0:T(8,128)(2,1)S(1)}, u32[]{:S(2)}, u32[]{:S(2)}) collective-permute-start(bf16[2,2,2,2,2,32,128]{6,5,4,3,2,1,0:T(8,128)(2,1)} %fusion.4), channel_id=1, source_target_pairs={{0,2},{1,3},{2,0},{3,1},{4,6},{5,7},{6,4},{7,5},{8,10},{9,11},{10,... | collective-permute-start | bytes 786440 | tf_op jit(solution)/shard_map/ppermute | solution.py:150
  143.4 7.3 %collective-permute-start.15 = (bf16[2,2,2,2,2,32,128]{6,5,4,3,2,1,0:T(8,128)(2,1)S(1)}, bf16[2,2,2,2,2,32,128]{6,5,4,3,2,1,0:T(8,128)(2,1)S(1)}, u32[]{:S(2)}, u32[]{:S(2)}) collective-permute-start(bf16[2,2,2,2,2,32,128]{6,5,4,3,2,1,0:T(8,128)(2,1)S(1)} %fusion.3), channel_id=1, source_target_pairs={{0,4},{1,5},{2,6},{3,7},{4,0},{5,1},{6,2},{7,3},{8,12},{9,13},{10,... | collective-permute-start | bytes 786440 | tf_op jit(solution)/shard_map/ppermute | solution.py:150
  151.9 5.3 %collective-permute-start.18 = (bf16[2,2,2,64,128]{4,3,2,1,0:T(8,128)(2,1)S(1)}, bf16[2,2,2,64,128]{4,3,2,1,0:T(8,128)(2,1)S(1)}, u32[]{:S(2)}, u32[]{:S(2)}) collective-permute-start(bf16[2,2,2,64,128]{4,3,2,1,0:T(8,128)(2,1)S(1)} %get-tuple-element.11), channel_id=1, source_target_pairs={{0,64},{1,65},{2,66},{3,67},{4,68},{5,69},{6,70},{7,71},{8,72},{9,... | collective-permute-start | bytes 393224 | tf_op jit(solution)/shard_map/ppermute | solution.py:174
  152.7 11.4 %collective-permute-start.19 = (bf16[2,2,2,64,128]{4,3,2,1,0:T(8,128)(2,1)S(1)}, bf16[2,2,2,64,128]{4,3,2,1,0:T(8,128)(2,1)S(1)}, u32[]{:S(2)}, u32[]{:S(2)}) collective-permute-start(bf16[2,2,2,64,128]{4,3,2,1,0:T(8,128)(2,1)S(1)} %get-tuple-element.12), channel_id=1, source_target_pairs={{0,8},{1,9},{2,10},{3,11},{4,12},{5,13},{6,14},{7,15},{8,0},{9,1},... | collective-permute-start | bytes 393224 | tf_op jit(solution)/shard_map/ppermute | solution.py:174
  155.3 10.9 %collective-permute-start.20 = (bf16[2,2,2,64,128]{4,3,2,1,0:T(8,128)(2,1)S(1)}, bf16[2,2,2,64,128]{4,3,2,1,0:T(8,128)(2,1)S(1)}, u32[]{:S(2)}, u32[]{:S(2)}) collective-permute-start(bf16[2,2,2,64,128]{4,3,2,1,0:T(8,128)(2,1)S(1)} %get-tuple-element.13), channel_id=1, source_target_pairs={{0,72},{1,73},{2,74},{3,75},{4,76},{5,77},{6,78},{7,79},{8,64},{9,... | collective-permute-start | bytes 393224 | tf_op jit(solution)/shard_map/ppermute | solution.py:174
  166.4 6.8 %collective-permute-start.21 = (bf16[2,64,128]{2,1,0:T(8,128)(2,1)S(1)}, bf16[2,64,128]{2,1,0:T(8,128)(2,1)S(1)}, u32[]{:S(2)}, u32[]{:S(2)}) collective-permute-start(bf16[2,64,128]{2,1,0:T(8,128)(2,1)S(1)} %get-tuple-element.28), channel_id=1, source_target_pairs={{0,32},{1,33},{2,34},{3,35},{4,36},{5,37},{6,38},{7,39},{8,40},{9,... | collective-permute-start | bytes 98312 | tf_op jit(solution)/shard_map/ppermute | solution.py:174
  168.3 5.4 %collective-permute-start.22 = (bf16[2,64,128]{2,1,0:T(8,128)(2,1)S(1)}, bf16[2,64,128]{2,1,0:T(8,128)(2,1)S(1)}, u32[]{:S(2)}, u32[]{:S(2)}) collective-permute-start(bf16[2,64,128]{2,1,0:T(8,128)(2,1)S(1)} %get-tuple-element.30), channel_id=1, source_target_pairs={{0,128},{1,129},{2,130},{3,131},{4,132},{5,133},{6,134},{7,135},{8... | collective-permute-start | bytes 98312 | tf_op jit(solution)/shard_map/ppermute | solution.py:174
  171.1 7.8 %collective-permute-start.23 = (bf16[2,64,128]{2,1,0:T(8,128)(2,1)S(1)}, bf16[2,64,128]{2,1,0:T(8,128)(2,1)S(1)}, u32[]{:S(2)}, u32[]{:S(2)}) collective-permute-start(bf16[2,64,128]{2,1,0:T(8,128)(2,1)S(1)} %get-tuple-element.29), channel_id=1, source_target_pairs={{0,160},{1,161},{2,162},{3,163},{4,164},{5,165},{6,166},{7,167},{8... | collective-permute-start | bytes 98312 | tf_op jit(solution)/shard_map/ppermute | solution.py:174
  178.9 8.1 %collective-permute-start.24 = (bf16[64,128]{1,0:T(8,128)(2,1)S(1)}, bf16[64,128]{1,0:T(8,128)(2,1)S(1)}, u32[]{:S(2)}, u32[]{:S(2)}) collective-permute-start(bf16[64,128]{1,0:T(8,128)(2,1)S(1)} %fusion.28), channel_id=1, source_target_pairs={{0,16},{1,17},{2,18},{3,19},{4,20},{5,21},{6,22},{7,23},{8,24},{9,... | collective-permute-start | bytes 49160 | tf_op jit(solution)/shard_map/ppermute | solution.py:150

commit v12 on v10

--- a/solution.py
+++ b/solution.py
@@ -16,7 +16,7 @@
 SMALL_SEND = 0
 
 
-def ladder_kernel(n_p, n_aux, rpp, t_ref, fb_ref, fa_ref, out_ref, w_ref, r_ref, l_ref):
+def ladder_kernel(n_p, n_aux, rpp, ta_ref, tb_ref, fb_ref, fa_ref, out_ref, w_ref, r_ref, l_ref):
     @pl.when(pl.program_id(0) == 0)
     def _():
         for p in range(n_p):
@@ -24,19 +24,21 @@
             l_ref[:, p * C:(p + 1) * C] = fa_ref[p].astype(jnp.float32).T.astype(jnp.bfloat16)
 
     cq = C // n_aux
-    t_blk = t_ref[...].reshape(n_aux * I_BLOCK * cq, D)
-    for p0 in range(0, n_p, P_GROUP):
-        pn = min(P_GROUP, n_p - p0)
-        v = jnp.dot(
-            t_blk, r_ref[:, p0 * B:(p0 + pn) * B], preferred_element_type=jnp.float32
-        ).astype(jnp.bfloat16)
-        for dp in range(pn):
-            p = p0 + dp
-            for q in range(n_aux):
-                for i in range(I_BLOCK):
-                    r0 = (q * I_BLOCK + i) * cq
-                    w_ref[p * C + q * cq:p * C + (q + 1) * cq, i * B:(i + 1) * B] = (
-                        v[r0:r0 + cq, dp * B:(dp + 1) * B])
+    hq = cq // 2
+    for h, t_ref in enumerate((ta_ref, tb_ref)):
+        t_blk = t_ref[...].reshape(n_aux * I_BLOCK * hq, D)
+        for p0 in range(0, n_p, P_GROUP):
+            pn = min(P_GROUP, n_p - p0)
+            v = jnp.dot(
+                t_blk, r_ref[:, p0 * B:(p0 + pn) * B], preferred_element_type=jnp.float32
+            ).astype(jnp.bfloat16)
+            for dp in range(pn):
+                p = p0 + dp
+                for q in range(n_aux):
+                    for i in range(I_BLOCK):
+                        r0 = (q * I_BLOCK + i) * hq
+                        w0 = p * C + q * cq + h * hq
+                        w_ref[w0:w0 + hq, i * B:(i + 1) * B] = v[r0:r0 + hq, dp * B:(dp + 1) * B]
     y = jnp.dot(l_ref[...], w_ref[...], preferred_element_type=jnp.float32)
     apa = A // n_aux
     for i in range(I_BLOCK):
@@ -44,12 +46,11 @@
             out_ref[i // rpp, q, i % rpp] = y[q * apa:(q + 1) * apa, i * B:(i + 1) * B].astype(out_ref.dtype)
 
 
-def local_ladder(t_all, factor_ca, factor_db, n_pair, n_aux):
+def local_ladder(t_halves, factor_ca, factor_db, n_pair, n_aux):
     n_p = factor_ca.shape[0]
-    nij = t_all.shape[1]
+    nij = t_halves[0].shape[1]
     rpp = nij // n_pair
     apa = A // n_aux
-    t2 = t_all
     r2 = factor_db.reshape(n_p, D, B)
     l2 = factor_ca.reshape(n_p, C, A)
     steps = nij // I_BLOCK
@@ -60,7 +61,8 @@
         kernel,
         grid=(steps,),
         in_specs=[
-            pl.BlockSpec((n_aux, I_BLOCK, C // n_aux, D), lambda g: (0, g, 0, 0)),
+            pl.BlockSpec((n_aux, I_BLOCK, C // n_aux // 2, D), lambda g: (0, g, 0, 0)),
+            pl.BlockSpec((n_aux, I_BLOCK, C // n_aux // 2, D), lambda g: (0, g, 0, 0)),
             pl.BlockSpec((n_p, D, B), lambda g: (0, 0, 0)),
             pl.BlockSpec((n_p, C, A), lambda g: (0, 0, 0)),
         ],
@@ -75,9 +77,9 @@
             dimension_semantics=("arbitrary",), vmem_limit_bytes=48 * 1024 * 1024),
         cost_estimate=pl.CostEstimate(
             flops=flops, transcendentals=0,
-            bytes_accessed=2 * (t2.size + r2.size + l2.size) + 2 * nij * A * B,
+            bytes_accessed=2 * (2 * t_halves[0].size + r2.size + l2.size) + 2 * nij * A * B,
         ),
-    )(t2, r2, l2)
+    )(t_halves[0], t_halves[1], r2, l2)
 
 
 def plan(n_pair, n_aux):
@@ -116,7 +118,7 @@
             part = gather_step(part, axes, n, me, b, len(first) + k)
         perm = [order.index(b) for b in target]
         halves.append(part.transpose(perm + list(range(n_bits, part.ndim))))
-    return jnp.concatenate(halves, axis=n_bits + split_axis)
+    return halves
 
 
 def reduce_step(buf, axes, n, me, live, b):
@@ -168,8 +170,8 @@
     aux_bits = n_aux.bit_length() - 1
     target = list(range(aux_bits - 1, -1, -1)) + list(range(n_bits - 1, aux_bits - 1, -1))
     t_all = gather_bits(amps_q, both, n, last[::-1], [o[::-1] for o in pair_orders], first[::-1], target, 1)
-    t_all = t_all.reshape(n_aux, n_pair * rows, cq, D)
-    y = local_ladder(t_all, factor_ca, factor_db, n_pair, n_aux)
+    t_halves = [t.reshape(n_aux, n_pair * rows, cq // 2, D) for t in t_all]
+    y = local_ladder(t_halves, factor_ca, factor_db, n_pair, n_aux)
     rpp = y.shape[2]
     y = y.reshape(n, rpp * y.shape[3], B)
     mine = reduce_bits(y, both, n, first, pair_orders, last).astype(jnp.bfloat16)

time: 185 us -> 183 us (0.989)
  other arithmetic: 15.5 us -> 13.2 us
    concatenate x1 -> x0, other arithmetic: 2.49 us -> none  [gather_bits(): return jnp.concatenate(halves, axis=n_bits + split_axis)]
    unnamed x20 -> x18, local copies, waits for them, and re-layouts: 7.83 us -> 5.62 us
    another operation x20 -> x21, other arithmetic: 5.44 us -> 5.63 us  [gather_step(): return jnp.stack([lo, hi], axis=k)]
where the time goes in v12:
time: 183 us; the launch traced here: 182 us
  waiting for transfers between devices  72.7 us (40%)
  Pallas kernels  44.7 us (24%)
  starting transfers between devices  39.8 us (22%)
  other arithmetic  13.2 us (7%)
  local copies, waits for them, and re-layouts  11.4 us (6%)
    pallas_call x1, Pallas kernels, local_ladder(): pl.pallas_call(kernel, grid=(steps,), in_specs=[pl.BlockSpec((n_aux, I_BL...  44.7 us
    ppermute x10, waiting for transfers between devices, reduce_step(): recv = lax.ppermute(send.astype(wire), axes, xor_perm(n, b))  39.9 us
    ppermute x11, waiting for transfers between devices, gather_step(): recv = lax.ppermute(buf, axes, xor_perm(n, b))  32.8 us
    ppermute x11, starting transfers between devices, gather_step(): recv = lax.ppermute(buf, axes, xor_perm(n, b))  20.3 us
    ppermute x10, starting transfers between devices, reduce_step(): recv = lax.ppermute(send.astype(wire), axes, xor_perm(n, b))  19.5 us
    add x9, other arithmetic, reduce_step(): return keep.astype(jnp.float32) + recv.astype(jnp.float32)  7.31 us
    another operation x21, other arithmetic, gather_step(): return jnp.stack([lo, hi], axis=k)  5.63 us
    unnamed x18, local copies, waits for them, and re-layouts  5.62 us
  transfers between devices with their start and end apart: 21, of which 17 were waited for; matrix products, arithmetic and copies ran while one was open for 5% of the time, Pallas kernels for 0%

profile of v12, /device:TPU:2, one launch (start us, length us, event | category | flops | bytes accessed | tf_op | source)
XLA Modules:
  0.0 182.2 jit_solution(15707204961703629100)
XLA Ops:
  0.9 7.3 %collective-permute-start = (bf16[2,32,128]{2,1,0:T(8,128)(2,1)S(1)}, bf16[2,32,128]{2,1,0:T(8,128)(2,1)S(1)}, u32[]{:S(2)}, u32[]{:S(2)}) collective-permute-start(bf16[2,32,128]{2,1,0:T(8,128)(2,1)S(1)} %bitcast.135), channel_id=1, source_target_pairs={{0,16},{1,17},{2,18},{3,19},{4,20},{5,21},{6,22},{7,23},{8,24},{9,... | collective-permute-start | bytes 49160 | tf_op jit(solution)/shard_map/ppermute | solution.py:98
  8.1 1.7 collective-permute-done
  9.9 3.3 %collective-permute-start.1 = (bf16[2,2,32,128]{3,2,1,0:T(8,128)(2,1)S(1)}, bf16[2,2,32,128]{3,2,1,0:T(8,128)(2,1)S(1)}, u32[]{:S(2)}, u32[]{:S(2)}) collective-permute-start(bf16[2,2,32,128]{3,2,1,0:T(8,128)(2,1)S(1)} %pad_maximum_fusion.9), channel_id=1, source_target_pairs={{0,128},{1,129},{2,130},{3,131},{4,132},{5,133},{6,134},{7,135},{8... | collective-permute-start | bytes 98312 | tf_op jit(solution)/shard_map/ppermute | solution.py:98
  13.2 2.2 %collective-permute-done.1 = bf16[2,2,32,128]{3,2,1,0:T(8,128)(2,1)S(1)} collective-permute-done((bf16[2,2,32,128]{3,2,1,0:T(8,128)(2,1)S(1)}, bf16[2,2,32,128]{3,2,1,0:T(8,128)(2,1)S(1)}, u32[]{:S(2)}, u32[]{:S(2)}) %collective-permute-start.1) | collective-permute-done | bytes 32800 | tf_op jit(solution)/shard_map/ppermute | solution.py:98
  15.4 2.2 %collective-permute-start.2 = (bf16[2,2,2,32,128]{4,3,2,0,1:T(8,128)(2,1)S(1)}, bf16[2,2,2,32,128]{4,3,2,0,1:T(8,128)(2,1)S(1)}, u32[]{:S(2)}, u32[]{:S(2)}) collective-permute-start(bf16[2,2,2,32,128]{4,3,2,0,1:T(8,128)(2,1)S(1)} %pad_maximum_fusion.8), channel_id=1, source_target_pairs={{0,32},{1,33},{2,34},{3,35},{4,36},{5,37},{6,38},{7,39},{8,40},{9,... | collective-permute-start | bytes 196616 | tf_op jit(solution)/shard_map/ppermute | solution.py:98
  17.6 3.6 %collective-permute-done.2 = bf16[2,2,2,32,128]{4,3,2,0,1:T(8,128)(2,1)S(1)} collective-permute-done((bf16[2,2,2,32,128]{4,3,2,0,1:T(8,128)(2,1)S(1)}, bf16[2,2,2,32,128]{4,3,2,0,1:T(8,128)(2,1)S(1)}, u32[]{:S(2)}, u32[]{:S(2)}) %collective-permute-start.2) | collective-permute-done | bytes 65568 | tf_op jit(solution)/shard_map/ppermute | solution.py:98
  21.3 2.1 %collective-permute-start.3 = (bf16[2,2,2,2,32,128]{5,4,3,0,2,1:T(8,128)(2,1)S(1)}, bf16[2,2,2,2,32,128]{5,4,3,0,2,1:T(8,128)(2,1)S(1)}, u32[]{:S(2)}, u32[]{:S(2)}) collective-permute-start(bf16[2,2,2,2,32,128]{5,4,3,0,2,1:T(8,128)(2,1)S(1)} %pad_maximum_fusion.7), channel_id=1, source_target_pairs={{0,8},{1,9},{2,10},{3,11},{4,12},{5,13},{6,14},{7,15},{8,0},{9,1},... | collective-permute-start | bytes 393224 | tf_op jit(solution)/shard_map/ppermute | solution.py:98
  23.4 5.3 %collective-permute-done.3 = bf16[2,2,2,2,32,128]{5,4,3,0,2,1:T(8,128)(2,1)S(1)} collective-permute-done((bf16[2,2,2,2,32,128]{5,4,3,0,2,1:T(8,128)(2,1)S(1)}, bf16[2,2,2,2,32,128]{5,4,3,0,2,1:T(8,128)(2,1)S(1)}, u32[]{:S(2)}, u32[]{:S(2)}) %collective-permute-start.3) | collective-permute-done | bytes 131104 | tf_op jit(solution)/shard_map/ppermute | solution.py:98
  28.7 1.7 collective-permute-start.4
  30.4 4.8 %collective-permute-done.4 = bf16[2,2,2,2,2,32,128]{6,5,4,3,0,2,1:T(8,128)(2,1)S(1)} collective-permute-done((bf16[2,2,2,2,2,32,128]{6,5,4,3,0,2,1:T(8,128)(2,1)S(1)}, bf16[2,2,2,2,2,32,128]{6,5,4,3,0,2,1:T(8,128)(2,1)S(1)}, u32[]{:S(2)}, u32[]{:S(2)}) %collective-permute-start.4) | collective-permute-done | bytes 262176 | tf_op jit(solution)/shard_map/ppermute | solution.py:98
  36.5 8.0 %collective-permute-done.5 = bf16[2,2,2,2,2,2,16,128]{7,6,5,3,0,2,4,1:T(8,128)(2,1)S(1)} collective-permute-done((bf16[2,2,2,2,2,2,16,128]{7,6,5,3,0,2,4,1:T(8,128)(2,1)S(1)}, bf16[2,2,2,2,2,2,16,128]{7,6,5,3,0,2,4,1:T(8,128)(2,1)S(1)}, u32[]{:S(2)}, u32[]{:S(2)}) %collective-permute-start.5) | collective-permute-done | bytes 262176 | tf_op jit(solution)/shard_map/ppermute | solution.py:98
  46.8 7.1 %collective-permute-done.6 = bf16[2,2,2,2,2,2,2,16,128]{8,7,6,3,0,2,4,1,5:T(8,128)(2,1)S(1)} collective-permute-done((bf16[2,2,2,2,2,2,2,16,128]{8,7,6,3,0,2,4,1,5:T(8,128)(2,1)S(1)}, bf16[2,2,2,2,2,2,2,16,128]{8,7,6,3,0,2,4,1,5:T(8,128)(2,1)S(1)}, u32[]{:S(2)}, u32[]{:S(2)}) %collective-permute-start.6) | collective-permute-done | bytes 524320 | tf_op jit(solution)/shard_map/ppermute | solution.py:98
  59.1 1.4 select_bitcast_fusion.3
  61.7 1.4 select_bitcast_fusion.1
  63.2 44.7 %shard_map.37 = bf16[64,4,2,32,128]{4,3,2,1,0:T(8,128)(2,1)} custom-call(bf16[4,128,16,128]{3,2,1,0:T(8,128)(2,1)S(1)} %bitcast.127, bf16[4,128,16,128]{3,2,1,0:T(8,128)(2,1)S(1)} %bitcast.128, bf16[25,128,128]{2,1,0:T(8,128)(2,1)S(1)} %slice.20.fb_ref, bf16[25,128,128]{2,1,0:T(8,128)(2,1)S(1)} %slice.21.fa_ref), custom_call_target="tpu_custom_call" | custom-call | flops 26843545600 | bytes 10027008 | tf_op jit(solution)/shard_map/pallas_call | solution.py:60
  108.0 1.8 dynamic-slice_bitcast_fusion
  109.9 4.2 %collective-permute-done.11 = bf16[2,2,2,2,2,2,2,64,128]{8,7,6,5,4,3,2,1,0:T(8,128)(2,1)} collective-permute-done((bf16[2,2,2,2,2,2,2,64,128]{8,7,6,5,4,3,2,1,0:T(8,128)(2,1)S(1)}, bf16[2,2,2,2,2,2,2,64,128]{8,7,6,5,4,3,2,1,0:T(8,128)(2,1)}, u32[]{:S(2)}, u32[]{:S(2)}) %collective-permute-start.11) | collective-permute-done | bytes 2097184 | tf_op jit(solution)/shard_map/ppermute | solution.py:130
  114.2 3.2 %convert_add_fusion = f32[2,2,2,2,2,2,2,64,128]{8,7,6,5,4,3,2,1,0:T(8,128)S(1)} fusion(bf16[2,2,2,2,2,2,2,64,128]{8,7,6,5,4,3,2,1,0:T(8,128)(2,1)} %collective-permute-done.11, bf16[2,2,2,2,2,2,2,2,64,128]{9,8,7,6,5,4,3,2,1,0:T(8,128)(2,1)} %bitcast.130, s32[]{:T(128)S(6)} %select_n.221), kind=kLoop, calls=%fused_computation | loop fusion | flops 3145728 | bytes 8388612 | tf_op jit(solution)/shard_map/add | solution.py:132
  121.7 12.0 %collective-permute-done.14 = bf16[2,2,2,2,2,2,32,128]{7,6,5,4,3,2,1,0:T(8,128)(2,1)} collective-permute-done((bf16[2,2,2,2,2,2,32,128]{7,6,5,4,3,2,1,0:T(8,128)(2,1)S(1)}, bf16[2,2,2,2,2,2,32,128]{7,6,5,4,3,2,1,0:T(8,128)(2,1)}, u32[]{:S(2)}, u32[]{:S(2)}) %collective-permute-start.14) | collective-permute-done | bytes 524320 | tf_op jit(solution)/shard_map/ppermute | solution.py:130
  133.7 1.6 bitcast_add_fusion
  139.9 3.8 %collective-permute-done.15 = bf16[2,2,2,2,2,32,128]{6,5,4,3,2,1,0:T(8,128)(2,1)S(1)} collective-permute-done((bf16[2,2,2,2,2,32,128]{6,5,4,3,2,1,0:T(8,128)(2,1)}, bf16[2,2,2,2,2,32,128]{6,5,4,3,2,1,0:T(8,128)(2,1)S(1)}, u32[]{:S(2)}, u32[]{:S(2)}) %collective-permute-start.15) | collective-permute-done | bytes 262176 | tf_op jit(solution)/shard_map/ppermute | solution.py:130
  143.8 3.0 %collective-permute-done.13 = bf16[2,2,2,2,2,32,128]{6,5,4,3,2,1,0:T(8,128)(2,1)S(1)} collective-permute-done((bf16[2,2,2,2,2,32,128]{6,5,4,3,2,1,0:T(8,128)(2,1)S(1)}, bf16[2,2,2,2,2,32,128]{6,5,4,3,2,1,0:T(8,128)(2,1)S(1)}, u32[]{:S(2)}, u32[]{:S(2)}) %collective-permute-start.13) | collective-permute-done | bytes 262176 | tf_op jit(solution)/shard_map/ppermute | solution.py:130
  148.0 1.8 %collective-permute-start.16 = (bf16[2,2,2,2,64,128]{5,4,3,2,1,0:T(8,128)(2,1)S(1)}, bf16[2,2,2,2,64,128]{5,4,3,2,1,0:T(8,128)(2,1)S(1)}, u32[]{:S(2)}, u32[]{:S(2)}) collective-permute-start(bf16[2,2,2,2,64,128]{5,4,3,2,1,0:T(8,128)(2,1)S(1)} %fusion.11), channel_id=1, source_target_pairs={{0,64},{1,65},{2,66},{3,67},{4,68},{5,69},{6,70},{7,71},{8,72},{9,... | collective-permute-start | bytes 786440 | tf_op jit(solution)/shard_map/ppermute | solution.py:130
  149.8 4.8 %collective-permute-done.16 = bf16[2,2,2,2,64,128]{5,4,3,2,1,0:T(8,128)(2,1)S(1)} collective-permute-done((bf16[2,2,2,2,64,128]{5,4,3,2,1,0:T(8,128)(2,1)S(1)}, bf16[2,2,2,2,64,128]{5,4,3,2,1,0:T(8,128)(2,1)S(1)}, u32[]{:S(2)}, u32[]{:S(2)}) %collective-permute-start.16) | collective-permute-done | bytes 262176 | tf_op jit(solution)/shard_map/ppermute | solution.py:130
  154.8 2.5 %collective-permute-start.17 = (bf16[2,2,2,64,128]{4,3,2,1,0:T(8,128)(2,1)S(1)}, bf16[2,2,2,64,128]{4,3,2,1,0:T(8,128)(2,1)S(1)}, u32[]{:S(2)}, u32[]{:S(2)}) collective-permute-start(bf16[2,2,2,64,128]{4,3,2,1,0:T(8,128)(2,1)S(1)} %fusion.12), channel_id=1, source_target_pairs={{0,8},{1,9},{2,10},{3,11},{4,12},{5,13},{6,14},{7,15},{8,0},{9,1},... | collective-permute-start | bytes 393224 | tf_op jit(solution)/shard_map/ppermute | solution.py:130
  157.2 4.9 %collective-permute-done.17 = bf16[2,2,2,64,128]{4,3,2,1,0:T(8,128)(2,1)S(1)} collective-permute-done((bf16[2,2,2,64,128]{4,3,2,1,0:T(8,128)(2,1)S(1)}, bf16[2,2,2,64,128]{4,3,2,1,0:T(8,128)(2,1)S(1)}, u32[]{:S(2)}, u32[]{:S(2)}) %collective-permute-start.17) | collective-permute-done | bytes 131104 | tf_op jit(solution)/shard_map/ppermute | solution.py:130
  162.2 2.5 %collective-permute-start.18 = (bf16[2,2,64,128]{3,2,1,0:T(8,128)(2,1)S(1)}, bf16[2,2,64,128]{3,2,1,0:T(8,128)(2,1)S(1)}, u32[]{:S(2)}, u32[]{:S(2)}) collective-permute-start(bf16[2,2,64,128]{3,2,1,0:T(8,128)(2,1)S(1)} %fusion.13), channel_id=1, source_target_pairs={{0,32},{1,33},{2,34},{3,35},{4,36},{5,37},{6,38},{7,39},{8,40},{9,... | collective-permute-start | bytes 196616 | tf_op jit(solution)/shard_map/ppermute | solution.py:130
  164.6 3.4 %collective-permute-done.18 = bf16[2,2,64,128]{3,2,1,0:T(8,128)(2,1)S(1)} collective-permute-done((bf16[2,2,64,128]{3,2,1,0:T(8,128)(2,1)S(1)}, bf16[2,2,64,128]{3,2,1,0:T(8,128)(2,1)S(1)}, u32[]{:S(2)}, u32[]{:S(2)}) %collective-permute-start.18) | collective-permute-done | bytes 65568 | tf_op jit(solution)/shard_map/ppermute | solution.py:130
  168.1 3.4 %collective-permute-start.19 = (bf16[2,64,128]{2,1,0:T(8,128)(2,1)S(1)}, bf16[2,64,128]{2,1,0:T(8,128)(2,1)S(1)}, u32[]{:S(2)}, u32[]{:S(2)}) collective-permute-start(bf16[2,64,128]{2,1,0:T(8,128)(2,1)S(1)} %fusion.14), channel_id=1, source_target_pairs={{0,128},{1,129},{2,130},{3,131},{4,132},{5,133},{6,134},{7,135},{8... | collective-permute-start | bytes 98312 | tf_op jit(solution)/shard_map/ppermute | solution.py:130
  171.5 2.1 %collective-permute-done.19 = bf16[2,64,128]{2,1,0:T(8,128)(2,1)S(1)} collective-permute-done((bf16[2,64,128]{2,1,0:T(8,128)(2,1)S(1)}, bf16[2,64,128]{2,1,0:T(8,128)(2,1)S(1)}, u32[]{:S(2)}, u32[]{:S(2)}) %collective-permute-start.19) | collective-permute-done | bytes 32800 | tf_op jit(solution)/shard_map/ppermute | solution.py:130
  173.6 6.2 %collective-permute-start.20 = (bf16[64,128]{1,0:T(8,128)(2,1)S(1)}, bf16[64,128]{1,0:T(8,128)(2,1)S(1)}, u32[]{:S(2)}, u32[]{:S(2)}) collective-permute-start(bf16[64,128]{1,0:T(8,128)(2,1)S(1)} %fusion.16), channel_id=1, source_target_pairs={{0,16},{1,17},{2,18},{3,19},{4,20},{5,21},{6,22},{7,23},{8,24},{9,... | collective-permute-start | bytes 49160 | tf_op jit(solution)/shard_map/ppermute | solution.py:130
  179.8 1.7 collective-permute-done.20
  (76 shorter events, 22.2 us)
Async XLA Ops:
  0.0 0.8 copy-start
  0.9 9.0 %collective-permute-start = (bf16[2,32,128]{2,1,0:T(8,128)(2,1)S(1)}, bf16[2,32,128]{2,1,0:T(8,128)(2,1)S(1)}, u32[]{:S(2)}, u32[]{:S(2)}) collective-permute-start(bf16[2,32,128]{2,1,0:T(8,128)(2,1)S(1)} %bitcast.135), channel_id=1, source_target_pairs={{0,16},{1,17},{2,18},{3,19},{4,20},{5,21},{6,22},{7,23},{8,24},{9,... | collective-permute-start | bytes 49160 | tf_op jit(solution)/shard_map/ppermute | solution.py:98
  9.9 5.5 %collective-permute-start.1 = (bf16[2,2,32,128]{3,2,1,0:T(8,128)(2,1)S(1)}, bf16[2,2,32,128]{3,2,1,0:T(8,128)(2,1)S(1)}, u32[]{:S(2)}, u32[]{:S(2)}) collective-permute-start(bf16[2,2,32,128]{3,2,1,0:T(8,128)(2,1)S(1)} %pad_maximum_fusion.9), channel_id=1, source_target_pairs={{0,128},{1,129},{2,130},{3,131},{4,132},{5,133},{6,134},{7,135},{8... | collective-permute-start | bytes 98312 | tf_op jit(solution)/shard_map/ppermute | solution.py:98
  15.4 5.9 %collective-permute-start.2 = (bf16[2,2,2,32,128]{4,3,2,0,1:T(8,128)(2,1)S(1)}, bf16[2,2,2,32,128]{4,3,2,0,1:T(8,128)(2,1)S(1)}, u32[]{:S(2)}, u32[]{:S(2)}) collective-permute-start(bf16[2,2,2,32,128]{4,3,2,0,1:T(8,128)(2,1)S(1)} %pad_maximum_fusion.8), channel_id=1, source_target_pairs={{0,32},{1,33},{2,34},{3,35},{4,36},{5,37},{6,38},{7,39},{8,40},{9,... | collective-permute-start | bytes 196616 | tf_op jit(solution)/shard_map/ppermute | solution.py:98
  21.3 7.4 %collective-permute-start.3 = (bf16[2,2,2,2,32,128]{5,4,3,0,2,1:T(8,128)(2,1)S(1)}, bf16[2,2,2,2,32,128]{5,4,3,0,2,1:T(8,128)(2,1)S(1)}, u32[]{:S(2)}, u32[]{:S(2)}) collective-permute-start(bf16[2,2,2,2,32,128]{5,4,3,0,2,1:T(8,128)(2,1)S(1)} %pad_maximum_fusion.7), channel_id=1, source_target_pairs={{0,8},{1,9},{2,10},{3,11},{4,12},{5,13},{6,14},{7,15},{8,0},{9,1},... | collective-permute-start | bytes 393224 | tf_op jit(solution)/shard_map/ppermute | solution.py:98
  28.7 6.5 %collective-permute-start.4 = (bf16[2,2,2,2,2,32,128]{6,5,4,3,0,2,1:T(8,128)(2,1)S(1)}, bf16[2,2,2,2,2,32,128]{6,5,4,3,0,2,1:T(8,128)(2,1)S(1)}, u32[]{:S(2)}, u32[]{:S(2)}) collective-permute-start(bf16[2,2,2,2,2,32,128]{6,5,4,3,0,2,1:T(8,128)(2,1)S(1)} %pad_maximum_fusion.6), channel_id=1, source_target_pairs={{0,64},{1,65},{2,66},{3,67},{4,68},{5,69},{6,70},{7,71},{8,72},{9,... | collective-permute-start | bytes 786440 | tf_op jit(solution)/shard_map/ppermute | solution.py:98
  35.3 9.2 %collective-permute-start.5 = (bf16[2,2,2,2,2,2,16,128]{7,6,5,3,0,2,4,1:T(8,128)(2,1)S(1)}, bf16[2,2,2,2,2,2,16,128]{7,6,5,3,0,2,4,1:T(8,128)(2,1)S(1)}, u32[]{:S(2)}, u32[]{:S(2)}) collective-permute-start(bf16[2,2,2,2,2,2,16,128]{7,6,5,3,0,2,4,1:T(8,128)(2,1)S(1)} %get-tuple-element.18), channel_id=1, source_target_pairs={{0,4},{1,5},{2,6},{3,7},{4,0},{5,1},{6,2},{7,3},{8,12},{9,13},{10,... | collective-permute-start | bytes 786440 | tf_op jit(solution)/shard_map/ppermute | solution.py:98
  35.5 10.2 %collective-permute-start.8 = (bf16[2,2,2,2,2,2,16,128]{7,6,5,3,0,2,4,1:T(8,128)(2,1)S(1)}, bf16[2,2,2,2,2,2,16,128]{7,6,5,3,0,2,4,1:T(8,128)(2,1)S(1)}, u32[]{:S(2)}, u32[]{:S(2)}) collective-permute-start(bf16[2,2,2,2,2,2,16,128]{7,6,5,3,0,2,4,1:T(8,128)(2,1)S(1)} %get-tuple-element.17), channel_id=1, source_target_pairs={{0,2},{1,3},{2,0},{3,1},{4,6},{5,7},{6,4},{7,5},{8,10},{9,11},{10,... | collective-permute-start | bytes 786440 | tf_op jit(solution)/shard_map/ppermute | solution.py:98
  44.6 9.3 %collective-permute-start.6 = (bf16[2,2,2,2,2,2,2,16,128]{8,7,6,3,0,2,4,1,5:T(8,128)(2,1)S(1)}, bf16[2,2,2,2,2,2,2,16,128]{8,7,6,3,0,2,4,1,5:T(8,128)(2,1)S(1)}, u32[]{:S(2)}, u32[]{:S(2)}) collective-permute-start(bf16[2,2,2,2,2,2,2,16,128]{8,7,6,3,0,2,4,1,5:T(8,128)(2,1)S(1)} %pad_maximum_fusion.3), channel_id=1, source_target_pairs={{0,2},{1,3},{2,0},{3,1},{4,6},{5,7},{6,4},{7,5},{8,10},{9,11},{10,... | collective-permute-start | bytes 1572872 | tf_op jit(solution)/shard_map/ppermute | solution.py:98
  45.8 9.3 %collective-permute-start.9 = (bf16[2,2,2,2,2,2,2,16,128]{8,7,6,3,0,2,4,1,5:T(8,128)(2,1)S(1)}, bf16[2,2,2,2,2,2,2,16,128]{8,7,6,3,0,2,4,1,5:T(8,128)(2,1)S(1)}, u32[]{:S(2)}, u32[]{:S(2)}) collective-permute-start(bf16[2,2,2,2,2,2,2,16,128]{8,7,6,3,0,2,4,1,5:T(8,128)(2,1)S(1)} %pad_maximum_fusion.4), channel_id=1, source_target_pairs={{0,4},{1,5},{2,6},{3,7},{4,0},{5,1},{6,2},{7,3},{8,12},{9,13},{10,... | collective-permute-start | bytes 1572872 | tf_op jit(solution)/shard_map/ppermute | solution.py:98
  55.0 2.5 %copy-start.5 = (bf16[25,16384]{1,0:T(8,128)(2,1)S(1)}, bf16[25,16384]{1,0:T(8,128)(2,1)}, u32[]{:S(2)}) copy-start(bf16[25,16384]{1,0:T(8,128)(2,1)} %param.5) | copy-start | bytes 2457604
  55.0 4.0 %collective-permute-start.7 = (bf16[2,2,2,2,2,2,2,2,16,128]{9,8,7,6,3,0,2,4,1,5:T(8,128)(2,1)}, bf16[2,2,2,2,2,2,2,2,16,128]{9,8,7,6,3,0,2,4,1,5:T(8,128)(2,1)}, u32[]{:S(2)}, u32[]{:S(2)}) collective-permute-start(bf16[2,2,2,2,2,2,2,2,16,128]{9,8,7,6,3,0,2,4,1,5:T(8,128)(2,1)} %pad_maximum_fusion.1), channel_id=1, source_target_pairs={{0,1},{1,0},{2,3},{3,2},{4,5},{5,4},{6,7},{7,6},{8,9},{9,8},{10,11... | collective-permute-start | bytes 3145736 | tf_op jit(solution)/shard_map/ppermute | solution.py:98
  55.1 0.8 copy-start.2
  57.0 4.3 %collective-permute-start.10 = (bf16[2,2,2,2,2,2,2,2,16,128]{9,8,7,6,3,0,2,4,1,5:T(8,128)(2,1)}, bf16[2,2,2,2,2,2,2,2,16,128]{9,8,7,6,3,0,2,4,1,5:T(8,128)(2,1)}, u32[]{:S(2)}, u32[]{:S(2)}) collective-permute-start(bf16[2,2,2,2,2,2,2,2,16,128]{9,8,7,6,3,0,2,4,1,5:T(8,128)(2,1)} %pad_maximum_fusion.2), channel_id=1, source_target_pairs={{0,1},{1,0},{2,3},{3,2},{4,5},{5,4},{6,7},{7,6},{8,9},{9,8},{10,11... | collective-permute-start | bytes 3145736 | tf_op jit(solution)/shard_map/ppermute | solution.py:98
  57.5 1.2 copy-start.6
  60.6 1.0 copy-start.3
  109.8 4.4 %collective-permute-start.11 = (bf16[2,2,2,2,2,2,2,64,128]{8,7,6,5,4,3,2,1,0:T(8,128)(2,1)S(1)}, bf16[2,2,2,2,2,2,2,64,128]{8,7,6,5,4,3,2,1,0:T(8,128)(2,1)}, u32[]{:S(2)}, u32[]{:S(2)}) collective-permute-start(bf16[2,2,2,2,2,2,2,64,128]{8,7,6,5,4,3,2,1,0:T(8,128)(2,1)S(1)} %dynamic-slice_bitcast_fusion), channel_id=1, source_target_pairs={{0,1},{1,0},{2,3},{3,2},{4,5},{5,4},{6,7},{7,6},{8,9},{9,8},{10,11... | collective-permute-start | bytes 6291464 | tf_op jit(solution)/shard_map/ppermute | solution.py:130
  118.0 1.4 copy-start.1
  119.5 14.2 %collective-permute-start.14 = (bf16[2,2,2,2,2,2,32,128]{7,6,5,4,3,2,1,0:T(8,128)(2,1)S(1)}, bf16[2,2,2,2,2,2,32,128]{7,6,5,4,3,2,1,0:T(8,128)(2,1)}, u32[]{:S(2)}, u32[]{:S(2)}) collective-permute-start(bf16[2,2,2,2,2,2,32,128]{7,6,5,4,3,2,1,0:T(8,128)(2,1)S(1)} %fusion.1), channel_id=1, source_target_pairs={{0,4},{1,5},{2,6},{3,7},{4,0},{5,1},{6,2},{7,3},{8,12},{9,13},{10,... | collective-permute-start | bytes 1572872 | tf_op jit(solution)/shard_map/ppermute | solution.py:130
  121.1 15.9 %collective-permute-start.12 = (bf16[2,2,2,2,2,2,32,128]{7,6,4,3,2,1,0,5:T(8,128)(2,1)}, bf16[2,2,2,2,2,2,32,128]{7,6,4,3,2,1,0,5:T(8,128)(2,1)}, u32[]{:S(2)}, u32[]{:S(2)}) collective-permute-start(bf16[2,2,2,2,2,2,32,128]{7,6,4,3,2,1,0,5:T(8,128)(2,1)} %fusion.2), channel_id=1, source_target_pairs={{0,2},{1,3},{2,0},{3,1},{4,6},{5,7},{6,4},{7,5},{8,10},{9,11},{10,... | collective-permute-start | bytes 1572872 | tf_op jit(solution)/shard_map/ppermute | solution.py:130
  136.0 7.7 %collective-permute-start.15 = (bf16[2,2,2,2,2,32,128]{6,5,4,3,2,1,0:T(8,128)(2,1)}, bf16[2,2,2,2,2,32,128]{6,5,4,3,2,1,0:T(8,128)(2,1)S(1)}, u32[]{:S(2)}, u32[]{:S(2)}) collective-permute-start(bf16[2,2,2,2,2,32,128]{6,5,4,3,2,1,0:T(8,128)(2,1)} %fusion.9), channel_id=1, source_target_pairs={{0,2},{1,3},{2,0},{3,1},{4,6},{5,7},{6,4},{7,5},{8,10},{9,11},{10,... | collective-permute-start | bytes 786440 | tf_op jit(solution)/shard_map/ppermute | solution.py:130
  138.2 1.0 copy-start.4
  139.3 7.5 %collective-permute-start.13 = (bf16[2,2,2,2,2,32,128]{6,5,4,3,2,1,0:T(8,128)(2,1)S(1)}, bf16[2,2,2,2,2,32,128]{6,5,4,3,2,1,0:T(8,128)(2,1)S(1)}, u32[]{:S(2)}, u32[]{:S(2)}) collective-permute-start(bf16[2,2,2,2,2,32,128]{6,5,4,3,2,1,0:T(8,128)(2,1)S(1)} %fusion.8), channel_id=1, source_target_pairs={{0,4},{1,5},{2,6},{3,7},{4,0},{5,1},{6,2},{7,3},{8,12},{9,13},{10,... | collective-permute-start | bytes 786440 | tf_op jit(solution)/shard_map/ppermute | solution.py:130
  148.0 6.6 %collective-permute-start.16 = (bf16[2,2,2,2,64,128]{5,4,3,2,1,0:T(8,128)(2,1)S(1)}, bf16[2,2,2,2,64,128]{5,4,3,2,1,0:T(8,128)(2,1)S(1)}, u32[]{:S(2)}, u32[]{:S(2)}) collective-permute-start(bf16[2,2,2,2,64,128]{5,4,3,2,1,0:T(8,128)(2,1)S(1)} %fusion.11), channel_id=1, source_target_pairs={{0,64},{1,65},{2,66},{3,67},{4,68},{5,69},{6,70},{7,71},{8,72},{9,... | collective-permute-start | bytes 786440 | tf_op jit(solution)/shard_map/ppermute | solution.py:130
  154.8 7.4 %collective-permute-start.17 = (bf16[2,2,2,64,128]{4,3,2,1,0:T(8,128)(2,1)S(1)}, bf16[2,2,2,64,128]{4,3,2,1,0:T(8,128)(2,1)S(1)}, u32[]{:S(2)}, u32[]{:S(2)}) collective-permute-start(bf16[2,2,2,64,128]{4,3,2,1,0:T(8,128)(2,1)S(1)} %fusion.12), channel_id=1, source_target_pairs={{0,8},{1,9},{2,10},{3,11},{4,12},{5,13},{6,14},{7,15},{8,0},{9,1},... | collective-permute-start | bytes 393224 | tf_op jit(solution)/shard_map/ppermute | solution.py:130
  162.2 5.9 %collective-permute-start.18 = (bf16[2,2,64,128]{3,2,1,0:T(8,128)(2,1)S(1)}, bf16[2,2,64,128]{3,2,1,0:T(8,128)(2,1)S(1)}, u32[]{:S(2)}, u32[]{:S(2)}) collective-permute-start(bf16[2,2,64,128]{3,2,1,0:T(8,128)(2,1)S(1)} %fusion.13), channel_id=1, source_target_pairs={{0,32},{1,33},{2,34},{3,35},{4,36},{5,37},{6,38},{7,39},{8,40},{9,... | collective-permute-start | bytes 196616 | tf_op jit(solution)/shard_map/ppermute | solution.py:130
  168.1 5.5 %collective-permute-start.19 = (bf16[2,64,128]{2,1,0:T(8,128)(2,1)S(1)}, bf16[2,64,128]{2,1,0:T(8,128)(2,1)S(1)}, u32[]{:S(2)}, u32[]{:S(2)}) collective-permute-start(bf16[2,64,128]{2,1,0:T(8,128)(2,1)S(1)} %fusion.14), channel_id=1, source_target_pairs={{0,128},{1,129},{2,130},{3,131},{4,132},{5,133},{6,134},{7,135},{8... | collective-permute-start | bytes 98312 | tf_op jit(solution)/shard_map/ppermute | solution.py:130
  173.6 7.9 %collective-permute-start.20 = (bf16[64,128]{1,0:T(8,128)(2,1)S(1)}, bf16[64,128]{1,0:T(8,128)(2,1)S(1)}, u32[]{:S(2)}, u32[]{:S(2)}) collective-permute-start(bf16[64,128]{1,0:T(8,128)(2,1)S(1)} %fusion.16), channel_id=1, source_target_pairs={{0,16},{1,17},{2,18},{3,19},{4,20},{5,21},{6,22},{7,23},{8,24},{9,... | collective-permute-start | bytes 49160 | tf_op jit(solution)/shard_map/ppermute | solution.py:130

commit v13 on v12

--- a/solution.py
+++ b/solution.py
@@ -16,7 +16,7 @@
 SMALL_SEND = 0
 
 
-def ladder_kernel(n_p, n_aux, rpp, ta_ref, tb_ref, fb_ref, fa_ref, out_ref, w_ref, r_ref, l_ref):
+def ladder_kernel(n_p, n_aux, rpp, row_of, ta_ref, tb_ref, fb_ref, fa_ref, out_ref, w_ref, r_ref, l_ref):
     @pl.when(pl.program_id(0) == 0)
     def _():
         for p in range(n_p):
@@ -36,7 +36,7 @@
                 p = p0 + dp
                 for q in range(n_aux):
                     for i in range(I_BLOCK):
-                        r0 = (q * I_BLOCK + i) * hq
+                        r0 = row_of[h][q][i] * hq
                         w0 = p * C + q * cq + h * hq
                         w_ref[w0:w0 + hq, i * B:(i + 1) * B] = v[r0:r0 + hq, dp * B:(dp + 1) * B]
     y = jnp.dot(l_ref[...], w_ref[...], preferred_element_type=jnp.float32)
@@ -46,23 +46,45 @@
             out_ref[i // rpp, q, i % rpp] = y[q * apa:(q + 1) * apa, i * B:(i + 1) * B].astype(out_ref.dtype)
 
 
-def local_ladder(t_halves, factor_ca, factor_db, n_pair, n_aux):
+def local_ladder(t_halves, orders, factor_ca, factor_db, n_pair, n_aux):
     n_p = factor_ca.shape[0]
-    nij = t_halves[0].shape[1]
-    rpp = nij // n_pair
+    rpp = t_halves[0].shape[-3]
+    nij = n_pair * rpp
     apa = A // n_aux
+    aux_bits = n_aux.bit_length() - 1
+    pbits = (I_BLOCK // rpp).bit_length() - 1
+    in_chunk = set(range(aux_bits + pbits))
+
+    def row_index(order, q, i):
+        r = 0
+        for b in order:
+            if b in in_chunk:
+                v = (q >> b) & 1 if b < aux_bits else ((i // rpp) >> (b - aux_bits)) & 1
+                r = r * 2 + v
+        return r * rpp + i % rpp
+
+    row_of = [[[row_index(o, q, i) for i in range(I_BLOCK)] for q in range(n_aux)] for o in orders]
+
+    def t_spec(order):
+        shape = tuple(2 if b in in_chunk else 1 for b in order) + t_halves[0].shape[-3:]
+
+        def index(g):
+            bits = tuple(0 if b in in_chunk else (g >> (b - aux_bits - pbits)) & 1 for b in order)
+            return bits + (0, 0, 0)
+        return pl.BlockSpec(shape, index)
+
     r2 = factor_db.reshape(n_p, D, B)
     l2 = factor_ca.reshape(n_p, C, A)
     steps = nij // I_BLOCK
     pb = I_BLOCK // rpp
     flops = 4 * nij * C * D * n_p * B
-    kernel = functools.partial(ladder_kernel, n_p, n_aux, rpp)
+    kernel = functools.partial(ladder_kernel, n_p, n_aux, rpp, row_of)
     return pl.pallas_call(
         kernel,
         grid=(steps,),
         in_specs=[
-            pl.BlockSpec((n_aux, I_BLOCK, C // n_aux // 2, D), lambda g: (0, g, 0, 0)),
-            pl.BlockSpec((n_aux, I_BLOCK, C // n_aux // 2, D), lambda g: (0, g, 0, 0)),
+            t_spec(orders[0]),
+            t_spec(orders[1]),
             pl.BlockSpec((n_p, D, B), lambda g: (0, 0, 0)),
             pl.BlockSpec((n_p, C, A), lambda g: (0, 0, 0)),
         ],
@@ -116,8 +138,7 @@
         order = first + tail + last
         for k, b in enumerate(tail + last):
             part = gather_step(part, axes, n, me, b, len(first) + k)
-        perm = [order.index(b) for b in target]
-        halves.append(part.transpose(perm + list(range(n_bits, part.ndim))))
+        halves.append((part, order))
     return halves
 
 
@@ -170,8 +191,7 @@
     aux_bits = n_aux.bit_length() - 1
     target = list(range(aux_bits - 1, -1, -1)) + list(range(n_bits - 1, aux_bits - 1, -1))
     t_all = gather_bits(amps_q, both, n, last[::-1], [o[::-1] for o in pair_orders], first[::-1], target, 1)
-    t_halves = [t.reshape(n_aux, n_pair * rows, cq // 2, D) for t in t_all]
-    y = local_ladder(t_halves, factor_ca, factor_db, n_pair, n_aux)
+    y = local_ladder([t for t, _ in t_all], [o for _, o in t_all], factor_ca, factor_db, n_pair, n_aux)
     rpp = y.shape[2]
     y = y.reshape(n, rpp * y.shape[3], B)
     mine = reduce_bits(y, both, n, first, pair_orders, last).astype(jnp.bfloat16)

time: 183 us -> 183 us (level)
    another operation x21 -> x22, other arithmetic: 5.63 us -> 5.39 us  [gather_step(): return jnp.stack([lo, hi], axis=k)]
  transfers between devices with their start and end apart: 21 -> 21, of which waited for: 17 -> 17; matrix products, arithmetic and copies ran while one was open for 5% -> 6% of each run, Pallas kernels for 0% -> 0%
where the time goes in v13:
time: 183 us; the launch traced here: 182 us
  waiting for transfers between devices  72.6 us (40%)
  Pallas kernels  44.9 us (25%)
  starting transfers between devices  39.9 us (22%)
  other arithmetic  12.7 us (7%)
  local copies, waits for them, and re-layouts  11.9 us (7%)
    pallas_call x1, Pallas kernels, local_ladder(): pl.pallas_call(kernel, grid=(steps,), in_specs=[t_spec(orders[0]), t_spec...  44.9 us
    ppermute x10, waiting for transfers between devices, reduce_step(): recv = lax.ppermute(send.astype(wire), axes, xor_perm(n, b))  39.9 us
    ppermute x11, waiting for transfers between devices, gather_step(): recv = lax.ppermute(buf, axes, xor_perm(n, b))  32.8 us
    ppermute x11, starting transfers between devices, gather_step(): recv = lax.ppermute(buf, axes, xor_perm(n, b))  20.3 us
    ppermute x10, starting transfers between devices, reduce_step(): recv = lax.ppermute(send.astype(wire), axes, xor_perm(n, b))  19.6 us
    add x9, other arithmetic, reduce_step(): return keep.astype(jnp.float32) + recv.astype(jnp.float32)  7.31 us
    another operation x22, other arithmetic, gather_step(): return jnp.stack([lo, hi], axis=k)  5.39 us
    unnamed x18, local copies, waits for them, and re-layouts  4.99 us
  transfers between devices with their start and end apart: 21, of which 17 were waited for; matrix products, arithmetic and copies ran while one was open for 6% of the time, Pallas kernels for 0%

profile of v13, /device:TPU:2, one launch (start us, length us, event | category | flops | bytes accessed | tf_op | source)
XLA Modules:
  0.0 182.4 jit_solution(14843178745782011659)
XLA Ops:
  0.9 7.3 %collective-permute-start = (bf16[2,32,128]{2,1,0:T(8,128)(2,1)S(1)}, bf16[2,32,128]{2,1,0:T(8,128)(2,1)S(1)}, u32[]{:S(2)}, u32[]{:S(2)}) collective-permute-start(bf16[2,32,128]{2,1,0:T(8,128)(2,1)S(1)} %bitcast.127), channel_id=1, source_target_pairs={{0,16},{1,17},{2,18},{3,19},{4,20},{5,21},{6,22},{7,23},{8,24},{9,... | collective-permute-start | bytes 49160 | tf_op jit(solution)/shard_map/ppermute | solution.py:120
  8.1 1.7 collective-permute-done
  9.9 3.3 %collective-permute-start.1 = (bf16[2,2,32,128]{3,2,1,0:T(8,128)(2,1)S(1)}, bf16[2,2,32,128]{3,2,1,0:T(8,128)(2,1)S(1)}, u32[]{:S(2)}, u32[]{:S(2)}) collective-permute-start(bf16[2,2,32,128]{3,2,1,0:T(8,128)(2,1)S(1)} %pad_maximum_fusion.10), channel_id=1, source_target_pairs={{0,128},{1,129},{2,130},{3,131},{4,132},{5,133},{6,134},{7,135},{8... | collective-permute-start | bytes 98312 | tf_op jit(solution)/shard_map/ppermute | solution.py:120
  13.2 2.2 %collective-permute-done.1 = bf16[2,2,32,128]{3,2,1,0:T(8,128)(2,1)S(1)} collective-permute-done((bf16[2,2,32,128]{3,2,1,0:T(8,128)(2,1)S(1)}, bf16[2,2,32,128]{3,2,1,0:T(8,128)(2,1)S(1)}, u32[]{:S(2)}, u32[]{:S(2)}) %collective-permute-start.1) | collective-permute-done | bytes 32800 | tf_op jit(solution)/shard_map/ppermute | solution.py:120
  15.4 2.2 %collective-permute-start.2 = (bf16[2,2,2,32,128]{4,3,2,1,0:T(8,128)(2,1)S(1)}, bf16[2,2,2,32,128]{4,3,2,1,0:T(8,128)(2,1)S(1)}, u32[]{:S(2)}, u32[]{:S(2)}) collective-permute-start(bf16[2,2,2,32,128]{4,3,2,1,0:T(8,128)(2,1)S(1)} %pad_maximum_fusion.9), channel_id=1, source_target_pairs={{0,32},{1,33},{2,34},{3,35},{4,36},{5,37},{6,38},{7,39},{8,40},{9,... | collective-permute-start | bytes 196616 | tf_op jit(solution)/shard_map/ppermute | solution.py:120
  17.6 3.6 %collective-permute-done.2 = bf16[2,2,2,32,128]{4,3,2,1,0:T(8,128)(2,1)S(1)} collective-permute-done((bf16[2,2,2,32,128]{4,3,2,1,0:T(8,128)(2,1)S(1)}, bf16[2,2,2,32,128]{4,3,2,1,0:T(8,128)(2,1)S(1)}, u32[]{:S(2)}, u32[]{:S(2)}) %collective-permute-start.2) | collective-permute-done | bytes 65568 | tf_op jit(solution)/shard_map/ppermute | solution.py:120
  21.3 2.1 %collective-permute-start.3 = (bf16[2,2,2,2,32,128]{5,4,3,2,1,0:T(8,128)(2,1)S(1)}, bf16[2,2,2,2,32,128]{5,4,3,2,1,0:T(8,128)(2,1)S(1)}, u32[]{:S(2)}, u32[]{:S(2)}) collective-permute-start(bf16[2,2,2,2,32,128]{5,4,3,2,1,0:T(8,128)(2,1)S(1)} %pad_maximum_fusion.8), channel_id=1, source_target_pairs={{0,8},{1,9},{2,10},{3,11},{4,12},{5,13},{6,14},{7,15},{8,0},{9,1},... | collective-permute-start | bytes 393224 | tf_op jit(solution)/shard_map/ppermute | solution.py:120
  23.4 5.3 %collective-permute-done.3 = bf16[2,2,2,2,32,128]{5,4,3,2,1,0:T(8,128)(2,1)S(1)} collective-permute-done((bf16[2,2,2,2,32,128]{5,4,3,2,1,0:T(8,128)(2,1)S(1)}, bf16[2,2,2,2,32,128]{5,4,3,2,1,0:T(8,128)(2,1)S(1)}, u32[]{:S(2)}, u32[]{:S(2)}) %collective-permute-start.3) | collective-permute-done | bytes 131104 | tf_op jit(solution)/shard_map/ppermute | solution.py:120
  28.7 1.7 collective-permute-start.4
  30.4 4.8 %collective-permute-done.4 = bf16[2,2,2,2,2,32,128]{6,5,4,3,2,1,0:T(8,128)(2,1)S(1)} collective-permute-done((bf16[2,2,2,2,2,32,128]{6,5,4,3,2,1,0:T(8,128)(2,1)S(1)}, bf16[2,2,2,2,2,32,128]{6,5,4,3,2,1,0:T(8,128)(2,1)S(1)}, u32[]{:S(2)}, u32[]{:S(2)}) %collective-permute-start.4) | collective-permute-done | bytes 262176 | tf_op jit(solution)/shard_map/ppermute | solution.py:120
  36.5 8.0 %collective-permute-done.5 = bf16[2,2,2,2,2,2,16,128]{7,6,5,4,3,2,1,0:T(8,128)(2,1)S(1)} collective-permute-done((bf16[2,2,2,2,2,2,16,128]{7,6,5,4,3,2,1,0:T(8,128)(2,1)S(1)}, bf16[2,2,2,2,2,2,16,128]{7,6,5,4,3,2,1,0:T(8,128)(2,1)S(1)}, u32[]{:S(2)}, u32[]{:S(2)}) %collective-permute-start.5) | collective-permute-done | bytes 262176 | tf_op jit(solution)/shard_map/ppermute | solution.py:120
  46.8 7.0 %collective-permute-done.6 = bf16[2,2,2,2,2,2,2,16,128]{8,7,6,5,4,3,2,1,0:T(8,128)(2,1)S(1)} collective-permute-done((bf16[2,2,2,2,2,2,2,16,128]{8,7,6,5,4,3,2,1,0:T(8,128)(2,1)S(1)}, bf16[2,2,2,2,2,2,2,16,128]{8,7,6,5,4,3,2,1,0:T(8,128)(2,1)S(1)}, u32[]{:S(2)}, u32[]{:S(2)}) %collective-permute-start.6) | collective-permute-done | bytes 524320 | tf_op jit(solution)/shard_map/ppermute | solution.py:120
  58.5 1.4 select_bitcast_fusion.3
  61.1 2.0 %select_bitcast_fusion.1 = (bf16[2,2,2,2,2,2,2,1,2,16,128]{10,9,8,7,6,5,4,3,2,1,0:T(8,128)(2,1)S(1)}, bf16[2,2,2,2,2,2,2,1,2,16,128]{10,9,8,7,6,5,4,3,2,1,0:T(8,128)(2,1)S(1)}) fusion(bf16[2,2,2,2,2,2,2,2,16,128]{9,8,7,6,5,4,3,2,1,0:T(8,128)(2,1)} %collective-permute-done.10, pred[]{:T(512)S(6)} %eq.27, ...), kind=kLoop, calls=%fused_computation.16 | loop fusion | flops 1572864 | bytes 4194305 | tf_op jit(solution)/shard_map/stack | solution.py:124
  63.3 44.9 %shard_map.37 = bf16[64,4,2,32,128]{4,3,2,1,0:T(8,128)(2,1)} custom-call(bf16[2,2,2,2,2,2,2,2,2,16,128]{10,9,8,7,6,5,4,3,2,1,0:T(8,128)(2,1)S(1)} %copy.13.ta_ref, bf16[2,2,2,2,2,2,2,2,2,16,128]{10,9,8,7,6,5,4,3,2,1,0:T(8,128)(2,1)S(1)} %pad_maximum_fusion.1.tb_ref, bf16[25,128,128]{2,1,0:T(8,128)(2,1)S(1)} %slice.20.fb_ref, ...), custom_call_target="tpu_custom_call" | custom-call | flops 26843545600 | bytes 10027008 | tf_op jit(solution)/shard_map/pallas_call | solution.py:82
  108.2 1.8 dynamic-slice_bitcast_fusion
  110.3 4.2 %collective-permute-done.11 = bf16[2,2,2,2,2,2,2,64,128]{8,7,6,5,4,3,2,1,0:T(8,128)(2,1)} collective-permute-done((bf16[2,2,2,2,2,2,2,64,128]{8,7,6,5,4,3,2,1,0:T(8,128)(2,1)S(1)}, bf16[2,2,2,2,2,2,2,64,128]{8,7,6,5,4,3,2,1,0:T(8,128)(2,1)}, u32[]{:S(2)}, u32[]{:S(2)}) %collective-permute-start.11) | collective-permute-done | bytes 2097184 | tf_op jit(solution)/shard_map/ppermute | solution.py:151
  114.4 3.2 %convert_add_fusion = f32[2,2,2,2,2,2,2,64,128]{8,7,6,5,4,3,2,1,0:T(8,128)S(1)} fusion(bf16[2,2,2,2,2,2,2,64,128]{8,7,6,5,4,3,2,1,0:T(8,128)(2,1)} %collective-permute-done.11, bf16[2,2,2,2,2,2,2,2,64,128]{9,8,7,6,5,4,3,2,1,0:T(8,128)(2,1)} %bitcast.122, s32[]{:T(128)S(6)} %select_n.221), kind=kLoop, calls=%fused_computation | loop fusion | flops 3145728 | bytes 8388612 | tf_op jit(solution)/shard_map/add | solution.py:153
  121.9 12.0 %collective-permute-done.14 = bf16[2,2,2,2,2,2,32,128]{7,6,5,4,3,2,1,0:T(8,128)(2,1)} collective-permute-done((bf16[2,2,2,2,2,2,32,128]{7,6,5,4,3,2,1,0:T(8,128)(2,1)S(1)}, bf16[2,2,2,2,2,2,32,128]{7,6,5,4,3,2,1,0:T(8,128)(2,1)}, u32[]{:S(2)}, u32[]{:S(2)}) %collective-permute-start.14) | collective-permute-done | bytes 524320 | tf_op jit(solution)/shard_map/ppermute | solution.py:151
  133.9 1.6 bitcast_add_fusion
  140.2 3.8 %collective-permute-done.15 = bf16[2,2,2,2,2,32,128]{6,5,4,3,2,1,0:T(8,128)(2,1)S(1)} collective-permute-done((bf16[2,2,2,2,2,32,128]{6,5,4,3,2,1,0:T(8,128)(2,1)}, bf16[2,2,2,2,2,32,128]{6,5,4,3,2,1,0:T(8,128)(2,1)S(1)}, u32[]{:S(2)}, u32[]{:S(2)}) %collective-permute-start.15) | collective-permute-done | bytes 262176 | tf_op jit(solution)/shard_map/ppermute | solution.py:151
  144.0 3.0 %collective-permute-done.13 = bf16[2,2,2,2,2,32,128]{6,5,4,3,2,1,0:T(8,128)(2,1)S(1)} collective-permute-done((bf16[2,2,2,2,2,32,128]{6,5,4,3,2,1,0:T(8,128)(2,1)S(1)}, bf16[2,2,2,2,2,32,128]{6,5,4,3,2,1,0:T(8,128)(2,1)S(1)}, u32[]{:S(2)}, u32[]{:S(2)}) %collective-permute-start.13) | collective-permute-done | bytes 262176 | tf_op jit(solution)/shard_map/ppermute | solution.py:151
  148.2 1.8 %collective-permute-start.16 = (bf16[2,2,2,2,64,128]{5,4,3,2,1,0:T(8,128)(2,1)S(1)}, bf16[2,2,2,2,64,128]{5,4,3,2,1,0:T(8,128)(2,1)S(1)}, u32[]{:S(2)}, u32[]{:S(2)}) collective-permute-start(bf16[2,2,2,2,64,128]{5,4,3,2,1,0:T(8,128)(2,1)S(1)} %fusion.11), channel_id=1, source_target_pairs={{0,64},{1,65},{2,66},{3,67},{4,68},{5,69},{6,70},{7,71},{8,72},{9,... | collective-permute-start | bytes 786440 | tf_op jit(solution)/shard_map/ppermute | solution.py:151
  150.1 4.8 %collective-permute-done.16 = bf16[2,2,2,2,64,128]{5,4,3,2,1,0:T(8,128)(2,1)S(1)} collective-permute-done((bf16[2,2,2,2,64,128]{5,4,3,2,1,0:T(8,128)(2,1)S(1)}, bf16[2,2,2,2,64,128]{5,4,3,2,1,0:T(8,128)(2,1)S(1)}, u32[]{:S(2)}, u32[]{:S(2)}) %collective-permute-start.16) | collective-permute-done | bytes 262176 | tf_op jit(solution)/shard_map/ppermute | solution.py:151
  155.0 2.4 %collective-permute-start.17 = (bf16[2,2,2,64,128]{4,3,2,1,0:T(8,128)(2,1)S(1)}, bf16[2,2,2,64,128]{4,3,2,1,0:T(8,128)(2,1)S(1)}, u32[]{:S(2)}, u32[]{:S(2)}) collective-permute-start(bf16[2,2,2,64,128]{4,3,2,1,0:T(8,128)(2,1)S(1)} %fusion.12), channel_id=1, source_target_pairs={{0,8},{1,9},{2,10},{3,11},{4,12},{5,13},{6,14},{7,15},{8,0},{9,1},... | collective-permute-start | bytes 393224 | tf_op jit(solution)/shard_map/ppermute | solution.py:151
  157.5 4.9 %collective-permute-done.17 = bf16[2,2,2,64,128]{4,3,2,1,0:T(8,128)(2,1)S(1)} collective-permute-done((bf16[2,2,2,64,128]{4,3,2,1,0:T(8,128)(2,1)S(1)}, bf16[2,2,2,64,128]{4,3,2,1,0:T(8,128)(2,1)S(1)}, u32[]{:S(2)}, u32[]{:S(2)}) %collective-permute-start.17) | collective-permute-done | bytes 131104 | tf_op jit(solution)/shard_map/ppermute | solution.py:151
  162.4 2.5 %collective-permute-start.18 = (bf16[2,2,64,128]{3,2,1,0:T(8,128)(2,1)S(1)}, bf16[2,2,64,128]{3,2,1,0:T(8,128)(2,1)S(1)}, u32[]{:S(2)}, u32[]{:S(2)}) collective-permute-start(bf16[2,2,64,128]{3,2,1,0:T(8,128)(2,1)S(1)} %fusion.13), channel_id=1, source_target_pairs={{0,32},{1,33},{2,34},{3,35},{4,36},{5,37},{6,38},{7,39},{8,40},{9,... | collective-permute-start | bytes 196616 | tf_op jit(solution)/shard_map/ppermute | solution.py:151
  164.9 3.4 %collective-permute-done.18 = bf16[2,2,64,128]{3,2,1,0:T(8,128)(2,1)S(1)} collective-permute-done((bf16[2,2,64,128]{3,2,1,0:T(8,128)(2,1)S(1)}, bf16[2,2,64,128]{3,2,1,0:T(8,128)(2,1)S(1)}, u32[]{:S(2)}, u32[]{:S(2)}) %collective-permute-start.18) | collective-permute-done | bytes 65568 | tf_op jit(solution)/shard_map/ppermute | solution.py:151
  168.3 3.4 %collective-permute-start.19 = (bf16[2,64,128]{2,1,0:T(8,128)(2,1)S(1)}, bf16[2,64,128]{2,1,0:T(8,128)(2,1)S(1)}, u32[]{:S(2)}, u32[]{:S(2)}) collective-permute-start(bf16[2,64,128]{2,1,0:T(8,128)(2,1)S(1)} %fusion.14), channel_id=1, source_target_pairs={{0,128},{1,129},{2,130},{3,131},{4,132},{5,133},{6,134},{7,135},{8... | collective-permute-start | bytes 98312 | tf_op jit(solution)/shard_map/ppermute | solution.py:151
  171.8 2.1 %collective-permute-done.19 = bf16[2,64,128]{2,1,0:T(8,128)(2,1)S(1)} collective-permute-done((bf16[2,64,128]{2,1,0:T(8,128)(2,1)S(1)}, bf16[2,64,128]{2,1,0:T(8,128)(2,1)S(1)}, u32[]{:S(2)}, u32[]{:S(2)}) %collective-permute-start.19) | collective-permute-done | bytes 32800 | tf_op jit(solution)/shard_map/ppermute | solution.py:151
  173.9 6.2 %collective-permute-start.20 = (bf16[64,128]{1,0:T(8,128)(2,1)S(1)}, bf16[64,128]{1,0:T(8,128)(2,1)S(1)}, u32[]{:S(2)}, u32[]{:S(2)}) collective-permute-start(bf16[64,128]{1,0:T(8,128)(2,1)S(1)} %fusion.16), channel_id=1, source_target_pairs={{0,16},{1,17},{2,18},{3,19},{4,20},{5,21},{6,22},{7,23},{8,24},{9,... | collective-permute-start | bytes 49160 | tf_op jit(solution)/shard_map/ppermute | solution.py:151
  180.1 1.7 collective-permute-done.20
  (77 shorter events, 21.7 us)
Async XLA Ops:
  0.0 0.8 copy-start
  0.9 9.0 %collective-permute-start = (bf16[2,32,128]{2,1,0:T(8,128)(2,1)S(1)}, bf16[2,32,128]{2,1,0:T(8,128)(2,1)S(1)}, u32[]{:S(2)}, u32[]{:S(2)}) collective-permute-start(bf16[2,32,128]{2,1,0:T(8,128)(2,1)S(1)} %bitcast.127), channel_id=1, source_target_pairs={{0,16},{1,17},{2,18},{3,19},{4,20},{5,21},{6,22},{7,23},{8,24},{9,... | collective-permute-start | bytes 49160 | tf_op jit(solution)/shard_map/ppermute | solution.py:120
  9.9 5.5 %collective-permute-start.1 = (bf16[2,2,32,128]{3,2,1,0:T(8,128)(2,1)S(1)}, bf16[2,2,32,128]{3,2,1,0:T(8,128)(2,1)S(1)}, u32[]{:S(2)}, u32[]{:S(2)}) collective-permute-start(bf16[2,2,32,128]{3,2,1,0:T(8,128)(2,1)S(1)} %pad_maximum_fusion.10), channel_id=1, source_target_pairs={{0,128},{1,129},{2,130},{3,131},{4,132},{5,133},{6,134},{7,135},{8... | collective-permute-start | bytes 98312 | tf_op jit(solution)/shard_map/ppermute | solution.py:120
  15.4 5.9 %collective-permute-start.2 = (bf16[2,2,2,32,128]{4,3,2,1,0:T(8,128)(2,1)S(1)}, bf16[2,2,2,32,128]{4,3,2,1,0:T(8,128)(2,1)S(1)}, u32[]{:S(2)}, u32[]{:S(2)}) collective-permute-start(bf16[2,2,2,32,128]{4,3,2,1,0:T(8,128)(2,1)S(1)} %pad_maximum_fusion.9), channel_id=1, source_target_pairs={{0,32},{1,33},{2,34},{3,35},{4,36},{5,37},{6,38},{7,39},{8,40},{9,... | collective-permute-start | bytes 196616 | tf_op jit(solution)/shard_map/ppermute | solution.py:120
  21.3 7.4 %collective-permute-start.3 = (bf16[2,2,2,2,32,128]{5,4,3,2,1,0:T(8,128)(2,1)S(1)}, bf16[2,2,2,2,32,128]{5,4,3,2,1,0:T(8,128)(2,1)S(1)}, u32[]{:S(2)}, u32[]{:S(2)}) collective-permute-start(bf16[2,2,2,2,32,128]{5,4,3,2,1,0:T(8,128)(2,1)S(1)} %pad_maximum_fusion.8), channel_id=1, source_target_pairs={{0,8},{1,9},{2,10},{3,11},{4,12},{5,13},{6,14},{7,15},{8,0},{9,1},... | collective-permute-start | bytes 393224 | tf_op jit(solution)/shard_map/ppermute | solution.py:120
  28.7 6.5 %collective-permute-start.4 = (bf16[2,2,2,2,2,32,128]{6,5,4,3,2,1,0:T(8,128)(2,1)S(1)}, bf16[2,2,2,2,2,32,128]{6,5,4,3,2,1,0:T(8,128)(2,1)S(1)}, u32[]{:S(2)}, u32[]{:S(2)}) collective-permute-start(bf16[2,2,2,2,2,32,128]{6,5,4,3,2,1,0:T(8,128)(2,1)S(1)} %pad_maximum_fusion.7), channel_id=1, source_target_pairs={{0,64},{1,65},{2,66},{3,67},{4,68},{5,69},{6,70},{7,71},{8,72},{9,... | collective-permute-start | bytes 786440 | tf_op jit(solution)/shard_map/ppermute | solution.py:120
  35.3 9.2 %collective-permute-start.5 = (bf16[2,2,2,2,2,2,16,128]{7,6,5,4,3,2,1,0:T(8,128)(2,1)S(1)}, bf16[2,2,2,2,2,2,16,128]{7,6,5,4,3,2,1,0:T(8,128)(2,1)S(1)}, u32[]{:S(2)}, u32[]{:S(2)}) collective-permute-start(bf16[2,2,2,2,2,2,16,128]{7,6,5,4,3,2,1,0:T(8,128)(2,1)S(1)} %get-tuple-element.18), channel_id=1, source_target_pairs={{0,4},{1,5},{2,6},{3,7},{4,0},{5,1},{6,2},{7,3},{8,12},{9,13},{10,... | collective-permute-start | bytes 786440 | tf_op jit(solution)/shard_map/ppermute | solution.py:120
  35.5 10.2 %collective-permute-start.8 = (bf16[2,2,2,2,2,2,16,128]{7,6,5,4,3,2,1,0:T(8,128)(2,1)S(1)}, bf16[2,2,2,2,2,2,16,128]{7,6,5,4,3,2,1,0:T(8,128)(2,1)S(1)}, u32[]{:S(2)}, u32[]{:S(2)}) collective-permute-start(bf16[2,2,2,2,2,2,16,128]{7,6,5,4,3,2,1,0:T(8,128)(2,1)S(1)} %get-tuple-element.17), channel_id=1, source_target_pairs={{0,2},{1,3},{2,0},{3,1},{4,6},{5,7},{6,4},{7,5},{8,10},{9,11},{10,... | collective-permute-start | bytes 786440 | tf_op jit(solution)/shard_map/ppermute | solution.py:120
  44.6 9.3 %collective-permute-start.6 = (bf16[2,2,2,2,2,2,2,16,128]{8,7,6,5,4,3,2,1,0:T(8,128)(2,1)S(1)}, bf16[2,2,2,2,2,2,2,16,128]{8,7,6,5,4,3,2,1,0:T(8,128)(2,1)S(1)}, u32[]{:S(2)}, u32[]{:S(2)}) collective-permute-start(bf16[2,2,2,2,2,2,2,16,128]{8,7,6,5,4,3,2,1,0:T(8,128)(2,1)S(1)} %pad_maximum_fusion.4), channel_id=1, source_target_pairs={{0,2},{1,3},{2,0},{3,1},{4,6},{5,7},{6,4},{7,5},{8,10},{9,11},{10,... | collective-permute-start | bytes 1572872 | tf_op jit(solution)/shard_map/ppermute | solution.py:120
  45.8 9.3 %collective-permute-start.9 = (bf16[2,2,2,2,2,2,2,16,128]{8,7,6,4,3,2,1,0,5:T(8,128)(2,1)S(1)}, bf16[2,2,2,2,2,2,2,16,128]{8,7,6,4,3,2,1,0,5:T(8,128)(2,1)S(1)}, u32[]{:S(2)}, u32[]{:S(2)}) collective-permute-start(bf16[2,2,2,2,2,2,2,16,128]{8,7,6,4,3,2,1,0,5:T(8,128)(2,1)S(1)} %pad_maximum_fusion.5), channel_id=1, source_target_pairs={{0,4},{1,5},{2,6},{3,7},{4,0},{5,1},{6,2},{7,3},{8,12},{9,13},{10,... | collective-permute-start | bytes 1572872 | tf_op jit(solution)/shard_map/ppermute | solution.py:120
  55.0 3.5 %collective-permute-start.7 = (bf16[2,2,2,2,2,2,2,2,16,128]{9,8,7,6,5,4,3,2,1,0:T(8,128)(2,1)}, bf16[2,2,2,2,2,2,2,2,16,128]{9,8,7,6,5,4,3,2,1,0:T(8,128)(2,1)}, u32[]{:S(2)}, u32[]{:S(2)}) collective-permute-start(bf16[2,2,2,2,2,2,2,2,16,128]{9,8,7,6,5,4,3,2,1,0:T(8,128)(2,1)} %pad_maximum_fusion.2), channel_id=1, source_target_pairs={{0,1},{1,0},{2,3},{3,2},{4,5},{5,4},{6,7},{7,6},{8,9},{9,8},{10,11... | collective-permute-start | bytes 3145736 | tf_op jit(solution)/shard_map/ppermute | solution.py:120
  55.1 1.4 copy-start.2
  55.1 1.8 copy-start.5
  56.5 4.2 %collective-permute-start.10 = (bf16[2,2,2,2,2,2,2,2,16,128]{9,8,7,6,5,4,3,2,1,0:T(8,128)(2,1)}, bf16[2,2,2,2,2,2,2,2,16,128]{9,8,7,6,5,4,3,2,1,0:T(8,128)(2,1)}, u32[]{:S(2)}, u32[]{:S(2)}) collective-permute-start(bf16[2,2,2,2,2,2,2,2,16,128]{9,8,7,6,5,4,3,2,1,0:T(8,128)(2,1)} %copy.15), channel_id=1, source_target_pairs={{0,1},{1,0},{2,3},{3,2},{4,5},{5,4},{6,7},{7,6},{8,9},{9,8},{10,11... | collective-permute-start | bytes 3145736 | tf_op jit(solution)/shard_map/ppermute | solution.py:120
  57.0 1.2 copy-start.6
  60.1 1.0 copy-start.3
  110.0 4.4 %collective-permute-start.11 = (bf16[2,2,2,2,2,2,2,64,128]{8,7,6,5,4,3,2,1,0:T(8,128)(2,1)S(1)}, bf16[2,2,2,2,2,2,2,64,128]{8,7,6,5,4,3,2,1,0:T(8,128)(2,1)}, u32[]{:S(2)}, u32[]{:S(2)}) collective-permute-start(bf16[2,2,2,2,2,2,2,64,128]{8,7,6,5,4,3,2,1,0:T(8,128)(2,1)S(1)} %dynamic-slice_bitcast_fusion), channel_id=1, source_target_pairs={{0,1},{1,0},{2,3},{3,2},{4,5},{5,4},{6,7},{7,6},{8,9},{9,8},{10,11... | collective-permute-start | bytes 6291464 | tf_op jit(solution)/shard_map/ppermute | solution.py:151
  118.3 1.4 copy-start.1
  119.7 14.2 %collective-permute-start.14 = (bf16[2,2,2,2,2,2,32,128]{7,6,5,4,3,2,1,0:T(8,128)(2,1)S(1)}, bf16[2,2,2,2,2,2,32,128]{7,6,5,4,3,2,1,0:T(8,128)(2,1)}, u32[]{:S(2)}, u32[]{:S(2)}) collective-permute-start(bf16[2,2,2,2,2,2,32,128]{7,6,5,4,3,2,1,0:T(8,128)(2,1)S(1)} %fusion.1), channel_id=1, source_target_pairs={{0,4},{1,5},{2,6},{3,7},{4,0},{5,1},{6,2},{7,3},{8,12},{9,13},{10,... | collective-permute-start | bytes 1572872 | tf_op jit(solution)/shard_map/ppermute | solution.py:151
  121.4 15.9 %collective-permute-start.12 = (bf16[2,2,2,2,2,2,32,128]{7,6,4,3,2,1,0,5:T(8,128)(2,1)}, bf16[2,2,2,2,2,2,32,128]{7,6,4,3,2,1,0,5:T(8,128)(2,1)}, u32[]{:S(2)}, u32[]{:S(2)}) collective-permute-start(bf16[2,2,2,2,2,2,32,128]{7,6,4,3,2,1,0,5:T(8,128)(2,1)} %fusion.2), channel_id=1, source_target_pairs={{0,2},{1,3},{2,0},{3,1},{4,6},{5,7},{6,4},{7,5},{8,10},{9,11},{10,... | collective-permute-start | bytes 1572872 | tf_op jit(solution)/shard_map/ppermute | solution.py:151
  136.2 7.7 %collective-permute-start.15 = (bf16[2,2,2,2,2,32,128]{6,5,4,3,2,1,0:T(8,128)(2,1)}, bf16[2,2,2,2,2,32,128]{6,5,4,3,2,1,0:T(8,128)(2,1)S(1)}, u32[]{:S(2)}, u32[]{:S(2)}) collective-permute-start(bf16[2,2,2,2,2,32,128]{6,5,4,3,2,1,0:T(8,128)(2,1)} %fusion.9), channel_id=1, source_target_pairs={{0,2},{1,3},{2,0},{3,1},{4,6},{5,7},{6,4},{7,5},{8,10},{9,11},{10,... | collective-permute-start | bytes 786440 | tf_op jit(solution)/shard_map/ppermute | solution.py:151
  138.5 1.0 copy-start.4
  139.5 7.5 %collective-permute-start.13 = (bf16[2,2,2,2,2,32,128]{6,5,4,3,2,1,0:T(8,128)(2,1)S(1)}, bf16[2,2,2,2,2,32,128]{6,5,4,3,2,1,0:T(8,128)(2,1)S(1)}, u32[]{:S(2)}, u32[]{:S(2)}) collective-permute-start(bf16[2,2,2,2,2,32,128]{6,5,4,3,2,1,0:T(8,128)(2,1)S(1)} %fusion.8), channel_id=1, source_target_pairs={{0,4},{1,5},{2,6},{3,7},{4,0},{5,1},{6,2},{7,3},{8,12},{9,13},{10,... | collective-permute-start | bytes 786440 | tf_op jit(solution)/shard_map/ppermute | solution.py:151
  148.2 6.7 %collective-permute-start.16 = (bf16[2,2,2,2,64,128]{5,4,3,2,1,0:T(8,128)(2,1)S(1)}, bf16[2,2,2,2,64,128]{5,4,3,2,1,0:T(8,128)(2,1)S(1)}, u32[]{:S(2)}, u32[]{:S(2)}) collective-permute-start(bf16[2,2,2,2,64,128]{5,4,3,2,1,0:T(8,128)(2,1)S(1)} %fusion.11), channel_id=1, source_target_pairs={{0,64},{1,65},{2,66},{3,67},{4,68},{5,69},{6,70},{7,71},{8,72},{9,... | collective-permute-start | bytes 786440 | tf_op jit(solution)/shard_map/ppermute | solution.py:151
  155.0 7.4 %collective-permute-start.17 = (bf16[2,2,2,64,128]{4,3,2,1,0:T(8,128)(2,1)S(1)}, bf16[2,2,2,64,128]{4,3,2,1,0:T(8,128)(2,1)S(1)}, u32[]{:S(2)}, u32[]{:S(2)}) collective-permute-start(bf16[2,2,2,64,128]{4,3,2,1,0:T(8,128)(2,1)S(1)} %fusion.12), channel_id=1, source_target_pairs={{0,8},{1,9},{2,10},{3,11},{4,12},{5,13},{6,14},{7,15},{8,0},{9,1},... | collective-permute-start | bytes 393224 | tf_op jit(solution)/shard_map/ppermute | solution.py:151
  162.4 5.9 %collective-permute-start.18 = (bf16[2,2,64,128]{3,2,1,0:T(8,128)(2,1)S(1)}, bf16[2,2,64,128]{3,2,1,0:T(8,128)(2,1)S(1)}, u32[]{:S(2)}, u32[]{:S(2)}) collective-permute-start(bf16[2,2,64,128]{3,2,1,0:T(8,128)(2,1)S(1)} %fusion.13), channel_id=1, source_target_pairs={{0,32},{1,33},{2,34},{3,35},{4,36},{5,37},{6,38},{7,39},{8,40},{9,... | collective-permute-start | bytes 196616 | tf_op jit(solution)/shard_map/ppermute | solution.py:151
  168.3 5.5 %collective-permute-start.19 = (bf16[2,64,128]{2,1,0:T(8,128)(2,1)S(1)}, bf16[2,64,128]{2,1,0:T(8,128)(2,1)S(1)}, u32[]{:S(2)}, u32[]{:S(2)}) collective-permute-start(bf16[2,64,128]{2,1,0:T(8,128)(2,1)S(1)} %fusion.14), channel_id=1, source_target_pairs={{0,128},{1,129},{2,130},{3,131},{4,132},{5,133},{6,134},{7,135},{8... | collective-permute-start | bytes 98312 | tf_op jit(solution)/shard_map/ppermute | solution.py:151
  173.9 7.9 %collective-permute-start.20 = (bf16[64,128]{1,0:T(8,128)(2,1)S(1)}, bf16[64,128]{1,0:T(8,128)(2,1)S(1)}, u32[]{:S(2)}, u32[]{:S(2)}) collective-permute-start(bf16[64,128]{1,0:T(8,128)(2,1)S(1)} %fusion.16), channel_id=1, source_target_pairs={{0,16},{1,17},{2,18},{3,19},{4,20},{5,21},{6,22},{7,23},{8,24},{9,... | collective-permute-start | bytes 49160 | tf_op jit(solution)/shard_map/ppermute | solution.py:151
